TPU v7x, 512 devices: a whole 4x4x16 slice. The times are simulated.
512 devices in a mesh: lon: 32 (over z, x_hi), lat: 16 (over x_lo, y, core).
Axes of the slice: x: 4 (x_hi: 2, x_lo: 2; x = x_hi * 2 + x_lo), y: 4, z: 16, core: 2. Of those that a mesh axis runs over, the one named last changes fastest.
Arguments:
- elevation: float32 [12, 1536, 4096], P(None, 'lat', 'lon'), may hold values from -6 to 6
- equilibrium: float32 [12, 1536, 4096], P(None, 'lat', 'lon'), may hold values from -4 to 4
- transport_u: float32 [12, 1536, 4096], P(None, 'lat', 'lon'), may hold values from -4 to 4
- transport_v: float32 [12, 1536, 4096], P(None, 'lat', 'lon'), may hold values from -4 to 4
- ocean_depth: float32 [1536, 4096], P('lat', 'lon'), may hold values from 0.3 to 3
- bottom_drag: float32 [1536, 4096], P('lat', 'lon'), may hold values from 0.2 to 2
- wet_mask: int32 [1536, 4096], P('lat', 'lon'), may hold values 0 or 1
- lon_green: float32 [4096, 128], P('lon'), may hold values from -0.5 to 0.5
- lat_green: float32 [1536, 49152], P('lat', 'lon'), may hold values from -0.0546875 to 0.0546875
Outputs:
- elevation_next: float32 [12, 1536, 4096], P(None, 'lat', 'lon')
- transport_u_next: float32 [12, 1536, 4096], P(None, 'lat', 'lon')
- transport_v_next: float32 [12, 1536, 4096], P(None, 'lat', 'lon')
All inputs are finite; a program needn't handle non-finite values. No bound on the sum of `wet_mask` on one device may be relied on, other than what follows from the above.
Results may differ from a plain program's by a relative error of at most 0.0001.
Values sent between devices are 32-bit elements; how exact they have to be, the bound alone decides.
No kernel may reach another device: no remote copies, remote signals or barrier semaphores. Data moves between devices by JAX's collectives and lax.ppermute only.
A program may use at most 64 MiB of HBM per device.

v0:
```python
import math

import jax
import jax.numpy as jnp
from jax import lax
from jax.sharding import PartitionSpec as P

FREQS = [1.9323, 2.0, 1.896, 2.0055, 1.0027, 0.9295]
VISCOSITY = 0.5


def extended(array, sides, width, wrap):
    for axis, dim in sides:
        size, length = (lax.axis_size(axis), array.shape[dim])
        up = [(i, (i + 1) % size) for i in range(size if wrap else size - 1)]
        down = [(j, i) for i, j in up]
        last = lax.slice_in_dim(array, length - width, length, axis=dim)
        initial = lax.slice_in_dim(array, 0, width, axis=dim)
        before = lax.ppermute(last, axis, up)
        after = lax.ppermute(initial, axis, down)
        array = jnp.concatenate([before, array, after], axis=dim)
    return array


def row_terms(rows, nlat):
    angle = (-80.0 + 160.0 * (rows.astype(jnp.float32) + 0.5) / nlat) * (math.pi / 180.0)
    return ((1.0 / jnp.cos(angle))[:, None], (2.0 * jnp.sin(angle))[:, None])


def extend(stack, width):
    widened = extended(stack, (("lon", 2),), width, True)
    return extended(widened, (("lat", 1),), width, False)


def slopes(potential_ext, stretch):
    east_slope = (potential_ext[:, 1:-1, 2:] - potential_ext[:, 1:-1, :-2]) * 0.5 * stretch
    north_slope = (potential_ext[:, 2:, 1:-1] - potential_ext[:, :-2, 1:-1]) * 0.5
    return (east_slope, north_slope)


def solve_cells(push_u, push_v, drag_field, wet_frac, coriolis):
    damping = drag_field + 4.0 * VISCOSITY
    frequency = jnp.array(FREQS, jnp.float32)[:, None, None]
    det_real = damping * damping - frequency * frequency + coriolis * coriolis
    det_imag = 2.0 * damping * frequency
    magnitude = det_real * det_real + det_imag * det_imag

    def combine(first, second, factor):
        top_real = damping * first[:6] - frequency * first[6:] + factor * coriolis * second[:6]
        top_imag = damping * first[6:] + frequency * first[:6] + factor * coriolis * second[6:]
        out_real = (top_real * det_real + top_imag * det_imag) / magnitude
        out_imag = (top_imag * det_real - top_real * det_imag) / magnitude
        return wet_frac * jnp.concatenate([out_real, out_imag], axis=0)

    return jnp.concatenate([combine(push_u, push_v, 1.0), combine(push_v, push_u, -1.0)], axis=0)


def relax(flow_ext, east_slope, north_slope, depth_field, drag_field, wet_frac, coriolis):
    beside_all = (
        flow_ext[:, :-2, 1:-1]
        + flow_ext[:, 2:, 1:-1]
        + flow_ext[:, 1:-1, :-2]
        + flow_ext[:, 1:-1, 2:]
    )
    push_u = -depth_field * east_slope + VISCOSITY * beside_all[:12]
    push_v = -depth_field * north_slope + VISCOSITY * beside_all[12:]
    return solve_cells(push_u, push_v, drag_field, wet_frac, coriolis)


def surface(east_ext, north_ext, stretch, wet_frac):
    spread = (east_ext[:, :, 2:] - east_ext[:, :, :-2]) * 0.5 * stretch + (
        north_ext[:, 2:, :] - north_ext[:, :-2, :]
    ) * 0.5
    frequency = jnp.array(FREQS, jnp.float32)[:, None, None]
    return wet_frac * jnp.concatenate([-spread[6:] / frequency, spread[:6] / frequency], axis=0)


def per_device(
    elevation,
    equilibrium,
    transport_u,
    transport_v,
    ocean_depth,
    bottom_drag,
    wet_mask,
    lon_green,
    lat_green,
):
    rows_here = elevation.shape[1]
    total_rows = rows_here * lax.axis_size("lat")
    wet_frac = wet_mask.astype(jnp.float32)
    source = wet_frac * elevation
    mixed = jnp.einsum("krj,cj->krc", source, lon_green, precision=lax.Precision.HIGHEST)
    sal = jnp.einsum(
        "rs,ksc->krc",
        lat_green,
        lax.all_gather(mixed, "lat", axis=1, tiled=True),
        precision=lax.Precision.HIGHEST,
    )
    potential = elevation - equilibrium - sal
    first_row = lax.axis_index("lat") * rows_here
    stretch, coriolis = row_terms(first_row + jnp.arange(rows_here), total_rows)
    flows = jnp.concatenate([transport_u, transport_v], axis=0)
    widened = extend(jnp.concatenate([potential, flows], axis=0), 1)
    east_slope, north_slope = slopes(widened[:12], stretch)
    flows = relax(
        widened[12:], east_slope, north_slope, ocean_depth, bottom_drag, wet_frac, coriolis
    )
    flows = relax(
        extend(flows, 1), east_slope, north_slope, ocean_depth, bottom_drag, wet_frac, coriolis
    )
    around_all = extend(flows, 1)
    east_ext = around_all[:12, 1:-1, :]
    north_ext = around_all[12:, :, 1:-1]
    elevation_next = surface(east_ext, north_ext, stretch, wet_frac)
    return (elevation_next, flows[:12], flows[12:])


def solution(mesh):
    placed = (
        P(None, "lat", "lon"),
        P(None, "lat", "lon"),
        P(None, "lat", "lon"),
        P(None, "lat", "lon"),
        P("lat", "lon"),
        P("lat", "lon"),
        P("lat", "lon"),
        P("lon", None),
        P("lat", "lon"),
    )
    return jax.shard_map(
        per_device,
        mesh=mesh,
        in_specs=placed,
        out_specs=(P(None, "lat", "lon"), P(None, "lat", "lon"), P(None, "lat", "lon")),
        check_vma=False,
    )
```

profile of v0, /device:TPU:2, one launch (start us, length us, event | category | flops | bytes accessed | tf_op | source)
XLA Modules:
  0.0 202.3 jit_solution(10215366285293022981)
XLA Ops:
  7.3 0.9 convert_element_type.21
  8.2 0.6 copy-done.13
  8.8 2.5 %fusion.20 = f32[12,96,128]{2,1,0:T(8,128)} fusion(f32[12,96,128]{2,1,0:T(8,128)} %param.12, f32[96,128]{1,0:T(8,128)S(1)} %convert_element_type.21, f32[128,128]{1,0:T(8,128)} %param.19), kind=kOutput, calls=%fused_computation.86 | convolution fusion | flops 226639872 | bytes 1294336 | tf_op jit(solution)/shard_map/krj,cj->krc/dot_general | solution.py:93
  11.3 0.6 broadcast_multiply_fusion.2
  12.0 0.7 broadcast_multiply_fusion
  12.7 0.7 broadcast_add_fusion
  13.3 67.3 %all-gather.2.cloned.1.call-done = f32[12,1536,128]{2,1,0:T(8,128)} async-done(((f32[12,96,128]{2,1,0:T(8,128)}), f32[12,1536,128]{2,1,0:T(8,128)}) %all-gather.2.cloned.1.call-update) | async-done | bytes 9437200 | tf_op jit(solution)/shard_map/all_gather | solution.py:97
  80.6 8.3 %fusion = f32[12,96,128]{2,1,0:T(8,128)S(1)} fusion(f32[12,1536,128]{2,1,0:T(8,128)} %all-gather.2.cloned.1.call-done, f32[96,1536]{1,0:T(8,128)S(1)} %copy-done, f32[12,96,128]{2,1,0:T(8,128)S(1)} %copy-done.11, f32[12,96,128]{2,1,0:T(8,128)S(1)} %copy-done.21), kind=kOutput, calls=%fused_computation.11 | convolution fusion | flops 2718203904 | bytes 11796480 | tf_op jit(solution)/shard_map/rs,ksc->krc/dot_general | solution.py:94
  89.0 0.1 pad_maximum_fusion
  89.1 1.9 fusion.56
  91.0 2.6 %copy.15 = f32[36,96,1]{1,2,0:T(1,128)} copy(f32[36,96,1]{2,1,0:T(8,128)} %get-tuple-element.26) | data formatting | bytes 27648 | tf_op jit(solution)/shard_map/slice | solution.py:18
  93.6 7.5 %collective-permute-start = (f32[36,96,1]{1,2,0:T(1,128)}, f32[36,96,1]{1,2,0:T(1,128)}, u32[]{:S(2)}, u32[]{:S(2)}) collective-permute-start(f32[36,96,1]{1,2,0:T(1,128)} %copy.15), channel_id=1, source_target_pairs={{16,0},{32,16},{48,32},{64,48},{80,64},{96,80},{112,96},{128,112},... | collective-permute-start | bytes 41480 | tf_op jit(solution)/shard_map/ppermute | solution.py:20
  101.0 1.1 copy.17
  102.2 1.9 collective-permute-start.1
  104.2 1.3 copy.16
  105.5 6.3 %collective-permute-done.1 = f32[36,96,1]{1,2,0:T(1,128)} collective-permute-done((f32[36,96,1]{1,2,0:T(1,128)}, f32[36,96,1]{1,2,0:T(1,128)}, u32[]{:S(2)}, u32[]{:S(2)}) %collective-permute-start.1) | collective-permute-done | bytes 13856 | tf_op jit(solution)/shard_map/ppermute | solution.py:19
  111.8 2.5 %copy.18 = f32[36,96,1]{2,1,0:T(8,128)} copy(f32[36,96,1]{1,2,0:T(1,128)} %collective-permute-done.1) | data formatting | bytes 27648 | tf_op jit(solution)/shard_map/ppermute | solution.py:19
  114.3 1.4 pad_maximum_fusion.47
  115.7 1.9 collective-permute-start.2
  117.7 5.8 %collective-permute-start.3 = (f32[36,1,130]{2,1,0:T(1,128)S(1)}, f32[36,1,130]{2,1,0:T(1,128)S(1)}, u32[]{:S(2)}, u32[]{:S(2)}) collective-permute-start(f32[36,1,130]{2,1,0:T(1,128)S(1)} %get-tuple-element.20), channel_id=1, source_target_pairs={{1,0},{2,1},{3,2},{4,3},{5,4},{6,5},{7,6},{8,7},{9,8},{10,9},{11,1... | collective-permute-start | bytes 56168 | tf_op jit(solution)/shard_map/ppermute | solution.py:20
  123.5 1.5 collective-permute-done.3
  125.0 2.3 %fusion.4 = f32[24,96,128]{2,1,0:T(8,128)S(1)} fusion(f32[36,96,1]{2,1,0:T(8,128)S(1)} %copy.16, f32[12,96,128]{2,1,0:T(8,128)S(1)} %copy-done.2, f32[12,96,128]{2,1,0:T(8,128)S(1)} %copy-done.4, f32[12,96,128]{2,1,0:T(8,128)S(1)} %fusion, f32[36,96,1]{2,1,0:T(8,128)S(1)} %copy-done.1, f32[36,1,130]{2,1,0:T(1,128)S(1)} %collective-permute-done.3, ...), kind=kLoop, calls=%fused_computation.32 | loop fusion | flops 5603328 | bytes 3014208 | tf_op jit(solution)/shard_map/add | solution.py:60
  127.4 1.4 fusion.16
  128.8 1.3 fusion.13
  130.2 0.5 fusion.23
  130.7 0.2 fusion.26
  131.0 0.5 copy-done.14
  131.5 0.1 maximum_multiply_fusion
  131.6 0.4 slice_maximum_fusion.1
  132.0 0.4 copy-done.8
  132.4 0.4 copy.21
  132.8 1.9 collective-permute-start.4
  134.7 0.4 copy.22
  135.1 7.5 %collective-permute-start.5 = (f32[24,96,1]{1,0,2:T(8,128)S(1)}, f32[24,96,1]{1,0,2:T(8,128)}, u32[]{:S(2)}, u32[]{:S(2)}) collective-permute-start(f32[24,96,1]{1,0,2:T(8,128)S(1)} %copy.22), channel_id=1, source_target_pairs={{16,0},{32,16},{48,32},{64,48},{80,64},{96,80},{112,96},{128,112},... | collective-permute-start | bytes 27656 | tf_op jit(solution)/shard_map/ppermute | solution.py:20
  142.7 0.4 copy.23
  143.1 1.0 collective-permute-done.5
  144.0 1.1 copy.24
  145.2 1.1 pad_maximum_fusion.55
  146.3 1.9 collective-permute-start.6
  148.2 6.1 %collective-permute-start.7 = (f32[24,1,130]{2,1,0:T(1,128)S(1)}, f32[24,1,130]{2,1,0:T(1,128)S(1)}, u32[]{:S(2)}, u32[]{:S(2)}) collective-permute-start(f32[24,1,130]{2,1,0:T(1,128)S(1)} %get-tuple-element.24), channel_id=1, source_target_pairs={{1,0},{2,1},{3,2},{4,3},{5,4},{6,5},{7,6},{8,7},{9,8},{10,9},{11,1... | collective-permute-start | bytes 37448 | tf_op jit(solution)/shard_map/ppermute | solution.py:20
  154.3 1.3 collective-permute-done.7
  155.6 1.6 fusion.1
  157.4 0.1 fusion.11
  157.5 0.6 copy-done.18
  158.1 0.6 fusion.32
  158.7 0.2 fusion.36
  159.0 0.6 copy-done.15
  159.6 0.4 pad_maximum_fusion.1
  160.0 0.4 copy-done.6
  160.4 0.4 copy.27
  160.8 7.9 %collective-permute-start.8 = (f32[24,96,1]{1,0,2:T(8,128)S(1)}, f32[24,96,1]{1,0,2:T(8,128)S(1)}, u32[]{:S(2)}, u32[]{:S(2)}) collective-permute-start(f32[24,96,1]{1,0,2:T(8,128)S(1)} %copy.27), channel_id=1, source_target_pairs={{16,0},{32,16},{48,32},{64,48},{80,64},{96,80},{112,96},{128,112},... | collective-permute-start | bytes 27656 | tf_op jit(solution)/shard_map/ppermute | solution.py:20
  168.7 0.4 copy.29
  169.1 1.9 collective-permute-start.9
  171.0 0.4 copy.28
  171.5 6.9 %collective-permute-done.9 = f32[24,96,1]{1,0,2:T(8,128)} collective-permute-done((f32[24,96,1]{1,0,2:T(8,128)S(1)}, f32[24,96,1]{1,0,2:T(8,128)}, u32[]{:S(2)}, u32[]{:S(2)}) %collective-permute-start.9) | collective-permute-done | bytes 9248 | tf_op jit(solution)/shard_map/ppermute | solution.py:19
  178.4 1.1 copy.30
  179.6 1.1 pad_maximum_fusion.51
  180.7 4.9 %collective-permute-start.10 = (f32[24,1,130]{2,1,0:T(1,128)S(1)}, f32[24,1,130]{2,1,0:T(1,128)S(1)}, u32[]{:S(2)}, u32[]{:S(2)}) collective-permute-start(f32[24,1,130]{2,1,0:T(1,128)S(1)} %get-tuple-element.21), channel_id=1, source_target_pairs={{1,0},{2,1},{3,2},{4,3},{5,4},{6,5},{7,6},{8,7},{9,8},{10,9},{11,1... | collective-permute-start | bytes 37448 | tf_op jit(solution)/shard_map/ppermute | solution.py:20
  185.6 1.9 collective-permute-start.11
  187.5 5.3 %collective-permute-done.11 = f32[24,1,130]{2,1,0:T(1,128)S(1)} collective-permute-done((f32[24,1,130]{2,1,0:T(1,128)S(1)}, f32[24,1,130]{2,1,0:T(1,128)S(1)}, u32[]{:S(2)}, u32[]{:S(2)}) %collective-permute-start.11) | collective-permute-done | bytes 12512 | tf_op jit(solution)/shard_map/ppermute | solution.py:19
  192.9 0.9 fusion.8
  193.8 0.1 fusion.39
  193.9 0.7 copy-done.16
  194.6 0.9 maximum_multiply_fusion.4
  (84 shorter events, 0.5 us)
Async XLA Ops:
  7.2 73.4 %copy-start = (f32[96,1536]{1,0:T(8,128)S(1)}, f32[96,1536]{1,0:T(8,128)}, u32[]{:S(2)}) copy-start(f32[96,1536]{1,0:T(8,128)} %param.20) | copy-start | bytes 1769476
  7.2 73.4 %copy-start.11 = (f32[12,96,128]{2,1,0:T(8,128)S(1)}, f32[12,96,128]{2,1,0:T(8,128)}, u32[]{:S(2)}) copy-start(f32[12,96,128]{2,1,0:T(8,128)} %param.12) | copy-start | bytes 1769476
  7.2 4.8 %copy-start.26 = (f32[96,128]{1,0:T(8,128)S(1)}, f32[96,128]{1,0:T(8,128)}, u32[]{:S(2)}) copy-start(f32[96,128]{1,0:T(8,128)} %param.16) | copy-start | bytes 147460
  7.2 5.4 %copy-start.27 = (f32[96,128]{1,0:T(8,128)S(1)}, f32[96,128]{1,0:T(8,128)}, u32[]{:S(2)}) copy-start(f32[96,128]{1,0:T(8,128)} %param.17) | copy-start | bytes 147460
  7.2 73.4 %copy-start.21 = (f32[12,96,128]{2,1,0:T(8,128)S(1)}, f32[12,96,128]{2,1,0:T(8,128)}, u32[]{:S(2)}) copy-start(f32[12,96,128]{2,1,0:T(8,128)} %param.13) | copy-start | bytes 1769476
  7.2 73.4 %all-gather.2.cloned.1.call-start = ((), (), s32[]{:S(2)}) async-start(), calls=%async_computation | async-start | bytes 10027008 | tf_op jit(solution)/shard_map/all_gather | solution.py:97
  8.2 0.6 copy-start.13
  12.0 118.2 %copy-start.35 = (f32[96]{0:T(128)}, f32[96]{0:T(128)S(1)}, u32[]{:S(2)}) copy-start(f32[96]{0:T(128)S(1)} %get-tuple-element.54) | copy-start | bytes 1156
  13.3 75.6 %copy-start.2 = (f32[12,96,128]{2,1,0:T(8,128)S(1)}, f32[12,96,128]{2,1,0:T(8,128)}, u32[]{:S(2)}) copy-start(f32[12,96,128]{2,1,0:T(8,128)} %param.15) | copy-start | bytes 1769476
  13.3 75.6 %copy-start.3 = (f32[12,96,128]{2,1,0:T(8,128)S(1)}, f32[12,96,128]{2,1,0:T(8,128)}, u32[]{:S(2)}) copy-start(f32[12,96,128]{2,1,0:T(8,128)} %param.14) | copy-start | bytes 1769476
  93.6 10.6 %collective-permute-start = (f32[36,96,1]{1,2,0:T(1,128)}, f32[36,96,1]{1,2,0:T(1,128)}, u32[]{:S(2)}, u32[]{:S(2)}) collective-permute-start(f32[36,96,1]{1,2,0:T(1,128)} %copy.15), channel_id=1, source_target_pairs={{16,0},{32,16},{48,32},{64,48},{80,64},{96,80},{112,96},{128,112},... | collective-permute-start | bytes 41480 | tf_op jit(solution)/shard_map/ppermute | solution.py:20
  102.2 9.6 %collective-permute-start.1 = (f32[36,96,1]{1,2,0:T(1,128)}, f32[36,96,1]{1,2,0:T(1,128)}, u32[]{:S(2)}, u32[]{:S(2)}) collective-permute-start(f32[36,96,1]{1,2,0:T(1,128)} %copy.17), channel_id=1, source_target_pairs={{0,16},{16,32},{32,48},{48,64},{64,80},{80,96},{96,112},{112,128},... | collective-permute-start | bytes 41480 | tf_op jit(solution)/shard_map/ppermute | solution.py:19
  104.2 23.2 %copy-start.33 = (f32[96]{0:T(128)}, f32[96]{0:T(128)S(1)}, u32[]{:S(2)}) copy-start(f32[96]{0:T(128)S(1)} %divide_multiply_fusion) | copy-start | bytes 1156
  114.3 10.7 %copy-start.1 = (f32[36,96,1]{2,1,0:T(8,128)S(1)}, f32[36,96,1]{2,1,0:T(8,128)}, u32[]{:S(2)}) copy-start(f32[36,96,1]{2,1,0:T(8,128)} %copy.18) | copy-start | bytes 41476
  114.3 10.7 %copy-start.4 = (f32[12,96,128]{2,1,0:T(8,128)S(1)}, f32[12,96,128]{2,1,0:T(8,128)}, u32[]{:S(2)}) copy-start(f32[12,96,128]{2,1,0:T(8,128)} %param.14) | copy-start | bytes 1769476
  115.7 7.8 %collective-permute-start.2 = (f32[36,1,130]{2,1,0:T(1,128)S(1)}, f32[36,1,130]{2,1,0:T(1,128)S(1)}, u32[]{:S(2)}, u32[]{:S(2)}) collective-permute-start(f32[36,1,130]{2,1,0:T(1,128)S(1)} %get-tuple-element.19), channel_id=1, source_target_pairs={{0,1},{1,2},{2,3},{3,4},{4,5},{5,6},{6,7},{7,8},{8,9},{9,10},{10,1... | collective-permute-start | bytes 56168 | tf_op jit(solution)/shard_map/ppermute | solution.py:19
  117.7 7.4 %collective-permute-start.3 = (f32[36,1,130]{2,1,0:T(1,128)S(1)}, f32[36,1,130]{2,1,0:T(1,128)S(1)}, u32[]{:S(2)}, u32[]{:S(2)}) collective-permute-start(f32[36,1,130]{2,1,0:T(1,128)S(1)} %get-tuple-element.20), channel_id=1, source_target_pairs={{1,0},{2,1},{3,2},{4,3},{5,4},{6,5},{7,6},{8,7},{9,8},{10,9},{11,1... | collective-permute-start | bytes 56168 | tf_op jit(solution)/shard_map/ppermute | solution.py:20
  123.5 7.3 %copy-start.31 = (f32[96]{0:T(128)}, f32[96]{0:T(128)S(1)}, u32[]{:S(2)}) copy-start(f32[96]{0:T(128)S(1)} %fusion.52) | copy-start | bytes 1156
  123.5 3.9 %copy-start.25 = (f32[96,128]{1,0:T(8,128)S(1)}, f32[96,128]{1,0:T(8,128)}, u32[]{:S(2)}) copy-start(f32[96,128]{1,0:T(8,128)} %get-tuple-element.53) | copy-start | bytes 147460
  127.4 1.4 copy-start.24
  128.8 1.4 copy-start.17
  128.8 1.4 copy-start.19
  128.8 1.4 copy-start.22
  128.8 1.4 copy-start.28
  128.8 1.4 copy-start.29
  128.8 1.4 copy-start.37
  130.7 0.8 copy-start.14
  131.6 0.8 copy-start.8
  132.8 9.9 %collective-permute-start.4 = (f32[24,96,1]{1,0,2:T(8,128)S(1)}, f32[24,96,1]{1,0,2:T(8,128)S(1)}, u32[]{:S(2)}, u32[]{:S(2)}) collective-permute-start(f32[24,96,1]{1,0,2:T(8,128)S(1)} %copy.21), channel_id=1, source_target_pairs={{0,16},{16,32},{32,48},{48,64},{64,80},{80,96},{96,112},{112,128},... | collective-permute-start | bytes 27656 | tf_op jit(solution)/shard_map/ppermute | solution.py:19
  135.1 8.9 %collective-permute-start.5 = (f32[24,96,1]{1,0,2:T(8,128)S(1)}, f32[24,96,1]{1,0,2:T(8,128)}, u32[]{:S(2)}, u32[]{:S(2)}) collective-permute-start(f32[24,96,1]{1,0,2:T(8,128)S(1)} %copy.22), channel_id=1, source_target_pairs={{16,0},{32,16},{48,32},{64,48},{80,64},{96,80},{112,96},{128,112},... | collective-permute-start | bytes 27656 | tf_op jit(solution)/shard_map/ppermute | solution.py:20
  145.2 10.5 %copy-start.9 = (f32[12,96,128]{2,1,0:T(8,128)S(1)}, f32[12,96,128]{2,1,0:T(8,128)}, u32[]{:S(2)}) copy-start(f32[12,96,128]{2,1,0:T(8,128)} %copy-done.8) | copy-start | bytes 1769476
  146.3 8.0 %collective-permute-start.6 = (f32[24,1,130]{2,1,0:T(1,128)S(1)}, f32[24,1,130]{2,1,0:T(1,128)S(1)}, u32[]{:S(2)}, u32[]{:S(2)}) collective-permute-start(f32[24,1,130]{2,1,0:T(1,128)S(1)} %get-tuple-element.23), channel_id=1, source_target_pairs={{0,1},{1,2},{2,3},{3,4},{4,5},{5,6},{6,7},{7,8},{8,9},{9,10},{10,1... | collective-permute-start | bytes 37448 | tf_op jit(solution)/shard_map/ppermute | solution.py:19
  148.2 9.1 %copy-start.10 = (f32[12,96,128]{2,1,0:T(8,128)S(1)}, f32[12,96,128]{2,1,0:T(8,128)}, u32[]{:S(2)}) copy-start(f32[12,96,128]{2,1,0:T(8,128)} %get-tuple-element.16) | copy-start | bytes 1769476
  148.2 9.1 %copy-start.12 = (f32[12,96,128]{2,1,0:T(8,128)S(1)}, f32[12,96,128]{2,1,0:T(8,128)}, u32[]{:S(2)}) copy-start(f32[12,96,128]{2,1,0:T(8,128)} %get-tuple-element.18) | copy-start | bytes 1769476
  148.2 7.4 %collective-permute-start.7 = (f32[24,1,130]{2,1,0:T(1,128)S(1)}, f32[24,1,130]{2,1,0:T(1,128)S(1)}, u32[]{:S(2)}, u32[]{:S(2)}) collective-permute-start(f32[24,1,130]{2,1,0:T(1,128)S(1)} %get-tuple-element.24), channel_id=1, source_target_pairs={{1,0},{2,1},{3,2},{4,3},{5,4},{6,5},{7,6},{8,7},{9,8},{10,9},{11,1... | collective-permute-start | bytes 37448 | tf_op jit(solution)/shard_map/ppermute | solution.py:20
  157.3 0.8 copy-start.18
  157.3 0.8 copy-start.20
  157.3 0.8 copy-start.23
  157.3 0.8 copy-start.30
  157.3 0.8 copy-start.32
  157.3 0.8 copy-start.36
  157.3 0.8 copy-start.38
  158.7 0.8 copy-start.15
  159.6 0.8 copy-start.6
  159.6 33.3 %copy-start.5 = (f32[12,96,128]{2,1,0:T(8,128)}, f32[12,96,128]{2,1,0:T(8,128)S(1)}, u32[]{:S(2)}) copy-start(f32[12,96,128]{2,1,0:T(8,128)S(1)} %get-tuple-element.45) | copy-start | bytes 1769476
  160.8 10.2 %collective-permute-start.8 = (f32[24,96,1]{1,0,2:T(8,128)S(1)}, f32[24,96,1]{1,0,2:T(8,128)S(1)}, u32[]{:S(2)}, u32[]{:S(2)}) collective-permute-start(f32[24,96,1]{1,0,2:T(8,128)S(1)} %copy.27), channel_id=1, source_target_pairs={{16,0},{32,16},{48,32},{64,48},{80,64},{96,80},{112,96},{128,112},... | collective-permute-start | bytes 27656 | tf_op jit(solution)/shard_map/ppermute | solution.py:20
  169.1 9.3 %collective-permute-start.9 = (f32[24,96,1]{1,0,2:T(8,128)S(1)}, f32[24,96,1]{1,0,2:T(8,128)}, u32[]{:S(2)}, u32[]{:S(2)}) collective-permute-start(f32[24,96,1]{1,0,2:T(8,128)S(1)} %copy.29), channel_id=1, source_target_pairs={{0,16},{16,32},{32,48},{48,64},{64,80},{80,96},{96,112},{112,128},... | collective-permute-start | bytes 27656 | tf_op jit(solution)/shard_map/ppermute | solution.py:19
  179.5 13.3 %copy-start.7 = (f32[12,96,128]{2,1,0:T(8,128)S(1)}, f32[12,96,128]{2,1,0:T(8,128)}, u32[]{:S(2)}) copy-start(f32[12,96,128]{2,1,0:T(8,128)} %copy-done.6) | copy-start | bytes 1769476
  179.5 13.3 %copy-start.34 = (f32[96]{0:T(128)S(1)}, f32[96]{0:T(128)}, u32[]{:S(2)}) copy-start(f32[96]{0:T(128)} %copy-done.33) | copy-start | bytes 1156
  180.7 6.9 %collective-permute-start.10 = (f32[24,1,130]{2,1,0:T(1,128)S(1)}, f32[24,1,130]{2,1,0:T(1,128)S(1)}, u32[]{:S(2)}, u32[]{:S(2)}) collective-permute-start(f32[24,1,130]{2,1,0:T(1,128)S(1)} %get-tuple-element.21), channel_id=1, source_target_pairs={{1,0},{2,1},{3,2},{4,3},{5,4},{6,5},{7,6},{8,7},{9,8},{10,9},{11,1... | collective-permute-start | bytes 37448 | tf_op jit(solution)/shard_map/ppermute | solution.py:20
  185.6 8.2 %copy-start.39 = (f32[6]{0:T(128)S(1)}, f32[6]{0:T(128)}, u32[]{:S(2)}) copy-start(f32[6]{0:T(128)} %constant.32) | copy-start | bytes 76
  185.6 7.3 %collective-permute-start.11 = (f32[24,1,130]{2,1,0:T(1,128)S(1)}, f32[24,1,130]{2,1,0:T(1,128)S(1)}, u32[]{:S(2)}, u32[]{:S(2)}) collective-permute-start(f32[24,1,130]{2,1,0:T(1,128)S(1)} %get-tuple-element.22), channel_id=1, source_target_pairs={{0,1},{1,2},{2,3},{3,4},{4,5},{5,6},{6,7},{7,8},{8,9},{9,10},{10,1... | collective-permute-start | bytes 37448 | tf_op jit(solution)/shard_map/ppermute | solution.py:19
  193.8 0.8 copy-start.16
Sparse Core Ops, SparseCore 0:
  11.5 69.0 all-gather.1
where the time goes:
time: 203 us; the launch traced here: 202 us
  waiting for transfers between devices  89.7 us (44%)
  starting transfers between devices  51.2 us (25%)
  local copies, waits for them, and re-layouts  17.9 us (9%)
  other arithmetic  17.9 us (9%)
  between operations  14.7 us (7%)
  matrix products  10.9 us (5%)
    all_gather x1, waiting for transfers between devices, per_device(): lax.all_gather(mixed, 'lat', axis=1, tiled=True)  67.3 us
    ppermute x6, starting transfers between devices, extended(): after = lax.ppermute(initial, axis, down)  39.7 us
    ppermute x6, waiting for transfers between devices, extended(): before = lax.ppermute(last, axis, up)  18.6 us
    ppermute x6, starting transfers between devices, extended(): before = lax.ppermute(last, axis, up)  11.5 us
    dot_general x1, matrix products, per_device(): jnp.einsum('rs,ksc->krc', lat_green, lax.all_gather(mixed, 'lat', axis=1,...  8.35 us
  transfers between devices with their start and end apart: 13, of which 7 were waited for; matrix products, arithmetic and copies ran while one was open for 3% of the time, Pallas kernels for 0%

commit v1 on v0

v1 whole, which is shorter than its diff:
```python
import math

import jax
import jax.numpy as jnp
from jax import lax
from jax.sharding import Mesh
from jax.sharding import PartitionSpec as P

FREQS = [1.9323, 2.0, 1.896, 2.0055, 1.0027, 0.9295]
VISCOSITY = 0.5
HALO = 3
LAT = ("chip", "core")


def lat_index():
    return lax.axis_index("chip") * lax.axis_size("core") + lax.axis_index("core")


def lat_size():
    return lax.axis_size("chip") * lax.axis_size("core")


def widen_lon(array, width, dim):
    size, length = lax.axis_size("lon"), array.shape[dim]
    up = [(i, (i + 1) % size) for i in range(size)]
    down = [(j, i) for i, j in up]
    last = lax.slice_in_dim(array, length - width, length, axis=dim)
    initial = lax.slice_in_dim(array, 0, width, axis=dim)
    before = lax.ppermute(last, "lon", up)
    after = lax.ppermute(initial, "lon", down)
    return jnp.concatenate([before, array, after], axis=dim)


def widen_lat(array, width, dim):
    size, length = lat_size(), array.shape[dim]
    up = [(i, i + 1) for i in range(size - 1)]
    down = [(j, i) for i, j in up]
    last = lax.slice_in_dim(array, length - width, length, axis=dim)
    initial = lax.slice_in_dim(array, 0, width, axis=dim)
    before = lax.ppermute(last, LAT, up)
    after = lax.ppermute(initial, LAT, down)
    return jnp.concatenate([before, array, after], axis=dim)


def row_terms(rows, nlat):
    angle = (-80.0 + 160.0 * (rows.astype(jnp.float32) + 0.5) / nlat) * (math.pi / 180.0)
    return ((1.0 / jnp.cos(angle))[:, None], (2.0 * jnp.sin(angle))[:, None])


def slopes(potential_ext, stretch):
    east_slope = (potential_ext[:, 1:-1, 2:] - potential_ext[:, 1:-1, :-2]) * 0.5 * stretch
    north_slope = (potential_ext[:, 2:, 1:-1] - potential_ext[:, :-2, 1:-1]) * 0.5
    return (east_slope, north_slope)


def solve_cells(push_u, push_v, drag_field, wet_frac, coriolis):
    damping = drag_field + 4.0 * VISCOSITY
    frequency = jnp.array(FREQS, jnp.float32)[:, None, None]
    det_real = damping * damping - frequency * frequency + coriolis * coriolis
    det_imag = 2.0 * damping * frequency
    magnitude = det_real * det_real + det_imag * det_imag

    def combine(first, second, factor):
        top_real = damping * first[:6] - frequency * first[6:] + factor * coriolis * second[:6]
        top_imag = damping * first[6:] + frequency * first[:6] + factor * coriolis * second[6:]
        out_real = (top_real * det_real + top_imag * det_imag) / magnitude
        out_imag = (top_imag * det_real - top_real * det_imag) / magnitude
        return wet_frac * jnp.concatenate([out_real, out_imag], axis=0)

    return jnp.concatenate([combine(push_u, push_v, 1.0), combine(push_v, push_u, -1.0)], axis=0)


def inner(field, trim):
    return field[..., trim : field.shape[-2] - trim, trim : field.shape[-1] - trim]


def relax(flow_ext, east_slope, north_slope, depth_field, drag_field, wet_frac, coriolis):
    beside_all = (
        flow_ext[:, :-2, 1:-1]
        + flow_ext[:, 2:, 1:-1]
        + flow_ext[:, 1:-1, :-2]
        + flow_ext[:, 1:-1, 2:]
    )
    push_u = -depth_field * east_slope + VISCOSITY * beside_all[:12]
    push_v = -depth_field * north_slope + VISCOSITY * beside_all[12:]
    return solve_cells(push_u, push_v, drag_field, wet_frac, coriolis)


def surface(east_ext, north_ext, stretch, wet_frac):
    spread = (east_ext[:, :, 2:] - east_ext[:, :, :-2]) * 0.5 * stretch + (
        north_ext[:, 2:, :] - north_ext[:, :-2, :]
    ) * 0.5
    frequency = jnp.array(FREQS, jnp.float32)[:, None, None]
    return wet_frac * jnp.concatenate([-spread[6:] / frequency, spread[:6] / frequency], axis=0)


def per_device(
    elevation,
    equilibrium,
    transport_u,
    transport_v,
    ocean_depth,
    bottom_drag,
    wet_mask,
    lon_green,
    lat_green,
):
    rows_here = elevation.shape[1]
    total_rows = rows_here * lat_size()
    wet_frac = wet_mask.astype(jnp.float32)
    source = wet_frac * elevation
    mixed = jnp.einsum("krj,cj->krc", source, lon_green, precision=lax.Precision.HIGHEST)
    gathered = lax.all_gather(mixed, LAT, axis=1, tiled=True)

    fields = jnp.stack([ocean_depth, bottom_drag, wet_frac], axis=0)
    stack = jnp.concatenate([elevation - equilibrium, transport_u, transport_v, fields], axis=0)
    stack = widen_lat(widen_lon(stack, HALO, 2), HALO, 1)
    green_ext = widen_lat(lat_green, HALO, 0)

    sal = jnp.einsum("rs,ksc->krc", green_ext, gathered, precision=lax.Precision.HIGHEST)
    sal = widen_lon(sal, HALO, 2)
    potential = stack[:12] - sal
    flows = stack[12:36]
    depth_ext, drag_ext, wet_ext = stack[36], stack[37], stack[38]

    first_row = lat_index() * rows_here - HALO
    stretch, coriolis = row_terms(first_row + jnp.arange(rows_here + 2 * HALO), total_rows)
    east_slope, north_slope = slopes(potential, stretch[1:-1])
    flows = relax(
        flows,
        east_slope,
        north_slope,
        inner(depth_ext, 1),
        inner(drag_ext, 1),
        inner(wet_ext, 1),
        coriolis[1:-1],
    )
    flows = relax(
        flows,
        inner(east_slope, 1),
        inner(north_slope, 1),
        inner(depth_ext, 2),
        inner(drag_ext, 2),
        inner(wet_ext, 2),
        coriolis[2:-2],
    )
    east_ext = flows[:12, 1:-1, :]
    north_ext = flows[12:, :, 1:-1]
    elevation_next = surface(east_ext, north_ext, stretch[HALO:-HALO], wet_frac)
    flows = inner(flows, 1)
    return (elevation_next, flows[:12], flows[12:])


def solution(mesh):
    lat_devices = mesh.shape["lat"]
    cores = 2 if lat_devices % 2 == 0 else 1
    devices = mesh.devices.reshape(mesh.shape["lon"], lat_devices // cores, cores)
    split = Mesh(devices, ("lon", "chip", "core"))
    grid = P(None, LAT, "lon")
    plane = P(LAT, "lon")
    placed = (grid, grid, grid, grid, plane, plane, plane, P("lon", None), plane)
    return jax.shard_map(
        per_device,
        mesh=split,
        in_specs=placed,
        out_specs=(grid, grid, grid),
        check_vma=False,
    )
```

time: 203 us -> 140 us (0.69)
  the two profiles are of different devices: /device:TPU:2 before, /device:TPU:1 now
where the time goes in v1:
time: 140 us; the launch traced here: 139 us
  starting transfers between devices  39.6 us (28%)
  local copies, waits for them, and re-layouts  26.6 us (19%)
  other arithmetic  24.3 us (17%)
  waiting for transfers between devices  23.1 us (16%)
  between operations  14.6 us (10%)
  matrix products  11 us (8%)
    ppermute x2, starting transfers between devices, widen_lon(): after = lax.ppermute(initial, 'lon', down)  17.9 us
    ppermute x2, starting transfers between devices, widen_lat(): before = lax.ppermute(last, LAT, up)  9.56 us
    dot_general x1, matrix products, per_device(): jnp.einsum('rs,ksc->krc', green_ext, gathered, precision=lax.Precision.HI...  8.49 us
    all_gather x1, waiting for transfers between devices, per_device(): gathered = lax.all_gather(mixed, LAT, axis=1, tiled=True)  8.15 us
    ppermute x2, starting transfers between devices, widen_lat(): after = lax.ppermute(initial, LAT, down)  8.11 us
    slice x4, local copies, waits for them, and re-layouts, widen_lon(): last = lax.slice_in_dim(array, length - width, length, axis=dim)  8.02 us
    ppermute x2, waiting for transfers between devices, widen_lon(): before = lax.ppermute(last, 'lon', up)  7.03 us
    ppermute x2, waiting for transfers between devices, widen_lat(): after = lax.ppermute(initial, LAT, down)  5.05 us
  transfers between devices with their start and end apart: 9, of which 5 were waited for; matrix products, arithmetic and copies ran while one was open for 22% of the time, Pallas kernels for 0%

profile of v1, /device:TPU:1, one launch (start us, length us, event | category | flops | bytes accessed | tf_op | source)
XLA Modules:
  0.0 139.2 jit_solution(9656131435580839244)
XLA Ops:
  7.2 0.0 copy-start
  7.2 0.0 all-gather.2.cloned.1.call-start
  7.2 0.9 convert_element_type.6
  8.1 2.5 %fusion.47 = f32[12,96,128]{2,1,0:T(8,128)} fusion(f32[12,96,128]{2,1,0:T(8,128)} %param.12, f32[96,128]{1,0:T(8,128)S(1)} %convert_element_type.6, f32[128,128]{1,0:T(8,128)S(1)} %copy-done), kind=kOutput, calls=%fused_computation.96 | convolution fusion | flops 226639872 | bytes 1294336 | tf_op jit(solution)/shard_map/krj,cj->krc/dot_general | solution.py:112
  10.7 0.0 all-gather.2.cloned.1.call-update
  10.7 1.4 %fusion.59 = (f32[3,1536]{1,0:T(4,128)}, f32[3,1536]{1,0:T(4,128)S(1)}) fusion(f32[96,1536]{1,0:T(8,128)} %param.20), kind=kLoop, calls=%fused_computation.137 | loop fusion | bytes 73728 | tf_op jit(solution)/shard_map/slice | solution.py:38
  12.1 4.6 %collective-permute-start.4 = (f32[3,1536]{1,0:T(4,128)}, f32[3,1536]{1,0:T(4,128)}, u32[]{:S(2)}, u32[]{:S(2)}) collective-permute-start(f32[3,1536]{1,0:T(4,128)} %get-tuple-element.43), channel_id=1, source_target_pairs={{0,1},{1,2},{2,3},{3,4},{4,5},{5,6},{6,7},{7,8},{8,9},{9,10},{10,1... | collective-permute-start | bytes 55304 | tf_op jit(solution)/shard_map/ppermute | solution.py:40
  16.7 6.2 %collective-permute-start.5 = (f32[3,1536]{1,0:T(4,128)S(1)}, f32[3,1536]{1,0:T(4,128)}, u32[]{:S(2)}, u32[]{:S(2)}) collective-permute-start(f32[3,1536]{1,0:T(4,128)S(1)} %get-tuple-element.44), channel_id=1, source_target_pairs={{1,0},{2,1},{3,2},{4,3},{5,4},{6,5},{7,6},{8,7},{9,8},{10,9},{11,1... | collective-permute-start | bytes 55304 | tf_op jit(solution)/shard_map/ppermute | solution.py:41
  22.9 0.1 subtract_dynamic-update-slice_fusion
  23.1 1.1 constant_dynamic-update-slice_fusion.1
  24.3 2.6 %fusion.56 = (f32[39,96,3]{2,1,0:T(8,128)}, f32[39,96,3]{2,1,0:T(8,128)}) fusion(f32[39,96,128]{2,1,0:T(8,128)S(1)} %bitcast_dynamic-update-slice_fusion), kind=kLoop, calls=%fused_computation.134 | loop fusion | bytes 179712 | tf_op jit(solution)/shard_map/slice | solution.py:27
  27.0 2.1 %copy.16 = f32[39,96,3]{1,0,2:T(8,128)S(1)} copy(f32[39,96,3]{2,1,0:T(8,128)} %get-tuple-element.35) | data formatting | bytes 89856 | tf_op jit(solution)/shard_map/slice | solution.py:28
  29.1 9.4 %collective-permute-start.1 = (f32[39,96,3]{1,0,2:T(8,128)S(1)}, f32[39,96,3]{1,0,2:T(8,128)S(1)}, u32[]{:S(2)}, u32[]{:S(2)}) collective-permute-start(f32[39,96,3]{1,0,2:T(8,128)S(1)} %copy.16), channel_id=1, source_target_pairs={{16,0},{32,16},{48,32},{64,48},{80,64},{96,80},{112,96},{128,112},... | collective-permute-start | bytes 134792 | tf_op jit(solution)/shard_map/ppermute | solution.py:30
  38.6 2.2 %copy.15 = f32[39,96,3]{1,0,2:T(8,128)S(1)} copy(f32[39,96,3]{2,1,0:T(8,128)} %get-tuple-element.34) | data formatting | bytes 89856 | tf_op jit(solution)/shard_map/slice | solution.py:27
  40.7 1.9 %collective-permute-start = (f32[39,96,3]{1,0,2:T(8,128)S(1)}, f32[39,96,3]{1,0,2:T(8,128)S(1)}, u32[]{:S(2)}, u32[]{:S(2)}) collective-permute-start(f32[39,96,3]{1,0,2:T(8,128)S(1)} %copy.15), channel_id=1, source_target_pairs={{0,16},{16,32},{32,48},{48,64},{64,80},{80,96},{96,112},{112,128},... | collective-permute-start | bytes 134792 | tf_op jit(solution)/shard_map/ppermute | solution.py:29
  42.7 0.1 cosine_divide_fusion
  42.7 0.7 fusion.60
  43.4 0.7 broadcast_multiply_fusion.4
  44.1 0.6 slice_multiply_fusion.7
  44.7 4.7 %collective-permute-done = f32[39,96,3]{1,0,2:T(8,128)S(1)} collective-permute-done((f32[39,96,3]{1,0,2:T(8,128)S(1)}, f32[39,96,3]{1,0,2:T(8,128)S(1)}, u32[]{:S(2)}, u32[]{:S(2)}) %collective-permute-start) | collective-permute-done | bytes 44960 | tf_op jit(solution)/shard_map/ppermute | solution.py:29
  49.4 2.0 %copy.17 = f32[39,96,3]{2,1,0:T(8,128)} copy(f32[39,96,3]{1,0,2:T(8,128)S(1)} %collective-permute-done) | data formatting | bytes 89856 | tf_op jit(solution)/shard_map/ppermute | solution.py:29
  51.4 1.9 %copy.18 = f32[39,96,3]{2,1,0:T(8,128)} copy(f32[39,96,3]{1,0,2:T(8,128)S(1)} %collective-permute-done.1) | data formatting | bytes 89856 | tf_op jit(solution)/shard_map/ppermute | solution.py:30
  53.2 1.7 %pad_maximum_fusion.4 = (f32[39,3,134]{2,1,0:T(4,128)S(1)}, f32[39,3,134]{2,1,0:T(4,128)S(1)}) fusion(f32[39,96,3]{2,1,0:T(8,128)} %copy.18, f32[39,96,128]{2,1,0:T(8,128)S(1)} %bitcast_dynamic-update-slice_fusion, f32[39,96,3]{2,1,0:T(8,128)} %copy.17), kind=kLoop, calls=%fused_computation.105 | loop fusion | flops 62712 | bytes 2132208 | tf_op jit(solution)/shard_map/slice | solution.py:38
  54.9 5.0 %collective-permute-start.2 = (f32[39,3,134]{2,1,0:T(4,128)S(1)}, f32[39,3,134]{2,1,0:T(4,128)S(1)}, u32[]{:S(2)}, u32[]{:S(2)}) collective-permute-start(f32[39,3,134]{2,1,0:T(4,128)S(1)} %get-tuple-element.22), channel_id=1, source_target_pairs={{0,1},{1,2},{2,3},{3,4},{4,5},{5,6},{6,7},{7,8},{8,9},{9,10},{10,1... | collective-permute-start | bytes 188144 | tf_op jit(solution)/shard_map/ppermute | solution.py:40
  59.9 1.9 %collective-permute-start.3 = (f32[39,3,134]{2,1,0:T(4,128)S(1)}, f32[39,3,134]{2,1,0:T(4,128)S(1)}, u32[]{:S(2)}, u32[]{:S(2)}) collective-permute-start(f32[39,3,134]{2,1,0:T(4,128)S(1)} %get-tuple-element.23), channel_id=1, source_target_pairs={{1,0},{2,1},{3,2},{4,3},{5,4},{6,5},{7,6},{8,7},{9,8},{10,9},{11,1... | collective-permute-start | bytes 188144 | tf_op jit(solution)/shard_map/ppermute | solution.py:41
  61.8 0.6 slice_multiply_fusion.8
  62.4 2.9 %collective-permute-done.2 = f32[39,3,134]{2,1,0:T(4,128)S(1)} collective-permute-done((f32[39,3,134]{2,1,0:T(4,128)S(1)}, f32[39,3,134]{2,1,0:T(4,128)S(1)}, u32[]{:S(2)}, u32[]{:S(2)}) %collective-permute-start.2) | collective-permute-done | bytes 62744 | tf_op jit(solution)/shard_map/ppermute | solution.py:40
  65.2 5.0 %collective-permute-done.3 = f32[39,3,134]{2,1,0:T(4,128)S(1)} collective-permute-done((f32[39,3,134]{2,1,0:T(4,128)S(1)}, f32[39,3,134]{2,1,0:T(4,128)S(1)}, u32[]{:S(2)}, u32[]{:S(2)}) %collective-permute-start.3) | collective-permute-done | bytes 62744 | tf_op jit(solution)/shard_map/ppermute | solution.py:41
  70.3 0.8 maximum_bitcast_fusion.4
  71.1 1.7 %pad_maximum_fusion = f32[39,102,134]{2,1,0:T(8,128)S(1)} fusion(f32[39,3,134]{2,1,0:T(4,128)S(1)} %collective-permute-done.3, f32[39,96,3]{2,1,0:T(8,128)S(1)} %copy-done.3, f32[39,96,128]{2,1,0:T(8,128)S(1)} %bitcast_dynamic-update-slice_fusion, f32[39,96,3]{2,1,0:T(8,128)S(1)} %copy-done.2, f32[39,3,134]{2,1,0:T(4,128)S(1)} %collective-permute-done.2), kind=kLoop, calls=%fused_computation | loop fusion | flops 2132208 | bytes 4264416 | tf_op jit(solution)/shard_map/concatenate | solution.py:42
  72.8 0.9 slice_add_fusion.4
  73.8 2.1 %slice_add_fusion = f32[24,100,132]{2,1,0:T(8,128)S(1)} fusion(f32[39,102,134]{2,1,0:T(8,128)S(1)} %pad_maximum_fusion), kind=kLoop, calls=%fused_computation.14 | loop fusion | flops 950400 | bytes 6336000 | tf_op jit(solution)/shard_map/add | solution.py:79
  75.9 0.8 slice_add_fusion.3
  76.7 8.1 %all-gather.2.cloned.1.call-done = f32[12,1536,128]{2,1,0:T(8,128)} async-done(((f32[12,96,128]{2,1,0:T(8,128)}), f32[12,1536,128]{2,1,0:T(8,128)}) %all-gather.2.cloned.1.call-update) | async-done | bytes 9437200 | tf_op jit(solution)/shard_map/all_gather | solution.py:113
  84.8 8.5 %convolution_bitcast_fusion = f32[12,102,128]{2,1,0:T(8,128)S(1)} fusion(f32[12,1536,128]{2,1,0:T(8,128)} %all-gather.2.cloned.1.call-done, f32[3,1536]{1,0:T(4,128)} %collective-permute-done.5, f32[96,1536]{1,0:T(8,128)} %param.20, f32[3,1536]{1,0:T(4,128)} %collective-permute-done.4), kind=kOutput, calls=%fused_computation.46 | convolution fusion | flops 2888091648 | bytes 10690560 | tf_op jit(solution)/shard_map/rs,ksc->krc/dot_general | solution.py:120
  93.3 1.2 fusion.58
  94.6 2.0 %copy.19 = f32[12,102,3]{1,0,2:T(8,128)} copy(f32[12,102,3]{2,1,0:T(8,128)} %get-tuple-element.39) | data formatting | bytes 29376 | tf_op jit(solution)/shard_map/slice | solution.py:27
  96.6 1.4 copy.20
  97.9 8.5 %collective-permute-start.7 = (f32[12,102,3]{1,0,2:T(8,128)S(1)}, f32[12,102,3]{1,0,2:T(8,128)}, u32[]{:S(2)}, u32[]{:S(2)}) collective-permute-start(f32[12,102,3]{1,0,2:T(8,128)S(1)} %copy.20), channel_id=1, source_target_pairs={{16,0},{32,16},{48,32},{64,48},{80,64},{96,80},{112,96},{128,112},... | collective-permute-start | bytes 44072 | tf_op jit(solution)/shard_map/ppermute | solution.py:30
  106.4 2.1 %collective-permute-start.6 = (f32[12,102,3]{1,0,2:T(8,128)}, f32[12,102,3]{1,0,2:T(8,128)}, u32[]{:S(2)}, u32[]{:S(2)}) collective-permute-start(f32[12,102,3]{1,0,2:T(8,128)} %copy.19), channel_id=1, source_target_pairs={{0,16},{16,32},{32,48},{48,64},{64,80},{80,96},{96,112},{112,128},... | collective-permute-start | bytes 44072 | tf_op jit(solution)/shard_map/ppermute | solution.py:29
  108.5 0.8 slice_negate_fusion.1
  109.3 1.6 %slice.271 = f32[100,132]{1,0:T(8,128)} slice(f32[102,134]{1,0:T(8,128)} %get-tuple-element.19), slice={[1:101], [1:133]} | slice | bytes 105600 | tf_op jit(solution)/shard_map/slice | solution.py:74
  110.9 1.6 %slice.262 = f32[98,130]{1,0:T(8,128)} slice(f32[102,134]{1,0:T(8,128)} %get-tuple-element.19), slice={[2:100], [2:132]} | slice | bytes 101920 | tf_op jit(solution)/shard_map/slice | solution.py:74
  112.6 2.3 %collective-permute-done.6 = f32[12,102,3]{1,0,2:T(8,128)} collective-permute-done((f32[12,102,3]{1,0,2:T(8,128)}, f32[12,102,3]{1,0,2:T(8,128)}, u32[]{:S(2)}, u32[]{:S(2)}) %collective-permute-start.6) | collective-permute-done | bytes 14720 | tf_op jit(solution)/shard_map/ppermute | solution.py:29
  114.9 1.9 %copy.21 = f32[12,102,3]{2,1,0:T(8,128)} copy(f32[12,102,3]{1,0,2:T(8,128)} %collective-permute-done.6) | data formatting | bytes 29376 | tf_op jit(solution)/shard_map/ppermute | solution.py:29
  116.8 1.9 %copy.22 = f32[12,102,3]{2,1,0:T(8,128)} copy(f32[12,102,3]{1,0,2:T(8,128)} %collective-permute-done.7) | data formatting | bytes 29376 | tf_op jit(solution)/shard_map/ppermute | solution.py:30
  118.6 2.3 %slice_subtract_fusion.2 = f32[12,102,134]{2,1,0:T(8,128)S(1)} fusion(f32[39,102,134]{2,1,0:T(8,128)} %copy-done.1, f32[12,102,3]{2,1,0:T(8,128)} %copy.22, f32[12,102,128]{2,1,0:T(8,128)S(1)} %convolution_bitcast_fusion, f32[12,102,3]{2,1,0:T(8,128)} %copy.21), kind=kLoop, calls=%fused_computation.41 | loop fusion | flops 492048 | bytes 1968192 | tf_op jit(solution)/shard_map/sub | solution.py:122
  121.0 1.1 fusion.10
  122.2 0.8 fusion.18
  123.0 0.4 fusion.20
  123.4 0.5 copy-done.15
  123.9 0.2 maximum_multiply_fusion.1
  124.1 2.1 %fusion.2 = f32[24,98,130]{2,1,0:T(8,128)S(1)} fusion(f32[12,100,132]{2,1,0:T(8,128)S(1)} %get-tuple-element.55, f32[12,100,132]{2,1,0:T(8,128)S(1)} %get-tuple-element.54), kind=kLoop, calls=%fused_computation.9 | loop fusion | flops 2140320 | bytes 2490240 | tf_op jit(solution)/shard_map/add | solution.py:79
  126.2 0.8 fusion.6
  127.0 0.0 copy-done.5
  127.1 0.1 copy-done.13
  127.1 0.8 fusion.22
  128.0 0.4 fusion.25
  128.4 0.5 copy-done.14
  128.9 0.2 maximum_multiply_fusion.2
  129.1 0.5 copy-done.27
  129.5 1.8 %fusion.57 = (f32[12,96,128]{2,1,0:T(8,128)}, f32[12,96,128]{2,1,0:T(8,128)S(1)}, f32[12,96,128]{2,1,0:T(8,128)}) fusion(f32[12,98,130]{2,1,0:T(8,128)S(1)} %get-tuple-element.50, f32[96]{0:T(128)S(1)} %copy-done.27, f32[12,98,130]{2,1,0:T(8,128)S(1)} %get-tuple-element.49), kind=kLoop, calls=%fused_computation.135 | loop fusion | flops 737280 | bytes 5308800 | tf_op jit(solution)/shard_map/slice | solution.py:151
  131.4 0.1 fusion.49
  131.5 0.9 maximum_multiply_fusion.4
  (61 shorter events, 0.2 us)
Async XLA Ops:
  7.2 1.0 copy-start
  7.2 15.7 %copy-start.4 = (f32[12,96,128]{2,1,0:T(8,128)S(1)}, f32[12,96,128]{2,1,0:T(8,128)}, u32[]{:S(2)}) copy-start(f32[12,96,128]{2,1,0:T(8,128)} %param.12) | copy-start | bytes 1769476
  7.2 15.7 %copy-start.8 = (f32[12,96,128]{2,1,0:T(8,128)S(1)}, f32[12,96,128]{2,1,0:T(8,128)}, u32[]{:S(2)}) copy-start(f32[12,96,128]{2,1,0:T(8,128)} %param.13) | copy-start | bytes 1769476
  7.2 77.6 %all-gather.2.cloned.1.call-start = ((), (), s32[]{:S(2)}) async-start(), calls=%async_computation | async-start | bytes 10027008 | tf_op jit(solution)/shard_map/all_gather | solution.py:113
  12.1 64.6 %collective-permute-start.4 = (f32[3,1536]{1,0:T(4,128)}, f32[3,1536]{1,0:T(4,128)}, u32[]{:S(2)}, u32[]{:S(2)}) collective-permute-start(f32[3,1536]{1,0:T(4,128)} %get-tuple-element.43), channel_id=1, source_target_pairs={{0,1},{1,2},{2,3},{3,4},{4,5},{5,6},{6,7},{7,8},{8,9},{9,10},{10,1... | collective-permute-start | bytes 55304 | tf_op jit(solution)/shard_map/ppermute | solution.py:40
  16.7 7.5 %copy-start.9 = (f32[12,96,128]{2,1,0:T(8,128)S(1)}, f32[12,96,128]{2,1,0:T(8,128)}, u32[]{:S(2)}) copy-start(f32[12,96,128]{2,1,0:T(8,128)} %param.15) | copy-start | bytes 1769476
  16.7 60.0 %collective-permute-start.5 = (f32[3,1536]{1,0:T(4,128)S(1)}, f32[3,1536]{1,0:T(4,128)}, u32[]{:S(2)}, u32[]{:S(2)}) collective-permute-start(f32[3,1536]{1,0:T(4,128)S(1)} %get-tuple-element.44), channel_id=1, source_target_pairs={{1,0},{2,1},{3,2},{4,3},{5,4},{6,5},{7,6},{8,7},{9,8},{10,9},{11,1... | collective-permute-start | bytes 55304 | tf_op jit(solution)/shard_map/ppermute | solution.py:41
  23.0 1.2 copy-start.18
  23.0 1.3 copy-start.19
  23.0 1.3 copy-start.17
  29.1 22.3 %collective-permute-start.1 = (f32[39,96,3]{1,0,2:T(8,128)S(1)}, f32[39,96,3]{1,0,2:T(8,128)S(1)}, u32[]{:S(2)}, u32[]{:S(2)}) collective-permute-start(f32[39,96,3]{1,0,2:T(8,128)S(1)} %copy.16), channel_id=1, source_target_pairs={{16,0},{32,16},{48,32},{64,48},{80,64},{96,80},{112,96},{128,112},... | collective-permute-start | bytes 134792 | tf_op jit(solution)/shard_map/ppermute | solution.py:30
  40.7 8.7 %collective-permute-start = (f32[39,96,3]{1,0,2:T(8,128)S(1)}, f32[39,96,3]{1,0,2:T(8,128)S(1)}, u32[]{:S(2)}, u32[]{:S(2)}) collective-permute-start(f32[39,96,3]{1,0,2:T(8,128)S(1)} %copy.15), channel_id=1, source_target_pairs={{0,16},{16,32},{32,48},{48,64},{64,80},{80,96},{96,112},{112,128},... | collective-permute-start | bytes 134792 | tf_op jit(solution)/shard_map/ppermute | solution.py:29
  53.2 17.0 %copy-start.2 = (f32[39,96,3]{2,1,0:T(8,128)S(1)}, f32[39,96,3]{2,1,0:T(8,128)}, u32[]{:S(2)}) copy-start(f32[39,96,3]{2,1,0:T(8,128)} %copy.17) | copy-start | bytes 134788
  53.2 17.0 %copy-start.3 = (f32[39,96,3]{2,1,0:T(8,128)S(1)}, f32[39,96,3]{2,1,0:T(8,128)}, u32[]{:S(2)}) copy-start(f32[39,96,3]{2,1,0:T(8,128)} %copy.18) | copy-start | bytes 134788
  54.9 10.3 %collective-permute-start.2 = (f32[39,3,134]{2,1,0:T(4,128)S(1)}, f32[39,3,134]{2,1,0:T(4,128)S(1)}, u32[]{:S(2)}, u32[]{:S(2)}) collective-permute-start(f32[39,3,134]{2,1,0:T(4,128)S(1)} %get-tuple-element.22), channel_id=1, source_target_pairs={{0,1},{1,2},{2,3},{3,4},{4,5},{5,6},{6,7},{7,8},{8,9},{9,10},{10,1... | collective-permute-start | bytes 188144 | tf_op jit(solution)/shard_map/ppermute | solution.py:40
  59.9 10.4 %collective-permute-start.3 = (f32[39,3,134]{2,1,0:T(4,128)S(1)}, f32[39,3,134]{2,1,0:T(4,128)S(1)}, u32[]{:S(2)}, u32[]{:S(2)}) collective-permute-start(f32[39,3,134]{2,1,0:T(4,128)S(1)} %get-tuple-element.23), channel_id=1, source_target_pairs={{1,0},{2,1},{3,2},{4,3},{5,4},{6,5},{7,6},{8,7},{9,8},{10,9},{11,1... | collective-permute-start | bytes 188144 | tf_op jit(solution)/shard_map/ppermute | solution.py:41
  72.8 3.1 %copy-start.1 = (f32[39,102,134]{2,1,0:T(8,128)}, f32[39,102,134]{2,1,0:T(8,128)S(1)}, u32[]{:S(2)}) copy-start(f32[39,102,134]{2,1,0:T(8,128)S(1)} %pad_maximum_fusion) | copy-start | bytes 6396628
  97.9 18.8 %collective-permute-start.7 = (f32[12,102,3]{1,0,2:T(8,128)S(1)}, f32[12,102,3]{1,0,2:T(8,128)}, u32[]{:S(2)}, u32[]{:S(2)}) collective-permute-start(f32[12,102,3]{1,0,2:T(8,128)S(1)} %copy.20), channel_id=1, source_target_pairs={{16,0},{32,16},{48,32},{64,48},{80,64},{96,80},{112,96},{128,112},... | collective-permute-start | bytes 44072 | tf_op jit(solution)/shard_map/ppermute | solution.py:30
  106.4 8.5 %collective-permute-start.6 = (f32[12,102,3]{1,0,2:T(8,128)}, f32[12,102,3]{1,0,2:T(8,128)}, u32[]{:S(2)}, u32[]{:S(2)}) collective-permute-start(f32[12,102,3]{1,0,2:T(8,128)} %copy.19), channel_id=1, source_target_pairs={{0,16},{16,32},{32,48},{48,64},{64,80},{80,96},{96,112},{112,128},... | collective-permute-start | bytes 44072 | tf_op jit(solution)/shard_map/ppermute | solution.py:29
  118.6 2.3 %copy-start.11 = (f32[100,132]{1,0:T(8,128)S(1)}, f32[100,132]{1,0:T(8,128)}, u32[]{:S(2)}) copy-start(f32[100,132]{1,0:T(8,128)} %get-tuple-element.59) | copy-start | bytes 158404
  118.6 2.3 %copy-start.12 = (f32[100,132]{1,0:T(8,128)S(1)}, f32[100,132]{1,0:T(8,128)}, u32[]{:S(2)}) copy-start(f32[100,132]{1,0:T(8,128)} %get-tuple-element.60) | copy-start | bytes 158404
  118.6 2.3 %copy-start.28 = (f32[100]{0:T(128)S(1)}, f32[100]{0:T(128)}, u32[]{:S(2)}) copy-start(f32[100]{0:T(128)} %slice_multiply_fusion.8) | copy-start | bytes 1204
  120.9 1.2 copy-start.6
  121.0 1.2 copy-start.7
  121.0 1.2 copy-start.16
  121.0 1.2 copy-start.20
  121.0 1.2 copy-start.21
  121.0 1.2 copy-start.24
  121.0 1.2 copy-start.25
  123.0 0.9 copy-start.15
  124.1 2.1 %copy-start.10 = (f32[98,130]{1,0:T(8,128)S(1)}, f32[98,130]{1,0:T(8,128)}, u32[]{:S(2)}) copy-start(f32[98,130]{1,0:T(8,128)} %get-tuple-element.67) | copy-start | bytes 152884
  126.2 0.9 copy-start.5
  126.2 0.9 copy-start.13
  126.2 0.9 copy-start.22
  126.2 0.9 copy-start.23
  128.0 0.9 copy-start.14
  128.8 0.7 copy-start.27
  129.5 1.9 %copy-start.26 = (f32[6]{0:T(128)S(1)}, f32[6]{0:T(128)}, u32[]{:S(2)}) copy-start(f32[6]{0:T(128)} %constant.12) | copy-start | bytes 76
Sparse Core Ops, SparseCore 0:
  10.8 74.0 all-gather.1

commit v2 on v1

--- a/solution.py
+++ b/solution.py
@@ -9,15 +9,18 @@
 FREQS = [1.9323, 2.0, 1.896, 2.0055, 1.0027, 0.9295]
 VISCOSITY = 0.5
 HALO = 3
-LAT = ("chip", "core")
+LAT = ("half", "row", "core")
+ROW = ("row", "core")
 
 
 def lat_index():
-    return lax.axis_index("chip") * lax.axis_size("core") + lax.axis_index("core")
+    return (
+        lax.axis_index("half") * lax.axis_size("row") + lax.axis_index("row")
+    ) * lax.axis_size("core") + lax.axis_index("core")
 
 
 def lat_size():
-    return lax.axis_size("chip") * lax.axis_size("core")
+    return lax.axis_size("half") * lax.axis_size("row") * lax.axis_size("core")
 
 
 def widen_lon(array, width, dim):
@@ -110,14 +113,26 @@
     wet_frac = wet_mask.astype(jnp.float32)
     source = wet_frac * elevation
     mixed = jnp.einsum("krj,cj->krc", source, lon_green, precision=lax.Precision.HIGHEST)
-    gathered = lax.all_gather(mixed, LAT, axis=1, tiled=True)
+    gathered = lax.all_gather(mixed, ROW, axis=1, tiled=True)
 
     fields = jnp.stack([ocean_depth, bottom_drag, wet_frac], axis=0)
     stack = jnp.concatenate([elevation - equilibrium, transport_u, transport_v, fields], axis=0)
     stack = widen_lat(widen_lon(stack, HALO, 2), HALO, 1)
     green_ext = widen_lat(lat_green, HALO, 0)
 
-    sal = jnp.einsum("rs,ksc->krc", green_ext, gathered, precision=lax.Precision.HIGHEST)
+    halves = lax.axis_size("half")
+    half = lax.axis_index("half")
+    green_split = green_ext.reshape(green_ext.shape[0], halves, -1)
+    swap = [(i, (i + 1) % halves) for i in range(halves)]
+    green_away = lax.ppermute(
+        lax.dynamic_index_in_dim(green_split, (half + 1) % halves, axis=1, keepdims=False), "half", swap
+    )
+    green_home = lax.dynamic_index_in_dim(green_split, half, axis=1, keepdims=False)
+    for_partner = jnp.einsum("rs,ksc->krc", green_away, gathered, precision=lax.Precision.HIGHEST)
+    back = [(j, i) for i, j in swap]
+    from_partner = lax.ppermute(for_partner, "half", back)
+    sal = jnp.einsum("rs,ksc->krc", green_home, gathered, precision=lax.Precision.HIGHEST)
+    sal = sal + from_partner
     sal = widen_lon(sal, HALO, 2)
     potential = stack[:12] - sal
     flows = stack[12:36]
@@ -153,9 +168,8 @@
 
 def solution(mesh):
     lat_devices = mesh.shape["lat"]
-    cores = 2 if lat_devices % 2 == 0 else 1
-    devices = mesh.devices.reshape(mesh.shape["lon"], lat_devices // cores, cores)
-    split = Mesh(devices, ("lon", "chip", "core"))
+    devices = mesh.devices.reshape(mesh.shape["lon"], 2, lat_devices // 4, 2)
+    split = Mesh(devices, ("lon", "half", "row", "core"))
     grid = P(None, LAT, "lon")
     plane = P(LAT, "lon")
     placed = (grid, grid, grid, grid, plane, plane, plane, P("lon", None), plane)

time: 140 us -> 145 us (1.036)
  the two profiles are of different devices: /device:TPU:1 before, /device:TPU:24 now
where the time goes in v2:
time: 145 us; the launch traced here: 144 us
  starting transfers between devices  39.8 us (27%)
  local copies, waits for them, and re-layouts  28.5 us (20%)
  other arithmetic  26 us (18%)
  waiting for transfers between devices  24.6 us (17%)
  between operations  14.7 us (10%)
  matrix products  10.5 us (7%)
    ppermute x2, starting transfers between devices, widen_lon(): after = lax.ppermute(initial, 'lon', down)  17.4 us
    ppermute x1, waiting for transfers between devices, per_device(): from_partner = lax.ppermute(for_partner, 'half', back)  11.1 us
    slice x4, local copies, waits for them, and re-layouts, widen_lon(): last = lax.slice_in_dim(array, length - width, length, axis=dim)  8 us
    ppermute x1, waiting for transfers between devices, per_device(): lax.ppermute(lax.dynamic_index_in_dim(green_split, (half + 1) % halves, a...  7.86 us
    ppermute x2, starting transfers between devices, widen_lat(): after = lax.ppermute(initial, LAT, down)  7.42 us
    ppermute x2, starting transfers between devices, widen_lon(): before = lax.ppermute(last, 'lon', up)  5.94 us
    ppermute x2, waiting for transfers between devices, widen_lon(): before = lax.ppermute(last, 'lon', up)  5.67 us
    dot_general x1, matrix products, per_device(): jnp.einsum('rs,ksc->krc', green_away, gathered, precision=lax.Precision.H...  5.23 us
  transfers between devices with their start and end apart: 11, of which 4 were waited for; matrix products, arithmetic and copies ran while one was open for 23% of the time, Pallas kernels for 0%

profile of v2, /device:TPU:24, one launch (start us, length us, event | category | flops | bytes accessed | tf_op | source)
XLA Modules:
  0.0 144.0 jit_solution(9679816847709279858)
XLA Ops:
  7.2 0.9 convert_element_type.6
  8.2 2.5 %fusion.43 = f32[12,96,128]{2,1,0:T(8,128)} fusion(f32[12,96,128]{2,1,0:T(8,128)} %param.12, f32[96,128]{1,0:T(8,128)S(1)} %convert_element_type.6, f32[128,128]{1,0:T(8,128)S(1)} %copy-done), kind=kOutput, calls=%fused_computation.93 | convolution fusion | flops 226639872 | bytes 1294336 | tf_op jit(solution)/shard_map/krj,cj->krc/dot_general | solution.py:115
  10.8 2.1 %collective-permute-start.4 = (f32[3,1536]{1,0:T(4,128)S(1)}, f32[3,1536]{1,0:T(4,128)}, u32[]{:S(2)}, u32[]{:S(2)}) collective-permute-start(f32[3,1536]{1,0:T(4,128)S(1)} %get-tuple-element.45), channel_id=1, source_target_pairs={{0,1},{1,2},{2,3},{3,4},{4,5},{5,6},{6,7},{7,8},{8,9},{9,10},{10,1... | collective-permute-start | bytes 55304 | tf_op jit(solution)/shard_map/ppermute | solution.py:43
  12.9 3.8 %collective-permute-start.5 = (f32[3,1536]{1,0:T(4,128)S(1)}, f32[3,1536]{1,0:T(4,128)}, u32[]{:S(2)}, u32[]{:S(2)}) collective-permute-start(f32[3,1536]{1,0:T(4,128)S(1)} %get-tuple-element.46), channel_id=1, source_target_pairs={{1,0},{2,1},{3,2},{4,3},{5,4},{6,5},{7,6},{8,7},{9,8},{10,9},{11,1... | collective-permute-start | bytes 55304 | tf_op jit(solution)/shard_map/ppermute | solution.py:44
  16.7 1.1 subtract_dynamic-update-slice_fusion
  17.9 1.1 constant_dynamic-update-slice_fusion
  19.0 2.6 %fusion.53 = (f32[39,96,3]{2,1,0:T(8,128)}, f32[39,96,3]{2,1,0:T(8,128)}) fusion(f32[39,96,128]{2,1,0:T(8,128)S(1)} %bitcast_dynamic-update-slice_fusion), kind=kLoop, calls=%fused_computation.136 | loop fusion | bytes 179712 | tf_op jit(solution)/shard_map/slice | solution.py:30
  21.6 2.1 %copy.18 = f32[39,96,3]{1,0,2:T(8,128)S(1)} copy(f32[39,96,3]{2,1,0:T(8,128)} %get-tuple-element.35) | data formatting | bytes 89856 | tf_op jit(solution)/shard_map/slice | solution.py:31
  23.8 13.9 %collective-permute-start.1 = (f32[39,96,3]{1,0,2:T(8,128)S(1)}, f32[39,96,3]{1,0,2:T(8,128)S(1)}, u32[]{:S(2)}, u32[]{:S(2)}) collective-permute-start(f32[39,96,3]{1,0,2:T(8,128)S(1)} %copy.18), channel_id=1, source_target_pairs={{16,0},{32,16},{48,32},{64,48},{80,64},{96,80},{112,96},{128,112},... | collective-permute-start | bytes 134792 | tf_op jit(solution)/shard_map/ppermute | solution.py:33
  37.6 2.2 %copy.17 = f32[39,96,3]{1,0,2:T(8,128)S(1)} copy(f32[39,96,3]{2,1,0:T(8,128)} %get-tuple-element.34) | data formatting | bytes 89856 | tf_op jit(solution)/shard_map/slice | solution.py:30
  39.8 1.9 %collective-permute-start = (f32[39,96,3]{1,0,2:T(8,128)S(1)}, f32[39,96,3]{1,0,2:T(8,128)}, u32[]{:S(2)}, u32[]{:S(2)}) collective-permute-start(f32[39,96,3]{1,0,2:T(8,128)S(1)} %copy.17), channel_id=1, source_target_pairs={{0,16},{16,32},{32,48},{48,64},{64,80},{80,96},{96,112},{112,128},... | collective-permute-start | bytes 134792 | tf_op jit(solution)/shard_map/ppermute | solution.py:32
  41.8 0.7 slice_multiply_fusion.7
  42.5 0.6 fusion.57
  43.1 0.6 broadcast_multiply_fusion.4
  43.7 0.6 slice_multiply_fusion.8
  44.3 0.8 pad_maximum_fusion.2
  45.1 0.4 reshape.51
  45.6 4.1 %collective-permute-done = f32[39,96,3]{1,0,2:T(8,128)} collective-permute-done((f32[39,96,3]{1,0,2:T(8,128)S(1)}, f32[39,96,3]{1,0,2:T(8,128)}, u32[]{:S(2)}, u32[]{:S(2)}) %collective-permute-start) | collective-permute-done | bytes 44960 | tf_op jit(solution)/shard_map/ppermute | solution.py:32
  49.6 2.7 %copy.19 = f32[39,96,3]{2,1,0:T(8,128)} copy(f32[39,96,3]{1,0,2:T(8,128)} %collective-permute-done) | data formatting | bytes 89856 | tf_op jit(solution)/shard_map/ppermute | solution.py:32
  52.3 2.0 %copy.20 = f32[39,96,3]{2,1,0:T(8,128)} copy(f32[39,96,3]{1,0,2:T(8,128)S(1)} %collective-permute-done.1) | data formatting | bytes 89856 | tf_op jit(solution)/shard_map/ppermute | solution.py:33
  54.3 1.6 %pad_maximum_fusion.5 = (f32[39,3,134]{2,1,0:T(4,128)S(1)}, f32[39,3,134]{2,1,0:T(4,128)S(1)}) fusion(f32[39,96,3]{2,1,0:T(8,128)} %copy.20, f32[39,96,128]{2,1,0:T(8,128)S(1)} %bitcast_dynamic-update-slice_fusion, f32[39,96,3]{2,1,0:T(8,128)} %copy.19), kind=kLoop, calls=%fused_computation.106 | loop fusion | flops 62712 | bytes 2132208 | tf_op jit(solution)/shard_map/slice | solution.py:41
  55.9 1.9 %collective-permute-start.2 = (f32[39,3,134]{2,1,0:T(4,128)S(1)}, f32[39,3,134]{2,1,0:T(4,128)S(1)}, u32[]{:S(2)}, u32[]{:S(2)}) collective-permute-start(f32[39,3,134]{2,1,0:T(4,128)S(1)} %get-tuple-element.22), channel_id=1, source_target_pairs={{0,1},{1,2},{2,3},{3,4},{4,5},{5,6},{6,7},{7,8},{8,9},{9,10},{10,1... | collective-permute-start | bytes 188144 | tf_op jit(solution)/shard_map/ppermute | solution.py:43
  57.9 3.6 %collective-permute-start.3 = (f32[39,3,134]{2,1,0:T(4,128)S(1)}, f32[39,3,134]{2,1,0:T(4,128)S(1)}, u32[]{:S(2)}, u32[]{:S(2)}) collective-permute-start(f32[39,3,134]{2,1,0:T(4,128)S(1)} %get-tuple-element.23), channel_id=1, source_target_pairs={{1,0},{2,1},{3,2},{4,3},{5,4},{6,5},{7,6},{8,7},{9,8},{10,9},{11,1... | collective-permute-start | bytes 188144 | tf_op jit(solution)/shard_map/ppermute | solution.py:44
  61.5 1.3 constant_dynamic-slice_fusion.1
  62.8 2.6 %collective-permute-start.6 = (f32[102,768]{1,0:T(8,128)S(1)}, f32[102,768]{1,0:T(8,128)S(1)}, u32[]{:S(2)}, u32[]{:S(2)}) collective-permute-start(f32[102,768]{1,0:T(8,128)S(1)} %bitcast.37), channel_id=1, source_target_pairs={{0,8},{8,0},{1,9},{9,1},{2,10},{10,2},{3,11},{11,3},{4,12},{12,4},... | collective-permute-start | bytes 940040 | tf_op jit(solution)/shard_map/ppermute | solution.py:127
  65.4 0.8 maximum_bitcast_fusion.2
  66.2 0.8 slice_add_fusion.3
  67.1 7.9 %collective-permute-done.6 = f32[102,768]{1,0:T(8,128)S(1)} collective-permute-done((f32[102,768]{1,0:T(8,128)S(1)}, f32[102,768]{1,0:T(8,128)S(1)}, u32[]{:S(2)}, u32[]{:S(2)}) %collective-permute-start.6) | collective-permute-done | bytes 313376 | tf_op jit(solution)/shard_map/ppermute | solution.py:127
  74.9 0.7 copy-done.20
  75.7 5.2 %convolution_bitcast_fusion = f32[12,102,128]{2,1,0:T(8,128)S(1)} fusion(f32[12,768,128]{2,1,0:T(8,128)} %all-gather.2.cloned.1.call-done, f32[102,768]{1,0:T(8,128)} %copy-done.20), kind=kOutput, calls=%fused_computation.46 | convolution fusion | flops 1443889152 | bytes 5658624 | tf_op jit(solution)/shard_map/rs,ksc->krc/dot_general | solution.py:131
  80.9 2.4 %collective-permute-start.7 = (f32[12,102,128]{2,1,0:T(8,128)S(1)}, f32[12,102,128]{2,1,0:T(8,128)S(1)}, u32[]{:S(2)}, u32[]{:S(2)}) collective-permute-start(f32[12,102,128]{2,1,0:T(8,128)S(1)} %convolution_bitcast_fusion), channel_id=1, source_target_pairs={{8,0},{0,8},{9,1},{1,9},{10,2},{2,10},{11,3},{3,11},{12,4},{4,12},... | collective-permute-start | bytes 1880072 | tf_op jit(solution)/shard_map/ppermute | solution.py:133
  83.3 1.7 %pad_maximum_fusion = f32[39,102,134]{2,1,0:T(8,128)S(1)} fusion(f32[39,3,134]{2,1,0:T(4,128)S(1)} %collective-permute-done.3, f32[39,96,3]{2,1,0:T(8,128)S(1)} %copy-done.5, f32[39,96,128]{2,1,0:T(8,128)S(1)} %bitcast_dynamic-update-slice_fusion, f32[39,96,3]{2,1,0:T(8,128)S(1)} %copy-done.3, f32[39,3,134]{2,1,0:T(4,128)S(1)} %collective-permute-done.2), kind=kLoop, calls=%fused_computation | loop fusion | flops 2132208 | bytes 4264416 | tf_op jit(solution)/shard_map/concatenate | solution.py:45
  85.0 0.8 slice_add_fusion.4
  85.8 2.1 %slice_add_fusion = f32[24,100,132]{2,1,0:T(8,128)S(1)} fusion(f32[39,102,134]{2,1,0:T(8,128)S(1)} %pad_maximum_fusion), kind=kLoop, calls=%fused_computation.14 | loop fusion | flops 950400 | bytes 6336000 | tf_op jit(solution)/shard_map/add | solution.py:82
  88.0 11.1 %collective-permute-done.7 = f32[12,102,128]{2,1,0:T(8,128)S(1)} collective-permute-done((f32[12,102,128]{2,1,0:T(8,128)S(1)}, f32[12,102,128]{2,1,0:T(8,128)S(1)}, u32[]{:S(2)}, u32[]{:S(2)}) %collective-permute-start.7) | collective-permute-done | bytes 626720 | tf_op jit(solution)/shard_map/ppermute | solution.py:133
  99.1 2.7 %fusion.45 = f32[12,102,128]{2,1,0:T(8,128)S(1)} fusion(f32[12,102,128]{2,1,0:T(8,128)S(1)} %collective-permute-done.7, f32[12,768,128]{2,1,0:T(8,128)S(1)} %bitcast.36, f32[102,1,768]{2,1,0:T(1,128)S(1)} %copy-done.7), kind=kOutput, calls=%fused_computation.98 | convolution fusion | flops 1444045824 | bytes 6285312 | tf_op jit(solution)/shard_map/rs,ksc->krc/dot_general | solution.py:134
  101.8 1.3 fusion.55
  103.1 2.0 %copy.23 = f32[12,102,3]{1,0,2:T(8,128)} copy(f32[12,102,3]{2,1,0:T(8,128)} %get-tuple-element.39) | data formatting | bytes 29376 | tf_op jit(solution)/shard_map/slice | solution.py:30
  105.1 1.4 copy.24
  106.4 3.6 %collective-permute-start.9 = (f32[12,102,3]{1,0,2:T(8,128)S(1)}, f32[12,102,3]{1,0,2:T(8,128)}, u32[]{:S(2)}, u32[]{:S(2)}) collective-permute-start(f32[12,102,3]{1,0,2:T(8,128)S(1)} %copy.24), channel_id=1, source_target_pairs={{16,0},{32,16},{48,32},{64,48},{80,64},{96,80},{112,96},{128,112},... | collective-permute-start | bytes 44072 | tf_op jit(solution)/shard_map/ppermute | solution.py:33
  110.0 4.0 %collective-permute-start.8 = (f32[12,102,3]{1,0,2:T(8,128)}, f32[12,102,3]{1,0,2:T(8,128)}, u32[]{:S(2)}, u32[]{:S(2)}) collective-permute-start(f32[12,102,3]{1,0,2:T(8,128)} %copy.23), channel_id=1, source_target_pairs={{0,16},{16,32},{32,48},{48,64},{64,80},{80,96},{96,112},{112,128},... | collective-permute-start | bytes 44072 | tf_op jit(solution)/shard_map/ppermute | solution.py:32
  114.0 0.8 slice_negate_fusion.1
  114.8 1.6 %slice.271 = f32[100,132]{1,0:T(8,128)} slice(f32[102,134]{1,0:T(8,128)} %get-tuple-element.19), slice={[1:101], [1:133]} | slice | bytes 105600 | tf_op jit(solution)/shard_map/slice | solution.py:77
  116.4 1.6 %slice.262 = f32[98,130]{1,0:T(8,128)} slice(f32[102,134]{1,0:T(8,128)} %get-tuple-element.19), slice={[2:100], [2:132]} | slice | bytes 101920 | tf_op jit(solution)/shard_map/slice | solution.py:77
  118.0 1.6 %collective-permute-done.8 = f32[12,102,3]{1,0,2:T(8,128)} collective-permute-done((f32[12,102,3]{1,0,2:T(8,128)}, f32[12,102,3]{1,0,2:T(8,128)}, u32[]{:S(2)}, u32[]{:S(2)}) %collective-permute-start.8) | collective-permute-done | bytes 14720 | tf_op jit(solution)/shard_map/ppermute | solution.py:32
  119.6 1.9 %copy.25 = f32[12,102,3]{2,1,0:T(8,128)} copy(f32[12,102,3]{1,0,2:T(8,128)} %collective-permute-done.8) | data formatting | bytes 29376 | tf_op jit(solution)/shard_map/ppermute | solution.py:32
  121.5 1.9 %copy.26 = f32[12,102,3]{2,1,0:T(8,128)} copy(f32[12,102,3]{1,0,2:T(8,128)} %collective-permute-done.9) | data formatting | bytes 29376 | tf_op jit(solution)/shard_map/ppermute | solution.py:33
  123.4 2.3 %slice_subtract_fusion.2 = f32[12,102,134]{2,1,0:T(8,128)S(1)} fusion(f32[39,102,134]{2,1,0:T(8,128)} %copy-done.1, f32[12,102,3]{2,1,0:T(8,128)} %copy.26, f32[12,102,128]{2,1,0:T(8,128)S(1)} %fusion.45, f32[12,102,3]{2,1,0:T(8,128)} %copy.25), kind=kLoop, calls=%fused_computation.41 | loop fusion | flops 492048 | bytes 1968192 | tf_op jit(solution)/shard_map/sub | solution.py:137
  125.8 1.1 fusion.10
  127.0 0.8 fusion.18
  127.8 0.4 fusion.20
  128.2 0.5 copy-done.18
  128.7 0.2 maximum_multiply_fusion.1
  128.9 2.1 %fusion.2 = f32[24,98,130]{2,1,0:T(8,128)S(1)} fusion(f32[12,100,132]{2,1,0:T(8,128)S(1)} %get-tuple-element.57, f32[12,100,132]{2,1,0:T(8,128)S(1)} %get-tuple-element.56), kind=kLoop, calls=%fused_computation.9 | loop fusion | flops 2140320 | bytes 2490240 | tf_op jit(solution)/shard_map/add | solution.py:82
  131.0 0.8 fusion.6
  131.9 0.1 copy-done.16
  131.9 0.8 fusion.22
  132.7 0.4 fusion.25
  133.2 0.5 copy-done.17
  133.6 0.2 maximum_multiply_fusion.2
  133.8 0.5 copy-done.31
  134.3 1.8 %fusion.54 = (f32[12,96,128]{2,1,0:T(8,128)}, f32[12,96,128]{2,1,0:T(8,128)S(1)}, f32[12,96,128]{2,1,0:T(8,128)}) fusion(f32[12,98,130]{2,1,0:T(8,128)S(1)} %get-tuple-element.52, f32[96]{0:T(128)S(1)} %copy-done.31, f32[12,98,130]{2,1,0:T(8,128)S(1)} %get-tuple-element.51), kind=kLoop, calls=%fused_computation.137 | loop fusion | flops 737280 | bytes 5308800 | tf_op jit(solution)/shard_map/slice | solution.py:166
  136.2 0.1 fusion.47
  136.3 0.9 maximum_multiply_fusion.4
  (83 shorter events, 0.5 us)
Async XLA Ops:
  7.2 1.0 copy-start
  7.2 9.5 %copy-start.6 = (f32[12,96,128]{2,1,0:T(8,128)S(1)}, f32[12,96,128]{2,1,0:T(8,128)}, u32[]{:S(2)}) copy-start(f32[12,96,128]{2,1,0:T(8,128)} %param.12) | copy-start | bytes 1769476
  7.2 3.5 %copy-start.11 = (f32[96,1536]{1,0:T(8,128)S(1)}, f32[96,1536]{1,0:T(8,128)}, u32[]{:S(2)}) copy-start(f32[96,1536]{1,0:T(8,128)} %param.20) | copy-start | bytes 1769476
  7.2 68.4 %all-gather.2.cloned.1.call-start = ((), (), s32[]{:S(2)}) async-start(), calls=%async_computation | async-start | bytes 5308416 | tf_op jit(solution)/shard_map/all_gather | solution.py:116
  10.7 7.1 %copy-start.12 = (f32[12,96,128]{2,1,0:T(8,128)S(1)}, f32[12,96,128]{2,1,0:T(8,128)}, u32[]{:S(2)}) copy-start(f32[12,96,128]{2,1,0:T(8,128)} %param.14) | copy-start | bytes 1769476
  10.8 33.5 %collective-permute-start.4 = (f32[3,1536]{1,0:T(4,128)S(1)}, f32[3,1536]{1,0:T(4,128)}, u32[]{:S(2)}, u32[]{:S(2)}) collective-permute-start(f32[3,1536]{1,0:T(4,128)S(1)} %get-tuple-element.45), channel_id=1, source_target_pairs={{0,1},{1,2},{2,3},{3,4},{4,5},{5,6},{6,7},{7,8},{8,9},{9,10},{10,1... | collective-permute-start | bytes 55304 | tf_op jit(solution)/shard_map/ppermute | solution.py:43
  12.8 6.1 %copy-start.22 = (f32[96,128]{1,0:T(8,128)S(1)}, f32[96,128]{1,0:T(8,128)}, u32[]{:S(2)}) copy-start(f32[96,128]{1,0:T(8,128)} %param.16) | copy-start | bytes 147460
  12.8 6.2 %copy-start.23 = (f32[96,128]{1,0:T(8,128)S(1)}, f32[96,128]{1,0:T(8,128)}, u32[]{:S(2)}) copy-start(f32[96,128]{1,0:T(8,128)} %param.17) | copy-start | bytes 147460
  12.9 6.2 %copy-start.21 = (s32[96,128]{1,0:T(8,128)S(1)}, s32[96,128]{1,0:T(8,128)}, u32[]{:S(2)}) copy-start(s32[96,128]{1,0:T(8,128)} %param.18) | copy-start | bytes 147460
  12.9 31.4 %collective-permute-start.5 = (f32[3,1536]{1,0:T(4,128)S(1)}, f32[3,1536]{1,0:T(4,128)}, u32[]{:S(2)}, u32[]{:S(2)}) collective-permute-start(f32[3,1536]{1,0:T(4,128)S(1)} %get-tuple-element.46), channel_id=1, source_target_pairs={{1,0},{2,1},{3,2},{4,3},{5,4},{6,5},{7,6},{8,7},{9,8},{10,9},{11,1... | collective-permute-start | bytes 55304 | tf_op jit(solution)/shard_map/ppermute | solution.py:44
  23.8 28.6 %collective-permute-start.1 = (f32[39,96,3]{1,0,2:T(8,128)S(1)}, f32[39,96,3]{1,0,2:T(8,128)S(1)}, u32[]{:S(2)}, u32[]{:S(2)}) collective-permute-start(f32[39,96,3]{1,0,2:T(8,128)S(1)} %copy.18), channel_id=1, source_target_pairs={{16,0},{32,16},{48,32},{64,48},{80,64},{96,80},{112,96},{128,112},... | collective-permute-start | bytes 134792 | tf_op jit(solution)/shard_map/ppermute | solution.py:33
  39.8 9.8 %collective-permute-start = (f32[39,96,3]{1,0,2:T(8,128)S(1)}, f32[39,96,3]{1,0,2:T(8,128)}, u32[]{:S(2)}, u32[]{:S(2)}) collective-permute-start(f32[39,96,3]{1,0,2:T(8,128)S(1)} %copy.17), channel_id=1, source_target_pairs={{0,16},{16,32},{32,48},{48,64},{64,80},{80,96},{96,112},{112,128},... | collective-permute-start | bytes 134792 | tf_op jit(solution)/shard_map/ppermute | solution.py:32
  54.3 11.1 %copy-start.2 = (f32[39,96,3]{2,1,0:T(8,128)S(1)}, f32[39,96,3]{2,1,0:T(8,128)}, u32[]{:S(2)}) copy-start(f32[39,96,3]{2,1,0:T(8,128)} %copy.19) | copy-start | bytes 134788
  54.3 11.1 %copy-start.4 = (f32[39,96,3]{2,1,0:T(8,128)S(1)}, f32[39,96,3]{2,1,0:T(8,128)}, u32[]{:S(2)}) copy-start(f32[39,96,3]{2,1,0:T(8,128)} %copy.20) | copy-start | bytes 134788
  55.9 9.5 %collective-permute-start.2 = (f32[39,3,134]{2,1,0:T(4,128)S(1)}, f32[39,3,134]{2,1,0:T(4,128)S(1)}, u32[]{:S(2)}, u32[]{:S(2)}) collective-permute-start(f32[39,3,134]{2,1,0:T(4,128)S(1)} %get-tuple-element.22), channel_id=1, source_target_pairs={{0,1},{1,2},{2,3},{3,4},{4,5},{5,6},{6,7},{7,8},{8,9},{9,10},{10,1... | collective-permute-start | bytes 188144 | tf_op jit(solution)/shard_map/ppermute | solution.py:43
  57.9 7.5 %collective-permute-start.3 = (f32[39,3,134]{2,1,0:T(4,128)S(1)}, f32[39,3,134]{2,1,0:T(4,128)S(1)}, u32[]{:S(2)}, u32[]{:S(2)}) collective-permute-start(f32[39,3,134]{2,1,0:T(4,128)S(1)} %get-tuple-element.23), channel_id=1, source_target_pairs={{1,0},{2,1},{3,2},{4,3},{5,4},{6,5},{7,6},{8,7},{9,8},{10,9},{11,1... | collective-permute-start | bytes 188144 | tf_op jit(solution)/shard_map/ppermute | solution.py:44
  62.8 12.1 %collective-permute-start.6 = (f32[102,768]{1,0:T(8,128)S(1)}, f32[102,768]{1,0:T(8,128)S(1)}, u32[]{:S(2)}, u32[]{:S(2)}) collective-permute-start(f32[102,768]{1,0:T(8,128)S(1)} %bitcast.37), channel_id=1, source_target_pairs={{0,8},{8,0},{1,9},{9,1},{2,10},{10,2},{3,11},{11,3},{4,12},{12,4},... | collective-permute-start | bytes 940040 | tf_op jit(solution)/shard_map/ppermute | solution.py:127
  74.9 0.7 copy-start.20
  75.7 7.6 %copy-start.3 = (f32[39,96,3]{2,1,0:T(8,128)S(1)}, f32[39,96,3]{2,1,0:T(8,128)}, u32[]{:S(2)}) copy-start(f32[39,96,3]{2,1,0:T(8,128)} %copy.19) | copy-start | bytes 134788
  75.7 7.6 %copy-start.5 = (f32[39,96,3]{2,1,0:T(8,128)S(1)}, f32[39,96,3]{2,1,0:T(8,128)}, u32[]{:S(2)}) copy-start(f32[39,96,3]{2,1,0:T(8,128)} %copy.20) | copy-start | bytes 134788
  80.9 18.1 %collective-permute-start.7 = (f32[12,102,128]{2,1,0:T(8,128)S(1)}, f32[12,102,128]{2,1,0:T(8,128)S(1)}, u32[]{:S(2)}, u32[]{:S(2)}) collective-permute-start(f32[12,102,128]{2,1,0:T(8,128)S(1)} %convolution_bitcast_fusion), channel_id=1, source_target_pairs={{8,0},{0,8},{9,1},{1,9},{10,2},{2,10},{11,3},{3,11},{12,4},{4,12},... | collective-permute-start | bytes 1880072 | tf_op jit(solution)/shard_map/ppermute | solution.py:133
  85.0 2.9 %copy-start.1 = (f32[39,102,134]{2,1,0:T(8,128)}, f32[39,102,134]{2,1,0:T(8,128)S(1)}, u32[]{:S(2)}) copy-start(f32[39,102,134]{2,1,0:T(8,128)S(1)} %pad_maximum_fusion) | copy-start | bytes 6396628
  85.0 14.0 %slice-start = ((s8[4718592]{0:T(1024)(128)(4,1)}), s8[4194304]{0:T(1024)(128)(4,1)S(1)}, s32[]{:S(2)}) async-start(s8[4718592]{0:T(1024)(128)(4,1)} %bitcast.35), calls=%async_computation.1 | async-start | bytes 8388608
  85.8 13.2 %slice-start.1 = ((s8[4718592]{0:T(1024)(128)(4,1)}), s8[524288]{0:T(1024)(128)(4,1)S(1)}, s32[]{:S(2)}) async-start(s8[4718592]{0:T(1024)(128)(4,1)} %bitcast.35), calls=%async_computation.2 | async-start | bytes 1048576
  85.8 13.2 %copy-start.7 = (f32[102,1,768]{2,1,0:T(1,128)S(1)}, f32[102,1,768]{2,1,0:T(1,128)}, u32[]{:S(2)}) copy-start(f32[102,1,768]{2,1,0:T(1,128)} %get-tuple-element.41) | copy-start | bytes 940036
  106.4 15.1 %collective-permute-start.9 = (f32[12,102,3]{1,0,2:T(8,128)S(1)}, f32[12,102,3]{1,0,2:T(8,128)}, u32[]{:S(2)}, u32[]{:S(2)}) collective-permute-start(f32[12,102,3]{1,0,2:T(8,128)S(1)} %copy.24), channel_id=1, source_target_pairs={{16,0},{32,16},{48,32},{64,48},{80,64},{96,80},{112,96},{128,112},... | collective-permute-start | bytes 44072 | tf_op jit(solution)/shard_map/ppermute | solution.py:33
  110.0 9.7 %collective-permute-start.8 = (f32[12,102,3]{1,0,2:T(8,128)}, f32[12,102,3]{1,0,2:T(8,128)}, u32[]{:S(2)}, u32[]{:S(2)}) collective-permute-start(f32[12,102,3]{1,0,2:T(8,128)} %copy.23), channel_id=1, source_target_pairs={{0,16},{16,32},{32,48},{48,64},{64,80},{80,96},{96,112},{112,128},... | collective-permute-start | bytes 44072 | tf_op jit(solution)/shard_map/ppermute | solution.py:32
  123.4 2.3 %copy-start.14 = (f32[100,132]{1,0:T(8,128)S(1)}, f32[100,132]{1,0:T(8,128)}, u32[]{:S(2)}) copy-start(f32[100,132]{1,0:T(8,128)} %get-tuple-element.61) | copy-start | bytes 158404
  123.4 2.3 %copy-start.15 = (f32[100,132]{1,0:T(8,128)S(1)}, f32[100,132]{1,0:T(8,128)}, u32[]{:S(2)}) copy-start(f32[100,132]{1,0:T(8,128)} %get-tuple-element.62) | copy-start | bytes 158404
  123.4 2.3 %copy-start.32 = (f32[100]{0:T(128)S(1)}, f32[100]{0:T(128)}, u32[]{:S(2)}) copy-start(f32[100]{0:T(128)} %slice_multiply_fusion.8) | copy-start | bytes 1204
  125.7 1.2 copy-start.9
  125.7 1.2 copy-start.10
  125.7 1.2 copy-start.19
  125.8 1.2 copy-start.24
  125.8 1.2 copy-start.25
  125.8 1.2 copy-start.28
  125.8 1.2 copy-start.29
  127.8 0.9 copy-start.18
  128.9 2.1 %copy-start.13 = (f32[98,130]{1,0:T(8,128)S(1)}, f32[98,130]{1,0:T(8,128)}, u32[]{:S(2)}) copy-start(f32[98,130]{1,0:T(8,128)} %get-tuple-element.69) | copy-start | bytes 152884
  131.0 0.9 copy-start.8
  131.0 0.9 copy-start.16
  131.0 0.9 copy-start.26
  131.0 0.9 copy-start.27
  132.7 0.9 copy-start.17
  133.6 0.7 copy-start.31
  134.3 1.9 %copy-start.30 = (f32[6]{0:T(128)S(1)}, f32[6]{0:T(128)}, u32[]{:S(2)}) copy-start(f32[6]{0:T(128)} %constant.64) | copy-start | bytes 76
Sparse Core Ops, SparseCore 0:
  10.9 44.2 all-gather.1

commit v3 on v1

--- a/solution.py
+++ b/solution.py
@@ -117,8 +117,20 @@
     stack = widen_lat(widen_lon(stack, HALO, 2), HALO, 1)
     green_ext = widen_lat(lat_green, HALO, 0)
 
+    columns = gathered.shape[2]
+    size = lax.axis_size("lon")
+    up = [(i, (i + 1) % size) for i in range(size)]
+    down = [(j, i) for i, j in up]
+    last = jnp.einsum(
+        "rs,ksc->krc", green_ext, gathered[:, :, columns - HALO :], precision=lax.Precision.HIGHEST
+    )
+    initial = jnp.einsum(
+        "rs,ksc->krc", green_ext, gathered[:, :, :HALO], precision=lax.Precision.HIGHEST
+    )
+    before = lax.ppermute(last, "lon", up)
+    after = lax.ppermute(initial, "lon", down)
     sal = jnp.einsum("rs,ksc->krc", green_ext, gathered, precision=lax.Precision.HIGHEST)
-    sal = widen_lon(sal, HALO, 2)
+    sal = jnp.concatenate([before, sal, after], axis=2)
     potential = stack[:12] - sal
     flows = stack[12:36]
     depth_ext, drag_ext, wet_ext = stack[36], stack[37], stack[38]

time: 140 us -> 156 us (1.11)
  local copies, waits for them, and re-layouts: 26.6 us -> 45.9 us
  matrix products: 11 us -> 14.4 us
  waiting for transfers between devices: 23.1 us -> 19.9 us
  starting transfers between devices: 39.6 us -> 37.6 us
    slice x0 -> x3, local copies, waits for them, and re-layouts: none -> 26.8 us  [the longest x2 20.6 us: per_device(): gathered[:, :, columns - HALO:]]
    ppermute x0 -> x2, starting transfers between devices: none -> 9.87 us  [the longest x1 7.78 us: per_device(): after = lax.ppermute(initial, 'lon', down)]
    ppermute x2 -> x1, waiting for transfers between devices: 7.03 us -> 0.01 us  [widen_lon(): before = lax.ppermute(last, 'lon', up)]
    all_gather x1, waiting for transfers between devices: 8.15 us -> 15 us  [per_device(): gathered = lax.all_gather(mixed, LAT, axis=1, tiled=True)]
    ppermute x2, starting transfers between devices: 8.11 us -> 4.43 us  [widen_lat(): after = lax.ppermute(initial, LAT, down)]
    ppermute x2 -> x1, starting transfers between devices: 17.9 us -> 14.4 us  [widen_lon(): after = lax.ppermute(initial, 'lon', down)]
    slice x4 -> x2, local copies, waits for them, and re-layouts: 8.02 us -> 5.1 us  [widen_lon(): last = lax.slice_in_dim(array, length - width, length, axis=dim)]
    dot_general x0 -> x2, matrix products: none -> 2.8 us  [the longest x1 1.4 us: per_device(): jnp.einsum('rs,ksc->krc', green_ext, gathered[:, :, :HALO], precision=lax...]
  transfers between devices with their start and end apart: 9 -> 9, of which waited for: 5 -> 3; matrix products, arithmetic and copies ran while one was open for 22% -> 41% of each run, Pallas kernels for 0% -> 0%
where the time goes in v3:
time: 156 us
  local copies, waits for them, and re-layouts  45.9 us (29%)
  starting transfers between devices  37.6 us (24%)
  other arithmetic  23.4 us (15%)
  waiting for transfers between devices  19.9 us (13%)
  between operations  14.6 us (9%)
  matrix products  14.4 us (9%)
    slice x2, local copies, waits for them, and re-layouts, per_device(): gathered[:, :, columns - HALO:]  20.6 us
    all_gather x1, waiting for transfers between devices, per_device(): gathered = lax.all_gather(mixed, LAT, axis=1, tiled=True)  15 us
    ppermute x1, starting transfers between devices, widen_lon(): after = lax.ppermute(initial, 'lon', down)  14.4 us
    dot_general x1, matrix products, per_device(): jnp.einsum('rs,ksc->krc', green_ext, gathered, precision=lax.Precision.HI...  9.06 us
    ppermute x1, starting transfers between devices, per_device(): after = lax.ppermute(initial, 'lon', down)  7.78 us
    ppermute x2, starting transfers between devices, widen_lat(): before = lax.ppermute(last, LAT, up)  6.9 us
    slice x1, local copies, waits for them, and re-layouts, per_device(): gathered[:, :, :HALO]  6.27 us
    slice x2, local copies, waits for them, and re-layouts, widen_lon(): last = lax.slice_in_dim(array, length - width, length, axis=dim)  5.1 us
  transfers between devices with their start and end apart: 9, of which 3 were waited for; matrix products, arithmetic and copies ran while one was open for 41% of the time, Pallas kernels for 0%

profile of v3, /device:TPU:1, one launch (start us, length us, event | category | flops | bytes accessed | tf_op | source)
XLA Modules:
  0.0 155.8 jit_solution(4488761481685078521)
XLA Ops:
  7.2 0.0 all-gather.2.cloned.1.call-start
  7.2 0.9 convert_element_type.6
  8.1 2.5 %fusion.43 = f32[12,96,128]{2,1,0:T(8,128)} fusion(f32[12,96,128]{2,1,0:T(8,128)} %param.12, f32[96,128]{1,0:T(8,128)S(1)} %convert_element_type.6, f32[128,128]{1,0:T(8,128)S(1)} %copy-done), kind=kOutput, calls=%fused_computation.94 | convolution fusion | flops 226639872 | bytes 1294336 | tf_op jit(solution)/shard_map/krj,cj->krc/dot_general | solution.py:112
  10.7 0.1 subtract_dynamic-update-slice_fusion
  10.8 0.9 copy-done.12
  11.8 1.1 constant_dynamic-update-slice_fusion
  13.0 2.6 %fusion.55 = (f32[39,96,3]{2,1,0:T(8,128)}, f32[39,96,3]{2,1,0:T(8,128)}) fusion(f32[39,96,128]{2,1,0:T(8,128)S(1)} %bitcast_dynamic-update-slice_fusion), kind=kLoop, calls=%fused_computation.135 | loop fusion | bytes 179712 | tf_op jit(solution)/shard_map/slice | solution.py:27
  15.6 2.2 %copy.20 = f32[39,96,3]{1,0,2:T(8,128)S(1)} copy(f32[39,96,3]{2,1,0:T(8,128)} %get-tuple-element.37) | data formatting | bytes 89856 | tf_op jit(solution)/shard_map/slice | solution.py:28
  17.8 14.4 %collective-permute-start.1 = (f32[39,96,3]{1,0,2:T(8,128)S(1)}, f32[39,96,3]{1,0,2:T(8,128)S(1)}, u32[]{:S(2)}, u32[]{:S(2)}) collective-permute-start(f32[39,96,3]{1,0,2:T(8,128)S(1)} %copy.20), channel_id=1, source_target_pairs={{16,0},{32,16},{48,32},{64,48},{80,64},{96,80},{112,96},{128,112},... | collective-permute-start | bytes 134792 | tf_op jit(solution)/shard_map/ppermute | solution.py:30
  32.2 2.5 %copy.19 = f32[39,96,3]{1,0,2:T(8,128)S(1)} copy(f32[39,96,3]{2,1,0:T(8,128)} %get-tuple-element.36) | data formatting | bytes 89856 | tf_op jit(solution)/shard_map/slice | solution.py:27
  34.7 1.9 %collective-permute-start = (f32[39,96,3]{1,0,2:T(8,128)S(1)}, f32[39,96,3]{1,0,2:T(8,128)S(1)}, u32[]{:S(2)}, u32[]{:S(2)}) collective-permute-start(f32[39,96,3]{1,0,2:T(8,128)S(1)} %copy.19), channel_id=1, source_target_pairs={{0,16},{16,32},{32,48},{48,64},{64,80},{80,96},{96,112},{112,128},... | collective-permute-start | bytes 134792 | tf_op jit(solution)/shard_map/ppermute | solution.py:29
  36.7 0.6 fusion.57
  37.3 2.5 %collective-permute-start.5 = (f32[3,1536]{1,0:T(4,128)}, f32[3,1536]{1,0:T(4,128)S(1)}, u32[]{:S(2)}, u32[]{:S(2)}) collective-permute-start(f32[3,1536]{1,0:T(4,128)} %get-tuple-element.44), channel_id=1, source_target_pairs={{1,0},{2,1},{3,2},{4,3},{5,4},{6,5},{7,6},{8,7},{9,8},{10,9},{11,1... | collective-permute-start | bytes 55304 | tf_op jit(solution)/shard_map/ppermute | solution.py:41
  39.8 3.3 %collective-permute-start.4 = (f32[3,1536]{1,0:T(4,128)}, f32[3,1536]{1,0:T(4,128)S(1)}, u32[]{:S(2)}, u32[]{:S(2)}) collective-permute-start(f32[3,1536]{1,0:T(4,128)} %get-tuple-element.43), channel_id=1, source_target_pairs={{0,1},{1,2},{2,3},{3,4},{4,5},{5,6},{6,7},{7,8},{8,9},{9,10},{10,1... | collective-permute-start | bytes 55304 | tf_op jit(solution)/shard_map/ppermute | solution.py:40
  43.1 0.1 cosine_divide_fusion
  43.2 0.1 fusion.58
  43.3 0.6 broadcast_multiply_fusion.4
  43.9 0.6 slice_multiply_fusion.8
  44.5 1.9 %copy.22 = f32[39,96,3]{2,1,0:T(8,128)} copy(f32[39,96,3]{1,0,2:T(8,128)S(1)} %collective-permute-done.1) | data formatting | bytes 89856 | tf_op jit(solution)/shard_map/ppermute | solution.py:30
  46.4 1.9 %copy.21 = f32[39,96,3]{2,1,0:T(8,128)} copy(f32[39,96,3]{1,0,2:T(8,128)S(1)} %collective-permute-done) | data formatting | bytes 89856 | tf_op jit(solution)/shard_map/ppermute | solution.py:29
  48.3 1.6 %pad_maximum_fusion.4 = (f32[39,3,134]{2,1,0:T(4,128)S(1)}, f32[39,3,134]{2,1,0:T(4,128)S(1)}) fusion(f32[39,96,3]{2,1,0:T(8,128)} %copy.22, f32[39,96,128]{2,1,0:T(8,128)S(1)} %bitcast_dynamic-update-slice_fusion, f32[39,96,3]{2,1,0:T(8,128)} %copy.21), kind=kLoop, calls=%fused_computation.103 | loop fusion | flops 62712 | bytes 2132208 | tf_op jit(solution)/shard_map/slice | solution.py:38
  49.9 1.9 %collective-permute-start.3 = (f32[39,3,134]{2,1,0:T(4,128)S(1)}, f32[39,3,134]{2,1,0:T(4,128)S(1)}, u32[]{:S(2)}, u32[]{:S(2)}) collective-permute-start(f32[39,3,134]{2,1,0:T(4,128)S(1)} %get-tuple-element.25), channel_id=1, source_target_pairs={{1,0},{2,1},{3,2},{4,3},{5,4},{6,5},{7,6},{8,7},{9,8},{10,9},{11,1... | collective-permute-start | bytes 188144 | tf_op jit(solution)/shard_map/ppermute | solution.py:41
  51.9 3.6 %collective-permute-start.2 = (f32[39,3,134]{2,1,0:T(4,128)S(1)}, f32[39,3,134]{2,1,0:T(4,128)S(1)}, u32[]{:S(2)}, u32[]{:S(2)}) collective-permute-start(f32[39,3,134]{2,1,0:T(4,128)S(1)} %get-tuple-element.24), channel_id=1, source_target_pairs={{0,1},{1,2},{2,3},{3,4},{4,5},{5,6},{6,7},{7,8},{8,9},{9,10},{10,1... | collective-permute-start | bytes 188144 | tf_op jit(solution)/shard_map/ppermute | solution.py:40
  55.5 0.6 slice_multiply_fusion.7
  56.1 4.3 %collective-permute-done.3 = f32[39,3,134]{2,1,0:T(4,128)S(1)} collective-permute-done((f32[39,3,134]{2,1,0:T(4,128)S(1)}, f32[39,3,134]{2,1,0:T(4,128)S(1)}, u32[]{:S(2)}, u32[]{:S(2)}) %collective-permute-start.3) | collective-permute-done | bytes 62744 | tf_op jit(solution)/shard_map/ppermute | solution.py:41
  60.3 0.7 collective-permute-done.2
  61.0 0.2 maximum_bitcast_fusion.6
  61.2 0.7 slice.271
  62.0 0.7 slice.262
  62.7 1.7 %pad_maximum_fusion = f32[39,102,134]{2,1,0:T(8,128)S(1)} fusion(f32[39,3,134]{2,1,0:T(4,128)S(1)} %collective-permute-done.3, f32[39,96,3]{2,1,0:T(8,128)S(1)} %copy-done.3, f32[39,96,128]{2,1,0:T(8,128)S(1)} %bitcast_dynamic-update-slice_fusion, f32[39,96,3]{2,1,0:T(8,128)S(1)} %copy-done.4, f32[39,3,134]{2,1,0:T(4,128)S(1)} %collective-permute-done.2), kind=kLoop, calls=%fused_computation | loop fusion | flops 2132208 | bytes 4264416 | tf_op jit(solution)/shard_map/concatenate | solution.py:42
  64.4 0.9 slice_negate_fusion.1
  65.3 1.2 slice_add_fusion.3
  66.5 0.8 slice_add_fusion.4
  67.4 2.1 %slice_add_fusion = f32[24,100,132]{2,1,0:T(8,128)S(1)} fusion(f32[39,102,134]{2,1,0:T(8,128)S(1)} %pad_maximum_fusion), kind=kLoop, calls=%fused_computation.14 | loop fusion | flops 950400 | bytes 6336000 | tf_op jit(solution)/shard_map/add | solution.py:79
  69.5 15.0 %all-gather.2.cloned.1.call-done = f32[12,1536,128]{2,1,0:T(8,128)} async-done(((f32[12,96,128]{2,1,0:T(8,128)}), f32[12,1536,128]{2,1,0:T(8,128)}) %all-gather.2.cloned.1.call-update) | async-done | bytes 9437200 | tf_op jit(solution)/shard_map/all_gather | solution.py:113
  84.5 14.3 %fusion.54 = (f32[12,1536,3]{2,1,0:T(8,128)}, f32[12,1536,3]{2,1,0:T(8,128)}) fusion(f32[12,1536,128]{2,1,0:T(8,128)} %all-gather.2.cloned.1.call-done), kind=kLoop, calls=%fused_computation.134 | loop fusion | bytes 884736 | tf_op jit(solution)/shard_map/slice | solution.py:125
  98.7 6.3 %copy.24 = f32[12,1536,3]{1,0,2:T(8,128)S(1)} copy(f32[12,1536,3]{2,1,0:T(8,128)} %get-tuple-element.20) | data formatting | bytes 442368 | tf_op jit(solution)/shard_map/slice | solution.py:128
  105.0 1.4 convolution_bitcast_fusion.1
  106.4 7.8 %collective-permute-start.7 = (f32[12,102,3]{1,0,2:T(8,128)}, f32[12,102,3]{1,0,2:T(8,128)}, u32[]{:S(2)}, u32[]{:S(2)}) collective-permute-start(f32[12,102,3]{1,0,2:T(8,128)} %convolution_bitcast_fusion.1), channel_id=1, source_target_pairs={{16,0},{32,16},{48,32},{64,48},{80,64},{96,80},{112,96},{128,112},... | collective-permute-start | bytes 44072 | tf_op jit(solution)/shard_map/ppermute | solution.py:131
  114.2 6.3 %copy.23 = f32[12,1536,3]{1,0,2:T(8,128)S(1)} copy(f32[12,1536,3]{2,1,0:T(8,128)} %get-tuple-element.19) | data formatting | bytes 442368 | tf_op jit(solution)/shard_map/slice | solution.py:125
  120.5 1.4 convolution_bitcast_fusion.2
  121.9 2.1 %collective-permute-start.6 = (f32[12,102,3]{1,0,2:T(8,128)}, f32[12,102,3]{1,0,2:T(8,128)S(1)}, u32[]{:S(2)}, u32[]{:S(2)}) collective-permute-start(f32[12,102,3]{1,0,2:T(8,128)} %convolution_bitcast_fusion.2), channel_id=1, source_target_pairs={{0,16},{16,32},{32,48},{48,64},{64,80},{80,96},{96,112},{112,128},... | collective-permute-start | bytes 44072 | tf_op jit(solution)/shard_map/ppermute | solution.py:130
  124.0 9.1 %convolution_bitcast_fusion = f32[12,102,128]{2,1,0:T(8,128)} fusion(f32[12,1536,128]{2,1,0:T(8,128)} %all-gather.2.cloned.1.call-done, f32[3,1536]{1,0:T(4,128)S(1)} %collective-permute-done.5, f32[96,1536]{1,0:T(8,128)S(1)} %copy-done.5, f32[3,1536]{1,0:T(4,128)S(1)} %collective-permute-done.4), kind=kOutput, calls=%fused_computation.46 | convolution fusion | flops 2888091648 | bytes 10690560 | tf_op jit(solution)/shard_map/rs,ksc->krc/dot_general | solution.py:132
  133.1 1.0 copy.26
  134.1 1.1 copy.25
  135.3 2.3 %slice_subtract_fusion.2 = f32[12,102,134]{2,1,0:T(8,128)S(1)} fusion(f32[39,102,134]{2,1,0:T(8,128)} %copy-done.2, f32[12,102,3]{2,1,0:T(8,128)S(1)} %copy.26, f32[12,102,128]{2,1,0:T(8,128)} %convolution_bitcast_fusion, f32[12,102,3]{2,1,0:T(8,128)} %copy.25), kind=kLoop, calls=%fused_computation.41 | loop fusion | flops 492048 | bytes 1968192 | tf_op jit(solution)/shard_map/sub | solution.py:134
  137.6 1.1 fusion.10
  138.8 0.8 fusion.18
  139.6 0.4 fusion.20
  140.0 0.5 copy-done.18
  140.5 0.2 maximum_multiply_fusion.1
  140.7 2.1 %fusion.2 = f32[24,98,130]{2,1,0:T(8,128)S(1)} fusion(f32[12,100,132]{2,1,0:T(8,128)S(1)} %get-tuple-element.55, f32[12,100,132]{2,1,0:T(8,128)S(1)} %get-tuple-element.54), kind=kLoop, calls=%fused_computation.9 | loop fusion | flops 2140320 | bytes 2490240 | tf_op jit(solution)/shard_map/add | solution.py:79
  142.8 0.8 fusion.6
  143.6 0.1 copy-done.7
  143.7 0.1 copy-done.8
  143.7 0.1 copy-done.16
  143.8 0.8 fusion.22
  144.6 0.4 fusion.25
  145.0 0.5 copy-done.17
  145.5 0.2 maximum_multiply_fusion.2
  145.7 0.4 copy-done.28
  146.1 1.8 %fusion.56 = (f32[12,96,128]{2,1,0:T(8,128)}, f32[12,96,128]{2,1,0:T(8,128)S(1)}, f32[12,96,128]{2,1,0:T(8,128)}) fusion(f32[12,98,130]{2,1,0:T(8,128)S(1)} %get-tuple-element.50, f32[96]{0:T(128)S(1)} %copy-done.28, f32[12,98,130]{2,1,0:T(8,128)S(1)} %get-tuple-element.49), kind=kLoop, calls=%fused_computation.136 | loop fusion | flops 737280 | bytes 5308800 | tf_op jit(solution)/shard_map/slice | solution.py:163
  147.9 0.1 fusion.45
  148.1 0.9 maximum_multiply_fusion.4
  (65 shorter events, 0.3 us)
Async XLA Ops:
  7.2 1.0 copy-start
  7.2 3.5 %copy-start.6 = (f32[12,96,128]{2,1,0:T(8,128)S(1)}, f32[12,96,128]{2,1,0:T(8,128)}, u32[]{:S(2)}) copy-start(f32[12,96,128]{2,1,0:T(8,128)} %param.12) | copy-start | bytes 1769476
  7.2 3.5 %copy-start.11 = (f32[12,96,128]{2,1,0:T(8,128)S(1)}, f32[12,96,128]{2,1,0:T(8,128)}, u32[]{:S(2)}) copy-start(f32[12,96,128]{2,1,0:T(8,128)} %param.13) | copy-start | bytes 1769476
  7.2 77.2 %all-gather.2.cloned.1.call-start = ((), (), s32[]{:S(2)}) async-start(), calls=%async_computation | async-start | bytes 10027008 | tf_op jit(solution)/shard_map/all_gather | solution.py:113
  10.7 1.1 copy-start.12
  10.7 2.2 %copy-start.21 = (f32[96,128]{1,0:T(8,128)S(1)}, f32[96,128]{1,0:T(8,128)}, u32[]{:S(2)}) copy-start(f32[96,128]{1,0:T(8,128)} %param.16) | copy-start | bytes 147460
  10.7 2.2 %copy-start.22 = (f32[96,128]{1,0:T(8,128)S(1)}, f32[96,128]{1,0:T(8,128)}, u32[]{:S(2)}) copy-start(f32[96,128]{1,0:T(8,128)} %param.17) | copy-start | bytes 147460
  10.7 2.2 %copy-start.20 = (s32[96,128]{1,0:T(8,128)S(1)}, s32[96,128]{1,0:T(8,128)}, u32[]{:S(2)}) copy-start(s32[96,128]{1,0:T(8,128)} %param.18) | copy-start | bytes 147460
  15.6 21.0 %copy-start.5 = (f32[96,1536]{1,0:T(8,128)S(1)}, f32[96,1536]{1,0:T(8,128)}, u32[]{:S(2)}) copy-start(f32[96,1536]{1,0:T(8,128)} %param.20) | copy-start | bytes 1769476
  17.8 26.6 %collective-permute-start.1 = (f32[39,96,3]{1,0,2:T(8,128)S(1)}, f32[39,96,3]{1,0,2:T(8,128)S(1)}, u32[]{:S(2)}, u32[]{:S(2)}) collective-permute-start(f32[39,96,3]{1,0,2:T(8,128)S(1)} %copy.20), channel_id=1, source_target_pairs={{16,0},{32,16},{48,32},{64,48},{80,64},{96,80},{112,96},{128,112},... | collective-permute-start | bytes 134792 | tf_op jit(solution)/shard_map/ppermute | solution.py:30
  34.7 11.6 %collective-permute-start = (f32[39,96,3]{1,0,2:T(8,128)S(1)}, f32[39,96,3]{1,0,2:T(8,128)S(1)}, u32[]{:S(2)}, u32[]{:S(2)}) collective-permute-start(f32[39,96,3]{1,0,2:T(8,128)S(1)} %copy.19), channel_id=1, source_target_pairs={{0,16},{16,32},{32,48},{48,64},{64,80},{80,96},{96,112},{112,128},... | collective-permute-start | bytes 134792 | tf_op jit(solution)/shard_map/ppermute | solution.py:29
  37.3 67.7 %collective-permute-start.5 = (f32[3,1536]{1,0:T(4,128)}, f32[3,1536]{1,0:T(4,128)S(1)}, u32[]{:S(2)}, u32[]{:S(2)}) collective-permute-start(f32[3,1536]{1,0:T(4,128)} %get-tuple-element.44), channel_id=1, source_target_pairs={{1,0},{2,1},{3,2},{4,3},{5,4},{6,5},{7,6},{8,7},{9,8},{10,9},{11,1... | collective-permute-start | bytes 55304 | tf_op jit(solution)/shard_map/ppermute | solution.py:41
  39.8 65.2 %collective-permute-start.4 = (f32[3,1536]{1,0:T(4,128)}, f32[3,1536]{1,0:T(4,128)S(1)}, u32[]{:S(2)}, u32[]{:S(2)}) collective-permute-start(f32[3,1536]{1,0:T(4,128)} %get-tuple-element.43), channel_id=1, source_target_pairs={{0,1},{1,2},{2,3},{3,4},{4,5},{5,6},{6,7},{7,8},{8,9},{9,10},{10,1... | collective-permute-start | bytes 55304 | tf_op jit(solution)/shard_map/ppermute | solution.py:40
  48.3 12.7 %copy-start.3 = (f32[39,96,3]{2,1,0:T(8,128)S(1)}, f32[39,96,3]{2,1,0:T(8,128)}, u32[]{:S(2)}) copy-start(f32[39,96,3]{2,1,0:T(8,128)} %copy.22) | copy-start | bytes 134788
  48.3 12.7 %copy-start.4 = (f32[39,96,3]{2,1,0:T(8,128)S(1)}, f32[39,96,3]{2,1,0:T(8,128)}, u32[]{:S(2)}) copy-start(f32[39,96,3]{2,1,0:T(8,128)} %copy.21) | copy-start | bytes 134788
  49.9 10.4 %collective-permute-start.3 = (f32[39,3,134]{2,1,0:T(4,128)S(1)}, f32[39,3,134]{2,1,0:T(4,128)S(1)}, u32[]{:S(2)}, u32[]{:S(2)}) collective-permute-start(f32[39,3,134]{2,1,0:T(4,128)S(1)} %get-tuple-element.25), channel_id=1, source_target_pairs={{1,0},{2,1},{3,2},{4,3},{5,4},{6,5},{7,6},{8,7},{9,8},{10,9},{11,1... | collective-permute-start | bytes 188144 | tf_op jit(solution)/shard_map/ppermute | solution.py:41
  51.9 9.1 %collective-permute-start.2 = (f32[39,3,134]{2,1,0:T(4,128)S(1)}, f32[39,3,134]{2,1,0:T(4,128)S(1)}, u32[]{:S(2)}, u32[]{:S(2)}) collective-permute-start(f32[39,3,134]{2,1,0:T(4,128)S(1)} %get-tuple-element.24), channel_id=1, source_target_pairs={{0,1},{1,2},{2,3},{3,4},{4,5},{5,6},{6,7},{7,8},{8,9},{9,10},{10,1... | collective-permute-start | bytes 188144 | tf_op jit(solution)/shard_map/ppermute | solution.py:40
  64.4 3.0 %copy-start.2 = (f32[39,102,134]{2,1,0:T(8,128)}, f32[39,102,134]{2,1,0:T(8,128)S(1)}, u32[]{:S(2)}) copy-start(f32[39,102,134]{2,1,0:T(8,128)S(1)} %pad_maximum_fusion) | copy-start | bytes 6396628
  106.4 26.6 %collective-permute-start.7 = (f32[12,102,3]{1,0,2:T(8,128)}, f32[12,102,3]{1,0,2:T(8,128)}, u32[]{:S(2)}, u32[]{:S(2)}) collective-permute-start(f32[12,102,3]{1,0,2:T(8,128)} %convolution_bitcast_fusion.1), channel_id=1, source_target_pairs={{16,0},{32,16},{48,32},{64,48},{80,64},{96,80},{112,96},{128,112},... | collective-permute-start | bytes 44072 | tf_op jit(solution)/shard_map/ppermute | solution.py:131
  121.9 12.2 %collective-permute-start.6 = (f32[12,102,3]{1,0,2:T(8,128)}, f32[12,102,3]{1,0,2:T(8,128)S(1)}, u32[]{:S(2)}, u32[]{:S(2)}) collective-permute-start(f32[12,102,3]{1,0,2:T(8,128)} %convolution_bitcast_fusion.2), channel_id=1, source_target_pairs={{0,16},{16,32},{32,48},{48,64},{64,80},{80,96},{96,112},{112,128},... | collective-permute-start | bytes 44072 | tf_op jit(solution)/shard_map/ppermute | solution.py:130
  135.2 2.3 %copy-start.14 = (f32[100,132]{1,0:T(8,128)S(1)}, f32[100,132]{1,0:T(8,128)}, u32[]{:S(2)}) copy-start(f32[100,132]{1,0:T(8,128)} %get-tuple-element.59) | copy-start | bytes 158404
  135.2 2.3 %copy-start.15 = (f32[100,132]{1,0:T(8,128)S(1)}, f32[100,132]{1,0:T(8,128)}, u32[]{:S(2)}) copy-start(f32[100,132]{1,0:T(8,128)} %get-tuple-element.60) | copy-start | bytes 158404
  135.2 2.3 %copy-start.29 = (f32[100]{0:T(128)S(1)}, f32[100]{0:T(128)}, u32[]{:S(2)}) copy-start(f32[100]{0:T(128)} %slice_multiply_fusion.8) | copy-start | bytes 1204
  137.5 1.2 copy-start.9
  137.6 1.2 copy-start.10
  137.6 1.2 copy-start.19
  137.6 1.2 copy-start.23
  137.6 1.2 copy-start.24
  137.6 1.2 copy-start.25
  137.6 1.2 copy-start.26
  139.6 0.9 copy-start.18
  140.7 2.1 %copy-start.13 = (f32[98,130]{1,0:T(8,128)S(1)}, f32[98,130]{1,0:T(8,128)}, u32[]{:S(2)}) copy-start(f32[98,130]{1,0:T(8,128)} %get-tuple-element.67) | copy-start | bytes 152884
  142.8 0.9 copy-start.7
  142.8 0.9 copy-start.8
  142.8 1.0 copy-start.16
  144.6 0.9 copy-start.17
  145.5 0.6 copy-start.28
  146.1 1.9 %copy-start.27 = (f32[6]{0:T(128)S(1)}, f32[6]{0:T(128)}, u32[]{:S(2)}) copy-start(f32[6]{0:T(128)} %constant.12) | copy-start | bytes 76
  146.1 2.8 %copy-start.1 = (f32[128,128]{1,0:T(8,128)S(1)}, f32[128,128]{1,0:T(8,128)}, u32[]{:S(2)}) copy-start(f32[128,128]{1,0:T(8,128)} %param.19) | copy-start | bytes 196612
Sparse Core Ops, SparseCore 0:
  10.8 73.6 all-gather.1

commit v4 on v1

--- a/solution.py
+++ b/solution.py
@@ -110,15 +110,32 @@
     wet_frac = wet_mask.astype(jnp.float32)
     source = wet_frac * elevation
     mixed = jnp.einsum("krj,cj->krc", source, lon_green, precision=lax.Precision.HIGHEST)
-    gathered = lax.all_gather(mixed, LAT, axis=1, tiled=True)
+    columns = mixed.shape[2]
+    edge_rows = jnp.concatenate([lon_green[:HALO], lon_green[columns - HALO :]], axis=0)
+    edges = jnp.einsum("ej,krj->ker", edge_rows, source, precision=lax.Precision.HIGHEST)
+    spare = 8 * ((2 * HALO + 7) // 8)
+    edges = jnp.pad(edges, ((0, 0), (0, spare - 2 * HALO), (0, columns - rows_here)))
+    packed = jnp.concatenate([mixed, edges], axis=1)
+    gathered = lax.all_gather(packed, LAT, axis=1, tiled=True)
 
     fields = jnp.stack([ocean_depth, bottom_drag, wet_frac], axis=0)
     stack = jnp.concatenate([elevation - equilibrium, transport_u, transport_v, fields], axis=0)
     stack = widen_lat(widen_lon(stack, HALO, 2), HALO, 1)
     green_ext = widen_lat(lat_green, HALO, 0)
 
-    sal = jnp.einsum("rs,ksc->krc", green_ext, gathered, precision=lax.Precision.HIGHEST)
-    sal = widen_lon(sal, HALO, 2)
+    blocks = lat_size()
+    block = rows_here + spare
+    green_blocks = green_ext.reshape(green_ext.shape[0], blocks, rows_here)
+    lanes = gathered.reshape(12, blocks, block, columns)[:, :, rows_here : rows_here + 2 * HALO, :rows_here]
+    edge_sal = jnp.einsum("rbj,kbej->kre", green_blocks, lanes, precision=lax.Precision.HIGHEST)
+    size = lax.axis_size("lon")
+    up = [(i, (i + 1) % size) for i in range(size)]
+    down = [(j, i) for i, j in up]
+    before = lax.ppermute(edge_sal[:, :, HALO:], "lon", up)
+    after = lax.ppermute(edge_sal[:, :, :HALO], "lon", down)
+    green_pad = jnp.pad(green_blocks, ((0, 0), (0, 0), (0, spare))).reshape(green_ext.shape[0], -1)
+    sal = jnp.einsum("rs,ksc->krc", green_pad, gathered, precision=lax.Precision.HIGHEST)
+    sal = jnp.concatenate([before, sal, after], axis=2)
     potential = stack[:12] - sal
     flows = stack[12:36]
     depth_ext, drag_ext, wet_ext = stack[36], stack[37], stack[38]

time: 140 us -> 137 us (0.979)
  local copies, waits for them, and re-layouts: 26.6 us -> 20.5 us
  waiting for transfers between devices: 23.1 us -> 18.5 us
  other arithmetic: 24.3 us -> 28.6 us
  matrix products: 11 us -> 13.5 us
    ppermute x0 -> x2, starting transfers between devices: none -> 10.9 us  [the longest x1 6.9 us: per_device(): after = lax.ppermute(edge_sal[:, :, :HALO], 'lon', down)]
    ppermute x2 -> x1, starting transfers between devices: 17.9 us -> 10 us  [widen_lon(): after = lax.ppermute(initial, 'lon', down)]
    dot_general x1 -> x3, matrix products: 8.49 us -> 11.8 us  [the longest x1 9.34 us: per_device(): jnp.einsum('rs,ksc->krc', green_pad, gathered, precision=lax.Precision.HI...]
    slice x4 -> x2, local copies, waits for them, and re-layouts: 8.02 us -> 4.77 us  [widen_lon(): last = lax.slice_in_dim(array, length - width, length, axis=dim)]
    ppermute x2 -> x1, waiting for transfers between devices: 7.03 us -> 4 us  [widen_lon(): before = lax.ppermute(last, 'lon', up)]
    ppermute x0 -> x2, local copies, waits for them, and re-layouts: none -> 2.26 us  [the longest x1 1.13 us: per_device(): before = lax.ppermute(edge_sal[:, :, HALO:], 'lon', up)]
    ppermute x2 -> x1, starting transfers between devices: 4.03 us -> 1.92 us  [widen_lon(): before = lax.ppermute(last, 'lon', up)]
    slice x0 -> x3, local copies, waits for them, and re-layouts: none -> 2.03 us  [the longest x1 1.26 us: per_device(): gathered.reshape(12, blocks, block, columns)]
  transfers between devices with their start and end apart: 9 -> 9, of which waited for: 5 -> 4; matrix products, arithmetic and copies ran while one was open for 22% -> 30% of each run, Pallas kernels for 0% -> 0%
where the time goes in v4:
time: 137 us; the launch traced here: 136 us
  starting transfers between devices  40 us (29%)
  other arithmetic  28.6 us (21%)
  local copies, waits for them, and re-layouts  20.5 us (15%)
  waiting for transfers between devices  18.5 us (14%)
  between operations  14.7 us (11%)
  matrix products  13.5 us (10%)
    ppermute x1, starting transfers between devices, widen_lon(): after = lax.ppermute(initial, 'lon', down)  10 us
    ppermute x2, starting transfers between devices, widen_lat(): before = lax.ppermute(last, LAT, up)  9.59 us
    dot_general x1, matrix products, per_device(): jnp.einsum('rs,ksc->krc', green_pad, gathered, precision=lax.Precision.HI...  9.34 us
    ppermute x2, starting transfers between devices, widen_lat(): after = lax.ppermute(initial, LAT, down)  7.52 us
    all_gather x1, waiting for transfers between devices, per_device(): gathered = lax.all_gather(packed, LAT, axis=1, tiled=True)  7.14 us
    ppermute x1, starting transfers between devices, per_device(): after = lax.ppermute(edge_sal[:, :, :HALO], 'lon', down)  6.9 us
    ppermute x2, waiting for transfers between devices, widen_lat(): after = lax.ppermute(initial, LAT, down)  4.93 us
    slice x2, local copies, waits for them, and re-layouts, widen_lon(): last = lax.slice_in_dim(array, length - width, length, axis=dim)  4.77 us
  transfers between devices with their start and end apart: 9, of which 4 were waited for; matrix products, arithmetic and copies ran while one was open for 30% of the time, Pallas kernels for 0%

profile of v4, /device:TPU:1, one launch (start us, length us, event | category | flops | bytes accessed | tf_op | source)
XLA Modules:
  0.0 135.8 jit_solution(12874723545811327905)
XLA Ops:
  7.2 0.0 all-gather.2.cloned.1.call-start
  7.2 0.8 fusion.60
  8.0 0.8 convert_element_type.10
  8.8 1.7 %fusion.45 = f32[12,96,128]{2,1,0:T(8,128)S(1)} fusion(f32[12,96,128]{2,1,0:T(8,128)} %param.12, f32[96,128]{1,0:T(8,128)S(1)} %convert_element_type.10, f32[128,128]{1,0:T(8,128)} %param.19), kind=kOutput, calls=%fused_computation.99 | convolution fusion | flops 226639872 | bytes 1294336 | tf_op jit(solution)/shard_map/krj,cj->krc/dot_general | solution.py:112
  10.5 1.2 convolution_bitcast_fusion.2
  11.7 0.9 select_maximum_fusion
  12.7 4.6 %collective-permute-start.4 = (f32[3,1536]{1,0:T(4,128)S(1)}, f32[3,1536]{1,0:T(4,128)S(1)}, u32[]{:S(2)}, u32[]{:S(2)}) collective-permute-start(f32[3,1536]{1,0:T(4,128)S(1)} %get-tuple-element.41), channel_id=1, source_target_pairs={{0,1},{1,2},{2,3},{3,4},{4,5},{5,6},{6,7},{7,8},{8,9},{9,10},{10,1... | collective-permute-start | bytes 55304 | tf_op jit(solution)/shard_map/ppermute | solution.py:40
  17.3 5.6 %collective-permute-start.5 = (f32[3,1536]{1,0:T(4,128)S(1)}, f32[3,1536]{1,0:T(4,128)S(1)}, u32[]{:S(2)}, u32[]{:S(2)}) collective-permute-start(f32[3,1536]{1,0:T(4,128)S(1)} %get-tuple-element.42), channel_id=1, source_target_pairs={{1,0},{2,1},{3,2},{4,3},{5,4},{6,5},{7,6},{8,7},{9,8},{10,9},{11,1... | collective-permute-start | bytes 55304 | tf_op jit(solution)/shard_map/ppermute | solution.py:41
  22.9 1.1 subtract_dynamic-update-slice_fusion
  24.1 1.1 constant_dynamic-update-slice_fusion.1
  25.4 2.6 %fusion.57 = (f32[39,96,3]{2,1,0:T(8,128)}, f32[39,96,3]{2,1,0:T(8,128)}) fusion(f32[39,96,128]{2,1,0:T(8,128)S(1)} %bitcast_dynamic-update-slice_fusion), kind=kLoop, calls=%fused_computation.140 | loop fusion | bytes 179712 | tf_op jit(solution)/shard_map/slice | solution.py:27
  28.0 2.1 %copy.21 = f32[39,96,3]{1,0,2:T(8,128)S(1)} copy(f32[39,96,3]{2,1,0:T(8,128)} %get-tuple-element.35) | data formatting | bytes 89856 | tf_op jit(solution)/shard_map/slice | solution.py:28
  30.1 10.0 %collective-permute-start.1 = (f32[39,96,3]{1,0,2:T(8,128)S(1)}, f32[39,96,3]{1,0,2:T(8,128)S(1)}, u32[]{:S(2)}, u32[]{:S(2)}) collective-permute-start(f32[39,96,3]{1,0,2:T(8,128)S(1)} %copy.21), channel_id=1, source_target_pairs={{16,0},{32,16},{48,32},{64,48},{80,64},{96,80},{112,96},{128,112},... | collective-permute-start | bytes 134792 | tf_op jit(solution)/shard_map/ppermute | solution.py:30
  40.2 2.1 %copy.20 = f32[39,96,3]{1,0,2:T(8,128)S(1)} copy(f32[39,96,3]{2,1,0:T(8,128)} %get-tuple-element.34) | data formatting | bytes 89856 | tf_op jit(solution)/shard_map/slice | solution.py:27
  42.3 1.9 %collective-permute-start = (f32[39,96,3]{1,0,2:T(8,128)S(1)}, f32[39,96,3]{1,0,2:T(8,128)S(1)}, u32[]{:S(2)}, u32[]{:S(2)}) collective-permute-start(f32[39,96,3]{1,0,2:T(8,128)S(1)} %copy.20), channel_id=1, source_target_pairs={{0,16},{16,32},{32,48},{48,64},{64,80},{80,96},{96,112},{112,128},... | collective-permute-start | bytes 134792 | tf_op jit(solution)/shard_map/ppermute | solution.py:29
  44.3 0.1 cosine_divide_fusion
  44.3 0.7 slice_multiply_fusion.7
  45.0 0.7 fusion.62
  45.7 0.7 broadcast_multiply_fusion.4
  46.3 0.7 slice_multiply_fusion.8
  47.0 4.0 %collective-permute-done = f32[39,96,3]{1,0,2:T(8,128)S(1)} collective-permute-done((f32[39,96,3]{1,0,2:T(8,128)S(1)}, f32[39,96,3]{1,0,2:T(8,128)S(1)}, u32[]{:S(2)}, u32[]{:S(2)}) %collective-permute-start) | collective-permute-done | bytes 44960 | tf_op jit(solution)/shard_map/ppermute | solution.py:29
  51.0 1.9 %copy.22 = f32[39,96,3]{2,1,0:T(8,128)} copy(f32[39,96,3]{1,0,2:T(8,128)S(1)} %collective-permute-done) | data formatting | bytes 89856 | tf_op jit(solution)/shard_map/ppermute | solution.py:29
  52.9 1.9 %copy.23 = f32[39,96,3]{2,1,0:T(8,128)} copy(f32[39,96,3]{1,0,2:T(8,128)S(1)} %collective-permute-done.1) | data formatting | bytes 89856 | tf_op jit(solution)/shard_map/ppermute | solution.py:30
  54.8 2.2 %pad_maximum_fusion.5 = (f32[39,3,134]{2,1,0:T(4,128)}, f32[39,3,134]{2,1,0:T(4,128)}) fusion(f32[39,96,3]{2,1,0:T(8,128)} %copy.23, f32[39,96,128]{2,1,0:T(8,128)S(1)} %bitcast_dynamic-update-slice_fusion, f32[39,96,3]{2,1,0:T(8,128)} %copy.22), kind=kLoop, calls=%fused_computation.108 | loop fusion | flops 62712 | bytes 2132208 | tf_op jit(solution)/shard_map/slice | solution.py:38
  57.0 5.0 %collective-permute-start.2 = (f32[39,3,134]{2,1,0:T(4,128)}, f32[39,3,134]{2,1,0:T(4,128)S(1)}, u32[]{:S(2)}, u32[]{:S(2)}) collective-permute-start(f32[39,3,134]{2,1,0:T(4,128)} %get-tuple-element.22), channel_id=1, source_target_pairs={{0,1},{1,2},{2,3},{3,4},{4,5},{5,6},{6,7},{7,8},{8,9},{9,10},{10,1... | collective-permute-start | bytes 188144 | tf_op jit(solution)/shard_map/ppermute | solution.py:40
  62.0 1.9 %collective-permute-start.3 = (f32[39,3,134]{2,1,0:T(4,128)}, f32[39,3,134]{2,1,0:T(4,128)}, u32[]{:S(2)}, u32[]{:S(2)}) collective-permute-start(f32[39,3,134]{2,1,0:T(4,128)} %get-tuple-element.23), channel_id=1, source_target_pairs={{1,0},{2,1},{3,2},{4,3},{5,4},{6,5},{7,6},{8,7},{9,8},{10,9},{11,1... | collective-permute-start | bytes 188144 | tf_op jit(solution)/shard_map/ppermute | solution.py:41
  63.9 0.1 pad_maximum_fusion.2
  64.0 0.3 copy.25
  64.3 1.0 pad.9
  65.3 2.4 %collective-permute-done.2 = f32[39,3,134]{2,1,0:T(4,128)S(1)} collective-permute-done((f32[39,3,134]{2,1,0:T(4,128)}, f32[39,3,134]{2,1,0:T(4,128)S(1)}, u32[]{:S(2)}, u32[]{:S(2)}) %collective-permute-start.2) | collective-permute-done | bytes 62744 | tf_op jit(solution)/shard_map/ppermute | solution.py:40
  67.7 4.9 %collective-permute-done.3 = f32[39,3,134]{2,1,0:T(4,128)} collective-permute-done((f32[39,3,134]{2,1,0:T(4,128)}, f32[39,3,134]{2,1,0:T(4,128)}, u32[]{:S(2)}, u32[]{:S(2)}) %collective-permute-start.3) | collective-permute-done | bytes 62744 | tf_op jit(solution)/shard_map/ppermute | solution.py:41
  72.6 1.3 maximum_bitcast_fusion.2
  73.9 0.7 slice.284
  74.6 0.8 slice.274
  75.4 2.6 %pad_maximum_fusion = f32[39,102,134]{2,1,0:T(8,128)S(1)} fusion(f32[39,3,134]{2,1,0:T(4,128)} %collective-permute-done.3, f32[39,96,3]{2,1,0:T(8,128)S(1)} %copy-done.2, f32[39,96,128]{2,1,0:T(8,128)S(1)} %bitcast_dynamic-update-slice_fusion, f32[39,96,3]{2,1,0:T(8,128)S(1)} %copy-done.1, f32[39,3,134]{2,1,0:T(4,128)S(1)} %collective-permute-done.2), kind=kLoop, calls=%fused_computation | loop fusion | flops 2132208 | bytes 4264416 | tf_op jit(solution)/shard_map/concatenate | solution.py:42
  78.0 0.9 slice_negate_fusion.1
  78.9 1.2 slice_add_fusion.3
  80.1 0.8 slice_add_fusion.4
  80.9 2.1 %slice_add_fusion = f32[24,100,132]{2,1,0:T(8,128)S(1)} fusion(f32[39,102,134]{2,1,0:T(8,128)S(1)} %pad_maximum_fusion), kind=kLoop, calls=%fused_computation.14 | loop fusion | flops 950400 | bytes 6336000 | tf_op jit(solution)/shard_map/add | solution.py:79
  83.0 7.1 %all-gather.2.cloned.1.call-done = f32[12,1664,128]{2,1,0:T(8,128)} async-done(((f32[12,104,128]{2,1,0:T(8,128)}), f32[12,1664,128]{2,1,0:T(8,128)}) %all-gather.2.cloned.1.call-update) | async-done | bytes 10223632 | tf_op jit(solution)/shard_map/all_gather | solution.py:119
  90.2 1.3 slice.278
  91.4 1.3 convolution_bitcast_fusion.1
  92.7 4.0 %collective-permute-start.6 = (f32[12,102,3]{1,0,2:T(8,128)S(1)}, f32[12,102,3]{1,0,2:T(8,128)S(1)}, u32[]{:S(2)}, u32[]{:S(2)}) collective-permute-start(f32[12,102,3]{1,0,2:T(8,128)S(1)} %get-tuple-element.61), channel_id=1, source_target_pairs={{0,16},{16,32},{32,48},{48,64},{64,80},{80,96},{96,112},{112,128},... | collective-permute-start | bytes 44072 | tf_op jit(solution)/shard_map/ppermute | solution.py:134
  96.7 6.9 %collective-permute-start.7 = (f32[12,102,3]{1,0,2:T(8,128)S(1)}, f32[12,102,3]{1,0,2:T(8,128)S(1)}, u32[]{:S(2)}, u32[]{:S(2)}) collective-permute-start(f32[12,102,3]{1,0,2:T(8,128)S(1)} %get-tuple-element.62), channel_id=1, source_target_pairs={{16,0},{32,16},{48,32},{64,48},{80,64},{96,80},{112,96},{128,112},... | collective-permute-start | bytes 44072 | tf_op jit(solution)/shard_map/ppermute | solution.py:135
  103.6 9.3 %convolution_bitcast_fusion = f32[12,102,128]{2,1,0:T(8,128)S(1)} fusion(f32[12,1664,128]{2,1,0:T(8,128)} %all-gather.2.cloned.1.call-done, f32[102,1664,1]{0,1,2:T(8,128)S(1)} %bitcast.40), kind=kOutput, calls=%fused_computation.46 | convolution fusion | flops 3128426496 | bytes 11529216 | tf_op jit(solution)/shard_map/rs,ksc->krc/dot_general | solution.py:137
  113.0 1.1 copy.28
  114.1 1.1 copy.27
  115.3 2.3 %slice_subtract_fusion.2 = f32[12,102,134]{2,1,0:T(8,128)S(1)} fusion(f32[39,102,134]{2,1,0:T(8,128)} %copy-done, f32[12,102,3]{2,1,0:T(8,128)} %copy.28, f32[12,102,128]{2,1,0:T(8,128)S(1)} %convolution_bitcast_fusion, f32[12,102,3]{2,1,0:T(8,128)} %copy.27), kind=kLoop, calls=%fused_computation.41 | loop fusion | flops 492048 | bytes 1968192 | tf_op jit(solution)/shard_map/sub | solution.py:139
  117.6 1.1 fusion.10
  118.8 0.8 fusion.19
  119.7 0.4 fusion.21
  120.1 0.5 copy-done.16
  120.5 0.2 maximum_multiply_fusion.1
  120.7 2.1 %fusion.2 = f32[24,98,130]{2,1,0:T(8,128)S(1)} fusion(f32[12,100,132]{2,1,0:T(8,128)S(1)} %get-tuple-element.53, f32[12,100,132]{2,1,0:T(8,128)S(1)} %get-tuple-element.52), kind=kLoop, calls=%fused_computation.9 | loop fusion | flops 2140320 | bytes 2490240 | tf_op jit(solution)/shard_map/add | solution.py:79
  122.8 0.8 fusion.6
  123.7 0.0 copy-done.14
  123.7 0.8 fusion.23
  124.5 0.4 fusion.26
  125.0 0.5 copy-done.15
  125.4 0.2 maximum_multiply_fusion.2
  125.6 0.5 copy-done.30
  126.1 1.8 %fusion.58 = (f32[12,96,128]{2,1,0:T(8,128)}, f32[12,96,128]{2,1,0:T(8,128)S(1)}, f32[12,96,128]{2,1,0:T(8,128)}) fusion(f32[12,98,130]{2,1,0:T(8,128)S(1)} %get-tuple-element.48, f32[96]{0:T(128)S(1)} %copy-done.30, f32[12,98,130]{2,1,0:T(8,128)S(1)} %get-tuple-element.47), kind=kLoop, calls=%fused_computation.141 | loop fusion | flops 737280 | bytes 5308800 | tf_op jit(solution)/shard_map/slice | solution.py:168
  128.0 0.1 fusion.47
  128.1 0.9 maximum_multiply_fusion.4
  (73 shorter events, 0.3 us)
Async XLA Ops:
  7.2 3.4 %copy-start.3 = (f32[12,96,128]{2,1,0:T(8,128)S(1)}, f32[12,96,128]{2,1,0:T(8,128)}, u32[]{:S(2)}) copy-start(f32[12,96,128]{2,1,0:T(8,128)} %param.12) | copy-start | bytes 1769476
  7.2 83.0 %all-gather.2.cloned.1.call-start = ((), (), s32[]{:S(2)}) async-start(), calls=%async_computation | async-start | bytes 10862592 | tf_op jit(solution)/shard_map/all_gather | solution.py:119
  8.8 1.7 %copy-start.7 = (f32[96,128]{1,0:T(8,128)}, f32[96,128]{1,0:T(8,128)S(1)}, u32[]{:S(2)}) copy-start(f32[96,128]{1,0:T(8,128)S(1)} %convert_element_type.10) | copy-start | bytes 147460
  10.5 2.1 %copy-start.9 = (f32[96,1536]{1,0:T(8,128)S(1)}, f32[96,1536]{1,0:T(8,128)}, u32[]{:S(2)}) copy-start(f32[96,1536]{1,0:T(8,128)} %param.20) | copy-start | bytes 1769476
  12.7 51.2 %collective-permute-start.4 = (f32[3,1536]{1,0:T(4,128)S(1)}, f32[3,1536]{1,0:T(4,128)S(1)}, u32[]{:S(2)}, u32[]{:S(2)}) collective-permute-start(f32[3,1536]{1,0:T(4,128)S(1)} %get-tuple-element.41), channel_id=1, source_target_pairs={{0,1},{1,2},{2,3},{3,4},{4,5},{5,6},{6,7},{7,8},{8,9},{9,10},{10,1... | collective-permute-start | bytes 55304 | tf_op jit(solution)/shard_map/ppermute | solution.py:40
  17.3 7.9 %copy-start.10 = (f32[12,96,128]{2,1,0:T(8,128)S(1)}, f32[12,96,128]{2,1,0:T(8,128)}, u32[]{:S(2)}) copy-start(f32[12,96,128]{2,1,0:T(8,128)} %param.15) | copy-start | bytes 1769476
  17.3 46.6 %collective-permute-start.5 = (f32[3,1536]{1,0:T(4,128)S(1)}, f32[3,1536]{1,0:T(4,128)S(1)}, u32[]{:S(2)}, u32[]{:S(2)}) collective-permute-start(f32[3,1536]{1,0:T(4,128)S(1)} %get-tuple-element.42), channel_id=1, source_target_pairs={{1,0},{2,1},{3,2},{4,3},{5,4},{6,5},{7,6},{8,7},{9,8},{10,9},{11,1... | collective-permute-start | bytes 55304 | tf_op jit(solution)/shard_map/ppermute | solution.py:41
  24.0 1.2 copy-start.19
  24.1 1.3 copy-start.20
  24.1 1.3 copy-start.18
  30.1 22.7 %collective-permute-start.1 = (f32[39,96,3]{1,0,2:T(8,128)S(1)}, f32[39,96,3]{1,0,2:T(8,128)S(1)}, u32[]{:S(2)}, u32[]{:S(2)}) collective-permute-start(f32[39,96,3]{1,0,2:T(8,128)S(1)} %copy.21), channel_id=1, source_target_pairs={{16,0},{32,16},{48,32},{64,48},{80,64},{96,80},{112,96},{128,112},... | collective-permute-start | bytes 134792 | tf_op jit(solution)/shard_map/ppermute | solution.py:30
  42.3 8.7 %collective-permute-start = (f32[39,96,3]{1,0,2:T(8,128)S(1)}, f32[39,96,3]{1,0,2:T(8,128)S(1)}, u32[]{:S(2)}, u32[]{:S(2)}) collective-permute-start(f32[39,96,3]{1,0,2:T(8,128)S(1)} %copy.20), channel_id=1, source_target_pairs={{0,16},{16,32},{32,48},{48,64},{64,80},{80,96},{96,112},{112,128},... | collective-permute-start | bytes 134792 | tf_op jit(solution)/shard_map/ppermute | solution.py:29
  57.0 10.7 %collective-permute-start.2 = (f32[39,3,134]{2,1,0:T(4,128)}, f32[39,3,134]{2,1,0:T(4,128)S(1)}, u32[]{:S(2)}, u32[]{:S(2)}) collective-permute-start(f32[39,3,134]{2,1,0:T(4,128)} %get-tuple-element.22), channel_id=1, source_target_pairs={{0,1},{1,2},{2,3},{3,4},{4,5},{5,6},{6,7},{7,8},{8,9},{9,10},{10,1... | collective-permute-start | bytes 188144 | tf_op jit(solution)/shard_map/ppermute | solution.py:40
  62.0 10.6 %collective-permute-start.3 = (f32[39,3,134]{2,1,0:T(4,128)}, f32[39,3,134]{2,1,0:T(4,128)}, u32[]{:S(2)}, u32[]{:S(2)}) collective-permute-start(f32[39,3,134]{2,1,0:T(4,128)} %get-tuple-element.23), channel_id=1, source_target_pairs={{1,0},{2,1},{3,2},{4,3},{5,4},{6,5},{7,6},{8,7},{9,8},{10,9},{11,1... | collective-permute-start | bytes 188144 | tf_op jit(solution)/shard_map/ppermute | solution.py:41
  72.6 2.8 %copy-start.1 = (f32[39,96,3]{2,1,0:T(8,128)S(1)}, f32[39,96,3]{2,1,0:T(8,128)}, u32[]{:S(2)}) copy-start(f32[39,96,3]{2,1,0:T(8,128)} %copy.22) | copy-start | bytes 134788
  72.6 2.8 %copy-start.2 = (f32[39,96,3]{2,1,0:T(8,128)S(1)}, f32[39,96,3]{2,1,0:T(8,128)}, u32[]{:S(2)}) copy-start(f32[39,96,3]{2,1,0:T(8,128)} %copy.23) | copy-start | bytes 134788
  78.0 2.9 %copy-start = (f32[39,102,134]{2,1,0:T(8,128)}, f32[39,102,134]{2,1,0:T(8,128)S(1)}, u32[]{:S(2)}) copy-start(f32[39,102,134]{2,1,0:T(8,128)S(1)} %pad_maximum_fusion) | copy-start | bytes 6396628
  90.2 13.4 %copy-start.4 = (f32[102,16,104]{0,2,1:T(8,128)S(1)}, f32[102,16,104]{0,2,1:T(8,128)}, u32[]{:S(2)}) copy-start(f32[102,16,104]{0,2,1:T(8,128)} %pad.9) | copy-start | bytes 2036740
  92.7 21.4 %collective-permute-start.6 = (f32[12,102,3]{1,0,2:T(8,128)S(1)}, f32[12,102,3]{1,0,2:T(8,128)S(1)}, u32[]{:S(2)}, u32[]{:S(2)}) collective-permute-start(f32[12,102,3]{1,0,2:T(8,128)S(1)} %get-tuple-element.61), channel_id=1, source_target_pairs={{0,16},{16,32},{32,48},{48,64},{64,80},{80,96},{96,112},{112,128},... | collective-permute-start | bytes 44072 | tf_op jit(solution)/shard_map/ppermute | solution.py:134
  96.7 16.3 %collective-permute-start.7 = (f32[12,102,3]{1,0,2:T(8,128)S(1)}, f32[12,102,3]{1,0,2:T(8,128)S(1)}, u32[]{:S(2)}, u32[]{:S(2)}) collective-permute-start(f32[12,102,3]{1,0,2:T(8,128)S(1)} %get-tuple-element.62), channel_id=1, source_target_pairs={{16,0},{32,16},{48,32},{64,48},{80,64},{96,80},{112,96},{128,112},... | collective-permute-start | bytes 44072 | tf_op jit(solution)/shard_map/ppermute | solution.py:135
  115.2 2.3 %copy-start.12 = (f32[100,132]{1,0:T(8,128)S(1)}, f32[100,132]{1,0:T(8,128)}, u32[]{:S(2)}) copy-start(f32[100,132]{1,0:T(8,128)} %get-tuple-element.57) | copy-start | bytes 158404
  115.2 2.3 %copy-start.13 = (f32[100,132]{1,0:T(8,128)S(1)}, f32[100,132]{1,0:T(8,128)}, u32[]{:S(2)}) copy-start(f32[100,132]{1,0:T(8,128)} %get-tuple-element.58) | copy-start | bytes 158404
  115.2 2.3 %copy-start.31 = (f32[100]{0:T(128)S(1)}, f32[100]{0:T(128)}, u32[]{:S(2)}) copy-start(f32[100]{0:T(128)} %slice_multiply_fusion.8) | copy-start | bytes 1204
  117.5 1.2 copy-start.5
  117.6 1.2 copy-start.6
  117.6 1.2 copy-start.17
  117.6 1.2 copy-start.21
  117.6 1.2 copy-start.22
  117.6 1.2 copy-start.24
  117.6 1.2 copy-start.27
  117.6 1.2 copy-start.28
  119.6 0.9 copy-start.16
  120.7 2.1 %copy-start.11 = (f32[98,130]{1,0:T(8,128)S(1)}, f32[98,130]{1,0:T(8,128)}, u32[]{:S(2)}) copy-start(f32[98,130]{1,0:T(8,128)} %get-tuple-element.69) | copy-start | bytes 152884
  122.8 0.9 copy-start.14
  122.8 0.9 copy-start.23
  122.8 0.9 copy-start.25
  122.8 0.9 copy-start.26
  124.5 0.9 copy-start.15
  125.4 0.7 copy-start.30
  126.1 1.9 %copy-start.29 = (f32[6]{0:T(128)S(1)}, f32[6]{0:T(128)}, u32[]{:S(2)}) copy-start(f32[6]{0:T(128)} %constant.48) | copy-start | bytes 76
  126.1 2.0 %copy-start.8 = (f32[96,128]{1,0:T(8,128)S(1)}, f32[96,128]{1,0:T(8,128)}, u32[]{:S(2)}) copy-start(f32[96,128]{1,0:T(8,128)} %copy-done.7) | copy-start | bytes 147460
Sparse Core Ops, SparseCore 0:
  12.8 77.3 all-gather.1

commit v5 on v1

--- a/solution.py
+++ b/solution.py
@@ -117,8 +117,26 @@
     stack = widen_lat(widen_lon(stack, HALO, 2), HALO, 1)
     green_ext = widen_lat(lat_green, HALO, 0)
 
+    columns = mixed.shape[2]
+    edge_rows = jnp.concatenate([lon_green[:HALO], lon_green[columns - HALO :]], axis=0)
+    edges = jnp.einsum("ej,krj->ker", edge_rows, source, precision=lax.Precision.HIGHEST)
+    size = lax.axis_size("lon")
+    up = [(i, (i + 1) % size) for i in range(size)]
+    down = [(j, i) for i, j in up]
+    near_edges = jnp.concatenate(
+        [lax.ppermute(edges[:, HALO:], "lon", up), lax.ppermute(edges[:, :HALO], "lon", down)], axis=1
+    )
+    near_edges = lax.all_gather(near_edges, LAT, axis=2, tiled=True)
+    green_before = lax.ppermute(green_ext, "lon", up)
+    green_after = lax.ppermute(green_ext, "lon", down)
     sal = jnp.einsum("rs,ksc->krc", green_ext, gathered, precision=lax.Precision.HIGHEST)
-    sal = widen_lon(sal, HALO, 2)
+    sal_before = jnp.einsum(
+        "rs,kes->kre", green_before, near_edges[:, :HALO], precision=lax.Precision.HIGHEST
+    )
+    sal_after = jnp.einsum(
+        "rs,kes->kre", green_after, near_edges[:, HALO:], precision=lax.Precision.HIGHEST
+    )
+    sal = jnp.concatenate([sal_before, sal, sal_after], axis=2)
     potential = stack[:12] - sal
     flows = stack[12:36]
     depth_ext, drag_ext, wet_ext = stack[36], stack[37], stack[38]

time: 140 us -> 213 us (1.52)
  the two profiles are of different devices: /device:TPU:1 before, /device:TPU:3 now
where the time goes in v5:
time: 213 us
  blocking collectives  68.2 us (32%)
  starting transfers between devices  44.3 us (21%)
  other arithmetic  24.2 us (11%)
  local copies, waits for them, and re-layouts  23.6 us (11%)
  matrix products  22 us (10%)
  waiting for transfers between devices  15.6 us (7%)
  between operations  14.7 us (7%)
    all_gather x1, blocking collectives, per_device(): near_edges = lax.all_gather(near_edges, LAT, axis=2, tiled=True)  68.2 us
    ppermute x1, waiting for transfers between devices, per_device(): green_after = lax.ppermute(green_ext, 'lon', down)  15.6 us
    ppermute x1, starting transfers between devices, widen_lon(): after = lax.ppermute(initial, 'lon', down)  12.7 us
    dot_general x1, matrix products, per_device(): jnp.einsum('rs,ksc->krc', green_ext, gathered, precision=lax.Precision.HI...  8.68 us
    ppermute x1, starting transfers between devices, per_device(): lax.ppermute(edges[:, :HALO], 'lon', down)  6.98 us
    ppermute x2, starting transfers between devices, widen_lat(): before = lax.ppermute(last, LAT, up)  6.61 us
    ppermute x1, starting transfers between devices, per_device(): green_after = lax.ppermute(green_ext, 'lon', down)  6.57 us
    dot_general x1, matrix products, per_device(): jnp.einsum('rs,kes->kre', green_before, near_edges[:, :HALO], precision=l...  5.81 us
  transfers between devices with their start and end apart: 11, of which 1 were waited for; matrix products, arithmetic and copies ran while one was open for 20% of the time, Pallas kernels for 0%

profile of v5, /device:TPU:3, one launch (start us, length us, event | category | flops | bytes accessed | tf_op | source)
XLA Modules:
  0.0 212.6 jit_solution(18060015593502591270)
XLA Ops:
  7.2 0.9 convert_element_type.6
  8.1 2.5 %fusion.53 = f32[12,96,128]{2,1,0:T(8,128)} fusion(f32[12,96,128]{2,1,0:T(8,128)} %param.12, f32[96,128]{1,0:T(8,128)S(1)} %convert_element_type.6, f32[128,128]{1,0:T(8,128)} %param.19), kind=kOutput, calls=%fused_computation.102 | convolution fusion | flops 226639872 | bytes 1294336 | tf_op jit(solution)/shard_map/krj,cj->krc/dot_general | solution.py:112
  10.7 0.1 subtract_dynamic-update-slice_fusion
  10.8 0.9 copy-done.10
  11.8 1.1 constant_dynamic-update-slice_fusion
  13.0 2.6 %fusion.67 = (f32[39,96,3]{2,1,0:T(8,128)}, f32[39,96,3]{2,1,0:T(8,128)}) fusion(f32[39,96,128]{2,1,0:T(8,128)S(1)} %bitcast_dynamic-update-slice_fusion), kind=kLoop, calls=%fused_computation.146 | loop fusion | bytes 179712 | tf_op jit(solution)/shard_map/slice | solution.py:27
  15.6 2.2 %copy.20 = f32[39,96,3]{1,0,2:T(8,128)S(1)} copy(f32[39,96,3]{2,1,0:T(8,128)} %get-tuple-element.37) | data formatting | bytes 89856 | tf_op jit(solution)/shard_map/slice | solution.py:28
  17.8 12.7 %collective-permute-start.1 = (f32[39,96,3]{1,0,2:T(8,128)S(1)}, f32[39,96,3]{1,0,2:T(8,128)S(1)}, u32[]{:S(2)}, u32[]{:S(2)}) collective-permute-start(f32[39,96,3]{1,0,2:T(8,128)S(1)} %copy.20), channel_id=1, source_target_pairs={{16,0},{32,16},{48,32},{64,48},{80,64},{96,80},{112,96},{128,112},... | collective-permute-start | bytes 134792 | tf_op jit(solution)/shard_map/ppermute | solution.py:30
  30.5 2.1 %copy.19 = f32[39,96,3]{1,0,2:T(8,128)S(1)} copy(f32[39,96,3]{2,1,0:T(8,128)} %get-tuple-element.36) | data formatting | bytes 89856 | tf_op jit(solution)/shard_map/slice | solution.py:27
  32.6 1.9 collective-permute-start
  34.5 0.7 fusion.70
  35.3 1.2 convolution_bitcast_fusion.1
  36.5 7.0 %collective-permute-start.5 = (f32[12,3,96]{2,1,0:T(4,128)S(1)}, f32[12,3,96]{2,1,0:T(4,128)S(1)}, u32[]{:S(2)}, u32[]{:S(2)}) collective-permute-start(f32[12,3,96]{2,1,0:T(4,128)S(1)} %get-tuple-element.64), channel_id=1, source_target_pairs={{16,0},{32,16},{48,32},{64,48},{80,64},{96,80},{112,96},{128,112},... | collective-permute-start | bytes 41480 | tf_op jit(solution)/shard_map/ppermute | solution.py:127
  43.5 1.9 collective-permute-start.4
  45.4 0.6 fusion.69
  46.0 3.4 %collective-permute-start.7 = (f32[3,1536]{1,0:T(4,128)}, f32[3,1536]{1,0:T(4,128)S(1)}, u32[]{:S(2)}, u32[]{:S(2)}) collective-permute-start(f32[3,1536]{1,0:T(4,128)} %get-tuple-element.44), channel_id=1, source_target_pairs={{1,0},{2,1},{3,2},{4,3},{5,4},{6,5},{7,6},{8,7},{9,8},{10,9},{11,1... | collective-permute-start | bytes 55304 | tf_op jit(solution)/shard_map/ppermute | solution.py:41
  49.5 0.1 cosine_divide_fusion
  49.5 0.6 slice_multiply_fusion.8
  50.2 0.1 fusion.72
  50.2 0.6 broadcast_multiply_fusion.4
  50.9 0.6 slice_multiply_fusion.7
  51.5 3.1 %collective-permute-start.6 = (f32[3,1536]{1,0:T(4,128)}, f32[3,1536]{1,0:T(4,128)}, u32[]{:S(2)}, u32[]{:S(2)}) collective-permute-start(f32[3,1536]{1,0:T(4,128)} %get-tuple-element.43), channel_id=1, source_target_pairs={{0,1},{1,2},{2,3},{3,4},{4,5},{5,6},{6,7},{7,8},{8,9},{9,10},{10,1... | collective-permute-start | bytes 55304 | tf_op jit(solution)/shard_map/ppermute | solution.py:40
  54.7 0.2 copy.23
  54.9 68.2 %all_gather.6 = f32[12,6,1536]{0,1,2:T(8,128)S(1)} all-gather(f32[12,6,96]{0,1,2:T(8,128)S(1)} %copy.23), channel_id=1, replica_groups=mesh['lon'=32,'chip'=8,'core'=2] {'chip','core'}, dimensions={2}, use_global_device_ids=true | all-gather | bytes 470016 | tf_op jit(solution)/shard_map/all_gather | solution.py:129
  123.1 3.2 %fusion.66 = (f32[12,3,1536]{0,1,2:T(4,128)}, f32[12,3,1536]{0,1,2:T(4,128)}) fusion(f32[12,6,1536]{0,1,2:T(8,128)S(1)} %all_gather.6), kind=kLoop, calls=%fused_computation.145 | loop fusion | bytes 884736 | tf_op jit(solution)/shard_map/slice | solution.py:134
  126.3 1.9 copy.22
  128.2 1.9 copy.21
  130.1 1.6 pad_maximum_fusion.5
  131.8 2.0 collective-permute-start.3
  133.8 3.5 %collective-permute-start.2 = (f32[39,3,134]{2,1,0:T(4,128)S(1)}, f32[39,3,134]{2,1,0:T(4,128)S(1)}, u32[]{:S(2)}, u32[]{:S(2)}) collective-permute-start(f32[39,3,134]{2,1,0:T(4,128)S(1)} %get-tuple-element.24), channel_id=1, source_target_pairs={{0,1},{1,2},{2,3},{3,4},{4,5},{5,6},{6,7},{7,8},{8,9},{9,10},{10,1... | collective-permute-start | bytes 188144 | tf_op jit(solution)/shard_map/ppermute | solution.py:40
  137.4 1.7 pad_maximum_fusion.2
  139.0 6.6 %collective-permute-start.9 = (f32[102,1536]{1,0:T(8,128)}, f32[102,1536]{1,0:T(8,128)S(1)}, u32[]{:S(2)}, u32[]{:S(2)}) collective-permute-start(f32[102,1536]{1,0:T(8,128)} %pad_maximum_fusion.2), channel_id=1, source_target_pairs={{16,0},{32,16},{48,32},{64,48},{80,64},{96,80},{112,96},{128,112},... | collective-permute-start | bytes 1880072 | tf_op jit(solution)/shard_map/ppermute | solution.py:131
  145.6 2.1 collective-permute-start.8
  147.8 0.2 maximum_bitcast_fusion.2
  148.0 0.8 slice_negate_fusion.1
  148.7 0.8 slice_add_fusion.3
  149.5 1.7 pad_maximum_fusion
  151.2 0.9 slice.289
  152.1 1.2 slice.278
  153.3 0.8 slice_add_fusion.4
  154.1 2.1 slice_add_fusion
  156.2 15.6 %collective-permute-done.9 = f32[102,1536]{1,0:T(8,128)S(1)} collective-permute-done((f32[102,1536]{1,0:T(8,128)}, f32[102,1536]{1,0:T(8,128)S(1)}, u32[]{:S(2)}, u32[]{:S(2)}) %collective-permute-start.9) | collective-permute-done | bytes 626720 | tf_op jit(solution)/shard_map/ppermute | solution.py:131
  171.8 3.8 %fusion.6 = f32[12,3,102]{2,0,1:T(8,128)S(1)} fusion(f32[12,3,1536]{0,1,2:T(4,128)S(1)} %copy-done.3, f32[102,1536]{1,0:T(8,128)S(1)} %collective-permute-done.9), kind=kOutput, calls=%fused_computation.17 | convolution fusion | flops 67682304 | bytes 862560 | tf_op jit(solution)/shard_map/rs,kes->kre/dot_general | solution.py:136
  175.6 1.2 copy.26
  176.7 5.8 %fusion.16 = f32[12,102,3]{1,0,2:T(8,128)S(1)} fusion(f32[12,3,1536]{0,1,2:T(4,128)} %get-tuple-element.19, f32[102,1536]{1,0:T(8,128)} %collective-permute-done.8), kind=kOutput, calls=%fused_computation.52 | convolution fusion | flops 67682304 | bytes 862560 | tf_op jit(solution)/shard_map/rs,kes->kre/dot_general | solution.py:133
  182.5 1.1 copy.27
  183.7 8.7 %convolution_bitcast_fusion = f32[12,102,128]{2,1,0:T(8,128)S(1)} fusion(f32[12,1536,128]{2,1,0:T(8,128)} %all-gather.2.cloned.1.call-done, f32[3,1536]{1,0:T(4,128)} %copy-done.19, f32[96,1536]{1,0:T(8,128)S(1)} %copy-done.5, f32[3,1536]{1,0:T(4,128)} %collective-permute-done.6), kind=kOutput, calls=%fused_computation.50 | convolution fusion | flops 2888091648 | bytes 10690560 | tf_op jit(solution)/shard_map/rs,ksc->krc/dot_general | solution.py:132
  192.4 1.9 slice_subtract_fusion.2
  194.5 1.1 fusion.14
  195.6 0.8 fusion.25
  196.5 0.4 fusion.27
  196.9 0.5 copy-done.16
  197.3 0.2 maximum_multiply_fusion.1
  197.5 2.1 fusion.2
  199.6 0.8 fusion.10
  200.4 0.1 copy-done.14
  200.5 0.8 fusion.29
  201.3 0.4 fusion.32
  201.7 0.5 copy-done.15
  202.2 0.2 maximum_multiply_fusion.2
  202.4 0.5 copy-done.27
  202.9 1.8 fusion.68
  204.7 0.1 fusion.56
  204.9 0.9 maximum_multiply_fusion.4
  (72 shorter events, 0.4 us)
Async XLA Ops:
  7.2 3.5 %copy-start.4 = (f32[12,96,128]{2,1,0:T(8,128)S(1)}, f32[12,96,128]{2,1,0:T(8,128)}, u32[]{:S(2)}) copy-start(f32[12,96,128]{2,1,0:T(8,128)} %param.12) | copy-start | bytes 1769476
  7.2 3.5 %copy-start.9 = (f32[12,96,128]{2,1,0:T(8,128)S(1)}, f32[12,96,128]{2,1,0:T(8,128)}, u32[]{:S(2)}) copy-start(f32[12,96,128]{2,1,0:T(8,128)} %param.13) | copy-start | bytes 1769476
  7.2 176.5 %all-gather.2.cloned.1.call-start = ((), (), s32[]{:S(2)}) async-start(), calls=%async_computation | async-start | bytes 10027008 | tf_op jit(solution)/shard_map/all_gather | solution.py:113
  10.7 1.1 copy-start.10
  10.7 2.2 %copy-start.20 = (f32[96,128]{1,0:T(8,128)S(1)}, f32[96,128]{1,0:T(8,128)}, u32[]{:S(2)}) copy-start(f32[96,128]{1,0:T(8,128)} %param.16) | copy-start | bytes 147460
  10.7 2.2 %copy-start.21 = (f32[96,128]{1,0:T(8,128)S(1)}, f32[96,128]{1,0:T(8,128)}, u32[]{:S(2)}) copy-start(f32[96,128]{1,0:T(8,128)} %param.17) | copy-start | bytes 147460
  10.7 2.2 %copy-start.18 = (s32[96,128]{1,0:T(8,128)S(1)}, s32[96,128]{1,0:T(8,128)}, u32[]{:S(2)}) copy-start(s32[96,128]{1,0:T(8,128)} %param.18) | copy-start | bytes 147460
  15.6 29.8 %copy-start.5 = (f32[96,1536]{1,0:T(8,128)S(1)}, f32[96,1536]{1,0:T(8,128)}, u32[]{:S(2)}) copy-start(f32[96,1536]{1,0:T(8,128)} %param.20) | copy-start | bytes 1769476
  17.8 108.5 %collective-permute-start.1 = (f32[39,96,3]{1,0,2:T(8,128)S(1)}, f32[39,96,3]{1,0,2:T(8,128)S(1)}, u32[]{:S(2)}, u32[]{:S(2)}) collective-permute-start(f32[39,96,3]{1,0,2:T(8,128)S(1)} %copy.20), channel_id=1, source_target_pairs={{16,0},{32,16},{48,32},{64,48},{80,64},{96,80},{112,96},{128,112},... | collective-permute-start | bytes 134792 | tf_op jit(solution)/shard_map/ppermute | solution.py:30
  32.6 95.6 %collective-permute-start = (f32[39,96,3]{1,0,2:T(8,128)S(1)}, f32[39,96,3]{1,0,2:T(8,128)S(1)}, u32[]{:S(2)}, u32[]{:S(2)}) collective-permute-start(f32[39,96,3]{1,0,2:T(8,128)S(1)} %copy.19), channel_id=1, source_target_pairs={{0,16},{16,32},{32,48},{48,64},{64,80},{80,96},{96,112},{112,128},... | collective-permute-start | bytes 134792 | tf_op jit(solution)/shard_map/ppermute | solution.py:29
  36.5 15.1 %collective-permute-start.5 = (f32[12,3,96]{2,1,0:T(4,128)S(1)}, f32[12,3,96]{2,1,0:T(4,128)S(1)}, u32[]{:S(2)}, u32[]{:S(2)}) collective-permute-start(f32[12,3,96]{2,1,0:T(4,128)S(1)} %get-tuple-element.64), channel_id=1, source_target_pairs={{16,0},{32,16},{48,32},{64,48},{80,64},{96,80},{112,96},{128,112},... | collective-permute-start | bytes 41480 | tf_op jit(solution)/shard_map/ppermute | solution.py:127
  43.5 11.2 %collective-permute-start.4 = (f32[12,3,96]{2,1,0:T(4,128)S(1)}, f32[12,3,96]{2,1,0:T(4,128)S(1)}, u32[]{:S(2)}, u32[]{:S(2)}) collective-permute-start(f32[12,3,96]{2,1,0:T(4,128)S(1)} %get-tuple-element.63), channel_id=1, source_target_pairs={{0,16},{16,32},{32,48},{48,64},{64,80},{80,96},{96,112},{112,128},... | collective-permute-start | bytes 41480 | tf_op jit(solution)/shard_map/ppermute | solution.py:127
  46.0 91.3 %collective-permute-start.7 = (f32[3,1536]{1,0:T(4,128)}, f32[3,1536]{1,0:T(4,128)S(1)}, u32[]{:S(2)}, u32[]{:S(2)}) collective-permute-start(f32[3,1536]{1,0:T(4,128)} %get-tuple-element.44), channel_id=1, source_target_pairs={{1,0},{2,1},{3,2},{4,3},{5,4},{6,5},{7,6},{8,7},{9,8},{10,9},{11,1... | collective-permute-start | bytes 55304 | tf_op jit(solution)/shard_map/ppermute | solution.py:41
  51.5 85.8 %collective-permute-start.6 = (f32[3,1536]{1,0:T(4,128)}, f32[3,1536]{1,0:T(4,128)}, u32[]{:S(2)}, u32[]{:S(2)}) collective-permute-start(f32[3,1536]{1,0:T(4,128)} %get-tuple-element.43), channel_id=1, source_target_pairs={{0,1},{1,2},{2,3},{3,4},{4,5},{5,6},{6,7},{7,8},{8,9},{9,10},{10,1... | collective-permute-start | bytes 55304 | tf_op jit(solution)/shard_map/ppermute | solution.py:40
  130.1 17.6 %copy-start.1 = (f32[39,96,3]{2,1,0:T(8,128)S(1)}, f32[39,96,3]{2,1,0:T(8,128)}, u32[]{:S(2)}) copy-start(f32[39,96,3]{2,1,0:T(8,128)} %copy.22) | copy-start | bytes 134788
  130.1 17.6 %copy-start.2 = (f32[39,96,3]{2,1,0:T(8,128)S(1)}, f32[39,96,3]{2,1,0:T(8,128)}, u32[]{:S(2)}) copy-start(f32[39,96,3]{2,1,0:T(8,128)} %copy.21) | copy-start | bytes 134788
  131.8 16.0 %collective-permute-start.3 = (f32[39,3,134]{2,1,0:T(4,128)S(1)}, f32[39,3,134]{2,1,0:T(4,128)S(1)}, u32[]{:S(2)}, u32[]{:S(2)}) collective-permute-start(f32[39,3,134]{2,1,0:T(4,128)S(1)} %get-tuple-element.25), channel_id=1, source_target_pairs={{1,0},{2,1},{3,2},{4,3},{5,4},{6,5},{7,6},{8,7},{9,8},{10,9},{11,1... | collective-permute-start | bytes 188144 | tf_op jit(solution)/shard_map/ppermute | solution.py:41
  133.8 13.9 %collective-permute-start.2 = (f32[39,3,134]{2,1,0:T(4,128)S(1)}, f32[39,3,134]{2,1,0:T(4,128)S(1)}, u32[]{:S(2)}, u32[]{:S(2)}) collective-permute-start(f32[39,3,134]{2,1,0:T(4,128)S(1)} %get-tuple-element.24), channel_id=1, source_target_pairs={{0,1},{1,2},{2,3},{3,4},{4,5},{5,6},{6,7},{7,8},{8,9},{9,10},{10,1... | collective-permute-start | bytes 188144 | tf_op jit(solution)/shard_map/ppermute | solution.py:40
  137.3 10.6 %copy-start.19 = (f32[3,1536]{1,0:T(4,128)}, f32[3,1536]{1,0:T(4,128)S(1)}, u32[]{:S(2)}) copy-start(f32[3,1536]{1,0:T(4,128)S(1)} %collective-permute-done.7) | copy-start | bytes 55300
  139.0 32.8 %collective-permute-start.9 = (f32[102,1536]{1,0:T(8,128)}, f32[102,1536]{1,0:T(8,128)S(1)}, u32[]{:S(2)}, u32[]{:S(2)}) collective-permute-start(f32[102,1536]{1,0:T(8,128)} %pad_maximum_fusion.2), channel_id=1, source_target_pairs={{16,0},{32,16},{48,32},{64,48},{80,64},{96,80},{112,96},{128,112},... | collective-permute-start | bytes 1880072 | tf_op jit(solution)/shard_map/ppermute | solution.py:131
  145.6 31.1 %collective-permute-start.8 = (f32[102,1536]{1,0:T(8,128)}, f32[102,1536]{1,0:T(8,128)}, u32[]{:S(2)}, u32[]{:S(2)}) collective-permute-start(f32[102,1536]{1,0:T(8,128)} %pad_maximum_fusion.2), channel_id=1, source_target_pairs={{0,16},{16,32},{32,48},{48,64},{64,80},{80,96},{96,112},{112,128},... | collective-permute-start | bytes 1880072 | tf_op jit(solution)/shard_map/ppermute | solution.py:130
  151.2 5.0 %copy-start = (f32[39,102,134]{2,1,0:T(8,128)}, f32[39,102,134]{2,1,0:T(8,128)S(1)}, u32[]{:S(2)}) copy-start(f32[39,102,134]{2,1,0:T(8,128)S(1)} %pad_maximum_fusion) | copy-start | bytes 6396628
  154.1 17.7 %copy-start.3 = (f32[12,3,1536]{0,1,2:T(4,128)S(1)}, f32[12,3,1536]{0,1,2:T(4,128)}, u32[]{:S(2)}) copy-start(f32[12,3,1536]{0,1,2:T(4,128)} %get-tuple-element.20) | copy-start | bytes 663556
  183.7 8.7 %copy-start.6 = (f32[12,3,102]{1,2,0:T(8,128)S(1)}, f32[12,3,102]{1,2,0:T(8,128)}, u32[]{:S(2)}) copy-start(f32[12,3,102]{1,2,0:T(8,128)} %copy.26) | copy-start | bytes 44068
  183.7 8.7 %copy-start.7 = (f32[12,102,3]{2,1,0:T(8,128)S(1)}, f32[12,102,3]{2,1,0:T(8,128)}, u32[]{:S(2)}) copy-start(f32[12,102,3]{2,1,0:T(8,128)} %copy.27) | copy-start | bytes 44068
  192.4 2.0 copy-start.12
  192.4 2.0 copy-start.13
  192.4 2.0 copy-start.28
  194.4 1.2 copy-start.8
  194.4 1.2 copy-start.17
  194.4 1.2 copy-start.22
  194.4 1.2 copy-start.23
  194.4 1.2 copy-start.24
  194.5 1.2 copy-start.25
  196.5 0.9 copy-start.16
  197.5 2.1 copy-start.11
  199.6 0.9 copy-start.14
  201.3 0.9 copy-start.15
  202.2 0.7 copy-start.27
  202.9 1.9 copy-start.26
Sparse Core Ops, SparseCore 0:
  10.8 87.6 all-gather.1

commit v6 on v4

--- a/solution.py
+++ b/solution.py
@@ -116,25 +116,42 @@
     spare = 8 * ((2 * HALO + 7) // 8)
     edges = jnp.pad(edges, ((0, 0), (0, spare - 2 * HALO), (0, columns - rows_here)))
     packed = jnp.concatenate([mixed, edges], axis=1)
-    gathered = lax.all_gather(packed, LAT, axis=1, tiled=True)
+    gathered = lax.all_gather(packed, "chip", axis=1, tiled=True)
+    cores = lax.axis_size("core")
+    core = lax.axis_index("core")
+    swap = [(i, (i + 1) % cores) for i in range(cores)]
 
     fields = jnp.stack([ocean_depth, bottom_drag, wet_frac], axis=0)
     stack = jnp.concatenate([elevation - equilibrium, transport_u, transport_v, fields], axis=0)
     stack = widen_lat(widen_lon(stack, HALO, 2), HALO, 1)
     green_ext = widen_lat(lat_green, HALO, 0)
-
-    blocks = lat_size()
+    gathered, stack, green_ext = lax.optimization_barrier((gathered, stack, green_ext))
+
+    swapped = lax.ppermute(gathered, "core", swap)
+    chips = lax.axis_size("chip")
     block = rows_here + spare
-    green_blocks = green_ext.reshape(green_ext.shape[0], blocks, rows_here)
-    lanes = gathered.reshape(12, blocks, block, columns)[:, :, rows_here : rows_here + 2 * HALO, :rows_here]
-    edge_sal = jnp.einsum("rbj,kbej->kre", green_blocks, lanes, precision=lax.Precision.HIGHEST)
+    ext_rows = green_ext.shape[0]
+    green_blocks = green_ext.reshape(ext_rows, chips, cores, rows_here)
+    green_own = lax.dynamic_index_in_dim(green_blocks, core, axis=2, keepdims=False)
+    green_other = lax.dynamic_index_in_dim(green_blocks, (core + 1) % cores, axis=2, keepdims=False)
+
+    def edge_part(green_part, part):
+        lanes = part.reshape(12, chips, block, columns)[:, :, rows_here : rows_here + 2 * HALO, :rows_here]
+        return jnp.einsum("rbj,kbej->kre", green_part, lanes, precision=lax.Precision.HIGHEST)
+
+    def bulk_part(green_part, part):
+        padded = jnp.pad(green_part, ((0, 0), (0, 0), (0, spare))).reshape(ext_rows, -1)
+        return jnp.einsum("rs,ksc->krc", padded, part, precision=lax.Precision.HIGHEST)
+
+    edge_own = edge_part(green_own, gathered)
+    sal_own = bulk_part(green_own, gathered)
+    edge_sal = edge_own + edge_part(green_other, swapped)
     size = lax.axis_size("lon")
     up = [(i, (i + 1) % size) for i in range(size)]
     down = [(j, i) for i, j in up]
     before = lax.ppermute(edge_sal[:, :, HALO:], "lon", up)
     after = lax.ppermute(edge_sal[:, :, :HALO], "lon", down)
-    green_pad = jnp.pad(green_blocks, ((0, 0), (0, 0), (0, spare))).reshape(green_ext.shape[0], -1)
-    sal = jnp.einsum("rs,ksc->krc", green_pad, gathered, precision=lax.Precision.HIGHEST)
+    sal = sal_own + bulk_part(green_other, swapped)
     sal = jnp.concatenate([before, sal, after], axis=2)
     potential = stack[:12] - sal
     flows = stack[12:36]

time: 137 us -> 152 us (1.11)
  waiting for transfers between devices: 18.5 us -> 28 us
  local copies, waits for them, and re-layouts: 20.5 us -> 25.6 us
  other arithmetic: 28.6 us -> 25.6 us
  matrix products: 13.5 us -> 15.4 us
    all_gather x1, waiting for transfers between devices: 7.14 us -> 19.6 us  [per_device(): gathered = lax.all_gather(packed, 'chip', axis=1, tiled=True)]
    ppermute x1, waiting for transfers between devices: 4 us -> 0.01 us  [widen_lon(): before = lax.ppermute(last, 'lon', up)]
    ppermute x2, starting transfers between devices: 7.52 us -> 3.84 us  [widen_lat(): after = lax.ppermute(initial, LAT, down)]
    ppermute x1, starting transfers between devices: 1.92 us -> 5.49 us  [widen_lon(): before = lax.ppermute(last, 'lon', up)]
    ppermute x0 -> x1, starting transfers between devices: none -> 2.63 us  [per_device(): swapped = lax.ppermute(gathered, 'core', swap)]
    ppermute x2, starting transfers between devices: 9.59 us -> 7.69 us  [widen_lat(): before = lax.ppermute(last, LAT, up)]
    unnamed x68 -> x60, local copies, waits for them, and re-layouts: 2.8 us -> 3.78 us
    dot_general x2 -> x4, matrix products: 10.6 us -> 11.3 us  [the longest x2 9.94 us: bulk_part(): jnp.einsum('rs,ksc->krc', padded, part, precision=lax.Precision.HIGHEST)]
  transfers between devices with their start and end apart: 9 -> 10, of which waited for: 4 -> 3; matrix products, arithmetic and copies ran while one was open for 30% -> 29% of each run, Pallas kernels for 0% -> 0%
where the time goes in v6:
time: 152 us; the launch traced here: 151 us
  starting transfers between devices  41.4 us (27%)
  waiting for transfers between devices  28 us (18%)
  other arithmetic  25.6 us (17%)
  local copies, waits for them, and re-layouts  25.6 us (17%)
  matrix products  15.4 us (10%)
  between operations  14.7 us (10%)
    all_gather x1, waiting for transfers between devices, per_device(): gathered = lax.all_gather(packed, 'chip', axis=1, tiled=True)  19.6 us
    ppermute x1, starting transfers between devices, widen_lon(): after = lax.ppermute(initial, 'lon', down)  10.9 us
    dot_general x2, matrix products, bulk_part(): jnp.einsum('rs,ksc->krc', padded, part, precision=lax.Precision.HIGHEST)  9.94 us
    ppermute x2, starting transfers between devices, widen_lat(): before = lax.ppermute(last, LAT, up)  7.69 us
    ppermute x1, starting transfers between devices, per_device(): after = lax.ppermute(edge_sal[:, :, :HALO], 'lon', down)  6.64 us
    ppermute x1, starting transfers between devices, widen_lon(): before = lax.ppermute(last, 'lon', up)  5.49 us
    ppermute x2, waiting for transfers between devices, widen_lat(): after = lax.ppermute(initial, LAT, down)  4.93 us
    slice x2, local copies, waits for them, and re-layouts, widen_lon(): last = lax.slice_in_dim(array, length - width, length, axis=dim)  4.78 us
  transfers between devices with their start and end apart: 10, of which 3 were waited for; matrix products, arithmetic and copies ran while one was open for 29% of the time, Pallas kernels for 0%

profile of v6, /device:TPU:1, one launch (start us, length us, event | category | flops | bytes accessed | tf_op | source)
XLA Modules:
  0.0 150.6 jit_solution(7128080408015224459)
XLA Ops:
  7.2 0.8 convert_element_type.11
  8.0 0.7 fusion.65
  8.7 1.8 %fusion.46 = f32[12,96,128]{2,1,0:T(8,128)S(1)} fusion(f32[12,96,128]{2,1,0:T(8,128)} %param.12, f32[96,128]{1,0:T(8,128)S(1)} %convert_element_type.11, f32[128,128]{1,0:T(8,128)} %param.19), kind=kOutput, calls=%fused_computation.99 | convolution fusion | flops 226639872 | bytes 1294336 | tf_op jit(solution)/shard_map/krj,cj->krc/dot_general | solution.py:112
  10.6 2.2 %convolution_bitcast_fusion.2 = f32[12,6,96]{2,1,0:T(8,128)S(1)} fusion(f32[12,96,128]{2,1,0:T(8,128)} %param.12, f32[96,128]{1,0:T(8,128)S(1)} %convert_element_type.11, f32[3,128]{1,0:T(4,128)S(1)} %get-tuple-element.68, f32[3,128]{1,0:T(4,128)S(1)} %get-tuple-element.67), kind=kOutput, calls=%fused_computation.46 | convolution fusion | flops 10765056 | bytes 669696 | tf_op jit(solution)/shard_map/ej,krj->ker/dot_general | solution.py:115
  12.8 0.9 select_maximum_fusion
  13.8 1.1 constant_dynamic-update-slice_fusion.1
  14.9 1.1 constant_dynamic-update-slice_fusion
  16.1 2.6 %fusion.62 = (f32[39,96,3]{2,1,0:T(8,128)}, f32[39,96,3]{2,1,0:T(8,128)}) fusion(f32[39,96,128]{2,1,0:T(8,128)S(1)} %bitcast_dynamic-update-slice_fusion), kind=kLoop, calls=%fused_computation.146 | loop fusion | bytes 179712 | tf_op jit(solution)/shard_map/slice | solution.py:27
  18.7 2.2 %copy.31 = f32[39,96,3]{1,0,2:T(8,128)S(1)} copy(f32[39,96,3]{2,1,0:T(8,128)} %get-tuple-element.40) | data formatting | bytes 89856 | tf_op jit(solution)/shard_map/slice | solution.py:27
  20.9 5.5 %collective-permute-start = (f32[39,96,3]{1,0,2:T(8,128)S(1)}, f32[39,96,3]{1,0,2:T(8,128)S(1)}, u32[]{:S(2)}, u32[]{:S(2)}) collective-permute-start(f32[39,96,3]{1,0,2:T(8,128)S(1)} %copy.31), channel_id=1, source_target_pairs={{0,16},{16,32},{32,48},{48,64},{64,80},{80,96},{96,112},{112,128},... | collective-permute-start | bytes 134792 | tf_op jit(solution)/shard_map/ppermute | solution.py:29
  26.4 2.1 %copy.32 = f32[39,96,3]{1,0,2:T(8,128)S(1)} copy(f32[39,96,3]{2,1,0:T(8,128)} %get-tuple-element.41) | data formatting | bytes 89856 | tf_op jit(solution)/shard_map/slice | solution.py:28
  28.5 10.9 %collective-permute-start.1 = (f32[39,96,3]{1,0,2:T(8,128)S(1)}, f32[39,96,3]{1,0,2:T(8,128)S(1)}, u32[]{:S(2)}, u32[]{:S(2)}) collective-permute-start(f32[39,96,3]{1,0,2:T(8,128)S(1)} %copy.32), channel_id=1, source_target_pairs={{16,0},{32,16},{48,32},{64,48},{80,64},{96,80},{112,96},{128,112},... | collective-permute-start | bytes 134792 | tf_op jit(solution)/shard_map/ppermute | solution.py:30
  39.4 4.0 %collective-permute-start.4 = (f32[3,1536]{1,0:T(4,128)S(1)}, f32[3,1536]{1,0:T(4,128)S(1)}, u32[]{:S(2)}, u32[]{:S(2)}) collective-permute-start(f32[3,1536]{1,0:T(4,128)S(1)} %get-tuple-element.49), channel_id=1, source_target_pairs={{0,1},{1,2},{2,3},{3,4},{4,5},{5,6},{6,7},{7,8},{8,9},{9,10},{10,1... | collective-permute-start | bytes 55304 | tf_op jit(solution)/shard_map/ppermute | solution.py:40
  43.5 1.9 %collective-permute-start.5 = (f32[3,1536]{1,0:T(4,128)S(1)}, f32[3,1536]{1,0:T(4,128)S(1)}, u32[]{:S(2)}, u32[]{:S(2)}) collective-permute-start(f32[3,1536]{1,0:T(4,128)S(1)} %get-tuple-element.50), channel_id=1, source_target_pairs={{1,0},{2,1},{3,2},{4,3},{5,4},{6,5},{7,6},{8,7},{9,8},{10,9},{11,1... | collective-permute-start | bytes 55304 | tf_op jit(solution)/shard_map/ppermute | solution.py:41
  45.4 2.0 %copy.33 = f32[39,96,3]{2,1,0:T(8,128)} copy(f32[39,96,3]{1,0,2:T(8,128)S(1)} %collective-permute-done) | data formatting | bytes 89856 | tf_op jit(solution)/shard_map/ppermute | solution.py:29
  47.4 1.9 %copy.34 = f32[39,96,3]{2,1,0:T(8,128)} copy(f32[39,96,3]{1,0,2:T(8,128)S(1)} %collective-permute-done.1) | data formatting | bytes 89856 | tf_op jit(solution)/shard_map/ppermute | solution.py:30
  49.3 1.6 %pad_maximum_fusion.5 = (f32[39,3,134]{2,1,0:T(4,128)S(1)}, f32[39,3,134]{2,1,0:T(4,128)S(1)}) fusion(f32[39,96,3]{2,1,0:T(8,128)} %copy.34, f32[39,96,128]{2,1,0:T(8,128)S(1)} %bitcast_dynamic-update-slice_fusion, f32[39,96,3]{2,1,0:T(8,128)} %copy.33), kind=kLoop, calls=%fused_computation.112 | loop fusion | flops 62712 | bytes 2132208 | tf_op jit(solution)/shard_map/slice | solution.py:38
  50.9 3.6 %collective-permute-start.2 = (f32[39,3,134]{2,1,0:T(4,128)S(1)}, f32[39,3,134]{2,1,0:T(4,128)S(1)}, u32[]{:S(2)}, u32[]{:S(2)}) collective-permute-start(f32[39,3,134]{2,1,0:T(4,128)S(1)} %get-tuple-element.25), channel_id=1, source_target_pairs={{0,1},{1,2},{2,3},{3,4},{4,5},{5,6},{6,7},{7,8},{8,9},{9,10},{10,1... | collective-permute-start | bytes 188144 | tf_op jit(solution)/shard_map/ppermute | solution.py:40
  54.6 1.9 %collective-permute-start.3 = (f32[39,3,134]{2,1,0:T(4,128)S(1)}, f32[39,3,134]{2,1,0:T(4,128)S(1)}, u32[]{:S(2)}, u32[]{:S(2)}) collective-permute-start(f32[39,3,134]{2,1,0:T(4,128)S(1)} %get-tuple-element.26), channel_id=1, source_target_pairs={{1,0},{2,1},{3,2},{4,3},{5,4},{6,5},{7,6},{8,7},{9,8},{10,9},{11,1... | collective-permute-start | bytes 188144 | tf_op jit(solution)/shard_map/ppermute | solution.py:41
  56.6 3.4 %collective-permute-done.2 = f32[39,3,134]{2,1,0:T(4,128)S(1)} collective-permute-done((f32[39,3,134]{2,1,0:T(4,128)S(1)}, f32[39,3,134]{2,1,0:T(4,128)S(1)}, u32[]{:S(2)}, u32[]{:S(2)}) %collective-permute-start.2) | collective-permute-done | bytes 62744 | tf_op jit(solution)/shard_map/ppermute | solution.py:40
  60.0 4.9 %collective-permute-done.3 = f32[39,3,134]{2,1,0:T(4,128)S(1)} collective-permute-done((f32[39,3,134]{2,1,0:T(4,128)S(1)}, f32[39,3,134]{2,1,0:T(4,128)S(1)}, u32[]{:S(2)}, u32[]{:S(2)}) %collective-permute-start.3) | collective-permute-done | bytes 62744 | tf_op jit(solution)/shard_map/ppermute | solution.py:41
  65.0 3.7 %pad_maximum_fusion = f32[39,102,134]{2,1,0:T(8,128)} fusion(f32[39,3,134]{2,1,0:T(4,128)S(1)} %collective-permute-done.3, f32[39,96,3]{2,1,0:T(8,128)S(1)} %copy-done.2, f32[39,96,128]{2,1,0:T(8,128)S(1)} %bitcast_dynamic-update-slice_fusion, f32[39,96,3]{2,1,0:T(8,128)S(1)} %copy-done.1, f32[39,3,134]{2,1,0:T(4,128)S(1)} %collective-permute-done.2), kind=kLoop, calls=%fused_computation | loop fusion | flops 2132208 | bytes 4264416 | tf_op jit(solution)/shard_map/concatenate | solution.py:42
  68.7 19.6 %all-gather.2.cloned.1.call-done = f32[12,832,128]{2,1,0:T(8,128)} async-done(((f32[12,104,128]{2,1,0:T(8,128)}), f32[12,832,128]{2,1,0:T(8,128)}) %all-gather.2.cloned.1.call-update) | async-done | bytes 5111824 | tf_op jit(solution)/shard_map/all_gather | solution.py:119
  88.3 2.6 %collective-permute-start.6 = (f32[12,832,128]{2,1,0:T(8,128)}, f32[12,832,128]{2,1,0:T(8,128)}, u32[]{:S(2)}, u32[]{:S(2)}) collective-permute-start(f32[12,832,128]{2,1,0:T(8,128)} %all-gather.2.cloned.1.call-done), channel_id=1, source_target_pairs={{0,1},{1,0},{2,3},{3,2},{4,5},{5,4},{6,7},{7,6},{8,9},{9,8},{10,11... | collective-permute-start | bytes 15335432 | tf_op jit(solution)/shard_map/ppermute | solution.py:130
  91.1 0.6 slice_multiply_fusion.8
  91.7 0.6 slice_multiply_fusion.7
  92.2 0.7 broadcast_multiply_fusion.4
  93.0 1.0 slice_bitcast_fusion.2
  94.0 0.7 slice.288
  94.7 0.7 slice.278
  95.5 1.2 reshape.64
  96.7 0.7 constant_dynamic-slice_fusion
  97.4 0.4 copy.38
  97.8 0.4 copy.36
  98.2 1.2 slice.281
  99.4 0.7 convolution_bitcast_fusion.1
  100.1 0.8 slice_negate_fusion.1
  100.9 0.8 slice_add_fusion.1
  101.6 0.8 slice_add_fusion.2
  102.4 2.1 %slice_add_fusion = f32[24,100,132]{2,1,0:T(8,128)S(1)} fusion(f32[39,102,134]{2,1,0:T(8,128)S(1)} %copy-done), kind=kLoop, calls=%fused_computation.14 | loop fusion | flops 950400 | bytes 6336000 | tf_op jit(solution)/shard_map/add | solution.py:79
  104.6 1.0 slice.282
  105.6 0.7 fusion.13
  106.3 4.3 %collective-permute-start.7 = (f32[12,102,3]{1,0,2:T(8,128)S(1)}, f32[12,102,3]{1,0,2:T(8,128)}, u32[]{:S(2)}, u32[]{:S(2)}) collective-permute-start(f32[12,102,3]{1,0,2:T(8,128)S(1)} %get-tuple-element.69), channel_id=1, source_target_pairs={{0,16},{16,32},{32,48},{48,64},{64,80},{80,96},{96,112},{112,128},... | collective-permute-start | bytes 44072 | tf_op jit(solution)/shard_map/ppermute | solution.py:152
  110.6 6.6 %collective-permute-start.8 = (f32[12,102,3]{1,0,2:T(8,128)S(1)}, f32[12,102,3]{1,0,2:T(8,128)}, u32[]{:S(2)}, u32[]{:S(2)}) collective-permute-start(f32[12,102,3]{1,0,2:T(8,128)S(1)} %get-tuple-element.70), channel_id=1, source_target_pairs={{16,0},{32,16},{48,32},{64,48},{80,64},{96,80},{112,96},{128,112},... | collective-permute-start | bytes 44072 | tf_op jit(solution)/shard_map/ppermute | solution.py:153
  117.2 5.7 %fusion.68 = f32[12,128,102]{1,2,0:T(8,128)S(1)} fusion(f32[12,832,128]{2,1,0:T(8,128)} %collective-permute-done.6, f32[102,832,1]{0,1,2:T(8,128)S(1)} %bitcast.59), kind=kOutput, calls=%fused_computation.152 | convolution fusion | flops 1564213248 | bytes 6077952 | tf_op jit(solution)/shard_map/rs,ksc->krc/dot_general | solution.py:144
  123.0 4.2 %add_bitcast_fusion = f32[12,102,128]{2,1,0:T(8,128)} fusion(f32[12,128,102]{1,2,0:T(8,128)S(1)} %fusion.68, f32[12,832,128]{2,1,0:T(8,128)S(1)} %bitcast.56, f32[102,832,1]{0,1,2:T(8,128)S(1)} %bitcast.60), kind=kOutput, calls=%fused_computation.90 | convolution fusion | flops 1564369920 | bytes 6704640 | tf_op jit(solution)/shard_map/rs,ksc->krc/dot_general | solution.py:144
  127.2 1.0 copy.41
  128.2 1.9 %copy.42 = f32[12,102,3]{2,1,0:T(8,128)} copy(f32[12,102,3]{1,0,2:T(8,128)} %collective-permute-done.8) | data formatting | bytes 29376 | tf_op jit(solution)/shard_map/ppermute | solution.py:153
  130.1 2.3 %maximum_subtract_fusion = f32[12,102,134]{2,1,0:T(8,128)S(1)} fusion(f32[12,102,3]{2,1,0:T(8,128)} %copy.42, f32[12,102,128]{2,1,0:T(8,128)} %add_bitcast_fusion, f32[12,102,3]{2,1,0:T(8,128)S(1)} %copy.41, f32[39,102,134]{2,1,0:T(8,128)} %pad_maximum_fusion), kind=kLoop, calls=%fused_computation.39 | loop fusion | flops 492048 | bytes 1968192 | tf_op jit(solution)/shard_map/sub | solution.py:156
  132.5 1.1 fusion.10
  133.7 0.8 fusion.20
  134.5 0.4 fusion.22
  134.9 0.5 copy-done.14
  135.4 0.2 maximum_multiply_fusion.1
  135.6 2.1 %fusion.2 = f32[24,98,130]{2,1,0:T(8,128)S(1)} fusion(f32[12,100,132]{2,1,0:T(8,128)S(1)} %get-tuple-element.61, f32[12,100,132]{2,1,0:T(8,128)S(1)} %get-tuple-element.60), kind=kLoop, calls=%fused_computation.9 | loop fusion | flops 2140320 | bytes 2490240 | tf_op jit(solution)/shard_map/add | solution.py:79
  137.7 0.8 fusion.6
  138.6 0.8 fusion.24
  139.4 0.4 fusion.27
  139.8 0.5 copy-done.13
  140.3 0.2 maximum_multiply_fusion.2
  140.5 0.4 copy-done.24
  140.9 1.8 %fusion.63 = (f32[12,96,128]{2,1,0:T(8,128)}, f32[12,96,128]{2,1,0:T(8,128)S(1)}, f32[12,96,128]{2,1,0:T(8,128)}) fusion(f32[12,98,130]{2,1,0:T(8,128)S(1)} %get-tuple-element.56, f32[96]{0:T(128)S(1)} %copy-done.24, f32[12,98,130]{2,1,0:T(8,128)S(1)} %get-tuple-element.55), kind=kLoop, calls=%fused_computation.147 | loop fusion | flops 737280 | bytes 5308800 | tf_op jit(solution)/shard_map/slice | solution.py:185
  142.7 0.1 fusion.52
  142.9 0.9 maximum_multiply_fusion.4
  (75 shorter events, 0.7 us)
Async XLA Ops:
  7.2 81.1 %all-gather.2.cloned.1.call-start = ((), (), s32[]{:S(2)}) async-start(), calls=%async_computation | async-start | bytes 5750784 | tf_op jit(solution)/shard_map/all_gather | solution.py:119
  8.0 2.5 %copy-start.5 = (f32[96,128]{1,0:T(8,128)}, f32[96,128]{1,0:T(8,128)S(1)}, u32[]{:S(2)}) copy-start(f32[96,128]{1,0:T(8,128)S(1)} %convert_element_type.11) | copy-start | bytes 147460
  8.7 5.0 %copy-start.3 = (f32[12,96,128]{2,1,0:T(8,128)S(1)}, f32[12,96,128]{2,1,0:T(8,128)}, u32[]{:S(2)}) copy-start(f32[12,96,128]{2,1,0:T(8,128)} %param.12) | copy-start | bytes 1769476
  8.7 5.0 %copy-start.8 = (f32[12,96,128]{2,1,0:T(8,128)S(1)}, f32[12,96,128]{2,1,0:T(8,128)}, u32[]{:S(2)}) copy-start(f32[12,96,128]{2,1,0:T(8,128)} %param.13) | copy-start | bytes 1769476
  13.7 2.3 %copy-start.17 = (f32[96,128]{1,0:T(8,128)S(1)}, f32[96,128]{1,0:T(8,128)}, u32[]{:S(2)}) copy-start(f32[96,128]{1,0:T(8,128)} %param.16) | copy-start | bytes 147460
  13.7 2.4 %copy-start.18 = (f32[96,128]{1,0:T(8,128)S(1)}, f32[96,128]{1,0:T(8,128)}, u32[]{:S(2)}) copy-start(f32[96,128]{1,0:T(8,128)} %param.17) | copy-start | bytes 147460
  13.7 2.4 %copy-start.16 = (s32[96,128]{1,0:T(8,128)S(1)}, s32[96,128]{1,0:T(8,128)}, u32[]{:S(2)}) copy-start(s32[96,128]{1,0:T(8,128)} %param.18) | copy-start | bytes 147460
  18.7 20.7 %copy-start.7 = (f32[96,1536]{1,0:T(8,128)S(1)}, f32[96,1536]{1,0:T(8,128)}, u32[]{:S(2)}) copy-start(f32[96,1536]{1,0:T(8,128)} %param.20) | copy-start | bytes 1769476
  20.9 24.5 %collective-permute-start = (f32[39,96,3]{1,0,2:T(8,128)S(1)}, f32[39,96,3]{1,0,2:T(8,128)S(1)}, u32[]{:S(2)}, u32[]{:S(2)}) collective-permute-start(f32[39,96,3]{1,0,2:T(8,128)S(1)} %copy.31), channel_id=1, source_target_pairs={{0,16},{16,32},{32,48},{48,64},{64,80},{80,96},{96,112},{112,128},... | collective-permute-start | bytes 134792 | tf_op jit(solution)/shard_map/ppermute | solution.py:29
  28.5 18.9 %collective-permute-start.1 = (f32[39,96,3]{1,0,2:T(8,128)S(1)}, f32[39,96,3]{1,0,2:T(8,128)S(1)}, u32[]{:S(2)}, u32[]{:S(2)}) collective-permute-start(f32[39,96,3]{1,0,2:T(8,128)S(1)} %copy.32), channel_id=1, source_target_pairs={{16,0},{32,16},{48,32},{64,48},{80,64},{96,80},{112,96},{128,112},... | collective-permute-start | bytes 134792 | tf_op jit(solution)/shard_map/ppermute | solution.py:30
  39.4 17.1 %collective-permute-start.4 = (f32[3,1536]{1,0:T(4,128)S(1)}, f32[3,1536]{1,0:T(4,128)S(1)}, u32[]{:S(2)}, u32[]{:S(2)}) collective-permute-start(f32[3,1536]{1,0:T(4,128)S(1)} %get-tuple-element.49), channel_id=1, source_target_pairs={{0,1},{1,2},{2,3},{3,4},{4,5},{5,6},{6,7},{7,8},{8,9},{9,10},{10,1... | collective-permute-start | bytes 55304 | tf_op jit(solution)/shard_map/ppermute | solution.py:40
  43.5 13.0 %collective-permute-start.5 = (f32[3,1536]{1,0:T(4,128)S(1)}, f32[3,1536]{1,0:T(4,128)S(1)}, u32[]{:S(2)}, u32[]{:S(2)}) collective-permute-start(f32[3,1536]{1,0:T(4,128)S(1)} %get-tuple-element.50), channel_id=1, source_target_pairs={{1,0},{2,1},{3,2},{4,3},{5,4},{6,5},{7,6},{8,7},{9,8},{10,9},{11,1... | collective-permute-start | bytes 55304 | tf_op jit(solution)/shard_map/ppermute | solution.py:41
  49.3 15.7 %copy-start.1 = (f32[39,96,3]{2,1,0:T(8,128)S(1)}, f32[39,96,3]{2,1,0:T(8,128)}, u32[]{:S(2)}) copy-start(f32[39,96,3]{2,1,0:T(8,128)} %copy.33) | copy-start | bytes 134788
  49.3 15.7 %copy-start.2 = (f32[39,96,3]{2,1,0:T(8,128)S(1)}, f32[39,96,3]{2,1,0:T(8,128)}, u32[]{:S(2)}) copy-start(f32[39,96,3]{2,1,0:T(8,128)} %copy.34) | copy-start | bytes 134788
  50.9 9.1 %collective-permute-start.2 = (f32[39,3,134]{2,1,0:T(4,128)S(1)}, f32[39,3,134]{2,1,0:T(4,128)S(1)}, u32[]{:S(2)}, u32[]{:S(2)}) collective-permute-start(f32[39,3,134]{2,1,0:T(4,128)S(1)} %get-tuple-element.25), channel_id=1, source_target_pairs={{0,1},{1,2},{2,3},{3,4},{4,5},{5,6},{6,7},{7,8},{8,9},{9,10},{10,1... | collective-permute-start | bytes 188144 | tf_op jit(solution)/shard_map/ppermute | solution.py:40
  54.6 10.4 %collective-permute-start.3 = (f32[39,3,134]{2,1,0:T(4,128)S(1)}, f32[39,3,134]{2,1,0:T(4,128)S(1)}, u32[]{:S(2)}, u32[]{:S(2)}) collective-permute-start(f32[39,3,134]{2,1,0:T(4,128)S(1)} %get-tuple-element.26), channel_id=1, source_target_pairs={{1,0},{2,1},{3,2},{4,3},{5,4},{6,5},{7,6},{8,7},{9,8},{10,9},{11,1... | collective-permute-start | bytes 188144 | tf_op jit(solution)/shard_map/ppermute | solution.py:41
  88.3 16.3 %collective-permute-start.6 = (f32[12,832,128]{2,1,0:T(8,128)}, f32[12,832,128]{2,1,0:T(8,128)}, u32[]{:S(2)}, u32[]{:S(2)}) collective-permute-start(f32[12,832,128]{2,1,0:T(8,128)} %all-gather.2.cloned.1.call-done), channel_id=1, source_target_pairs={{0,1},{1,0},{2,3},{3,2},{4,5},{5,4},{6,7},{7,6},{8,9},{9,8},{10,11... | collective-permute-start | bytes 15335432 | tf_op jit(solution)/shard_map/ppermute | solution.py:130
  98.1 4.3 %copy-start = (f32[39,102,134]{2,1,0:T(8,128)S(1)}, f32[39,102,134]{2,1,0:T(8,128)}, u32[]{:S(2)}) copy-start(f32[39,102,134]{2,1,0:T(8,128)} %pad_maximum_fusion) | copy-start | bytes 6396628
  101.6 21.3 %slice-start = ((s8[5111808]{0:T(1024)(128)(4,1)}), s8[4194304]{0:T(1024)(128)(4,1)S(1)}, s32[]{:S(2)}) async-start(s8[5111808]{0:T(1024)(128)(4,1)} %bitcast.55), calls=%async_computation.1 | async-start | bytes 8388608
  102.4 20.5 %slice-start.1 = ((s8[5111808]{0:T(1024)(128)(4,1)}), s8[917504]{0:T(1024)(128)(4,1)S(1)}, s32[]{:S(2)}) async-start(s8[5111808]{0:T(1024)(128)(4,1)} %bitcast.55), calls=%async_computation.2 | async-start | bytes 1835008
  106.3 20.9 %collective-permute-start.7 = (f32[12,102,3]{1,0,2:T(8,128)S(1)}, f32[12,102,3]{1,0,2:T(8,128)}, u32[]{:S(2)}, u32[]{:S(2)}) collective-permute-start(f32[12,102,3]{1,0,2:T(8,128)S(1)} %get-tuple-element.69), channel_id=1, source_target_pairs={{0,16},{16,32},{32,48},{48,64},{64,80},{80,96},{96,112},{112,128},... | collective-permute-start | bytes 44072 | tf_op jit(solution)/shard_map/ppermute | solution.py:152
  110.6 17.7 %collective-permute-start.8 = (f32[12,102,3]{1,0,2:T(8,128)S(1)}, f32[12,102,3]{1,0,2:T(8,128)}, u32[]{:S(2)}, u32[]{:S(2)}) collective-permute-start(f32[12,102,3]{1,0,2:T(8,128)S(1)} %get-tuple-element.70), channel_id=1, source_target_pairs={{16,0},{32,16},{48,32},{64,48},{80,64},{96,80},{112,96},{128,112},... | collective-permute-start | bytes 44072 | tf_op jit(solution)/shard_map/ppermute | solution.py:153
  130.1 2.3 %copy-start.10 = (f32[100,132]{1,0:T(8,128)S(1)}, f32[100,132]{1,0:T(8,128)}, u32[]{:S(2)}) copy-start(f32[100,132]{1,0:T(8,128)} %get-tuple-element.65) | copy-start | bytes 158404
  130.1 2.3 %copy-start.11 = (f32[100,132]{1,0:T(8,128)S(1)}, f32[100,132]{1,0:T(8,128)}, u32[]{:S(2)}) copy-start(f32[100,132]{1,0:T(8,128)} %get-tuple-element.66) | copy-start | bytes 158404
  130.1 2.3 %copy-start.25 = (f32[100]{0:T(128)S(1)}, f32[100]{0:T(128)}, u32[]{:S(2)}) copy-start(f32[100]{0:T(128)} %slice_multiply_fusion.8) | copy-start | bytes 1204
  132.4 1.2 copy-start.4
  132.5 1.2 copy-start.15
  132.5 1.2 copy-start.19
  132.5 1.2 copy-start.20
  132.5 1.2 copy-start.21
  132.5 1.2 copy-start.22
  134.5 0.9 copy-start.14
  135.6 2.1 %copy-start.9 = (f32[98,130]{1,0:T(8,128)S(1)}, f32[98,130]{1,0:T(8,128)}, u32[]{:S(2)}) copy-start(f32[98,130]{1,0:T(8,128)} %get-tuple-element.77) | copy-start | bytes 152884
  137.7 0.9 copy-start.12
  139.4 0.9 copy-start.13
  140.3 0.6 copy-start.24
  140.9 1.9 %copy-start.23 = (f32[6]{0:T(128)S(1)}, f32[6]{0:T(128)}, u32[]{:S(2)}) copy-start(f32[6]{0:T(128)} %constant.68) | copy-start | bytes 76
  140.9 2.0 %copy-start.6 = (f32[96,128]{1,0:T(8,128)S(1)}, f32[96,128]{1,0:T(8,128)}, u32[]{:S(2)}) copy-start(f32[96,128]{1,0:T(8,128)} %copy-done.5) | copy-start | bytes 147460
Sparse Core Ops, SparseCore 0:
  13.8 74.4 all-gather.1

commit v7 on v4

--- a/solution.py
+++ b/solution.py
@@ -131,10 +131,11 @@
     size = lax.axis_size("lon")
     up = [(i, (i + 1) % size) for i in range(size)]
     down = [(j, i) for i, j in up]
+    green_pad = jnp.pad(green_blocks, ((0, 0), (0, 0), (0, spare))).reshape(green_ext.shape[0], -1)
+    sal = jnp.einsum("rs,ksc->krc", green_pad, gathered, precision=lax.Precision.HIGHEST)
+    edge_sal, sal = lax.optimization_barrier((edge_sal, sal))
     before = lax.ppermute(edge_sal[:, :, HALO:], "lon", up)
     after = lax.ppermute(edge_sal[:, :, :HALO], "lon", down)
-    green_pad = jnp.pad(green_blocks, ((0, 0), (0, 0), (0, spare))).reshape(green_ext.shape[0], -1)
-    sal = jnp.einsum("rs,ksc->krc", green_pad, gathered, precision=lax.Precision.HIGHEST)
     sal = jnp.concatenate([before, sal, after], axis=2)
     potential = stack[:12] - sal
     flows = stack[12:36]

time: 137 us -> 140 us (1.022)
  local copies, waits for them, and re-layouts: 20.5 us -> 23.1 us
    unnamed x68 -> x76, local copies, waits for them, and re-layouts: 2.8 us -> 3.9 us
  transfers between devices with their start and end apart: 9 -> 9, of which waited for: 4 -> 4; matrix products, arithmetic and copies ran while one was open for 30% -> 23% of each run, Pallas kernels for 0% -> 0%
where the time goes in v7:
time: 140 us
  starting transfers between devices  40.2 us (29%)
  other arithmetic  29.2 us (21%)
  local copies, waits for them, and re-layouts  23.1 us (16%)
  waiting for transfers between devices  19 us (14%)
  between operations  14.7 us (10%)
  matrix products  13.5 us (10%)
    ppermute x1, starting transfers between devices, widen_lon(): after = lax.ppermute(initial, 'lon', down)  10 us
    ppermute x2, starting transfers between devices, widen_lat(): before = lax.ppermute(last, LAT, up)  9.56 us
    dot_general x1, matrix products, per_device(): jnp.einsum('rs,ksc->krc', green_pad, gathered, precision=lax.Precision.HI...  9.38 us
    all_gather x1, waiting for transfers between devices, per_device(): gathered = lax.all_gather(packed, LAT, axis=1, tiled=True)  8.31 us
    ppermute x2, starting transfers between devices, widen_lat(): after = lax.ppermute(initial, LAT, down)  7.7 us
    ppermute x1, starting transfers between devices, per_device(): after = lax.ppermute(edge_sal[:, :, :HALO], 'lon', down)  6.94 us
    slice x2, local copies, waits for them, and re-layouts, widen_lon(): last = lax.slice_in_dim(array, length - width, length, axis=dim)  4.74 us
    ppermute x2, waiting for transfers between devices, widen_lat(): after = lax.ppermute(initial, LAT, down)  4.27 us
  transfers between devices with their start and end apart: 9, of which 4 were waited for; matrix products, arithmetic and copies ran while one was open for 23% of the time, Pallas kernels for 0%

profile of v7, /device:TPU:1, one launch (start us, length us, event | category | flops | bytes accessed | tf_op | source)
XLA Modules:
  0.0 139.7 jit_solution(1967696804804820530)
XLA Ops:
  7.2 0.8 fusion.60
  8.0 0.8 convert_element_type.10
  8.8 1.7 %fusion.45 = f32[12,96,128]{2,1,0:T(8,128)S(1)} fusion(f32[12,96,128]{2,1,0:T(8,128)} %param.12, f32[96,128]{1,0:T(8,128)S(1)} %convert_element_type.10, f32[128,128]{1,0:T(8,128)} %param.19), kind=kOutput, calls=%fused_computation.99 | convolution fusion | flops 226639872 | bytes 1294336 | tf_op jit(solution)/shard_map/krj,cj->krc/dot_general | solution.py:112
  10.5 1.2 convolution_bitcast_fusion.2
  11.7 0.9 select_maximum_fusion
  12.7 4.6 %collective-permute-start.4 = (f32[3,1536]{1,0:T(4,128)S(1)}, f32[3,1536]{1,0:T(4,128)S(1)}, u32[]{:S(2)}, u32[]{:S(2)}) collective-permute-start(f32[3,1536]{1,0:T(4,128)S(1)} %get-tuple-element.45), channel_id=1, source_target_pairs={{0,1},{1,2},{2,3},{3,4},{4,5},{5,6},{6,7},{7,8},{8,9},{9,10},{10,1... | collective-permute-start | bytes 55304 | tf_op jit(solution)/shard_map/ppermute | solution.py:40
  17.3 5.6 %collective-permute-start.5 = (f32[3,1536]{1,0:T(4,128)S(1)}, f32[3,1536]{1,0:T(4,128)S(1)}, u32[]{:S(2)}, u32[]{:S(2)}) collective-permute-start(f32[3,1536]{1,0:T(4,128)S(1)} %get-tuple-element.46), channel_id=1, source_target_pairs={{1,0},{2,1},{3,2},{4,3},{5,4},{6,5},{7,6},{8,7},{9,8},{10,9},{11,1... | collective-permute-start | bytes 55304 | tf_op jit(solution)/shard_map/ppermute | solution.py:41
  22.9 1.1 subtract_dynamic-update-slice_fusion
  24.1 1.1 constant_dynamic-update-slice_fusion.1
  25.4 2.6 %fusion.57 = (f32[39,96,3]{2,1,0:T(8,128)}, f32[39,96,3]{2,1,0:T(8,128)}) fusion(f32[39,96,128]{2,1,0:T(8,128)S(1)} %bitcast_dynamic-update-slice_fusion), kind=kLoop, calls=%fused_computation.140 | loop fusion | bytes 179712 | tf_op jit(solution)/shard_map/slice | solution.py:27
  28.0 2.1 %copy.21 = f32[39,96,3]{1,0,2:T(8,128)S(1)} copy(f32[39,96,3]{2,1,0:T(8,128)} %get-tuple-element.39) | data formatting | bytes 89856 | tf_op jit(solution)/shard_map/slice | solution.py:28
  30.1 10.0 %collective-permute-start.1 = (f32[39,96,3]{1,0,2:T(8,128)S(1)}, f32[39,96,3]{1,0,2:T(8,128)S(1)}, u32[]{:S(2)}, u32[]{:S(2)}) collective-permute-start(f32[39,96,3]{1,0,2:T(8,128)S(1)} %copy.21), channel_id=1, source_target_pairs={{16,0},{32,16},{48,32},{64,48},{80,64},{96,80},{112,96},{128,112},... | collective-permute-start | bytes 134792 | tf_op jit(solution)/shard_map/ppermute | solution.py:30
  40.1 2.1 %copy.20 = f32[39,96,3]{1,0,2:T(8,128)S(1)} copy(f32[39,96,3]{2,1,0:T(8,128)} %get-tuple-element.38) | data formatting | bytes 89856 | tf_op jit(solution)/shard_map/slice | solution.py:27
  42.3 1.9 %collective-permute-start = (f32[39,96,3]{1,0,2:T(8,128)S(1)}, f32[39,96,3]{1,0,2:T(8,128)S(1)}, u32[]{:S(2)}, u32[]{:S(2)}) collective-permute-start(f32[39,96,3]{1,0,2:T(8,128)S(1)} %copy.20), channel_id=1, source_target_pairs={{0,16},{16,32},{32,48},{48,64},{64,80},{80,96},{96,112},{112,128},... | collective-permute-start | bytes 134792 | tf_op jit(solution)/shard_map/ppermute | solution.py:29
  44.3 0.6 slice_multiply_fusion.7
  44.9 0.6 fusion.62
  45.6 0.7 broadcast_multiply_fusion.4
  46.2 0.6 slice_multiply_fusion.8
  46.8 4.1 %collective-permute-done = f32[39,96,3]{1,0,2:T(8,128)S(1)} collective-permute-done((f32[39,96,3]{1,0,2:T(8,128)S(1)}, f32[39,96,3]{1,0,2:T(8,128)S(1)}, u32[]{:S(2)}, u32[]{:S(2)}) %collective-permute-start) | collective-permute-done | bytes 44960 | tf_op jit(solution)/shard_map/ppermute | solution.py:29
  51.0 1.9 %copy.22 = f32[39,96,3]{2,1,0:T(8,128)} copy(f32[39,96,3]{1,0,2:T(8,128)S(1)} %collective-permute-done) | data formatting | bytes 89856 | tf_op jit(solution)/shard_map/ppermute | solution.py:29
  52.8 1.9 %copy.23 = f32[39,96,3]{2,1,0:T(8,128)} copy(f32[39,96,3]{1,0,2:T(8,128)S(1)} %collective-permute-done.1) | data formatting | bytes 89856 | tf_op jit(solution)/shard_map/ppermute | solution.py:30
  54.8 2.2 %pad_maximum_fusion.5 = (f32[39,3,134]{2,1,0:T(4,128)}, f32[39,3,134]{2,1,0:T(4,128)}) fusion(f32[39,96,3]{2,1,0:T(8,128)} %copy.23, f32[39,96,128]{2,1,0:T(8,128)S(1)} %bitcast_dynamic-update-slice_fusion, f32[39,96,3]{2,1,0:T(8,128)} %copy.22), kind=kLoop, calls=%fused_computation.108 | loop fusion | flops 62712 | bytes 2132208 | tf_op jit(solution)/shard_map/slice | solution.py:38
  57.0 4.9 %collective-permute-start.2 = (f32[39,3,134]{2,1,0:T(4,128)}, f32[39,3,134]{2,1,0:T(4,128)S(1)}, u32[]{:S(2)}, u32[]{:S(2)}) collective-permute-start(f32[39,3,134]{2,1,0:T(4,128)} %get-tuple-element.26), channel_id=1, source_target_pairs={{0,1},{1,2},{2,3},{3,4},{4,5},{5,6},{6,7},{7,8},{8,9},{9,10},{10,1... | collective-permute-start | bytes 188144 | tf_op jit(solution)/shard_map/ppermute | solution.py:40
  61.9 2.1 %collective-permute-start.3 = (f32[39,3,134]{2,1,0:T(4,128)}, f32[39,3,134]{2,1,0:T(4,128)}, u32[]{:S(2)}, u32[]{:S(2)}) collective-permute-start(f32[39,3,134]{2,1,0:T(4,128)} %get-tuple-element.27), channel_id=1, source_target_pairs={{1,0},{2,1},{3,2},{4,3},{5,4},{6,5},{7,6},{8,7},{9,8},{10,9},{11,1... | collective-permute-start | bytes 188144 | tf_op jit(solution)/shard_map/ppermute | solution.py:41
  64.1 0.1 pad_maximum_fusion.2
  64.1 0.3 copy.25
  64.4 1.0 pad.9
  65.4 2.2 %collective-permute-done.2 = f32[39,3,134]{2,1,0:T(4,128)S(1)} collective-permute-done((f32[39,3,134]{2,1,0:T(4,128)}, f32[39,3,134]{2,1,0:T(4,128)S(1)}, u32[]{:S(2)}, u32[]{:S(2)}) %collective-permute-start.2) | collective-permute-done | bytes 62744 | tf_op jit(solution)/shard_map/ppermute | solution.py:40
  67.6 0.7 copy-done.12
  68.3 4.3 %collective-permute-done.3 = f32[39,3,134]{2,1,0:T(4,128)} collective-permute-done((f32[39,3,134]{2,1,0:T(4,128)}, f32[39,3,134]{2,1,0:T(4,128)}, u32[]{:S(2)}, u32[]{:S(2)}) %collective-permute-start.3) | collective-permute-done | bytes 62744 | tf_op jit(solution)/shard_map/ppermute | solution.py:41
  72.5 1.9 %maximum_bitcast_fusion.2 = (f32[102,134]{1,0:T(8,128)}, f32[102,134]{1,0:T(8,128)S(1)}, f32[102,134]{1,0:T(8,128)S(1)}) fusion(f32[39,3,134]{2,1,0:T(4,128)} %collective-permute-done.3, f32[39,3,134]{2,1,0:T(4,128)} %copy-done.12, f32[39,96,3]{2,1,0:T(8,128)} %copy.23, f32[39,96,128]{2,1,0:T(8,128)S(1)} %bitcast_dynamic-update-slice_fusion, ...), kind=kLoop, calls=%fused_computation.115 | loop fusion | flops 164016 | bytes 2296224 | tf_op jit(solution)/shard_map/squeeze | solution.py:142
  74.5 0.4 copy-done.2
  74.9 2.6 %pad_maximum_fusion = f32[39,102,134]{2,1,0:T(8,128)S(1)} fusion(f32[39,3,134]{2,1,0:T(4,128)} %collective-permute-done.3, f32[39,96,3]{2,1,0:T(8,128)S(1)} %copy-done.2, f32[39,96,128]{2,1,0:T(8,128)S(1)} %bitcast_dynamic-update-slice_fusion, f32[39,96,3]{2,1,0:T(8,128)S(1)} %copy-done.1, f32[39,3,134]{2,1,0:T(4,128)S(1)} %copy-done.13), kind=kLoop, calls=%fused_computation | loop fusion | flops 2132208 | bytes 4264416 | tf_op jit(solution)/shard_map/concatenate | solution.py:42
  77.6 0.9 slice_add_fusion.3
  78.5 1.2 slice_add_fusion.4
  79.7 2.1 %slice_add_fusion = f32[24,100,132]{2,1,0:T(8,128)S(1)} fusion(f32[39,102,134]{2,1,0:T(8,128)S(1)} %pad_maximum_fusion), kind=kLoop, calls=%fused_computation.14 | loop fusion | flops 950400 | bytes 6336000 | tf_op jit(solution)/shard_map/add | solution.py:79
  81.8 8.3 %all-gather.2.cloned.1.call-done = f32[12,1664,128]{2,1,0:T(8,128)} async-done(((f32[12,104,128]{2,1,0:T(8,128)}), f32[12,1664,128]{2,1,0:T(8,128)}) %all-gather.2.cloned.1.call-update) | async-done | bytes 10223632 | tf_op jit(solution)/shard_map/all_gather | solution.py:119
  90.2 1.3 slice.278
  91.4 1.3 convolution_bitcast_fusion.1
  92.7 9.4 %convolution_bitcast_fusion = f32[12,102,128]{2,1,0:T(8,128)S(1)} fusion(f32[12,1664,128]{2,1,0:T(8,128)} %all-gather.2.cloned.1.call-done, f32[102,1664,1]{0,1,2:T(8,128)S(1)} %bitcast.40), kind=kOutput, calls=%fused_computation.46 | convolution fusion | flops 3128426496 | bytes 11529216 | tf_op jit(solution)/shard_map/rs,ksc->krc/dot_general | solution.py:135
  102.1 4.0 %collective-permute-start.6 = (f32[12,102,3]{1,0,2:T(8,128)S(1)}, f32[12,102,3]{1,0,2:T(8,128)}, u32[]{:S(2)}, u32[]{:S(2)}) collective-permute-start(f32[12,102,3]{1,0,2:T(8,128)S(1)} %get-tuple-element.65), channel_id=1, source_target_pairs={{0,16},{16,32},{32,48},{48,64},{64,80},{80,96},{96,112},{112,128},... | collective-permute-start | bytes 44072 | tf_op jit(solution)/shard_map/ppermute | solution.py:137
  106.1 6.9 %collective-permute-start.7 = (f32[12,102,3]{1,0,2:T(8,128)S(1)}, f32[12,102,3]{1,0,2:T(8,128)}, u32[]{:S(2)}, u32[]{:S(2)}) collective-permute-start(f32[12,102,3]{1,0,2:T(8,128)S(1)} %get-tuple-element.66), channel_id=1, source_target_pairs={{16,0},{32,16},{48,32},{64,48},{80,64},{96,80},{112,96},{128,112},... | collective-permute-start | bytes 44072 | tf_op jit(solution)/shard_map/ppermute | solution.py:138
  113.1 0.8 slice_negate_fusion.1
  113.9 0.7 slice.282
  114.6 0.7 slice.274
  115.4 1.9 %copy.28 = f32[12,102,3]{2,1,0:T(8,128)} copy(f32[12,102,3]{1,0,2:T(8,128)} %collective-permute-done.7) | data formatting | bytes 29376 | tf_op jit(solution)/shard_map/ppermute | solution.py:138
  117.2 1.9 %copy.27 = f32[12,102,3]{2,1,0:T(8,128)} copy(f32[12,102,3]{1,0,2:T(8,128)} %collective-permute-done.6) | data formatting | bytes 29376 | tf_op jit(solution)/shard_map/ppermute | solution.py:137
  119.1 2.3 %slice_subtract_fusion.2 = f32[12,102,134]{2,1,0:T(8,128)S(1)} fusion(f32[39,102,134]{2,1,0:T(8,128)} %copy-done, f32[12,102,3]{2,1,0:T(8,128)} %copy.28, f32[12,102,128]{2,1,0:T(8,128)S(1)} %convolution_bitcast_fusion, f32[12,102,3]{2,1,0:T(8,128)} %copy.27), kind=kLoop, calls=%fused_computation.41 | loop fusion | flops 492048 | bytes 1968192 | tf_op jit(solution)/shard_map/sub | solution.py:140
  121.5 1.1 fusion.10
  122.7 0.8 fusion.19
  123.5 0.4 fusion.21
  123.9 0.5 copy-done.20
  124.4 0.2 maximum_multiply_fusion.1
  124.6 2.1 %fusion.2 = f32[24,98,130]{2,1,0:T(8,128)S(1)} fusion(f32[12,100,132]{2,1,0:T(8,128)S(1)} %get-tuple-element.57, f32[12,100,132]{2,1,0:T(8,128)S(1)} %get-tuple-element.56), kind=kLoop, calls=%fused_computation.9 | loop fusion | flops 2140320 | bytes 2490240 | tf_op jit(solution)/shard_map/add | solution.py:79
  126.7 0.8 fusion.6
  127.6 0.1 copy-done.18
  127.6 0.8 fusion.23
  128.5 0.4 fusion.26
  128.9 0.5 copy-done.19
  129.4 0.2 maximum_multiply_fusion.2
  129.6 0.4 copy-done.34
  130.0 1.8 %fusion.58 = (f32[12,96,128]{2,1,0:T(8,128)}, f32[12,96,128]{2,1,0:T(8,128)S(1)}, f32[12,96,128]{2,1,0:T(8,128)}) fusion(f32[12,98,130]{2,1,0:T(8,128)S(1)} %get-tuple-element.52, f32[96]{0:T(128)S(1)} %copy-done.34, f32[12,98,130]{2,1,0:T(8,128)S(1)} %get-tuple-element.51), kind=kLoop, calls=%fused_computation.141 | loop fusion | flops 737280 | bytes 5308800 | tf_op jit(solution)/shard_map/slice | solution.py:169
  131.8 0.1 fusion.47
  132.0 0.9 maximum_multiply_fusion.4
  (81 shorter events, 0.4 us)
Async XLA Ops:
  7.2 3.4 %copy-start.3 = (f32[12,96,128]{2,1,0:T(8,128)S(1)}, f32[12,96,128]{2,1,0:T(8,128)}, u32[]{:S(2)}) copy-start(f32[12,96,128]{2,1,0:T(8,128)} %param.12) | copy-start | bytes 1769476
  7.2 83.0 %all-gather.2.cloned.1.call-start = ((), (), s32[]{:S(2)}) async-start(), calls=%async_computation | async-start | bytes 10862592 | tf_op jit(solution)/shard_map/all_gather | solution.py:119
  8.8 1.7 %copy-start.9 = (f32[96,128]{1,0:T(8,128)}, f32[96,128]{1,0:T(8,128)S(1)}, u32[]{:S(2)}) copy-start(f32[96,128]{1,0:T(8,128)S(1)} %convert_element_type.10) | copy-start | bytes 147460
  10.5 2.1 %copy-start.11 = (f32[96,1536]{1,0:T(8,128)S(1)}, f32[96,1536]{1,0:T(8,128)}, u32[]{:S(2)}) copy-start(f32[96,1536]{1,0:T(8,128)} %param.20) | copy-start | bytes 1769476
  12.7 51.4 %collective-permute-start.4 = (f32[3,1536]{1,0:T(4,128)S(1)}, f32[3,1536]{1,0:T(4,128)S(1)}, u32[]{:S(2)}, u32[]{:S(2)}) collective-permute-start(f32[3,1536]{1,0:T(4,128)S(1)} %get-tuple-element.45), channel_id=1, source_target_pairs={{0,1},{1,2},{2,3},{3,4},{4,5},{5,6},{6,7},{7,8},{8,9},{9,10},{10,1... | collective-permute-start | bytes 55304 | tf_op jit(solution)/shard_map/ppermute | solution.py:40
  17.3 7.9 %copy-start.14 = (f32[12,96,128]{2,1,0:T(8,128)S(1)}, f32[12,96,128]{2,1,0:T(8,128)}, u32[]{:S(2)}) copy-start(f32[12,96,128]{2,1,0:T(8,128)} %param.15) | copy-start | bytes 1769476
  17.3 46.7 %collective-permute-start.5 = (f32[3,1536]{1,0:T(4,128)S(1)}, f32[3,1536]{1,0:T(4,128)S(1)}, u32[]{:S(2)}, u32[]{:S(2)}) collective-permute-start(f32[3,1536]{1,0:T(4,128)S(1)} %get-tuple-element.46), channel_id=1, source_target_pairs={{1,0},{2,1},{3,2},{4,3},{5,4},{6,5},{7,6},{8,7},{9,8},{10,9},{11,1... | collective-permute-start | bytes 55304 | tf_op jit(solution)/shard_map/ppermute | solution.py:41
  24.1 1.2 copy-start.23
  24.1 1.3 copy-start.24
  24.1 1.3 copy-start.22
  30.1 22.7 %collective-permute-start.1 = (f32[39,96,3]{1,0,2:T(8,128)S(1)}, f32[39,96,3]{1,0,2:T(8,128)S(1)}, u32[]{:S(2)}, u32[]{:S(2)}) collective-permute-start(f32[39,96,3]{1,0,2:T(8,128)S(1)} %copy.21), channel_id=1, source_target_pairs={{16,0},{32,16},{48,32},{64,48},{80,64},{96,80},{112,96},{128,112},... | collective-permute-start | bytes 134792 | tf_op jit(solution)/shard_map/ppermute | solution.py:30
  42.3 8.7 %collective-permute-start = (f32[39,96,3]{1,0,2:T(8,128)S(1)}, f32[39,96,3]{1,0,2:T(8,128)S(1)}, u32[]{:S(2)}, u32[]{:S(2)}) collective-permute-start(f32[39,96,3]{1,0,2:T(8,128)S(1)} %copy.20), channel_id=1, source_target_pairs={{0,16},{16,32},{32,48},{48,64},{64,80},{80,96},{96,112},{112,128},... | collective-permute-start | bytes 134792 | tf_op jit(solution)/shard_map/ppermute | solution.py:29
  57.0 10.6 %collective-permute-start.2 = (f32[39,3,134]{2,1,0:T(4,128)}, f32[39,3,134]{2,1,0:T(4,128)S(1)}, u32[]{:S(2)}, u32[]{:S(2)}) collective-permute-start(f32[39,3,134]{2,1,0:T(4,128)} %get-tuple-element.26), channel_id=1, source_target_pairs={{0,1},{1,2},{2,3},{3,4},{4,5},{5,6},{6,7},{7,8},{8,9},{9,10},{10,1... | collective-permute-start | bytes 188144 | tf_op jit(solution)/shard_map/ppermute | solution.py:40
  61.9 10.6 %collective-permute-start.3 = (f32[39,3,134]{2,1,0:T(4,128)}, f32[39,3,134]{2,1,0:T(4,128)}, u32[]{:S(2)}, u32[]{:S(2)}) collective-permute-start(f32[39,3,134]{2,1,0:T(4,128)} %get-tuple-element.27), channel_id=1, source_target_pairs={{1,0},{2,1},{3,2},{4,3},{5,4},{6,5},{7,6},{8,7},{9,8},{10,9},{11,1... | collective-permute-start | bytes 188144 | tf_op jit(solution)/shard_map/ppermute | solution.py:41
  67.6 0.7 copy-start.12
  72.5 1.9 %copy-start.1 = (f32[39,96,3]{2,1,0:T(8,128)S(1)}, f32[39,96,3]{2,1,0:T(8,128)}, u32[]{:S(2)}) copy-start(f32[39,96,3]{2,1,0:T(8,128)} %copy.22) | copy-start | bytes 134788
  72.5 2.4 %copy-start.2 = (f32[39,96,3]{2,1,0:T(8,128)S(1)}, f32[39,96,3]{2,1,0:T(8,128)}, u32[]{:S(2)}) copy-start(f32[39,96,3]{2,1,0:T(8,128)} %copy.23) | copy-start | bytes 134788
  72.5 2.4 %copy-start.13 = (f32[39,3,134]{2,1,0:T(4,128)S(1)}, f32[39,3,134]{2,1,0:T(4,128)}, u32[]{:S(2)}) copy-start(f32[39,3,134]{2,1,0:T(4,128)} %copy-done.12) | copy-start | bytes 188140
  77.6 2.2 %copy-start = (f32[39,102,134]{2,1,0:T(8,128)}, f32[39,102,134]{2,1,0:T(8,128)S(1)}, u32[]{:S(2)}) copy-start(f32[39,102,134]{2,1,0:T(8,128)S(1)} %pad_maximum_fusion) | copy-start | bytes 6396628
  90.2 2.5 %copy-start.4 = (f32[102,16,104]{0,2,1:T(8,128)S(1)}, f32[102,16,104]{0,2,1:T(8,128)}, u32[]{:S(2)}) copy-start(f32[102,16,104]{0,2,1:T(8,128)} %pad.9) | copy-start | bytes 2036740
  92.7 21.2 %copy-start.6 = (f32[102,134]{1,0:T(8,128)S(1)}, f32[102,134]{1,0:T(8,128)}, u32[]{:S(2)}) copy-start(f32[102,134]{1,0:T(8,128)} %get-tuple-element.23) | copy-start | bytes 164020
  102.1 15.1 %collective-permute-start.6 = (f32[12,102,3]{1,0,2:T(8,128)S(1)}, f32[12,102,3]{1,0,2:T(8,128)}, u32[]{:S(2)}, u32[]{:S(2)}) collective-permute-start(f32[12,102,3]{1,0,2:T(8,128)S(1)} %get-tuple-element.65), channel_id=1, source_target_pairs={{0,16},{16,32},{32,48},{48,64},{64,80},{80,96},{96,112},{112,128},... | collective-permute-start | bytes 44072 | tf_op jit(solution)/shard_map/ppermute | solution.py:137
  106.1 9.2 %collective-permute-start.7 = (f32[12,102,3]{1,0,2:T(8,128)S(1)}, f32[12,102,3]{1,0,2:T(8,128)}, u32[]{:S(2)}, u32[]{:S(2)}) collective-permute-start(f32[12,102,3]{1,0,2:T(8,128)S(1)} %get-tuple-element.66), channel_id=1, source_target_pairs={{16,0},{32,16},{48,32},{64,48},{80,64},{96,80},{112,96},{128,112},... | collective-permute-start | bytes 44072 | tf_op jit(solution)/shard_map/ppermute | solution.py:138
  119.1 2.3 %copy-start.16 = (f32[100,132]{1,0:T(8,128)S(1)}, f32[100,132]{1,0:T(8,128)}, u32[]{:S(2)}) copy-start(f32[100,132]{1,0:T(8,128)} %get-tuple-element.61) | copy-start | bytes 158404
  119.1 2.3 %copy-start.17 = (f32[100,132]{1,0:T(8,128)S(1)}, f32[100,132]{1,0:T(8,128)}, u32[]{:S(2)}) copy-start(f32[100,132]{1,0:T(8,128)} %get-tuple-element.62) | copy-start | bytes 158404
  119.1 2.3 %copy-start.35 = (f32[100]{0:T(128)S(1)}, f32[100]{0:T(128)}, u32[]{:S(2)}) copy-start(f32[100]{0:T(128)} %slice_multiply_fusion.8) | copy-start | bytes 1204
  121.4 1.2 copy-start.7
  121.4 1.2 copy-start.8
  121.4 1.2 copy-start.21
  121.5 1.2 copy-start.25
  121.5 1.2 copy-start.26
  121.5 1.2 copy-start.28
  121.5 1.2 copy-start.31
  121.5 1.2 copy-start.32
  123.5 0.9 copy-start.20
  124.6 2.1 %copy-start.15 = (f32[98,130]{1,0:T(8,128)S(1)}, f32[98,130]{1,0:T(8,128)}, u32[]{:S(2)}) copy-start(f32[98,130]{1,0:T(8,128)} %get-tuple-element.73) | copy-start | bytes 152884
  126.7 0.9 copy-start.5
  126.7 0.9 copy-start.18
  126.7 0.9 copy-start.27
  126.7 0.9 copy-start.29
  126.7 0.9 copy-start.30
  128.5 0.9 copy-start.19
  129.4 0.6 copy-start.34
  130.0 1.9 %copy-start.33 = (f32[6]{0:T(128)S(1)}, f32[6]{0:T(128)}, u32[]{:S(2)}) copy-start(f32[6]{0:T(128)} %constant.48) | copy-start | bytes 76
  130.0 2.0 %copy-start.10 = (f32[96,128]{1,0:T(8,128)S(1)}, f32[96,128]{1,0:T(8,128)}, u32[]{:S(2)}) copy-start(f32[96,128]{1,0:T(8,128)} %copy-done.9) | copy-start | bytes 147460
Sparse Core Ops, SparseCore 0:
  12.8 77.3 all-gather.1

commit v8 on v4

--- a/solution.py
+++ b/solution.py
@@ -113,6 +113,12 @@
     columns = mixed.shape[2]
     edge_rows = jnp.concatenate([lon_green[:HALO], lon_green[columns - HALO :]], axis=0)
     edges = jnp.einsum("ej,krj->ker", edge_rows, source, precision=lax.Precision.HIGHEST)
+    size = lax.axis_size("lon")
+    up = [(i, (i + 1) % size) for i in range(size)]
+    down = [(j, i) for i, j in up]
+    edges = jnp.concatenate(
+        [lax.ppermute(edges[:, HALO:], "lon", up), lax.ppermute(edges[:, :HALO], "lon", down)], axis=1
+    )
     spare = 8 * ((2 * HALO + 7) // 8)
     edges = jnp.pad(edges, ((0, 0), (0, spare - 2 * HALO), (0, columns - rows_here)))
     packed = jnp.concatenate([mixed, edges], axis=1)
@@ -127,12 +133,14 @@
     block = rows_here + spare
     green_blocks = green_ext.reshape(green_ext.shape[0], blocks, rows_here)
     lanes = gathered.reshape(12, blocks, block, columns)[:, :, rows_here : rows_here + 2 * HALO, :rows_here]
-    edge_sal = jnp.einsum("rbj,kbej->kre", green_blocks, lanes, precision=lax.Precision.HIGHEST)
-    size = lax.axis_size("lon")
-    up = [(i, (i + 1) % size) for i in range(size)]
-    down = [(j, i) for i, j in up]
-    before = lax.ppermute(edge_sal[:, :, HALO:], "lon", up)
-    after = lax.ppermute(edge_sal[:, :, :HALO], "lon", down)
+    green_before = lax.ppermute(green_blocks, "lon", up)
+    green_after = lax.ppermute(green_blocks, "lon", down)
+    before = jnp.einsum(
+        "rbj,kbej->kre", green_before, lanes[:, :, :HALO], precision=lax.Precision.HIGHEST
+    )
+    after = jnp.einsum(
+        "rbj,kbej->kre", green_after, lanes[:, :, HALO:], precision=lax.Precision.HIGHEST
+    )
     green_pad = jnp.pad(green_blocks, ((0, 0), (0, 0), (0, spare))).reshape(green_ext.shape[0], -1)
     sal = jnp.einsum("rs,ksc->krc", green_pad, gathered, precision=lax.Precision.HIGHEST)
     sal = jnp.concatenate([before, sal, after], axis=2)

time: 137 us -> 174 us (1.27)
  waiting for transfers between devices: 18.5 us -> 44.4 us
  starting transfers between devices: 40 us -> 45.4 us
  matrix products: 13.5 us -> 17.2 us
  local copies, waits for them, and re-layouts: 20.5 us -> 23.8 us
    all_gather x1, waiting for transfers between devices: 7.14 us -> 39.7 us  [per_device(): gathered = lax.all_gather(packed, LAT, axis=1, tiled=True)]
    ppermute x2 -> x4, starting transfers between devices: 10.9 us -> 23.2 us  [the longest x1 10.9 us: per_device(): lax.ppermute(edges[:, :HALO], 'lon', down)]
    ppermute x2, waiting for transfers between devices: 4.93 us -> 0.01 us  [widen_lat(): after = lax.ppermute(initial, LAT, down)]
    ppermute x2, starting transfers between devices: 7.52 us -> 3.97 us  [widen_lat(): after = lax.ppermute(initial, LAT, down)]
    dot_general x1 -> x2, matrix products: 1.25 us -> 4.22 us  [the longest x1 2.17 us: per_device(): jnp.einsum('rbj,kbej->kre', green_before, lanes[:, :, :HALO], precision=l...]
    ppermute x1, starting transfers between devices: 10 us -> 7.29 us  [widen_lon(): after = lax.ppermute(initial, 'lon', down)]
    ppermute x2, waiting for transfers between devices: 2.4 us -> 0.01 us  [widen_lat(): before = lax.ppermute(last, LAT, up)]
    ppermute x2 -> x0, local copies, waits for them, and re-layouts: 2.26 us -> none  [the longest x1 1.13 us: per_device(): before = lax.ppermute(edge_sal[:, :, HALO:], 'lon', up)]
  transfers between devices with their start and end apart: 9 -> 11, of which waited for: 4 -> 2; matrix products, arithmetic and copies ran while one was open for 30% -> 22% of each run, Pallas kernels for 0% -> 0%
where the time goes in v8:
time: 174 us; the launch traced here: 173 us
  starting transfers between devices  45.4 us (26%)
  waiting for transfers between devices  44.4 us (26%)
  other arithmetic  27.4 us (16%)
  local copies, waits for them, and re-layouts  23.8 us (14%)
  matrix products  17.2 us (10%)
  between operations  14.7 us (8%)
    all_gather x1, waiting for transfers between devices, per_device(): gathered = lax.all_gather(packed, LAT, axis=1, tiled=True)  39.7 us
    ppermute x1, starting transfers between devices, per_device(): lax.ppermute(edges[:, :HALO], 'lon', down)  10.9 us
    dot_general x1, matrix products, per_device(): jnp.einsum('rs,ksc->krc', green_pad, gathered, precision=lax.Precision.HI...  8.96 us
    ppermute x2, starting transfers between devices, widen_lat(): before = lax.ppermute(last, LAT, up)  8.94 us
    ppermute x1, starting transfers between devices, widen_lon(): after = lax.ppermute(initial, 'lon', down)  7.29 us
    ppermute x1, starting transfers between devices, per_device(): lax.ppermute(edges[:, HALO:], 'lon', up)  5.61 us
    ppermute x1, starting transfers between devices, per_device(): green_before = lax.ppermute(green_blocks, 'lon', up)  4.87 us
    slice x2, local copies, waits for them, and re-layouts, widen_lon(): last = lax.slice_in_dim(array, length - width, length, axis=dim)  4.78 us
  transfers between devices with their start and end apart: 11, of which 2 were waited for; matrix products, arithmetic and copies ran while one was open for 22% of the time, Pallas kernels for 0%

profile of v8, /device:TPU:1, one launch (start us, length us, event | category | flops | bytes accessed | tf_op | source)
XLA Modules:
  0.0 172.9 jit_solution(3593804458045081467)
XLA Ops:
  7.2 0.7 fusion.64
  7.9 0.8 convert_element_type.10
  8.7 2.3 %convolution_bitcast_fusion.1 = f32[12,6,96]{2,1,0:T(8,128)S(1)} fusion(f32[12,96,128]{2,1,0:T(8,128)} %param.12, f32[96,128]{1,0:T(8,128)S(1)} %convert_element_type.10, f32[3,128]{1,0:T(4,128)S(1)} %get-tuple-element.62, f32[3,128]{1,0:T(4,128)S(1)} %get-tuple-element.61), kind=kOutput, calls=%fused_computation.47 | convolution fusion | flops 10765056 | bytes 669696 | tf_op jit(solution)/shard_map/ej,krj->ker/dot_general | solution.py:115
  11.1 5.6 %collective-permute-start.4 = (f32[12,3,96]{2,1,0:T(4,128)S(1)}, f32[12,3,96]{2,1,0:T(4,128)S(1)}, u32[]{:S(2)}, u32[]{:S(2)}) collective-permute-start(f32[12,3,96]{2,1,0:T(4,128)S(1)} %get-tuple-element.63), channel_id=1, source_target_pairs={{0,16},{16,32},{32,48},{48,64},{64,80},{80,96},{96,112},{112,128},... | collective-permute-start | bytes 41480 | tf_op jit(solution)/shard_map/ppermute | solution.py:120
  16.7 10.9 %collective-permute-start.5 = (f32[12,3,96]{2,1,0:T(4,128)S(1)}, f32[12,3,96]{2,1,0:T(4,128)S(1)}, u32[]{:S(2)}, u32[]{:S(2)}) collective-permute-start(f32[12,3,96]{2,1,0:T(4,128)S(1)} %get-tuple-element.64), channel_id=1, source_target_pairs={{16,0},{32,16},{48,32},{64,48},{80,64},{96,80},{112,96},{128,112},... | collective-permute-start | bytes 41480 | tf_op jit(solution)/shard_map/ppermute | solution.py:120
  27.6 1.7 fusion.46
  29.3 0.9 pad_maximum_fusion.2
  30.3 4.1 %collective-permute-start.6 = (f32[3,1536]{1,0:T(4,128)S(1)}, f32[3,1536]{1,0:T(4,128)S(1)}, u32[]{:S(2)}, u32[]{:S(2)}) collective-permute-start(f32[3,1536]{1,0:T(4,128)S(1)} %get-tuple-element.43), channel_id=1, source_target_pairs={{0,1},{1,2},{2,3},{3,4},{4,5},{5,6},{6,7},{7,8},{8,9},{9,10},{10,1... | collective-permute-start | bytes 55304 | tf_op jit(solution)/shard_map/ppermute | solution.py:40
  34.4 2.1 %collective-permute-start.7 = (f32[3,1536]{1,0:T(4,128)S(1)}, f32[3,1536]{1,0:T(4,128)S(1)}, u32[]{:S(2)}, u32[]{:S(2)}) collective-permute-start(f32[3,1536]{1,0:T(4,128)S(1)} %get-tuple-element.44), channel_id=1, source_target_pairs={{1,0},{2,1},{3,2},{4,3},{5,4},{6,5},{7,6},{8,7},{9,8},{10,9},{11,1... | collective-permute-start | bytes 55304 | tf_op jit(solution)/shard_map/ppermute | solution.py:41
  36.4 1.1 subtract_dynamic-update-slice_fusion
  37.6 1.1 constant_dynamic-update-slice_fusion.1
  38.7 1.1 constant_dynamic-update-slice_fusion
  39.9 2.6 %fusion.61 = (f32[39,96,3]{2,1,0:T(8,128)}, f32[39,96,3]{2,1,0:T(8,128)}) fusion(f32[39,96,128]{2,1,0:T(8,128)S(1)} %bitcast_dynamic-update-slice_fusion), kind=kLoop, calls=%fused_computation.147 | loop fusion | bytes 179712 | tf_op jit(solution)/shard_map/slice | solution.py:27
  42.5 2.1 %copy.22 = f32[39,96,3]{1,0,2:T(8,128)S(1)} copy(f32[39,96,3]{2,1,0:T(8,128)} %get-tuple-element.37) | data formatting | bytes 89856 | tf_op jit(solution)/shard_map/slice | solution.py:28
  44.6 7.3 %collective-permute-start.1 = (f32[39,96,3]{1,0,2:T(8,128)S(1)}, f32[39,96,3]{1,0,2:T(8,128)S(1)}, u32[]{:S(2)}, u32[]{:S(2)}) collective-permute-start(f32[39,96,3]{1,0,2:T(8,128)S(1)} %copy.22), channel_id=1, source_target_pairs={{16,0},{32,16},{48,32},{64,48},{80,64},{96,80},{112,96},{128,112},... | collective-permute-start | bytes 134792 | tf_op jit(solution)/shard_map/ppermute | solution.py:30
  51.9 2.1 %copy.21 = f32[39,96,3]{1,0,2:T(8,128)S(1)} copy(f32[39,96,3]{2,1,0:T(8,128)} %get-tuple-element.36) | data formatting | bytes 89856 | tf_op jit(solution)/shard_map/slice | solution.py:27
  54.1 1.9 %collective-permute-start = (f32[39,96,3]{1,0,2:T(8,128)S(1)}, f32[39,96,3]{1,0,2:T(8,128)S(1)}, u32[]{:S(2)}, u32[]{:S(2)}) collective-permute-start(f32[39,96,3]{1,0,2:T(8,128)S(1)} %copy.21), channel_id=1, source_target_pairs={{0,16},{16,32},{32,48},{48,64},{64,80},{80,96},{96,112},{112,128},... | collective-permute-start | bytes 134792 | tf_op jit(solution)/shard_map/ppermute | solution.py:29
  56.1 0.7 slice_multiply_fusion.7
  56.8 0.1 fusion.66
  56.9 0.6 broadcast_multiply_fusion.4
  57.5 0.6 slice_multiply_fusion.8
  58.1 4.7 %collective-permute-done = f32[39,96,3]{1,0,2:T(8,128)S(1)} collective-permute-done((f32[39,96,3]{1,0,2:T(8,128)S(1)}, f32[39,96,3]{1,0,2:T(8,128)S(1)}, u32[]{:S(2)}, u32[]{:S(2)}) %collective-permute-start) | collective-permute-done | bytes 44960 | tf_op jit(solution)/shard_map/ppermute | solution.py:29
  62.8 1.9 %copy.23 = f32[39,96,3]{2,1,0:T(8,128)} copy(f32[39,96,3]{1,0,2:T(8,128)S(1)} %collective-permute-done) | data formatting | bytes 89856 | tf_op jit(solution)/shard_map/ppermute | solution.py:29
  64.6 1.9 %copy.24 = f32[39,96,3]{2,1,0:T(8,128)} copy(f32[39,96,3]{1,0,2:T(8,128)S(1)} %collective-permute-done.1) | data formatting | bytes 89856 | tf_op jit(solution)/shard_map/ppermute | solution.py:30
  66.6 2.3 %pad_maximum_fusion.6 = (f32[39,3,134]{2,1,0:T(4,128)}, f32[39,3,134]{2,1,0:T(4,128)}) fusion(f32[39,96,3]{2,1,0:T(8,128)} %copy.24, f32[39,96,128]{2,1,0:T(8,128)S(1)} %bitcast_dynamic-update-slice_fusion, f32[39,96,3]{2,1,0:T(8,128)} %copy.23), kind=kLoop, calls=%fused_computation.111 | loop fusion | flops 62712 | bytes 2132208 | tf_op jit(solution)/shard_map/slice | solution.py:38
  68.8 4.9 %collective-permute-start.2 = (f32[39,3,134]{2,1,0:T(4,128)}, f32[39,3,134]{2,1,0:T(4,128)}, u32[]{:S(2)}, u32[]{:S(2)}) collective-permute-start(f32[39,3,134]{2,1,0:T(4,128)} %get-tuple-element.24), channel_id=1, source_target_pairs={{0,1},{1,2},{2,3},{3,4},{4,5},{5,6},{6,7},{7,8},{8,9},{9,10},{10,1... | collective-permute-start | bytes 188144 | tf_op jit(solution)/shard_map/ppermute | solution.py:40
  73.7 1.9 %collective-permute-start.3 = (f32[39,3,134]{2,1,0:T(4,128)}, f32[39,3,134]{2,1,0:T(4,128)}, u32[]{:S(2)}, u32[]{:S(2)}) collective-permute-start(f32[39,3,134]{2,1,0:T(4,128)} %get-tuple-element.25), channel_id=1, source_target_pairs={{1,0},{2,1},{3,2},{4,3},{5,4},{6,5},{7,6},{8,7},{9,8},{10,9},{11,1... | collective-permute-start | bytes 188144 | tf_op jit(solution)/shard_map/ppermute | solution.py:41
  75.7 0.1 pad_maximum_fusion.3
  75.7 1.2 copy.26
  76.9 1.9 %collective-permute-start.9 = (f32[102,16,96]{0,2,1:T(8,128)}, f32[102,16,96]{0,2,1:T(8,128)}, u32[]{:S(2)}, u32[]{:S(2)}) collective-permute-start(f32[102,16,96]{0,2,1:T(8,128)} %bitcast.10), channel_id=1, source_target_pairs={{16,0},{32,16},{48,32},{64,48},{80,64},{96,80},{112,96},{128,112},... | collective-permute-start | bytes 1880072 | tf_op jit(solution)/shard_map/ppermute | solution.py:137
  78.8 4.9 %collective-permute-start.8 = (f32[102,16,96]{0,2,1:T(8,128)}, f32[102,16,96]{0,2,1:T(8,128)}, u32[]{:S(2)}, u32[]{:S(2)}) collective-permute-start(f32[102,16,96]{0,2,1:T(8,128)} %bitcast.10), channel_id=1, source_target_pairs={{0,16},{16,32},{32,48},{48,64},{64,80},{80,96},{96,112},{112,128},... | collective-permute-start | bytes 1880072 | tf_op jit(solution)/shard_map/ppermute | solution.py:136
  83.7 1.2 pad.9
  84.9 1.3 maximum_bitcast_fusion.2
  86.2 0.7 slice.292
  87.0 0.7 slice.281
  87.7 2.7 %pad_maximum_fusion = f32[39,102,134]{2,1,0:T(8,128)S(1)} fusion(f32[39,3,134]{2,1,0:T(4,128)} %collective-permute-done.3, f32[39,96,3]{2,1,0:T(8,128)S(1)} %copy-done.2, f32[39,96,128]{2,1,0:T(8,128)S(1)} %bitcast_dynamic-update-slice_fusion, f32[39,96,3]{2,1,0:T(8,128)S(1)} %copy-done.1, f32[39,3,134]{2,1,0:T(4,128)} %collective-permute-done.2), kind=kLoop, calls=%fused_computation | loop fusion | flops 2132208 | bytes 4264416 | tf_op jit(solution)/shard_map/concatenate | solution.py:42
  90.4 1.0 slice_add_fusion.4
  91.4 2.1 %slice_add_fusion = f32[24,100,132]{2,1,0:T(8,128)S(1)} fusion(f32[39,102,134]{2,1,0:T(8,128)S(1)} %pad_maximum_fusion), kind=kLoop, calls=%fused_computation.14 | loop fusion | flops 950400 | bytes 6336000 | tf_op jit(solution)/shard_map/add | solution.py:79
  93.5 0.8 slice_add_fusion.3
  94.3 0.8 slice_negate_fusion.1
  95.1 39.7 %all-gather.2.cloned.1.call-done = f32[12,1664,128]{2,1,0:T(8,128)} async-done(((f32[12,104,128]{2,1,0:T(8,128)}), f32[12,1664,128]{2,1,0:T(8,128)}) %all-gather.2.cloned.1.call-update) | async-done | bytes 10223632 | tf_op jit(solution)/shard_map/all_gather | solution.py:125
  134.8 2.3 %fusion.60 = (f32[12,16,3,96]{3,2,1,0:T(4,128)}, f32[12,16,3,96]{3,2,1,0:T(4,128)S(1)}) fusion(f32[12,16,104,128]{3,2,1,0:T(8,128)} %bitcast.44), kind=kLoop, calls=%fused_computation.146 | loop fusion | bytes 884736 | tf_op jit(solution)/shard_map/slice | solution.py:139
  137.1 2.0 %convolution_bitcast_fusion.2 = f32[12,3,102]{2,0,1:T(8,128)S(1)} fusion(f32[102,16,96]{0,2,1:T(8,128)} %collective-permute-done.9, f32[12,16,3,96]{3,2,1,0:T(4,128)S(1)} %get-tuple-element.20), kind=kOutput, calls=%fused_computation.48 | convolution fusion | flops 67682304 | bytes 862560 | tf_op jit(solution)/shard_map/rbj,kbej->kre/dot_general | solution.py:141
  139.2 1.1 copy.29
  140.3 2.2 %convolution_bitcast_fusion.3 = f32[12,102,3]{1,0,2:T(8,128)S(1)} fusion(f32[102,16,96]{0,2,1:T(8,128)} %collective-permute-done.8, f32[12,16,3,96]{3,2,1,0:T(4,128)} %get-tuple-element.19), kind=kOutput, calls=%fused_computation.49 | convolution fusion | flops 67682304 | bytes 862560 | tf_op jit(solution)/shard_map/rbj,kbej->kre/dot_general | solution.py:138
  142.5 1.1 copy.30
  143.6 9.0 %convolution_bitcast_fusion = f32[12,102,128]{2,1,0:T(8,128)S(1)} fusion(f32[12,1664,128]{2,1,0:T(8,128)} %all-gather.2.cloned.1.call-done, f32[102,1664,1]{0,1,2:T(8,128)S(1)} %bitcast.45), kind=kOutput, calls=%fused_computation.46 | convolution fusion | flops 3128426496 | bytes 11529216 | tf_op jit(solution)/shard_map/rs,ksc->krc/dot_general | solution.py:145
  152.7 1.9 %slice_subtract_fusion.2 = f32[12,102,134]{2,1,0:T(8,128)S(1)} fusion(f32[39,102,134]{2,1,0:T(8,128)} %copy-done, f32[12,102,3]{2,1,0:T(8,128)S(1)} %bitcast.46, f32[12,102,128]{2,1,0:T(8,128)S(1)} %convolution_bitcast_fusion, f32[12,102,3]{2,1,0:T(8,128)S(1)} %copy-done.5), kind=kLoop, calls=%fused_computation.41 | loop fusion | flops 492048 | bytes 1968192 | tf_op jit(solution)/shard_map/sub | solution.py:147
  154.7 1.1 fusion.10
  155.9 0.8 fusion.20
  156.7 0.4 fusion.22
  157.1 0.5 copy-done.17
  157.6 0.2 maximum_multiply_fusion.1
  157.8 2.1 %fusion.2 = f32[24,98,130]{2,1,0:T(8,128)S(1)} fusion(f32[12,100,132]{2,1,0:T(8,128)S(1)} %get-tuple-element.55, f32[12,100,132]{2,1,0:T(8,128)S(1)} %get-tuple-element.54), kind=kLoop, calls=%fused_computation.9 | loop fusion | flops 2140320 | bytes 2490240 | tf_op jit(solution)/shard_map/add | solution.py:79
  159.9 0.8 fusion.6
  160.7 0.1 copy-done.6
  160.8 0.8 fusion.24
  161.7 0.4 fusion.27
  162.1 0.5 copy-done.16
  162.5 0.2 maximum_multiply_fusion.2
  162.8 0.5 copy-done.27
  163.2 1.8 %fusion.62 = (f32[12,96,128]{2,1,0:T(8,128)}, f32[12,96,128]{2,1,0:T(8,128)S(1)}, f32[12,96,128]{2,1,0:T(8,128)}) fusion(f32[12,98,130]{2,1,0:T(8,128)S(1)} %get-tuple-element.50, f32[96]{0:T(128)S(1)} %copy-done.27, f32[12,98,130]{2,1,0:T(8,128)S(1)} %get-tuple-element.49), kind=kLoop, calls=%fused_computation.148 | loop fusion | flops 737280 | bytes 5308800 | tf_op jit(solution)/shard_map/slice | solution.py:176
  165.1 0.1 fusion.50
  165.2 0.9 maximum_multiply_fusion.4
  (73 shorter events, 0.4 us)
Async XLA Ops:
  7.2 127.6 %all-gather.2.cloned.1.call-start = ((), (), s32[]{:S(2)}) async-start(), calls=%async_computation | async-start | bytes 10862592 | tf_op jit(solution)/shard_map/all_gather | solution.py:125
  8.7 18.8 %copy-start.9 = (f32[96,128]{1,0:T(8,128)}, f32[96,128]{1,0:T(8,128)S(1)}, u32[]{:S(2)}) copy-start(f32[96,128]{1,0:T(8,128)S(1)} %convert_element_type.10) | copy-start | bytes 147460
  8.7 21.5 %copy-start.11 = (f32[96,1536]{1,0:T(8,128)S(1)}, f32[96,1536]{1,0:T(8,128)}, u32[]{:S(2)}) copy-start(f32[96,1536]{1,0:T(8,128)} %param.20) | copy-start | bytes 1769476
  11.0 25.4 %copy-start.3 = (f32[12,96,128]{2,1,0:T(8,128)S(1)}, f32[12,96,128]{2,1,0:T(8,128)}, u32[]{:S(2)}) copy-start(f32[12,96,128]{2,1,0:T(8,128)} %param.12) | copy-start | bytes 1769476
  11.1 18.2 %collective-permute-start.4 = (f32[12,3,96]{2,1,0:T(4,128)S(1)}, f32[12,3,96]{2,1,0:T(4,128)S(1)}, u32[]{:S(2)}, u32[]{:S(2)}) collective-permute-start(f32[12,3,96]{2,1,0:T(4,128)S(1)} %get-tuple-element.63), channel_id=1, source_target_pairs={{0,16},{16,32},{32,48},{48,64},{64,80},{80,96},{96,112},{112,128},... | collective-permute-start | bytes 41480 | tf_op jit(solution)/shard_map/ppermute | solution.py:120
  16.7 12.6 %collective-permute-start.5 = (f32[12,3,96]{2,1,0:T(4,128)S(1)}, f32[12,3,96]{2,1,0:T(4,128)S(1)}, u32[]{:S(2)}, u32[]{:S(2)}) collective-permute-start(f32[12,3,96]{2,1,0:T(4,128)S(1)} %get-tuple-element.64), channel_id=1, source_target_pairs={{16,0},{32,16},{48,32},{64,48},{80,64},{96,80},{112,96},{128,112},... | collective-permute-start | bytes 41480 | tf_op jit(solution)/shard_map/ppermute | solution.py:120
  30.3 45.4 %collective-permute-start.6 = (f32[3,1536]{1,0:T(4,128)S(1)}, f32[3,1536]{1,0:T(4,128)S(1)}, u32[]{:S(2)}, u32[]{:S(2)}) collective-permute-start(f32[3,1536]{1,0:T(4,128)S(1)} %get-tuple-element.43), channel_id=1, source_target_pairs={{0,1},{1,2},{2,3},{3,4},{4,5},{5,6},{6,7},{7,8},{8,9},{9,10},{10,1... | collective-permute-start | bytes 55304 | tf_op jit(solution)/shard_map/ppermute | solution.py:40
  34.3 5.5 %copy-start.20 = (f32[96,128]{1,0:T(8,128)S(1)}, f32[96,128]{1,0:T(8,128)}, u32[]{:S(2)}) copy-start(f32[96,128]{1,0:T(8,128)} %param.16) | copy-start | bytes 147460
  34.3 5.5 %copy-start.21 = (f32[96,128]{1,0:T(8,128)S(1)}, f32[96,128]{1,0:T(8,128)}, u32[]{:S(2)}) copy-start(f32[96,128]{1,0:T(8,128)} %param.17) | copy-start | bytes 147460
  34.4 5.5 %copy-start.19 = (s32[96,128]{1,0:T(8,128)S(1)}, s32[96,128]{1,0:T(8,128)}, u32[]{:S(2)}) copy-start(s32[96,128]{1,0:T(8,128)} %param.18) | copy-start | bytes 147460
  34.4 41.3 %collective-permute-start.7 = (f32[3,1536]{1,0:T(4,128)S(1)}, f32[3,1536]{1,0:T(4,128)S(1)}, u32[]{:S(2)}, u32[]{:S(2)}) collective-permute-start(f32[3,1536]{1,0:T(4,128)S(1)} %get-tuple-element.44), channel_id=1, source_target_pairs={{1,0},{2,1},{3,2},{4,3},{5,4},{6,5},{7,6},{8,7},{9,8},{10,9},{11,1... | collective-permute-start | bytes 55304 | tf_op jit(solution)/shard_map/ppermute | solution.py:41
  44.6 20.0 %collective-permute-start.1 = (f32[39,96,3]{1,0,2:T(8,128)S(1)}, f32[39,96,3]{1,0,2:T(8,128)S(1)}, u32[]{:S(2)}, u32[]{:S(2)}) collective-permute-start(f32[39,96,3]{1,0,2:T(8,128)S(1)} %copy.22), channel_id=1, source_target_pairs={{16,0},{32,16},{48,32},{64,48},{80,64},{96,80},{112,96},{128,112},... | collective-permute-start | bytes 134792 | tf_op jit(solution)/shard_map/ppermute | solution.py:30
  54.1 8.7 %collective-permute-start = (f32[39,96,3]{1,0,2:T(8,128)S(1)}, f32[39,96,3]{1,0,2:T(8,128)S(1)}, u32[]{:S(2)}, u32[]{:S(2)}) collective-permute-start(f32[39,96,3]{1,0,2:T(8,128)S(1)} %copy.21), channel_id=1, source_target_pairs={{0,16},{16,32},{32,48},{48,64},{64,80},{80,96},{96,112},{112,128},... | collective-permute-start | bytes 134792 | tf_op jit(solution)/shard_map/ppermute | solution.py:29
  68.8 16.1 %collective-permute-start.2 = (f32[39,3,134]{2,1,0:T(4,128)}, f32[39,3,134]{2,1,0:T(4,128)}, u32[]{:S(2)}, u32[]{:S(2)}) collective-permute-start(f32[39,3,134]{2,1,0:T(4,128)} %get-tuple-element.24), channel_id=1, source_target_pairs={{0,1},{1,2},{2,3},{3,4},{4,5},{5,6},{6,7},{7,8},{8,9},{9,10},{10,1... | collective-permute-start | bytes 188144 | tf_op jit(solution)/shard_map/ppermute | solution.py:40
  73.7 11.2 %collective-permute-start.3 = (f32[39,3,134]{2,1,0:T(4,128)}, f32[39,3,134]{2,1,0:T(4,128)}, u32[]{:S(2)}, u32[]{:S(2)}) collective-permute-start(f32[39,3,134]{2,1,0:T(4,128)} %get-tuple-element.25), channel_id=1, source_target_pairs={{1,0},{2,1},{3,2},{4,3},{5,4},{6,5},{7,6},{8,7},{9,8},{10,9},{11,1... | collective-permute-start | bytes 188144 | tf_op jit(solution)/shard_map/ppermute | solution.py:41
  76.9 60.2 %collective-permute-start.9 = (f32[102,16,96]{0,2,1:T(8,128)}, f32[102,16,96]{0,2,1:T(8,128)}, u32[]{:S(2)}, u32[]{:S(2)}) collective-permute-start(f32[102,16,96]{0,2,1:T(8,128)} %bitcast.10), channel_id=1, source_target_pairs={{16,0},{32,16},{48,32},{64,48},{80,64},{96,80},{112,96},{128,112},... | collective-permute-start | bytes 1880072 | tf_op jit(solution)/shard_map/ppermute | solution.py:137
  78.8 61.5 %collective-permute-start.8 = (f32[102,16,96]{0,2,1:T(8,128)}, f32[102,16,96]{0,2,1:T(8,128)}, u32[]{:S(2)}, u32[]{:S(2)}) collective-permute-start(f32[102,16,96]{0,2,1:T(8,128)} %bitcast.10), channel_id=1, source_target_pairs={{0,16},{16,32},{32,48},{48,64},{64,80},{80,96},{96,112},{112,128},... | collective-permute-start | bytes 1880072 | tf_op jit(solution)/shard_map/ppermute | solution.py:136
  84.9 2.8 %copy-start.1 = (f32[39,96,3]{2,1,0:T(8,128)S(1)}, f32[39,96,3]{2,1,0:T(8,128)}, u32[]{:S(2)}) copy-start(f32[39,96,3]{2,1,0:T(8,128)} %copy.23) | copy-start | bytes 134788
  84.9 2.8 %copy-start.2 = (f32[39,96,3]{2,1,0:T(8,128)S(1)}, f32[39,96,3]{2,1,0:T(8,128)}, u32[]{:S(2)}) copy-start(f32[39,96,3]{2,1,0:T(8,128)} %copy.24) | copy-start | bytes 134788
  90.4 3.1 %copy-start = (f32[39,102,134]{2,1,0:T(8,128)}, f32[39,102,134]{2,1,0:T(8,128)S(1)}, u32[]{:S(2)}) copy-start(f32[39,102,134]{2,1,0:T(8,128)S(1)} %pad_maximum_fusion) | copy-start | bytes 6396628
  143.6 9.0 %copy-start.4 = (f32[12,3,102]{1,2,0:T(8,128)S(1)}, f32[12,3,102]{1,2,0:T(8,128)}, u32[]{:S(2)}) copy-start(f32[12,3,102]{1,2,0:T(8,128)} %copy.29) | copy-start | bytes 44068
  143.6 9.0 %copy-start.5 = (f32[12,102,3]{2,1,0:T(8,128)S(1)}, f32[12,102,3]{2,1,0:T(8,128)}, u32[]{:S(2)}) copy-start(f32[12,102,3]{2,1,0:T(8,128)} %copy.30) | copy-start | bytes 44068
  152.6 2.0 %copy-start.13 = (f32[100,132]{1,0:T(8,128)S(1)}, f32[100,132]{1,0:T(8,128)}, u32[]{:S(2)}) copy-start(f32[100,132]{1,0:T(8,128)} %get-tuple-element.59) | copy-start | bytes 158404
  152.6 2.0 %copy-start.14 = (f32[100,132]{1,0:T(8,128)S(1)}, f32[100,132]{1,0:T(8,128)}, u32[]{:S(2)}) copy-start(f32[100,132]{1,0:T(8,128)} %get-tuple-element.60) | copy-start | bytes 158404
  152.6 2.0 %copy-start.28 = (f32[100]{0:T(128)S(1)}, f32[100]{0:T(128)}, u32[]{:S(2)}) copy-start(f32[100]{0:T(128)} %slice_multiply_fusion.8) | copy-start | bytes 1204
  154.6 1.2 copy-start.7
  154.7 1.2 copy-start.8
  154.7 1.2 copy-start.18
  154.7 1.2 copy-start.22
  154.7 1.2 copy-start.23
  154.7 1.2 copy-start.24
  154.7 1.2 copy-start.25
  156.7 0.9 copy-start.17
  157.8 2.1 %copy-start.12 = (f32[98,130]{1,0:T(8,128)S(1)}, f32[98,130]{1,0:T(8,128)}, u32[]{:S(2)}) copy-start(f32[98,130]{1,0:T(8,128)} %get-tuple-element.71) | copy-start | bytes 152884
  159.9 0.9 copy-start.6
  159.9 0.9 copy-start.15
  161.6 0.9 copy-start.16
  162.5 0.7 copy-start.27
  163.2 1.9 %copy-start.26 = (f32[6]{0:T(128)S(1)}, f32[6]{0:T(128)}, u32[]{:S(2)}) copy-start(f32[6]{0:T(128)} %constant.48) | copy-start | bytes 76
  163.2 2.0 %copy-start.10 = (f32[96,128]{1,0:T(8,128)S(1)}, f32[96,128]{1,0:T(8,128)}, u32[]{:S(2)}) copy-start(f32[96,128]{1,0:T(8,128)} %copy-done.9) | copy-start | bytes 147460
Sparse Core Ops, SparseCore 0:
  30.4 104.4 all-gather.1

commit v9 on v1

--- a/solution.py
+++ b/solution.py
@@ -10,6 +10,7 @@
 VISCOSITY = 0.5
 HALO = 3
 LAT = ("chip", "core")
+STREAMS = ((0, 1, 2), (3, 4, 5))
 
 
 def lat_index():
@@ -53,16 +54,17 @@
     return (east_slope, north_slope)
 
 
-def solve_cells(push_u, push_v, drag_field, wet_frac, coriolis):
+def solve_cells(push_u, push_v, drag_field, wet_frac, coriolis, freqs):
+    n = len(freqs)
     damping = drag_field + 4.0 * VISCOSITY
-    frequency = jnp.array(FREQS, jnp.float32)[:, None, None]
+    frequency = jnp.array(freqs, jnp.float32)[:, None, None]
     det_real = damping * damping - frequency * frequency + coriolis * coriolis
     det_imag = 2.0 * damping * frequency
     magnitude = det_real * det_real + det_imag * det_imag
 
     def combine(first, second, factor):
-        top_real = damping * first[:6] - frequency * first[6:] + factor * coriolis * second[:6]
-        top_imag = damping * first[6:] + frequency * first[:6] + factor * coriolis * second[6:]
+        top_real = damping * first[:n] - frequency * first[n:] + factor * coriolis * second[:n]
+        top_imag = damping * first[n:] + frequency * first[:n] + factor * coriolis * second[n:]
         out_real = (top_real * det_real + top_imag * det_imag) / magnitude
         out_imag = (top_imag * det_real - top_real * det_imag) / magnitude
         return wet_frac * jnp.concatenate([out_real, out_imag], axis=0)
@@ -74,24 +76,33 @@
     return field[..., trim : field.shape[-2] - trim, trim : field.shape[-1] - trim]
 
 
-def relax(flow_ext, east_slope, north_slope, depth_field, drag_field, wet_frac, coriolis):
+def relax(flow_ext, east_slope, north_slope, depth_field, drag_field, wet_frac, coriolis, freqs):
+    half = 2 * len(freqs)
     beside_all = (
         flow_ext[:, :-2, 1:-1]
         + flow_ext[:, 2:, 1:-1]
         + flow_ext[:, 1:-1, :-2]
         + flow_ext[:, 1:-1, 2:]
     )
-    push_u = -depth_field * east_slope + VISCOSITY * beside_all[:12]
-    push_v = -depth_field * north_slope + VISCOSITY * beside_all[12:]
-    return solve_cells(push_u, push_v, drag_field, wet_frac, coriolis)
-
-
-def surface(east_ext, north_ext, stretch, wet_frac):
+    push_u = -depth_field * east_slope + VISCOSITY * beside_all[:half]
+    push_v = -depth_field * north_slope + VISCOSITY * beside_all[half:]
+    return solve_cells(push_u, push_v, drag_field, wet_frac, coriolis, freqs)
+
+
+def surface(east_ext, north_ext, stretch, wet_frac, freqs):
+    n = len(freqs)
     spread = (east_ext[:, :, 2:] - east_ext[:, :, :-2]) * 0.5 * stretch + (
         north_ext[:, 2:, :] - north_ext[:, :-2, :]
     ) * 0.5
-    frequency = jnp.array(FREQS, jnp.float32)[:, None, None]
-    return wet_frac * jnp.concatenate([-spread[6:] / frequency, spread[:6] / frequency], axis=0)
+    frequency = jnp.array(freqs, jnp.float32)[:, None, None]
+    return wet_frac * jnp.concatenate([-spread[n:] / frequency, spread[:n] / frequency], axis=0)
+
+
+def pick(array, start, stream):
+    low, high = stream[0], stream[-1] + 1
+    return jnp.concatenate(
+        [array[start + low : start + high], array[start + 6 + low : start + 6 + high]], axis=0
+    )
 
 
 def per_device(
@@ -109,46 +120,86 @@
     total_rows = rows_here * lat_size()
     wet_frac = wet_mask.astype(jnp.float32)
     source = wet_frac * elevation
-    mixed = jnp.einsum("krj,cj->krc", source, lon_green, precision=lax.Precision.HIGHEST)
-    gathered = lax.all_gather(mixed, LAT, axis=1, tiled=True)
+    columns = source.shape[2]
+    edge_rows = jnp.concatenate([lon_green[:HALO], lon_green[columns - HALO :]], axis=0)
+    spare = 8 * ((2 * HALO + 7) // 8)
+    gathers = []
+    for stream in STREAMS:
+        part = pick(source, 0, stream)
+        mixed = jnp.einsum("krj,cj->krc", part, lon_green, precision=lax.Precision.HIGHEST)
+        edges = jnp.einsum("ej,krj->ker", edge_rows, part, precision=lax.Precision.HIGHEST)
+        edges = jnp.pad(edges, ((0, 0), (0, spare - 2 * HALO), (0, columns - rows_here)))
+        packed = jnp.concatenate([mixed, edges], axis=1)
+        gathers.append(lax.all_gather(packed, LAT, axis=1, tiled=True))
 
     fields = jnp.stack([ocean_depth, bottom_drag, wet_frac], axis=0)
     stack = jnp.concatenate([elevation - equilibrium, transport_u, transport_v, fields], axis=0)
     stack = widen_lat(widen_lon(stack, HALO, 2), HALO, 1)
     green_ext = widen_lat(lat_green, HALO, 0)
-
-    sal = jnp.einsum("rs,ksc->krc", green_ext, gathered, precision=lax.Precision.HIGHEST)
-    sal = widen_lon(sal, HALO, 2)
-    potential = stack[:12] - sal
-    flows = stack[12:36]
+    gathers[0], stack, green_ext = lax.optimization_barrier((gathers[0], stack, green_ext))
+
+    blocks = lat_size()
+    block = rows_here + spare
+    green_blocks = green_ext.reshape(green_ext.shape[0], blocks, rows_here)
+    green_pad = jnp.pad(green_blocks, ((0, 0), (0, 0), (0, spare))).reshape(green_ext.shape[0], -1)
+    size = lax.axis_size("lon")
+    up = [(i, (i + 1) % size) for i in range(size)]
+    down = [(j, i) for i, j in up]
     depth_ext, drag_ext, wet_ext = stack[36], stack[37], stack[38]
-
     first_row = lat_index() * rows_here - HALO
     stretch, coriolis = row_terms(first_row + jnp.arange(rows_here + 2 * HALO), total_rows)
-    east_slope, north_slope = slopes(potential, stretch[1:-1])
-    flows = relax(
-        flows,
-        east_slope,
-        north_slope,
-        inner(depth_ext, 1),
-        inner(drag_ext, 1),
-        inner(wet_ext, 1),
-        coriolis[1:-1],
-    )
-    flows = relax(
-        flows,
-        inner(east_slope, 1),
-        inner(north_slope, 1),
-        inner(depth_ext, 2),
-        inner(drag_ext, 2),
-        inner(wet_ext, 2),
-        coriolis[2:-2],
-    )
-    east_ext = flows[:12, 1:-1, :]
-    north_ext = flows[12:, :, 1:-1]
-    elevation_next = surface(east_ext, north_ext, stretch[HALO:-HALO], wet_frac)
-    flows = inner(flows, 1)
-    return (elevation_next, flows[:12], flows[12:])
+
+    results = []
+    for index, stream in enumerate(STREAMS):
+        gathered = gathers[index]
+        if results:
+            gathered = lax.optimization_barrier((gathered, results[-1]))[0]
+        freqs = tuple(FREQS[c] for c in stream)
+        channels = 2 * len(stream)
+        lanes = gathered.reshape(channels, blocks, block, columns)
+        lanes = lanes[:, :, rows_here : rows_here + 2 * HALO, :rows_here]
+        edge_sal = jnp.einsum("rbj,kbej->kre", green_blocks, lanes, precision=lax.Precision.HIGHEST)
+        before = lax.ppermute(edge_sal[:, :, HALO:], "lon", up)
+        after = lax.ppermute(edge_sal[:, :, :HALO], "lon", down)
+        sal = jnp.einsum("rs,ksc->krc", green_pad, gathered, precision=lax.Precision.HIGHEST)
+        sal = jnp.concatenate([before, sal, after], axis=2)
+        potential = pick(stack, 0, stream) - sal
+        flows = jnp.concatenate([pick(stack, 12, stream), pick(stack, 24, stream)], axis=0)
+
+        east_slope, north_slope = slopes(potential, stretch[1:-1])
+        flows = relax(
+            flows,
+            east_slope,
+            north_slope,
+            inner(depth_ext, 1),
+            inner(drag_ext, 1),
+            inner(wet_ext, 1),
+            coriolis[1:-1],
+            freqs,
+        )
+        flows = relax(
+            flows,
+            inner(east_slope, 1),
+            inner(north_slope, 1),
+            inner(depth_ext, 2),
+            inner(drag_ext, 2),
+            inner(wet_ext, 2),
+            coriolis[2:-2],
+            freqs,
+        )
+        east_ext = flows[:channels, 1:-1, :]
+        north_ext = flows[channels:, :, 1:-1]
+        elevation_next = surface(east_ext, north_ext, stretch[HALO:-HALO], wet_frac, freqs)
+        flows = inner(flows, 1)
+        results.append((elevation_next, flows[:channels], flows[channels:]))
+
+    def merge(outputs):
+        n = [len(stream) for stream in STREAMS]
+        real = [out[:k] for out, k in zip(outputs, n)]
+        imag = [out[k:] for out, k in zip(outputs, n)]
+        return jnp.concatenate(real + imag, axis=0)
+
+    return tuple(merge([result[i] for result in results]) for i in range(3))
 
 
 def solution(mesh):

time: 140 us -> 167 us (1.19)
  starting transfers between devices: 39.6 us -> 48.1 us
  matrix products: 11 us -> 18.2 us
  other arithmetic: 24.3 us -> 31.4 us
  local copies, waits for them, and re-layouts: 26.6 us -> 28.8 us
    ppermute x0 -> x4, starting transfers between devices: none -> 20 us  [the longest x2 12.2 us: per_device(): after = lax.ppermute(edge_sal[:, :, :HALO], 'lon', down)]
    ppermute x0 -> x4, waiting for transfers between devices: none -> 12.7 us  [the longest x2 7.62 us: per_device(): before = lax.ppermute(edge_sal[:, :, HALO:], 'lon', up)]
    dot_general x2 -> x8, matrix products: 11 us -> 18.2 us  [the longest x2 9.53 us: per_device(): jnp.einsum('rs,ksc->krc', green_pad, gathered, precision=lax.Precision.HI...]
    ppermute x2 -> x1, starting transfers between devices: 17.9 us -> 10.9 us  [widen_lon(): after = lax.ppermute(initial, 'lon', down)]
    ppermute x2 -> x1, waiting for transfers between devices: 7.03 us -> 0.01 us  [widen_lon(): before = lax.ppermute(last, 'lon', up)]
    slice x0 -> x11, local copies, waits for them, and re-layouts: none -> 5.47 us  [the longest x2 3.25 us: pick(): array[start + low:start + high]]
    concatenate x0 -> x7, other arithmetic: none -> 4.31 us  [the longest x3 2.57 us: merge(): return jnp.concatenate(real + imag, axis=0)]
    ppermute x2, starting transfers between devices: 8.11 us -> 3.84 us  [widen_lat(): after = lax.ppermute(initial, LAT, down)]
  transfers between devices with their start and end apart: 9 -> 12, of which waited for: 5 -> 5; matrix products, arithmetic and copies ran while one was open for 22% -> 30% of each run, Pallas kernels for 0% -> 0%
where the time goes in v9:
time: 167 us; the launch traced here: 166 us
  starting transfers between devices  48.1 us (29%)
  other arithmetic  31.4 us (19%)
  local copies, waits for them, and re-layouts  28.8 us (17%)
  waiting for transfers between devices  24.1 us (14%)
  matrix products  18.2 us (11%)
  between operations  14.9 us (9%)
    ppermute x2, starting transfers between devices, per_device(): after = lax.ppermute(edge_sal[:, :, :HALO], 'lon', down)  12.2 us
    ppermute x1, starting transfers between devices, widen_lon(): after = lax.ppermute(initial, 'lon', down)  10.9 us
    dot_general x2, matrix products, per_device(): jnp.einsum('rs,ksc->krc', green_pad, gathered, precision=lax.Precision.HI...  9.53 us
    ppermute x2, starting transfers between devices, per_device(): before = lax.ppermute(edge_sal[:, :, HALO:], 'lon', up)  7.77 us
    ppermute x2, starting transfers between devices, widen_lat(): before = lax.ppermute(last, LAT, up)  7.66 us
    ppermute x2, waiting for transfers between devices, per_device(): before = lax.ppermute(edge_sal[:, :, HALO:], 'lon', up)  7.62 us
    dot_general x2, matrix products, per_device(): jnp.einsum('rbj,kbej->kre', green_blocks, lanes, precision=lax.Precision....  6.59 us
    unnamed x106, local copies, waits for them, and re-layouts  6.45 us
  transfers between devices with their start and end apart: 12, of which 5 were waited for; matrix products, arithmetic and copies ran while one was open for 30% of the time, Pallas kernels for 0%

profile of v9, /device:TPU:1, one launch (start us, length us, event | category | flops | bytes accessed | tf_op | source)
XLA Modules:
  0.0 165.5 jit_solution(6539114359462233982)
XLA Ops:
  7.2 0.8 convert_element_type.11
  8.0 1.4 subtract_dynamic-update-slice_fusion
  9.9 0.6 convolution_bitcast_fusion.5
  10.5 0.8 select_maximum_fusion.1
  11.3 0.6 convolution_bitcast_fusion.3
  12.4 0.7 select_maximum_fusion
  13.3 0.6 copy-done.34
  14.0 2.6 %fusion.105 = (f32[39,96,3]{2,1,0:T(8,128)}, f32[39,96,3]{2,1,0:T(8,128)}) fusion(f32[39,96,128]{2,1,0:T(8,128)S(1)} %bitcast_dynamic-update-slice_fusion), kind=kLoop, calls=%fused_computation.247 | loop fusion | bytes 179712 | tf_op jit(solution)/shard_map/slice | solution.py:28
  16.6 2.1 %copy.28 = f32[39,96,3]{1,0,2:T(8,128)S(1)} copy(f32[39,96,3]{2,1,0:T(8,128)} %get-tuple-element.64) | data formatting | bytes 89856 | tf_op jit(solution)/shard_map/slice | solution.py:28
  18.7 5.6 %collective-permute-start = (f32[39,96,3]{1,0,2:T(8,128)S(1)}, f32[39,96,3]{1,0,2:T(8,128)S(1)}, u32[]{:S(2)}, u32[]{:S(2)}) collective-permute-start(f32[39,96,3]{1,0,2:T(8,128)S(1)} %copy.28), channel_id=1, source_target_pairs={{0,16},{16,32},{32,48},{48,64},{64,80},{80,96},{96,112},{112,128},... | collective-permute-start | bytes 134792 | tf_op jit(solution)/shard_map/ppermute | solution.py:30
  24.3 2.1 %copy.29 = f32[39,96,3]{1,0,2:T(8,128)S(1)} copy(f32[39,96,3]{2,1,0:T(8,128)} %get-tuple-element.65) | data formatting | bytes 89856 | tf_op jit(solution)/shard_map/slice | solution.py:29
  26.5 10.9 %collective-permute-start.1 = (f32[39,96,3]{1,0,2:T(8,128)S(1)}, f32[39,96,3]{1,0,2:T(8,128)S(1)}, u32[]{:S(2)}, u32[]{:S(2)}) collective-permute-start(f32[39,96,3]{1,0,2:T(8,128)S(1)} %copy.29), channel_id=1, source_target_pairs={{16,0},{32,16},{48,32},{64,48},{80,64},{96,80},{112,96},{128,112},... | collective-permute-start | bytes 134792 | tf_op jit(solution)/shard_map/ppermute | solution.py:31
  37.4 4.0 %collective-permute-start.4 = (f32[3,1536]{1,0:T(4,128)S(1)}, f32[3,1536]{1,0:T(4,128)S(1)}, u32[]{:S(2)}, u32[]{:S(2)}) collective-permute-start(f32[3,1536]{1,0:T(4,128)S(1)} %get-tuple-element.94), channel_id=1, source_target_pairs={{0,1},{1,2},{2,3},{3,4},{4,5},{5,6},{6,7},{7,8},{8,9},{9,10},{10,1... | collective-permute-start | bytes 55304 | tf_op jit(solution)/shard_map/ppermute | solution.py:41
  41.4 1.9 %collective-permute-start.5 = (f32[3,1536]{1,0:T(4,128)S(1)}, f32[3,1536]{1,0:T(4,128)}, u32[]{:S(2)}, u32[]{:S(2)}) collective-permute-start(f32[3,1536]{1,0:T(4,128)S(1)} %get-tuple-element.95), channel_id=1, source_target_pairs={{1,0},{2,1},{3,2},{4,3},{5,4},{6,5},{7,6},{8,7},{9,8},{10,9},{11,1... | collective-permute-start | bytes 55304 | tf_op jit(solution)/shard_map/ppermute | solution.py:42
  43.5 0.6 slice_multiply_fusion.15
  44.1 0.7 broadcast_multiply_fusion.5
  44.7 0.6 fusion.117
  45.4 0.6 slice_multiply_fusion.14
  46.0 1.9 %copy.30 = f32[39,96,3]{2,1,0:T(8,128)} copy(f32[39,96,3]{1,0,2:T(8,128)S(1)} %collective-permute-done) | data formatting | bytes 89856 | tf_op jit(solution)/shard_map/ppermute | solution.py:30
  47.9 2.0 %copy.31 = f32[39,96,3]{2,1,0:T(8,128)} copy(f32[39,96,3]{1,0,2:T(8,128)S(1)} %collective-permute-done.1) | data formatting | bytes 89856 | tf_op jit(solution)/shard_map/ppermute | solution.py:31
  49.9 1.6 pad_maximum_fusion.17
  51.6 3.6 %collective-permute-start.2 = (f32[39,3,134]{2,1,0:T(4,128)S(1)}, f32[39,3,134]{2,1,0:T(4,128)S(1)}, u32[]{:S(2)}, u32[]{:S(2)}) collective-permute-start(f32[39,3,134]{2,1,0:T(4,128)S(1)} %get-tuple-element.43), channel_id=1, source_target_pairs={{0,1},{1,2},{2,3},{3,4},{4,5},{5,6},{6,7},{7,8},{8,9},{9,10},{10,1... | collective-permute-start | bytes 188144 | tf_op jit(solution)/shard_map/ppermute | solution.py:41
  55.2 1.9 %collective-permute-start.3 = (f32[39,3,134]{2,1,0:T(4,128)S(1)}, f32[39,3,134]{2,1,0:T(4,128)S(1)}, u32[]{:S(2)}, u32[]{:S(2)}) collective-permute-start(f32[39,3,134]{2,1,0:T(4,128)S(1)} %get-tuple-element.44), channel_id=1, source_target_pairs={{1,0},{2,1},{3,2},{4,3},{5,4},{6,5},{7,6},{8,7},{9,8},{10,9},{11,1... | collective-permute-start | bytes 188144 | tf_op jit(solution)/shard_map/ppermute | solution.py:42
  57.1 0.8 pad_maximum_fusion.5
  57.9 2.3 %collective-permute-done.2 = f32[39,3,134]{2,1,0:T(4,128)S(1)} collective-permute-done((f32[39,3,134]{2,1,0:T(4,128)S(1)}, f32[39,3,134]{2,1,0:T(4,128)S(1)}, u32[]{:S(2)}, u32[]{:S(2)}) %collective-permute-start.2) | collective-permute-done | bytes 62744 | tf_op jit(solution)/shard_map/ppermute | solution.py:41
  60.3 2.6 %collective-permute-done.3 = f32[39,3,134]{2,1,0:T(4,128)S(1)} collective-permute-done((f32[39,3,134]{2,1,0:T(4,128)S(1)}, f32[39,3,134]{2,1,0:T(4,128)S(1)}, u32[]{:S(2)}, u32[]{:S(2)}) %collective-permute-start.3) | collective-permute-done | bytes 62744 | tf_op jit(solution)/shard_map/ppermute | solution.py:42
  62.9 3.7 %pad_maximum_fusion = f32[39,102,134]{2,1,0:T(8,128)} fusion(f32[39,3,134]{2,1,0:T(4,128)S(1)} %collective-permute-done.3, f32[39,96,3]{2,1,0:T(8,128)S(1)} %copy-done.1, f32[39,96,128]{2,1,0:T(8,128)S(1)} %bitcast_dynamic-update-slice_fusion, f32[39,96,3]{2,1,0:T(8,128)S(1)} %copy-done, f32[39,3,134]{2,1,0:T(4,128)S(1)} %collective-permute-done.2), kind=kLoop, calls=%fused_computation | loop fusion | flops 2132208 | bytes 4264416 | tf_op jit(solution)/shard_map/concatenate | solution.py:43
  67.2 2.4 %convolution_bitcast_fusion.4 = f32[6,102,6]{1,2,0:T(8,128)S(1)} fusion(f32[102,16,96]{0,2,1:T(8,128)S(1)} %copy.32, f32[6,16,104,128]{3,2,1,0:T(8,128)} %bitcast.50), kind=kOutput, calls=%fused_computation.39 | convolution fusion | flops 67682304 | bytes 1034592 | tf_op jit(solution)/shard_map/rbj,kbej->kre/dot_general | solution.py:161
  69.6 3.4 %collective-permute-start.6 = (f32[6,102,3]{1,2,0:T(4,128)S(1)}, f32[6,102,3]{1,2,0:T(4,128)}, u32[]{:S(2)}, u32[]{:S(2)}) collective-permute-start(f32[6,102,3]{1,2,0:T(4,128)S(1)} %get-tuple-element.134), channel_id=1, source_target_pairs={{0,16},{16,32},{32,48},{48,64},{64,80},{80,96},{96,112},{112,128},... | collective-permute-start | bytes 22040 | tf_op jit(solution)/shard_map/ppermute | solution.py:162
  73.0 6.5 %collective-permute-start.7 = (f32[6,102,3]{1,2,0:T(4,128)S(1)}, f32[6,102,3]{1,2,0:T(4,128)S(1)}, u32[]{:S(2)}, u32[]{:S(2)}) collective-permute-start(f32[6,102,3]{1,2,0:T(4,128)S(1)} %get-tuple-element.135), channel_id=1, source_target_pairs={{16,0},{32,16},{48,32},{64,48},{80,64},{96,80},{112,96},{128,112},... | collective-permute-start | bytes 22040 | tf_op jit(solution)/shard_map/ppermute | solution.py:163
  80.0 3.2 %fusion.104 = (f32[3,102,134]{2,1,0:T(8,128)}, f32[3,102,134]{2,1,0:T(8,128)S(1)}, f32[3,102,134]{2,1,0:T(8,128)S(1)}, f32[3,102,134]{2,1,0:T(8,128)S(1)}, f32[3...) fusion(f32[39,102,134]{2,1,0:T(8,128)} %pad_maximum_fusion), kind=kLoop, calls=%fused_computation.246 | loop fusion | bytes 3936384 | tf_op jit(solution)/shard_map/slice | solution.py:104
  83.4 1.0 slice_bitcast_fusion.2
  84.5 0.9 slice_add_fusion.6
  85.3 0.8 slice_add_fusion.7
  86.1 1.1 slice_add_fusion.3
  87.2 1.1 slice_add_fusion
  88.3 3.8 %convolution_bitcast_fusion.2 = f32[6,102,128]{2,1,0:T(8,128)} fusion(f32[6,1664,128]{2,1,0:T(8,128)S(1)} %bitcast.52, f32[102,1664,1]{1,0,2:T(8,128)S(1)} %reshape.75), kind=kOutput, calls=%fused_computation.37 | convolution fusion | flops 1564213248 | bytes 6104064 | tf_op jit(solution)/shard_map/rs,ksc->krc/dot_general | solution.py:164
  92.1 0.8 slice_negate_fusion.2
  92.9 0.7 slice.571
  93.7 0.7 slice.562
  94.4 1.6 copy.33
  96.0 0.9 copy.34
  96.9 1.8 %maximum_subtract_fusion = f32[6,102,134]{2,1,0:T(8,128)S(1)} fusion(f32[3,102,134]{2,1,0:T(8,128)} %get-tuple-element.59, f32[3,102,134]{2,1,0:T(8,128)} %get-tuple-element.48, f32[6,102,3]{2,1,0:T(8,128)} %copy.34, f32[6,102,128]{2,1,0:T(8,128)} %convolution_bitcast_fusion.2, f32[6,102,3]{2,1,0:T(8,128)} %copy.33), kind=kLoop, calls=%fused_computation.92 | loop fusion | flops 328032 | bytes 984096 | tf_op jit(solution)/shard_map/sub | solution.py:166
  100.6 0.6 copy-done.19
  101.4 1.1 fusion.8
  104.2 0.6 copy-done.17
  105.9 0.7 maximum_multiply_fusion.8
  106.7 0.9 fusion.106
  107.5 0.9 fusion.108
  108.4 6.4 %all-gather.5.cloned.1.call-done = f32[6,1664,128]{2,1,0:T(8,128)} async-done(((f32[6,104,128]{2,1,0:T(8,128)}), f32[6,1664,128]{2,1,0:T(8,128)}) %all-gather.5.cloned.1.call-update) | async-done | bytes 5111824 | tf_op jit(solution)/shard_map/all_gather | solution.py:133
  114.8 5.7 %convolution_bitcast_fusion.1 = f32[6,102,128]{2,1,0:T(8,128)S(1)} fusion(f32[6,1664,128]{2,1,0:T(8,128)} %all-gather.5.cloned.1.call-done, f32[102,1664,1]{1,0,2:T(8,128)S(1)} %reshape.75), kind=kOutput, calls=%fused_computation.36 | convolution fusion | flops 1564213248 | bytes 6104064 | tf_op jit(solution)/shard_map/rs,ksc->krc/dot_general | solution.py:164
  120.5 4.2 %convolution_bitcast_fusion = f32[6,102,6]{2,1,0:T(8,128)S(1)} fusion(f32[102,16,96]{0,2,1:T(8,128)S(1)} %copy-done.3, f32[6,16,104,128]{3,2,1,0:T(8,128)} %bitcast.53), kind=kOutput, calls=%fused_computation.35 | convolution fusion | flops 67682304 | bytes 1034592 | tf_op jit(solution)/shard_map/rbj,kbej->kre/dot_general | solution.py:161
  124.9 4.4 %collective-permute-start.8 = (f32[6,102,3]{2,1,0:T(8,128)S(1)}, f32[6,102,3]{2,1,0:T(8,128)S(1)}, u32[]{:S(2)}, u32[]{:S(2)}) collective-permute-start(f32[6,102,3]{2,1,0:T(8,128)S(1)} %get-tuple-element.98), channel_id=1, source_target_pairs={{0,16},{16,32},{32,48},{48,64},{64,80},{80,96},{96,112},{112,128},... | collective-permute-start | bytes 22040 | tf_op jit(solution)/shard_map/ppermute | solution.py:162
  129.4 5.8 %collective-permute-start.9 = (f32[6,102,3]{2,1,0:T(8,128)S(1)}, f32[6,102,3]{2,1,0:T(8,128)S(1)}, u32[]{:S(2)}, u32[]{:S(2)}) collective-permute-start(f32[6,102,3]{2,1,0:T(8,128)S(1)} %get-tuple-element.99), channel_id=1, source_target_pairs={{16,0},{32,16},{48,32},{64,48},{80,64},{96,80},{112,96},{128,112},... | collective-permute-start | bytes 22040 | tf_op jit(solution)/shard_map/ppermute | solution.py:163
  135.2 7.6 %collective-permute-done.8 = f32[6,102,3]{2,1,0:T(8,128)S(1)} collective-permute-done((f32[6,102,3]{2,1,0:T(8,128)S(1)}, f32[6,102,3]{2,1,0:T(8,128)S(1)}, u32[]{:S(2)}, u32[]{:S(2)}) %collective-permute-start.8) | collective-permute-done | bytes 7376 | tf_op jit(solution)/shard_map/ppermute | solution.py:162
  142.8 5.1 %collective-permute-done.9 = f32[6,102,3]{2,1,0:T(8,128)S(1)} collective-permute-done((f32[6,102,3]{2,1,0:T(8,128)S(1)}, f32[6,102,3]{2,1,0:T(8,128)S(1)}, u32[]{:S(2)}, u32[]{:S(2)}) %collective-permute-start.9) | collective-permute-done | bytes 7376 | tf_op jit(solution)/shard_map/ppermute | solution.py:163
  148.3 0.6 fusion.18
  150.1 0.6 copy-done.20
  150.9 1.1 fusion.2
  153.7 0.6 copy-done.18
  155.3 0.7 copy-done.28
  156.1 0.9 pad_maximum_fusion.8
  157.0 0.9 pad_maximum_fusion.7
  157.8 0.9 pad_maximum_fusion.6
  (153 shorter events, 11.9 us)
Async XLA Ops:
  7.2 59.4 %all-gather.3.cloned.1.call-start = ((), (), s32[]{:S(2)}) async-start(), calls=%async_computation | async-start | bytes 5431296 | tf_op jit(solution)/shard_map/all_gather | solution.py:133
  8.0 1.4 copy-start.32
  11.3 1.9 %copy-start.30 = (f32[12,96,128]{2,1,0:T(8,128)S(1)}, f32[12,96,128]{2,1,0:T(8,128)}, u32[]{:S(2)}) copy-start(f32[12,96,128]{2,1,0:T(8,128)} %param.17) | copy-start | bytes 1769476
  11.3 103.5 %all-gather.5.cloned.1.call-start = ((), (), s32[]{:S(2)}) async-start(), calls=%async_computation.1 | async-start | bytes 5431296 | tf_op jit(solution)/shard_map/all_gather | solution.py:133
  12.0 1.3 copy-start.31
  13.2 0.8 copy-start.34
  13.2 0.8 copy-start.35
  13.2 0.8 copy-start.33
  18.7 18.6 %copy-start.25 = (f32[96,1536]{1,0:T(8,128)S(1)}, f32[96,1536]{1,0:T(8,128)}, u32[]{:S(2)}) copy-start(f32[96,1536]{1,0:T(8,128)} %param.23) | copy-start | bytes 1769476
  18.7 27.3 %collective-permute-start = (f32[39,96,3]{1,0,2:T(8,128)S(1)}, f32[39,96,3]{1,0,2:T(8,128)S(1)}, u32[]{:S(2)}, u32[]{:S(2)}) collective-permute-start(f32[39,96,3]{1,0,2:T(8,128)S(1)} %copy.28), channel_id=1, source_target_pairs={{0,16},{16,32},{32,48},{48,64},{64,80},{80,96},{96,112},{112,128},... | collective-permute-start | bytes 134792 | tf_op jit(solution)/shard_map/ppermute | solution.py:30
  26.5 21.4 %collective-permute-start.1 = (f32[39,96,3]{1,0,2:T(8,128)S(1)}, f32[39,96,3]{1,0,2:T(8,128)S(1)}, u32[]{:S(2)}, u32[]{:S(2)}) collective-permute-start(f32[39,96,3]{1,0,2:T(8,128)S(1)} %copy.29), channel_id=1, source_target_pairs={{16,0},{32,16},{48,32},{64,48},{80,64},{96,80},{112,96},{128,112},... | collective-permute-start | bytes 134792 | tf_op jit(solution)/shard_map/ppermute | solution.py:31
  37.4 19.7 %collective-permute-start.4 = (f32[3,1536]{1,0:T(4,128)S(1)}, f32[3,1536]{1,0:T(4,128)S(1)}, u32[]{:S(2)}, u32[]{:S(2)}) collective-permute-start(f32[3,1536]{1,0:T(4,128)S(1)} %get-tuple-element.94), channel_id=1, source_target_pairs={{0,1},{1,2},{2,3},{3,4},{4,5},{5,6},{6,7},{7,8},{8,9},{9,10},{10,1... | collective-permute-start | bytes 55304 | tf_op jit(solution)/shard_map/ppermute | solution.py:41
  41.4 15.7 %collective-permute-start.5 = (f32[3,1536]{1,0:T(4,128)S(1)}, f32[3,1536]{1,0:T(4,128)}, u32[]{:S(2)}, u32[]{:S(2)}) collective-permute-start(f32[3,1536]{1,0:T(4,128)S(1)} %get-tuple-element.95), channel_id=1, source_target_pairs={{1,0},{2,1},{3,2},{4,3},{5,4},{6,5},{7,6},{8,7},{9,8},{10,9},{11,1... | collective-permute-start | bytes 55304 | tf_op jit(solution)/shard_map/ppermute | solution.py:42
  49.9 13.0 %copy-start = (f32[39,96,3]{2,1,0:T(8,128)S(1)}, f32[39,96,3]{2,1,0:T(8,128)}, u32[]{:S(2)}) copy-start(f32[39,96,3]{2,1,0:T(8,128)} %copy.30) | copy-start | bytes 134788
  49.9 13.0 %copy-start.1 = (f32[39,96,3]{2,1,0:T(8,128)S(1)}, f32[39,96,3]{2,1,0:T(8,128)}, u32[]{:S(2)}) copy-start(f32[39,96,3]{2,1,0:T(8,128)} %copy.31) | copy-start | bytes 134788
  51.6 8.7 %collective-permute-start.2 = (f32[39,3,134]{2,1,0:T(4,128)S(1)}, f32[39,3,134]{2,1,0:T(4,128)S(1)}, u32[]{:S(2)}, u32[]{:S(2)}) collective-permute-start(f32[39,3,134]{2,1,0:T(4,128)S(1)} %get-tuple-element.43), channel_id=1, source_target_pairs={{0,1},{1,2},{2,3},{3,4},{4,5},{5,6},{6,7},{7,8},{8,9},{9,10},{10,1... | collective-permute-start | bytes 188144 | tf_op jit(solution)/shard_map/ppermute | solution.py:41
  55.2 7.7 %collective-permute-start.3 = (f32[39,3,134]{2,1,0:T(4,128)S(1)}, f32[39,3,134]{2,1,0:T(4,128)S(1)}, u32[]{:S(2)}, u32[]{:S(2)}) collective-permute-start(f32[39,3,134]{2,1,0:T(4,128)S(1)} %get-tuple-element.44), channel_id=1, source_target_pairs={{1,0},{2,1},{3,2},{4,3},{5,4},{6,5},{7,6},{8,7},{9,8},{10,9},{11,1... | collective-permute-start | bytes 188144 | tf_op jit(solution)/shard_map/ppermute | solution.py:42
  67.2 5.8 %copy-start.2 = (f32[102,16,96]{0,2,1:T(8,128)}, f32[102,16,96]{0,2,1:T(8,128)S(1)}, u32[]{:S(2)}) copy-start(f32[102,16,96]{0,2,1:T(8,128)S(1)} %copy.32) | copy-start | bytes 1880068
  69.6 24.8 %collective-permute-start.6 = (f32[6,102,3]{1,2,0:T(4,128)S(1)}, f32[6,102,3]{1,2,0:T(4,128)}, u32[]{:S(2)}, u32[]{:S(2)}) collective-permute-start(f32[6,102,3]{1,2,0:T(4,128)S(1)} %get-tuple-element.134), channel_id=1, source_target_pairs={{0,16},{16,32},{32,48},{48,64},{64,80},{80,96},{96,112},{112,128},... | collective-permute-start | bytes 22040 | tf_op jit(solution)/shard_map/ppermute | solution.py:162
  73.0 23.0 %collective-permute-start.7 = (f32[6,102,3]{1,2,0:T(4,128)S(1)}, f32[6,102,3]{1,2,0:T(4,128)S(1)}, u32[]{:S(2)}, u32[]{:S(2)}) collective-permute-start(f32[6,102,3]{1,2,0:T(4,128)S(1)} %get-tuple-element.135), channel_id=1, source_target_pairs={{16,0},{32,16},{48,32},{64,48},{80,64},{96,80},{112,96},{128,112},... | collective-permute-start | bytes 22040 | tf_op jit(solution)/shard_map/ppermute | solution.py:163
  85.3 3.0 %slice-start = ((s8[5111808]{0:T(1024)(128)(4,1)}), s8[4194304]{0:T(1024)(128)(4,1)S(1)}, s32[]{:S(2)}) async-start(s8[5111808]{0:T(1024)(128)(4,1)} %bitcast.51), calls=%async_computation.2 | async-start | bytes 8388608
  86.1 2.2 %slice-start.1 = ((s8[5111808]{0:T(1024)(128)(4,1)}), s8[917504]{0:T(1024)(128)(4,1)S(1)}, s32[]{:S(2)}) async-start(s8[5111808]{0:T(1024)(128)(4,1)} %bitcast.51), calls=%async_computation.3 | async-start | bytes 1835008
  96.0 2.7 %copy-start.45 = (f32[100]{0:T(128)S(1)}, f32[100]{0:T(128)}, u32[]{:S(2)}) copy-start(f32[100]{0:T(128)} %slice_multiply_fusion.15) | copy-start | bytes 1204
  96.9 1.8 %copy-start.21 = (f32[100,132]{1,0:T(8,128)S(1)}, f32[100,132]{1,0:T(8,128)}, u32[]{:S(2)}) copy-start(f32[100,132]{1,0:T(8,128)} %get-tuple-element.130) | copy-start | bytes 158404
  96.9 1.8 %copy-start.23 = (f32[100,132]{1,0:T(8,128)S(1)}, f32[100,132]{1,0:T(8,128)}, u32[]{:S(2)}) copy-start(f32[100,132]{1,0:T(8,128)} %get-tuple-element.131) | copy-start | bytes 158404
  98.7 0.9 copy-start.4
  98.7 0.9 copy-start.6
  98.7 1.0 copy-start.15
  98.8 1.0 copy-start.38
  98.8 1.0 copy-start.39
  98.8 1.0 copy-start.42
  98.8 1.0 copy-start.43
  100.3 0.9 copy-start.19
  101.4 1.1 copy-start.13
  102.5 0.9 copy-start.11
  102.5 0.9 copy-start.40
  102.5 0.9 copy-start.41
  103.9 0.9 copy-start.17
  104.8 0.7 copy-start.44
  105.0 0.8 copy-start.48
  108.4 12.1 %copy-start.3 = (f32[102,16,96]{0,2,1:T(8,128)S(1)}, f32[102,16,96]{0,2,1:T(8,128)}, u32[]{:S(2)}) copy-start(f32[102,16,96]{0,2,1:T(8,128)} %copy-done.2) | copy-start | bytes 1880068
  120.5 14.7 %copy-start.10 = (f32[6,96,128]{2,1,0:T(8,128)S(1)}, f32[6,96,128]{2,1,0:T(8,128)}, u32[]{:S(2)}) copy-start(f32[6,96,128]{2,1,0:T(8,128)} %maximum_multiply_fusion.8) | copy-start | bytes 884740
  124.8 23.2 %copy-start.8 = (f32[3,102,134]{2,1,0:T(8,128)S(1)}, f32[3,102,134]{2,1,0:T(8,128)}, u32[]{:S(2)}) copy-start(f32[3,102,134]{2,1,0:T(8,128)} %get-tuple-element.53) | copy-start | bytes 492052
  124.8 23.2 %copy-start.9 = (f32[3,102,134]{2,1,0:T(8,128)S(1)}, f32[3,102,134]{2,1,0:T(8,128)}, u32[]{:S(2)}) copy-start(f32[3,102,134]{2,1,0:T(8,128)} %get-tuple-element.54) | copy-start | bytes 492052
  124.9 17.9 %collective-permute-start.8 = (f32[6,102,3]{2,1,0:T(8,128)S(1)}, f32[6,102,3]{2,1,0:T(8,128)S(1)}, u32[]{:S(2)}, u32[]{:S(2)}) collective-permute-start(f32[6,102,3]{2,1,0:T(8,128)S(1)} %get-tuple-element.98), channel_id=1, source_target_pairs={{0,16},{16,32},{32,48},{48,64},{64,80},{80,96},{96,112},{112,128},... | collective-permute-start | bytes 22040 | tf_op jit(solution)/shard_map/ppermute | solution.py:162
  129.4 18.9 %copy-start.22 = (f32[100,132]{1,0:T(8,128)S(1)}, f32[100,132]{1,0:T(8,128)}, u32[]{:S(2)}) copy-start(f32[100,132]{1,0:T(8,128)} %get-tuple-element.130) | copy-start | bytes 158404
  129.4 18.9 %copy-start.24 = (f32[100,132]{1,0:T(8,128)S(1)}, f32[100,132]{1,0:T(8,128)}, u32[]{:S(2)}) copy-start(f32[100,132]{1,0:T(8,128)} %get-tuple-element.131) | copy-start | bytes 158404
  129.4 18.9 %copy-start.46 = (f32[100]{0:T(128)S(1)}, f32[100]{0:T(128)}, u32[]{:S(2)}) copy-start(f32[100]{0:T(128)} %slice_multiply_fusion.15) | copy-start | bytes 1204
  129.4 18.5 %collective-permute-start.9 = (f32[6,102,3]{2,1,0:T(8,128)S(1)}, f32[6,102,3]{2,1,0:T(8,128)S(1)}, u32[]{:S(2)}, u32[]{:S(2)}) collective-permute-start(f32[6,102,3]{2,1,0:T(8,128)S(1)} %get-tuple-element.99), channel_id=1, source_target_pairs={{16,0},{32,16},{48,32},{64,48},{80,64},{96,80},{112,96},{128,112},... | collective-permute-start | bytes 22040 | tf_op jit(solution)/shard_map/ppermute | solution.py:163
  148.3 0.9 copy-start.5
  148.3 0.9 copy-start.7
  148.3 1.0 copy-start.16
  148.3 1.0 copy-start.36
  148.3 1.0 copy-start.37
  149.9 0.9 copy-start.20
  150.9 1.1 copy-start.14
  152.0 0.9 copy-start.12
  153.4 0.9 copy-start.18
  154.5 0.7 copy-start.47
  155.1 0.9 copy-start.28
  155.1 1.0 copy-start.29
  155.2 1.7 %copy-start.26 = (f32[3,96,128]{2,1,0:T(8,128)S(1)}, f32[3,96,128]{2,1,0:T(8,128)}, u32[]{:S(2)}) copy-start(f32[3,96,128]{2,1,0:T(8,128)} %get-tuple-element.86) | copy-start | bytes 442372
  155.2 1.7 %copy-start.27 = (f32[3,96,128]{2,1,0:T(8,128)S(1)}, f32[3,96,128]{2,1,0:T(8,128)}, u32[]{:S(2)}) copy-start(f32[3,96,128]{2,1,0:T(8,128)} %get-tuple-element.87) | copy-start | bytes 442372
Sparse Core Ops, SparseCore 0:
  11.4 52.9 all-gather.2
  66.6 48.2 all-gather.4

commit v10 on v4

--- a/solution.py
+++ b/solution.py
@@ -53,12 +53,18 @@
     return (east_slope, north_slope)
 
 
-def solve_cells(push_u, push_v, drag_field, wet_frac, coriolis):
+def cell_terms(drag_field, coriolis):
     damping = drag_field + 4.0 * VISCOSITY
     frequency = jnp.array(FREQS, jnp.float32)[:, None, None]
     det_real = damping * damping - frequency * frequency + coriolis * coriolis
     det_imag = 2.0 * damping * frequency
     magnitude = det_real * det_real + det_imag * det_imag
+    return (damping, det_real, det_imag, magnitude)
+
+
+def solve_cells(push_u, push_v, terms, wet_frac, coriolis):
+    damping, det_real, det_imag, magnitude = terms
+    frequency = jnp.array(FREQS, jnp.float32)[:, None, None]
 
     def combine(first, second, factor):
         top_real = damping * first[:6] - frequency * first[6:] + factor * coriolis * second[:6]
@@ -74,16 +80,19 @@
     return field[..., trim : field.shape[-2] - trim, trim : field.shape[-1] - trim]
 
 
-def relax(flow_ext, east_slope, north_slope, depth_field, drag_field, wet_frac, coriolis):
-    beside_all = (
+def beside(flow_ext):
+    return VISCOSITY * (
         flow_ext[:, :-2, 1:-1]
         + flow_ext[:, 2:, 1:-1]
         + flow_ext[:, 1:-1, :-2]
         + flow_ext[:, 1:-1, 2:]
     )
-    push_u = -depth_field * east_slope + VISCOSITY * beside_all[:12]
-    push_v = -depth_field * north_slope + VISCOSITY * beside_all[12:]
-    return solve_cells(push_u, push_v, drag_field, wet_frac, coriolis)
+
+
+def relax(around, east_slope, north_slope, depth_field, terms, wet_frac, coriolis):
+    push_u = -depth_field * east_slope + around[:12]
+    push_v = -depth_field * north_slope + around[12:]
+    return solve_cells(push_u, push_v, terms, wet_frac, coriolis)
 
 
 def surface(east_ext, north_ext, stretch, wet_frac):
@@ -122,42 +131,47 @@
     stack = jnp.concatenate([elevation - equilibrium, transport_u, transport_v, fields], axis=0)
     stack = widen_lat(widen_lon(stack, HALO, 2), HALO, 1)
     green_ext = widen_lat(lat_green, HALO, 0)
-
+    depth_ext, drag_ext, wet_ext = stack[36], stack[37], stack[38]
+    first_row = lat_index() * rows_here - HALO
+    stretch, coriolis = row_terms(first_row + jnp.arange(rows_here + 2 * HALO), total_rows)
+    around = beside(stack[12:36])
+    terms_first = cell_terms(inner(drag_ext, 1), coriolis[1:-1])
+    terms_second = cell_terms(inner(drag_ext, 2), coriolis[2:-2])
     blocks = lat_size()
     block = rows_here + spare
     green_blocks = green_ext.reshape(green_ext.shape[0], blocks, rows_here)
+    green_pad = jnp.pad(green_blocks, ((0, 0), (0, 0), (0, spare))).reshape(green_ext.shape[0], -1)
+    gathered, stack, green_pad, around, terms_first, terms_second = lax.optimization_barrier(
+        (gathered, stack, green_pad, around, terms_first, terms_second)
+    )
     lanes = gathered.reshape(12, blocks, block, columns)[:, :, rows_here : rows_here + 2 * HALO, :rows_here]
     edge_sal = jnp.einsum("rbj,kbej->kre", green_blocks, lanes, precision=lax.Precision.HIGHEST)
     size = lax.axis_size("lon")
     up = [(i, (i + 1) % size) for i in range(size)]
     down = [(j, i) for i, j in up]
+    edge_sal, gathered = lax.optimization_barrier((edge_sal, gathered))
     before = lax.ppermute(edge_sal[:, :, HALO:], "lon", up)
     after = lax.ppermute(edge_sal[:, :, :HALO], "lon", down)
-    green_pad = jnp.pad(green_blocks, ((0, 0), (0, 0), (0, spare))).reshape(green_ext.shape[0], -1)
     sal = jnp.einsum("rs,ksc->krc", green_pad, gathered, precision=lax.Precision.HIGHEST)
     sal = jnp.concatenate([before, sal, after], axis=2)
     potential = stack[:12] - sal
-    flows = stack[12:36]
-    depth_ext, drag_ext, wet_ext = stack[36], stack[37], stack[38]
-
-    first_row = lat_index() * rows_here - HALO
-    stretch, coriolis = row_terms(first_row + jnp.arange(rows_here + 2 * HALO), total_rows)
+    depth_ext, wet_ext = stack[36], stack[38]
     east_slope, north_slope = slopes(potential, stretch[1:-1])
     flows = relax(
-        flows,
+        around,
         east_slope,
         north_slope,
         inner(depth_ext, 1),
-        inner(drag_ext, 1),
+        terms_first,
         inner(wet_ext, 1),
         coriolis[1:-1],
     )
     flows = relax(
-        flows,
+        beside(flows),
         inner(east_slope, 1),
         inner(north_slope, 1),
         inner(depth_ext, 2),
-        inner(drag_ext, 2),
+        terms_second,
         inner(wet_ext, 2),
         coriolis[2:-2],
     )

time: 137 us -> 140 us (1.022)
  local copies, waits for them, and re-layouts: 20.5 us -> 24.2 us
  other arithmetic: 28.6 us -> 30.6 us
  waiting for transfers between devices: 18.5 us -> 16.5 us
    mul x0 -> x4, other arithmetic: none -> 6.13 us  [the longest x2 4.12 us: beside(): VISCOSITY * (flow_ext[:, :-2, 1:-1] + flow_ext[:, 2:, 1:-1] + flow_ext[:,...]
    ppermute x1, waiting for transfers between devices: 4 us -> 0.01 us  [widen_lon(): before = lax.ppermute(last, 'lon', up)]
    ppermute x2, starting transfers between devices: 7.52 us -> 3.84 us  [widen_lat(): after = lax.ppermute(initial, LAT, down)]
    ppermute x1, starting transfers between devices: 1.92 us -> 5.49 us  [widen_lon(): before = lax.ppermute(last, 'lon', up)]
    all_gather x1, waiting for transfers between devices: 7.14 us -> 10.6 us  [per_device(): gathered = lax.all_gather(packed, LAT, axis=1, tiled=True)]
    add x6 -> x4, other arithmetic: 8.1 us -> 4.81 us  [the longest x2 2.96 us: cell_terms(): magnitude = det_real * det_real + det_imag * det_imag]
    unnamed x68 -> x66, local copies, waits for them, and re-layouts: 2.8 us -> 5.51 us
    concatenate x2, other arithmetic: 2.69 us -> 4.77 us  [widen_lat(): return jnp.concatenate([before, array, after], axis=dim)]
  transfers between devices with their start and end apart: 9 -> 9, of which waited for: 4 -> 3; matrix products, arithmetic and copies ran while one was open for 30% -> 32% of each run, Pallas kernels for 0% -> 0%
where the time goes in v10:
time: 140 us
  starting transfers between devices  39 us (28%)
  other arithmetic  30.6 us (22%)
  local copies, waits for them, and re-layouts  24.2 us (17%)
  waiting for transfers between devices  16.5 us (12%)
  matrix products  14.6 us (10%)
  between operations  14.6 us (10%)
    ppermute x1, starting transfers between devices, widen_lon(): after = lax.ppermute(initial, 'lon', down)  10.9 us
    all_gather x1, waiting for transfers between devices, per_device(): gathered = lax.all_gather(packed, LAT, axis=1, tiled=True)  10.6 us
    dot_general x1, matrix products, per_device(): jnp.einsum('rs,ksc->krc', green_pad, gathered, precision=lax.Precision.HI...  9.34 us
    ppermute x2, starting transfers between devices, widen_lat(): before = lax.ppermute(last, LAT, up)  7.67 us
    ppermute x1, starting transfers between devices, per_device(): after = lax.ppermute(edge_sal[:, :, :HALO], 'lon', down)  6.48 us
    unnamed x66, local copies, waits for them, and re-layouts  5.51 us
    ppermute x1, starting transfers between devices, widen_lon(): before = lax.ppermute(last, 'lon', up)  5.49 us
    slice x2, local copies, waits for them, and re-layouts, widen_lon(): last = lax.slice_in_dim(array, length - width, length, axis=dim)  4.82 us
  transfers between devices with their start and end apart: 9, of which 3 were waited for; matrix products, arithmetic and copies ran while one was open for 32% of the time, Pallas kernels for 0%

profile of v10, /device:TPU:1, one launch (start us, length us, event | category | flops | bytes accessed | tf_op | source)
XLA Modules:
  0.0 139.6 jit_solution(9655201886937069207)
XLA Ops:
  7.2 0.8 convert_element_type.10
  8.0 0.7 fusion.31
  8.7 1.8 %fusion.16 = f32[12,96,128]{2,1,0:T(8,128)S(1)} fusion(f32[12,96,128]{2,1,0:T(8,128)} %param.14, f32[96,128]{1,0:T(8,128)S(1)} %convert_element_type.10, f32[128,128]{1,0:T(8,128)} %param.21), kind=kOutput, calls=%fused_computation.70 | convolution fusion | flops 226639872 | bytes 1294336 | tf_op jit(solution)/shard_map/krj,cj->krc/dot_general | solution.py:121
  10.5 2.2 %convolution_bitcast_fusion.2 = f32[12,6,96]{2,1,0:T(8,128)S(1)} fusion(f32[12,96,128]{2,1,0:T(8,128)} %param.14, f32[96,128]{1,0:T(8,128)S(1)} %convert_element_type.10, f32[3,128]{1,0:T(4,128)S(1)} %get-tuple-element.93, f32[3,128]{1,0:T(4,128)S(1)} %get-tuple-element.92), kind=kOutput, calls=%fused_computation.36 | convolution fusion | flops 10765056 | bytes 669696 | tf_op jit(solution)/shard_map/ej,krj->ker/dot_general | solution.py:124
  12.8 0.9 select_maximum_fusion
  13.8 1.1 constant_dynamic-update-slice_fusion.1
  14.9 1.1 constant_dynamic-update-slice_fusion
  16.1 2.6 %fusion.28 = (f32[39,96,3]{2,1,0:T(8,128)}, f32[39,96,3]{2,1,0:T(8,128)}) fusion(f32[39,96,128]{2,1,0:T(8,128)S(1)} %bitcast_dynamic-update-slice_fusion), kind=kLoop, calls=%fused_computation.113 | loop fusion | bytes 179712 | tf_op jit(solution)/shard_map/slice | solution.py:27
  18.8 2.2 %copy.22 = f32[39,96,3]{1,0,2:T(8,128)S(1)} copy(f32[39,96,3]{2,1,0:T(8,128)} %get-tuple-element.65) | data formatting | bytes 89856 | tf_op jit(solution)/shard_map/slice | solution.py:27
  20.9 5.5 %collective-permute-start = (f32[39,96,3]{1,0,2:T(8,128)S(1)}, f32[39,96,3]{1,0,2:T(8,128)S(1)}, u32[]{:S(2)}, u32[]{:S(2)}) collective-permute-start(f32[39,96,3]{1,0,2:T(8,128)S(1)} %copy.22), channel_id=1, source_target_pairs={{0,16},{16,32},{32,48},{48,64},{64,80},{80,96},{96,112},{112,128},... | collective-permute-start | bytes 134792 | tf_op jit(solution)/shard_map/ppermute | solution.py:29
  26.4 2.1 %copy.23 = f32[39,96,3]{1,0,2:T(8,128)S(1)} copy(f32[39,96,3]{2,1,0:T(8,128)} %get-tuple-element.66) | data formatting | bytes 89856 | tf_op jit(solution)/shard_map/slice | solution.py:28
  28.6 10.9 %collective-permute-start.1 = (f32[39,96,3]{1,0,2:T(8,128)S(1)}, f32[39,96,3]{1,0,2:T(8,128)S(1)}, u32[]{:S(2)}, u32[]{:S(2)}) collective-permute-start(f32[39,96,3]{1,0,2:T(8,128)S(1)} %copy.23), channel_id=1, source_target_pairs={{16,0},{32,16},{48,32},{64,48},{80,64},{96,80},{112,96},{128,112},... | collective-permute-start | bytes 134792 | tf_op jit(solution)/shard_map/ppermute | solution.py:30
  39.5 4.0 %collective-permute-start.4 = (f32[3,1536]{1,0:T(4,128)S(1)}, f32[3,1536]{1,0:T(4,128)S(1)}, u32[]{:S(2)}, u32[]{:S(2)}) collective-permute-start(f32[3,1536]{1,0:T(4,128)S(1)} %get-tuple-element.72), channel_id=1, source_target_pairs={{0,1},{1,2},{2,3},{3,4},{4,5},{5,6},{6,7},{7,8},{8,9},{9,10},{10,1... | collective-permute-start | bytes 55304 | tf_op jit(solution)/shard_map/ppermute | solution.py:40
  43.5 1.9 %collective-permute-start.5 = (f32[3,1536]{1,0:T(4,128)S(1)}, f32[3,1536]{1,0:T(4,128)}, u32[]{:S(2)}, u32[]{:S(2)}) collective-permute-start(f32[3,1536]{1,0:T(4,128)S(1)} %get-tuple-element.73), channel_id=1, source_target_pairs={{1,0},{2,1},{3,2},{4,3},{5,4},{6,5},{7,6},{8,7},{9,8},{10,9},{11,1... | collective-permute-start | bytes 55304 | tf_op jit(solution)/shard_map/ppermute | solution.py:41
  45.6 0.7 slice_multiply_fusion.4
  46.2 0.6 fusion.33
  46.8 0.7 broadcast_multiply_fusion.6
  47.5 0.6 slice_multiply_fusion.3
  48.1 1.9 %copy.24 = f32[39,96,3]{2,1,0:T(8,128)} copy(f32[39,96,3]{1,0,2:T(8,128)S(1)} %collective-permute-done) | data formatting | bytes 89856 | tf_op jit(solution)/shard_map/ppermute | solution.py:29
  50.0 1.9 %copy.25 = f32[39,96,3]{2,1,0:T(8,128)} copy(f32[39,96,3]{1,0,2:T(8,128)S(1)} %collective-permute-done.1) | data formatting | bytes 89856 | tf_op jit(solution)/shard_map/ppermute | solution.py:30
  51.9 2.2 %pad_maximum_fusion.5 = (f32[39,3,134]{2,1,0:T(4,128)}, f32[39,3,134]{2,1,0:T(4,128)}) fusion(f32[39,96,3]{2,1,0:T(8,128)} %copy.25, f32[39,96,128]{2,1,0:T(8,128)S(1)} %bitcast_dynamic-update-slice_fusion, f32[39,96,3]{2,1,0:T(8,128)} %copy.24), kind=kLoop, calls=%fused_computation.81 | loop fusion | flops 62712 | bytes 2132208 | tf_op jit(solution)/shard_map/slice | solution.py:38
  54.1 3.6 %collective-permute-start.2 = (f32[39,3,134]{2,1,0:T(4,128)}, f32[39,3,134]{2,1,0:T(4,128)S(1)}, u32[]{:S(2)}, u32[]{:S(2)}) collective-permute-start(f32[39,3,134]{2,1,0:T(4,128)} %get-tuple-element.47), channel_id=1, source_target_pairs={{0,1},{1,2},{2,3},{3,4},{4,5},{5,6},{6,7},{7,8},{8,9},{9,10},{10,1... | collective-permute-start | bytes 188144 | tf_op jit(solution)/shard_map/ppermute | solution.py:40
  57.8 1.9 %collective-permute-start.3 = (f32[39,3,134]{2,1,0:T(4,128)}, f32[39,3,134]{2,1,0:T(4,128)}, u32[]{:S(2)}, u32[]{:S(2)}) collective-permute-start(f32[39,3,134]{2,1,0:T(4,128)} %get-tuple-element.48), channel_id=1, source_target_pairs={{1,0},{2,1},{3,2},{4,3},{5,4},{6,5},{7,6},{8,7},{9,8},{10,9},{11,1... | collective-permute-start | bytes 188144 | tf_op jit(solution)/shard_map/ppermute | solution.py:41
  59.7 0.6 copy-done.19
  60.3 0.8 pad_maximum_fusion.2
  61.1 0.3 copy.26
  61.4 1.0 pad.9
  62.4 1.3 collective-permute-done.2
  63.7 4.7 %collective-permute-done.3 = f32[39,3,134]{2,1,0:T(4,128)} collective-permute-done((f32[39,3,134]{2,1,0:T(4,128)}, f32[39,3,134]{2,1,0:T(4,128)}, u32[]{:S(2)}, u32[]{:S(2)}) %collective-permute-start.3) | collective-permute-done | bytes 62744 | tf_op jit(solution)/shard_map/ppermute | solution.py:41
  68.4 4.0 %pad_maximum_fusion = f32[39,102,134]{2,1,0:T(8,128)S(1)} fusion(f32[39,3,134]{2,1,0:T(4,128)} %collective-permute-done.3, f32[39,96,3]{2,1,0:T(8,128)} %copy.25, f32[39,96,128]{2,1,0:T(8,128)S(1)} %bitcast_dynamic-update-slice_fusion, f32[39,96,3]{2,1,0:T(8,128)} %copy.24, f32[39,3,134]{2,1,0:T(4,128)S(1)} %collective-permute-done.2), kind=kLoop, calls=%fused_computation | loop fusion | flops 2132208 | bytes 4264416 | tf_op jit(solution)/shard_map/concatenate | solution.py:42
  72.4 0.9 broadcast_multiply_fusion.3
  73.2 1.1 broadcast_multiply_fusion.4
  74.4 1.5 %multiply_add_fusion.8 = (f32[6,98,130]{2,1,0:T(8,128)}, f32[6,98,130]{2,1,0:T(8,128)}, f32[6,98,130]{2,1,0:T(8,128)}) fusion(f32[6]{0:T(128)S(1)} %copy-done.20, f32[98,130]{1,0:T(8,128)S(1)} %get-tuple-element.86, f32[98]{0:T(128)S(1)} %copy-done.23, f32[6]{0:T(128)S(1)} %copy-done.21, f32[98,130]{1,0:T(8,128)S(1)} %get-tuple-element.87), kind=kLoop, calls=%fused_computation.60 | loop fusion | flops 458640 | bytes 1019640 | tf_op jit(solution)/shard_map/add | solution.py:61
  75.9 1.5 %multiply_add_fusion.9 = (f32[6,100,132]{2,1,0:T(8,128)}, f32[6,100,132]{2,1,0:T(8,128)}, f32[6,100,132]{2,1,0:T(8,128)}) fusion(f32[6]{0:T(128)S(1)} %copy-done.20, f32[100,132]{1,0:T(8,128)S(1)} %get-tuple-element.89, f32[100]{0:T(128)S(1)} %copy-done.22, f32[6]{0:T(128)S(1)} %copy-done.21, f32[100,132]{1,0:T(8,128)S(1)} %get-tuple-element.90), kind=kLoop, calls=%fused_computation.61 | loop fusion | flops 475200 | bytes 1056448 | tf_op jit(solution)/shard_map/add | solution.py:61
  77.3 2.1 %fusion.7 = f32[24,100,132]{2,1,0:T(8,128)S(1)} fusion(f32[39,102,134]{2,1,0:T(8,128)S(1)} %pad_maximum_fusion), kind=kLoop, calls=%fused_computation.16 | loop fusion | flops 1267200 | bytes 6336000 | tf_op jit(solution)/shard_map/mul | solution.py:84
  79.4 10.6 %all-gather.2.cloned.1.call-done = f32[12,1664,128]{2,1,0:T(8,128)} async-done(((f32[12,104,128]{2,1,0:T(8,128)}), f32[12,1664,128]{2,1,0:T(8,128)}) %all-gather.2.cloned.1.call-update) | async-done | bytes 10223632 | tf_op jit(solution)/shard_map/all_gather | solution.py:128
  90.0 1.3 slice.285
  91.2 1.3 convolution_bitcast_fusion.1
  92.5 4.6 %collective-permute-start.6 = (f32[12,102,3]{1,0,2:T(8,128)S(1)}, f32[12,102,3]{1,0,2:T(8,128)S(1)}, u32[]{:S(2)}, u32[]{:S(2)}) collective-permute-start(f32[12,102,3]{1,0,2:T(8,128)S(1)} %get-tuple-element.94), channel_id=1, source_target_pairs={{0,16},{16,32},{32,48},{48,64},{64,80},{80,96},{96,112},{112,128},... | collective-permute-start | bytes 44072 | tf_op jit(solution)/shard_map/ppermute | solution.py:153
  97.1 6.5 %collective-permute-start.7 = (f32[12,102,3]{1,0,2:T(8,128)S(1)}, f32[12,102,3]{1,0,2:T(8,128)S(1)}, u32[]{:S(2)}, u32[]{:S(2)}) collective-permute-start(f32[12,102,3]{1,0,2:T(8,128)S(1)} %get-tuple-element.95), channel_id=1, source_target_pairs={{16,0},{32,16},{48,32},{64,48},{80,64},{96,80},{112,96},{128,112},... | collective-permute-start | bytes 44072 | tf_op jit(solution)/shard_map/ppermute | solution.py:154
  103.6 1.0 slice_bitcast_fusion.2
  104.7 9.3 %convolution_bitcast_fusion = f32[12,102,128]{2,1,0:T(8,128)S(1)} fusion(f32[12,1664,128]{2,1,0:T(8,128)} %all-gather.2.cloned.1.call-done, f32[102,1664]{0,1:T(8,128)S(1)} %bitcast.40), kind=kOutput, calls=%fused_computation.34 | convolution fusion | flops 3128426496 | bytes 11529216 | tf_op jit(solution)/shard_map/rs,ksc->krc/dot_general | solution.py:155
  114.0 0.7 slice_negate_fusion.2
  114.8 0.7 slice.289
  115.5 0.7 slice.283
  116.3 1.2 copy.29
  117.4 1.1 copy.30
  118.6 2.3 %maximum_subtract_fusion = f32[12,102,134]{2,1,0:T(8,128)S(1)} fusion(f32[12,102,3]{2,1,0:T(8,128)} %copy.30, f32[12,102,128]{2,1,0:T(8,128)S(1)} %convolution_bitcast_fusion, f32[12,102,3]{2,1,0:T(8,128)} %copy.29, f32[39,102,134]{2,1,0:T(8,128)} %copy-done), kind=kLoop, calls=%fused_computation.27 | loop fusion | flops 492048 | bytes 1968192 | tf_op jit(solution)/shard_map/sub | solution.py:157
  120.9 1.1 slice_add_fusion.6
  122.1 0.2 copy-done.6
  122.3 0.7 add_divide_fusion.2
  123.0 0.3 subtract_divide_fusion.2
  123.3 0.6 copy-done.13
  124.1 2.0 %fusion.3 = f32[24,98,130]{2,1,0:T(8,128)S(1)} fusion(f32[12,100,132]{2,1,0:T(8,128)S(1)} %get-tuple-element.83, f32[12,100,132]{2,1,0:T(8,128)S(1)} %get-tuple-element.82), kind=kLoop, calls=%fused_computation.10 | loop fusion | flops 2446080 | bytes 2490240 | tf_op jit(solution)/shard_map/mul | solution.py:84
  126.2 0.8 slice_add_fusion.3
  127.0 0.3 copy-done.1
  127.2 0.2 copy-done.2
  127.4 0.2 copy-done.3
  127.6 0.7 add_divide_fusion.1
  128.4 0.3 subtract_divide_fusion.1
  128.7 0.6 copy-done.12
  129.5 0.5 copy-done.29
  129.9 1.8 %fusion.29 = (f32[12,96,128]{2,1,0:T(8,128)}, f32[12,96,128]{2,1,0:T(8,128)S(1)}, f32[12,96,128]{2,1,0:T(8,128)}) fusion(f32[12,98,130]{2,1,0:T(8,128)S(1)} %get-tuple-element.81, f32[96]{0:T(128)S(1)} %copy-done.29, f32[12,98,130]{2,1,0:T(8,128)S(1)} %get-tuple-element.80), kind=kLoop, calls=%fused_computation.114 | loop fusion | flops 737280 | bytes 5308800 | tf_op jit(solution)/shard_map/slice | solution.py:182
  131.9 0.9 maximum_multiply_fusion.4
  (75 shorter events, 1.1 us)
Async XLA Ops:
  7.2 82.8 %all-gather.2.cloned.1.call-start = ((), (), s32[]{:S(2)}) async-start(), calls=%async_computation | async-start | bytes 10862592 | tf_op jit(solution)/shard_map/all_gather | solution.py:128
  8.7 5.0 %copy-start.7 = (f32[12,96,128]{2,1,0:T(8,128)S(1)}, f32[12,96,128]{2,1,0:T(8,128)}, u32[]{:S(2)}) copy-start(f32[12,96,128]{2,1,0:T(8,128)} %param.14) | copy-start | bytes 1769476
  8.7 5.0 %copy-start.10 = (f32[12,96,128]{2,1,0:T(8,128)S(1)}, f32[12,96,128]{2,1,0:T(8,128)}, u32[]{:S(2)}) copy-start(f32[12,96,128]{2,1,0:T(8,128)} %param.15) | copy-start | bytes 1769476
  13.7 2.3 %copy-start.17 = (f32[96,128]{1,0:T(8,128)S(1)}, f32[96,128]{1,0:T(8,128)}, u32[]{:S(2)}) copy-start(f32[96,128]{1,0:T(8,128)} %param.18) | copy-start | bytes 147460
  13.7 2.4 %copy-start.18 = (f32[96,128]{1,0:T(8,128)S(1)}, f32[96,128]{1,0:T(8,128)}, u32[]{:S(2)}) copy-start(f32[96,128]{1,0:T(8,128)} %param.19) | copy-start | bytes 147460
  13.7 2.4 %copy-start.16 = (s32[96,128]{1,0:T(8,128)S(1)}, s32[96,128]{1,0:T(8,128)}, u32[]{:S(2)}) copy-start(s32[96,128]{1,0:T(8,128)} %param.20) | copy-start | bytes 147460
  18.8 20.7 %copy-start.9 = (f32[96,1536]{1,0:T(8,128)S(1)}, f32[96,1536]{1,0:T(8,128)}, u32[]{:S(2)}) copy-start(f32[96,1536]{1,0:T(8,128)} %param.22) | copy-start | bytes 1769476
  20.9 27.2 %collective-permute-start = (f32[39,96,3]{1,0,2:T(8,128)S(1)}, f32[39,96,3]{1,0,2:T(8,128)S(1)}, u32[]{:S(2)}, u32[]{:S(2)}) collective-permute-start(f32[39,96,3]{1,0,2:T(8,128)S(1)} %copy.22), channel_id=1, source_target_pairs={{0,16},{16,32},{32,48},{48,64},{64,80},{80,96},{96,112},{112,128},... | collective-permute-start | bytes 134792 | tf_op jit(solution)/shard_map/ppermute | solution.py:29
  28.6 21.4 %collective-permute-start.1 = (f32[39,96,3]{1,0,2:T(8,128)S(1)}, f32[39,96,3]{1,0,2:T(8,128)S(1)}, u32[]{:S(2)}, u32[]{:S(2)}) collective-permute-start(f32[39,96,3]{1,0,2:T(8,128)S(1)} %copy.23), channel_id=1, source_target_pairs={{16,0},{32,16},{48,32},{64,48},{80,64},{96,80},{112,96},{128,112},... | collective-permute-start | bytes 134792 | tf_op jit(solution)/shard_map/ppermute | solution.py:30
  39.5 20.2 %collective-permute-start.4 = (f32[3,1536]{1,0:T(4,128)S(1)}, f32[3,1536]{1,0:T(4,128)S(1)}, u32[]{:S(2)}, u32[]{:S(2)}) collective-permute-start(f32[3,1536]{1,0:T(4,128)S(1)} %get-tuple-element.72), channel_id=1, source_target_pairs={{0,1},{1,2},{2,3},{3,4},{4,5},{5,6},{6,7},{7,8},{8,9},{9,10},{10,1... | collective-permute-start | bytes 55304 | tf_op jit(solution)/shard_map/ppermute | solution.py:40
  43.5 16.8 %collective-permute-start.5 = (f32[3,1536]{1,0:T(4,128)S(1)}, f32[3,1536]{1,0:T(4,128)}, u32[]{:S(2)}, u32[]{:S(2)}) collective-permute-start(f32[3,1536]{1,0:T(4,128)S(1)} %get-tuple-element.73), channel_id=1, source_target_pairs={{1,0},{2,1},{3,2},{4,3},{5,4},{6,5},{7,6},{8,7},{9,8},{10,9},{11,1... | collective-permute-start | bytes 55304 | tf_op jit(solution)/shard_map/ppermute | solution.py:41
  54.1 9.5 %collective-permute-start.2 = (f32[39,3,134]{2,1,0:T(4,128)}, f32[39,3,134]{2,1,0:T(4,128)S(1)}, u32[]{:S(2)}, u32[]{:S(2)}) collective-permute-start(f32[39,3,134]{2,1,0:T(4,128)} %get-tuple-element.47), channel_id=1, source_target_pairs={{0,1},{1,2},{2,3},{3,4},{4,5},{5,6},{6,7},{7,8},{8,9},{9,10},{10,1... | collective-permute-start | bytes 188144 | tf_op jit(solution)/shard_map/ppermute | solution.py:40
  57.8 10.6 %collective-permute-start.3 = (f32[39,3,134]{2,1,0:T(4,128)}, f32[39,3,134]{2,1,0:T(4,128)}, u32[]{:S(2)}, u32[]{:S(2)}) collective-permute-start(f32[39,3,134]{2,1,0:T(4,128)} %get-tuple-element.48), channel_id=1, source_target_pairs={{1,0},{2,1},{3,2},{4,3},{5,4},{6,5},{7,6},{8,7},{9,8},{10,9},{11,1... | collective-permute-start | bytes 188144 | tf_op jit(solution)/shard_map/ppermute | solution.py:41
  59.7 0.6 copy-start.19
  62.4 12.0 %copy-start.20 = (f32[6]{0:T(128)S(1)}, f32[6]{0:T(128)}, u32[]{:S(2)}) copy-start(f32[6]{0:T(128)} %constant.12.clone) | copy-start | bytes 76
  62.4 12.0 %copy-start.21 = (f32[6]{0:T(128)S(1)}, f32[6]{0:T(128)}, u32[]{:S(2)}) copy-start(f32[6]{0:T(128)} %constant.52) | copy-start | bytes 76
  62.4 12.0 %copy-start.23 = (f32[98]{0:T(128)S(1)}, f32[98]{0:T(128)}, u32[]{:S(2)}) copy-start(f32[98]{0:T(128)} %get-tuple-element.97) | copy-start | bytes 1180
  72.3 5.0 %copy-start = (f32[39,102,134]{2,1,0:T(8,128)}, f32[39,102,134]{2,1,0:T(8,128)S(1)}, u32[]{:S(2)}) copy-start(f32[39,102,134]{2,1,0:T(8,128)S(1)} %pad_maximum_fusion) | copy-start | bytes 6396628
  72.3 3.5 %copy-start.22 = (f32[100]{0:T(128)S(1)}, f32[100]{0:T(128)}, u32[]{:S(2)}) copy-start(f32[100]{0:T(128)} %get-tuple-element.100) | copy-start | bytes 1204
  90.0 14.7 %copy-start.8 = (f32[102,16,104]{0,2,1:T(8,128)S(1)}, f32[102,16,104]{0,2,1:T(8,128)}, u32[]{:S(2)}) copy-start(f32[102,16,104]{0,2,1:T(8,128)} %pad.9) | copy-start | bytes 2036740
  92.5 23.8 %collective-permute-start.6 = (f32[12,102,3]{1,0,2:T(8,128)S(1)}, f32[12,102,3]{1,0,2:T(8,128)S(1)}, u32[]{:S(2)}, u32[]{:S(2)}) collective-permute-start(f32[12,102,3]{1,0,2:T(8,128)S(1)} %get-tuple-element.94), channel_id=1, source_target_pairs={{0,16},{16,32},{32,48},{48,64},{64,80},{80,96},{96,112},{112,128},... | collective-permute-start | bytes 44072 | tf_op jit(solution)/shard_map/ppermute | solution.py:153
  97.1 20.3 %collective-permute-start.7 = (f32[12,102,3]{1,0,2:T(8,128)S(1)}, f32[12,102,3]{1,0,2:T(8,128)S(1)}, u32[]{:S(2)}, u32[]{:S(2)}) collective-permute-start(f32[12,102,3]{1,0,2:T(8,128)S(1)} %get-tuple-element.95), channel_id=1, source_target_pairs={{16,0},{32,16},{48,32},{64,48},{80,64},{96,80},{112,96},{128,112},... | collective-permute-start | bytes 44072 | tf_op jit(solution)/shard_map/ppermute | solution.py:154
  118.6 2.3 %copy-start.30 = (f32[100]{0:T(128)S(1)}, f32[100]{0:T(128)}, u32[]{:S(2)}) copy-start(f32[100]{0:T(128)} %slice_multiply_fusion.4) | copy-start | bytes 1204
  120.8 1.2 copy-start.4
  120.8 1.3 copy-start.5
  120.9 1.5 %copy-start.6 = (f32[6,100,132]{2,1,0:T(8,128)S(1)}, f32[6,100,132]{2,1,0:T(8,128)}, u32[]{:S(2)}) copy-start(f32[6,100,132]{2,1,0:T(8,128)} %get-tuple-element.26) | copy-start | bytes 950404
  120.9 1.4 %copy-start.15 = (f32[100,132]{1,0:T(8,128)S(1)}, f32[100,132]{1,0:T(8,128)}, u32[]{:S(2)}) copy-start(f32[100,132]{1,0:T(8,128)} %get-tuple-element.23) | copy-start | bytes 158404
  120.9 1.4 %copy-start.26 = (f32[100]{0:T(128)S(1)}, f32[100]{0:T(128)}, u32[]{:S(2)}) copy-start(f32[100]{0:T(128)} %get-tuple-element.99) | copy-start | bytes 1204
  120.9 1.4 %copy-start.27 = (f32[100]{0:T(128)S(1)}, f32[100]{0:T(128)}, u32[]{:S(2)}) copy-start(f32[100]{0:T(128)} %get-tuple-element.101) | copy-start | bytes 1204
  123.0 0.9 copy-start.13
  124.1 2.1 %copy-start.11 = (f32[98,130]{1,0:T(8,128)S(1)}, f32[98,130]{1,0:T(8,128)}, u32[]{:S(2)}) copy-start(f32[98,130]{1,0:T(8,128)} %slice_negate_fusion.2) | copy-start | bytes 152884
  126.1 1.1 copy-start.1
  126.2 1.3 copy-start.2
  126.2 1.5 %copy-start.3 = (f32[6,98,130]{2,1,0:T(8,128)S(1)}, f32[6,98,130]{2,1,0:T(8,128)}, u32[]{:S(2)}) copy-start(f32[6,98,130]{2,1,0:T(8,128)} %get-tuple-element.29) | copy-start | bytes 917284
  126.2 1.4 %copy-start.14 = (f32[98,130]{1,0:T(8,128)S(1)}, f32[98,130]{1,0:T(8,128)}, u32[]{:S(2)}) copy-start(f32[98,130]{1,0:T(8,128)} %get-tuple-element.18) | copy-start | bytes 152884
  126.2 1.4 %copy-start.24 = (f32[98]{0:T(128)S(1)}, f32[98]{0:T(128)}, u32[]{:S(2)}) copy-start(f32[98]{0:T(128)} %get-tuple-element.96) | copy-start | bytes 1180
  126.2 1.4 %copy-start.25 = (f32[98]{0:T(128)S(1)}, f32[98]{0:T(128)}, u32[]{:S(2)}) copy-start(f32[98]{0:T(128)} %get-tuple-element.98) | copy-start | bytes 1180
  128.4 0.9 copy-start.12
  129.3 0.7 copy-start.29
  129.9 1.9 %copy-start.28 = (f32[6]{0:T(128)S(1)}, f32[6]{0:T(128)}, u32[]{:S(2)}) copy-start(f32[6]{0:T(128)} %constant.49) | copy-start | bytes 76
Sparse Core Ops, SparseCore 0:
  13.8 76.1 all-gather.1

commit v11 on v2

--- a/solution.py
+++ b/solution.py
@@ -124,10 +124,27 @@
     half = lax.axis_index("half")
     green_split = green_ext.reshape(green_ext.shape[0], halves, -1)
     swap = [(i, (i + 1) % halves) for i in range(halves)]
-    green_away = lax.ppermute(
-        lax.dynamic_index_in_dim(green_split, (half + 1) % halves, axis=1, keepdims=False), "half", swap
+    green_home = lax.dynamic_index_in_dim(green_split, half, axis=1, keepdims=False)
+    lat_here, lat_count = lat_index(), lat_size()
+    per_half = lat_count // halves
+    own_split = lat_green.reshape(rows_here, halves, -1)
+
+    def partner(i):
+        return (i + per_half) % lat_count
+
+    def columns_for(owner):
+        return lax.dynamic_index_in_dim(own_split, (owner // per_half + 1) % halves, axis=1, keepdims=False)
+
+    middle = lax.ppermute(columns_for(lat_here), LAT, [(i, partner(i)) for i in range(lat_count)])
+    top = lax.ppermute(
+        columns_for(lat_here + 1)[rows_here - HALO :],
+        LAT,
+        [(i, partner(i + 1)) for i in range(lat_count - 1)],
     )
-    green_home = lax.dynamic_index_in_dim(green_split, half, axis=1, keepdims=False)
+    bottom = lax.ppermute(
+        columns_for(lat_here - 1)[:HALO], LAT, [(i, partner(i - 1)) for i in range(1, lat_count)]
+    )
+    green_away = jnp.concatenate([top, middle, bottom], axis=0)
     for_partner = jnp.einsum("rs,ksc->krc", green_away, gathered, precision=lax.Precision.HIGHEST)
     back = [(j, i) for i, j in swap]
     from_partner = lax.ppermute(for_partner, "half", back)

time: 145 us -> 149 us (1.028)
  the two profiles are of different devices: /device:TPU:24 before, /device:TPU:1 now
where the time goes in v11:
time: 149 us; the launch traced here: 148 us
  starting transfers between devices  47.9 us (32%)
  local copies, waits for them, and re-layouts  30.6 us (21%)
  other arithmetic  25.9 us (17%)
  waiting for transfers between devices  18.1 us (12%)
  between operations  14.8 us (10%)
  matrix products  10.7 us (7%)
    ppermute x2, starting transfers between devices, widen_lon(): after = lax.ppermute(initial, 'lon', down)  13 us
    ppermute x1, waiting for transfers between devices, per_device(): from_partner = lax.ppermute(for_partner, 'half', back)  10.4 us
    ppermute x2, starting transfers between devices, widen_lat(): before = lax.ppermute(last, LAT, up)  9.32 us
    ppermute x2, starting transfers between devices, widen_lat(): after = lax.ppermute(initial, LAT, down)  7.98 us
    slice x4, local copies, waits for them, and re-layouts, widen_lon(): last = lax.slice_in_dim(array, length - width, length, axis=dim)  7.96 us
    ppermute x2, starting transfers between devices, widen_lon(): before = lax.ppermute(last, 'lon', up)  7.01 us
    dot_general x1, matrix products, per_device(): jnp.einsum('rs,ksc->krc', green_away, gathered, precision=lax.Precision.H...  5.47 us
    unnamed x75, local copies, waits for them, and re-layouts  5.24 us
  transfers between devices with their start and end apart: 13, of which 3 were waited for; matrix products, arithmetic and copies ran while one was open for 24% of the time, Pallas kernels for 0%

profile of v11, /device:TPU:1, one launch (start us, length us, event | category | flops | bytes accessed | tf_op | source)
XLA Modules:
  0.0 148.0 jit_solution(10777502277146569823)
XLA Ops:
  7.2 0.9 convert_element_type.6
  8.1 2.5 %fusion.43 = f32[12,96,128]{2,1,0:T(8,128)} fusion(f32[12,96,128]{2,1,0:T(8,128)} %param.12, f32[96,128]{1,0:T(8,128)S(1)} %convert_element_type.6, f32[128,128]{1,0:T(8,128)S(1)} %copy-done), kind=kOutput, calls=%fused_computation.93 | convolution fusion | flops 226639872 | bytes 1294336 | tf_op jit(solution)/shard_map/krj,cj->krc/dot_general | solution.py:115
  10.7 4.7 %collective-permute-start.4 = (f32[3,1536]{1,0:T(4,128)S(1)}, f32[3,1536]{1,0:T(4,128)S(1)}, u32[]{:S(2)}, u32[]{:S(2)}) collective-permute-start(f32[3,1536]{1,0:T(4,128)S(1)} %get-tuple-element.43), channel_id=1, source_target_pairs={{0,1},{1,2},{2,3},{3,4},{4,5},{5,6},{6,7},{7,8},{8,9},{9,10},{10,1... | collective-permute-start | bytes 55304 | tf_op jit(solution)/shard_map/ppermute | solution.py:43
  15.4 5.5 %collective-permute-start.5 = (f32[3,1536]{1,0:T(4,128)S(1)}, f32[3,1536]{1,0:T(4,128)}, u32[]{:S(2)}, u32[]{:S(2)}) collective-permute-start(f32[3,1536]{1,0:T(4,128)S(1)} %get-tuple-element.44), channel_id=1, source_target_pairs={{1,0},{2,1},{3,2},{4,3},{5,4},{6,5},{7,6},{8,7},{9,8},{10,9},{11,1... | collective-permute-start | bytes 55304 | tf_op jit(solution)/shard_map/ppermute | solution.py:44
  21.0 0.4 reshape.57
  21.4 2.1 %collective-permute-start.8 = (f32[3,768]{1,0:T(4,128)S(1)}, f32[3,768]{1,0:T(4,128)}, u32[]{:S(2)}, u32[]{:S(2)}) collective-permute-start(f32[3,768]{1,0:T(4,128)S(1)} %bitcast.43), channel_id=1, source_target_pairs={{1,8},{2,9},{3,10},{4,11},{5,12},{6,13},{7,14},{8,15},{9,0},{10,1}... | collective-permute-start | bytes 27656 | tf_op jit(solution)/shard_map/ppermute | solution.py:144
  23.5 0.6 copy.45
  24.1 4.3 %collective-permute-start.6 = (f32[3,768]{1,0:T(4,128)}, f32[3,768]{1,0:T(4,128)}, u32[]{:S(2)}, u32[]{:S(2)}) collective-permute-start(f32[3,768]{1,0:T(4,128)} %bitcast.40), channel_id=1, source_target_pairs={{0,9},{1,10},{2,11},{3,12},{4,13},{5,14},{6,15},{7,0},{8,1},{9,2},... | collective-permute-start | bytes 27656 | tf_op jit(solution)/shard_map/ppermute | solution.py:139
  28.8 0.7 copy.43
  29.5 1.9 %collective-permute-start.7 = (f32[96,768]{1,0:T(8,128)}, f32[96,768]{1,0:T(8,128)}, u32[]{:S(2)}, u32[]{:S(2)}) collective-permute-start(f32[96,768]{1,0:T(8,128)} %bitcast.38), channel_id=1, source_target_pairs={{0,8},{1,9},{2,10},{3,11},{4,12},{5,13},{6,14},{7,15},{8,0},{9,1},... | collective-permute-start | bytes 884744 | tf_op jit(solution)/shard_map/ppermute | solution.py:138
  31.6 1.2 subtract_dynamic-update-slice_fusion
  32.8 1.1 constant_dynamic-update-slice_fusion.1
  34.0 1.1 constant_dynamic-update-slice_fusion
  35.1 0.6 slice_multiply_fusion.7
  35.7 0.6 fusion.61
  36.3 0.6 broadcast_multiply_fusion.4
  36.9 2.6 %fusion.57 = (f32[39,96,3]{2,1,0:T(8,128)}, f32[39,96,3]{2,1,0:T(8,128)}) fusion(f32[39,96,128]{2,1,0:T(8,128)S(1)} %bitcast_dynamic-update-slice_fusion), kind=kLoop, calls=%fused_computation.145 | loop fusion | bytes 179712 | tf_op jit(solution)/shard_map/slice | solution.py:30
  39.5 0.6 slice_multiply_fusion.8
  40.1 2.1 %copy.19 = f32[39,96,3]{1,0,2:T(8,128)S(1)} copy(f32[39,96,3]{2,1,0:T(8,128)} %get-tuple-element.34) | data formatting | bytes 89856 | tf_op jit(solution)/shard_map/slice | solution.py:30
  42.2 2.2 %copy.20 = f32[39,96,3]{1,0,2:T(8,128)S(1)} copy(f32[39,96,3]{2,1,0:T(8,128)} %get-tuple-element.35) | data formatting | bytes 89856 | tf_op jit(solution)/shard_map/slice | solution.py:31
  44.5 11.1 %collective-permute-start.1 = (f32[39,96,3]{1,0,2:T(8,128)S(1)}, f32[39,96,3]{1,0,2:T(8,128)S(1)}, u32[]{:S(2)}, u32[]{:S(2)}) collective-permute-start(f32[39,96,3]{1,0,2:T(8,128)S(1)} %copy.20), channel_id=1, source_target_pairs={{16,0},{32,16},{48,32},{64,48},{80,64},{96,80},{112,96},{128,112},... | collective-permute-start | bytes 134792 | tf_op jit(solution)/shard_map/ppermute | solution.py:33
  55.6 1.9 %collective-permute-start = (f32[39,96,3]{1,0,2:T(8,128)S(1)}, f32[39,96,3]{1,0,2:T(8,128)S(1)}, u32[]{:S(2)}, u32[]{:S(2)}) collective-permute-start(f32[39,96,3]{1,0,2:T(8,128)S(1)} %copy.19), channel_id=1, source_target_pairs={{0,16},{16,32},{32,48},{48,64},{64,80},{80,96},{96,112},{112,128},... | collective-permute-start | bytes 134792 | tf_op jit(solution)/shard_map/ppermute | solution.py:32
  57.5 0.8 pad_maximum_fusion.2
  58.3 1.2 reshape.56
  59.6 4.6 %collective-permute-done = f32[39,96,3]{1,0,2:T(8,128)S(1)} collective-permute-done((f32[39,96,3]{1,0,2:T(8,128)S(1)}, f32[39,96,3]{1,0,2:T(8,128)S(1)}, u32[]{:S(2)}, u32[]{:S(2)}) %collective-permute-start) | collective-permute-done | bytes 44960 | tf_op jit(solution)/shard_map/ppermute | solution.py:32
  64.2 2.0 %copy.21 = f32[39,96,3]{2,1,0:T(8,128)} copy(f32[39,96,3]{1,0,2:T(8,128)S(1)} %collective-permute-done) | data formatting | bytes 89856 | tf_op jit(solution)/shard_map/ppermute | solution.py:32
  66.1 1.9 %copy.22 = f32[39,96,3]{2,1,0:T(8,128)} copy(f32[39,96,3]{1,0,2:T(8,128)S(1)} %collective-permute-done.1) | data formatting | bytes 89856 | tf_op jit(solution)/shard_map/ppermute | solution.py:33
  68.0 1.6 %pad_maximum_fusion.5 = (f32[39,3,134]{2,1,0:T(4,128)S(1)}, f32[39,3,134]{2,1,0:T(4,128)S(1)}) fusion(f32[39,96,3]{2,1,0:T(8,128)} %copy.22, f32[39,96,128]{2,1,0:T(8,128)S(1)} %bitcast_dynamic-update-slice_fusion, f32[39,96,3]{2,1,0:T(8,128)} %copy.21), kind=kLoop, calls=%fused_computation.110 | loop fusion | flops 62712 | bytes 2132208 | tf_op jit(solution)/shard_map/slice | solution.py:41
  69.7 4.6 %collective-permute-start.2 = (f32[39,3,134]{2,1,0:T(4,128)S(1)}, f32[39,3,134]{2,1,0:T(4,128)S(1)}, u32[]{:S(2)}, u32[]{:S(2)}) collective-permute-start(f32[39,3,134]{2,1,0:T(4,128)S(1)} %get-tuple-element.22), channel_id=1, source_target_pairs={{0,1},{1,2},{2,3},{3,4},{4,5},{5,6},{6,7},{7,8},{8,9},{9,10},{10,1... | collective-permute-start | bytes 188144 | tf_op jit(solution)/shard_map/ppermute | solution.py:43
  74.3 2.5 %collective-permute-start.3 = (f32[39,3,134]{2,1,0:T(4,128)S(1)}, f32[39,3,134]{2,1,0:T(4,128)S(1)}, u32[]{:S(2)}, u32[]{:S(2)}) collective-permute-start(f32[39,3,134]{2,1,0:T(4,128)S(1)} %get-tuple-element.23), channel_id=1, source_target_pairs={{1,0},{2,1},{3,2},{4,3},{5,4},{6,5},{7,6},{8,7},{9,8},{10,9},{11,1... | collective-permute-start | bytes 188144 | tf_op jit(solution)/shard_map/ppermute | solution.py:44
  76.8 1.0 constant_dynamic-slice_fusion.3
  77.8 3.1 %collective-permute-done.3 = f32[39,3,134]{2,1,0:T(4,128)S(1)} collective-permute-done((f32[39,3,134]{2,1,0:T(4,128)S(1)}, f32[39,3,134]{2,1,0:T(4,128)S(1)}, u32[]{:S(2)}, u32[]{:S(2)}) %collective-permute-start.3) | collective-permute-done | bytes 62744 | tf_op jit(solution)/shard_map/ppermute | solution.py:44
  80.9 0.8 maximum_bitcast_fusion.4
  81.7 0.8 slice_add_fusion.3
  82.6 5.5 %convolution_bitcast_fusion = f32[12,102,128]{2,1,0:T(8,128)S(1)} fusion(f32[12,768,128]{2,1,0:T(8,128)} %all-gather.2.cloned.1.call-done, f32[3,768]{1,0:T(4,128)} %collective-permute-done.8, f32[96,768]{1,0:T(8,128)} %collective-permute-done.7, f32[3,768]{1,0:T(4,128)} %collective-permute-done.6), kind=kOutput, calls=%fused_computation.46 | convolution fusion | flops 1444045824 | bytes 5658624 | tf_op jit(solution)/shard_map/rs,ksc->krc/dot_general | solution.py:148
  88.1 2.2 %collective-permute-start.9 = (f32[12,102,128]{2,1,0:T(8,128)S(1)}, f32[12,102,128]{2,1,0:T(8,128)S(1)}, u32[]{:S(2)}, u32[]{:S(2)}) collective-permute-start(f32[12,102,128]{2,1,0:T(8,128)S(1)} %convolution_bitcast_fusion), channel_id=1, source_target_pairs={{8,0},{0,8},{9,1},{1,9},{10,2},{2,10},{11,3},{3,11},{12,4},{4,12},... | collective-permute-start | bytes 1880072 | tf_op jit(solution)/shard_map/ppermute | solution.py:150
  90.3 1.7 %pad_maximum_fusion = f32[39,102,134]{2,1,0:T(8,128)S(1)} fusion(f32[39,3,134]{2,1,0:T(4,128)S(1)} %collective-permute-done.3, f32[39,96,3]{2,1,0:T(8,128)S(1)} %copy-done.5, f32[39,96,128]{2,1,0:T(8,128)S(1)} %bitcast_dynamic-update-slice_fusion, f32[39,96,3]{2,1,0:T(8,128)S(1)} %copy-done.3, f32[39,3,134]{2,1,0:T(4,128)S(1)} %collective-permute-done.2), kind=kLoop, calls=%fused_computation | loop fusion | flops 2132208 | bytes 4264416 | tf_op jit(solution)/shard_map/concatenate | solution.py:45
  92.0 0.8 slice_add_fusion.4
  92.8 2.1 %slice_add_fusion = f32[24,100,132]{2,1,0:T(8,128)S(1)} fusion(f32[39,102,134]{2,1,0:T(8,128)S(1)} %pad_maximum_fusion), kind=kLoop, calls=%fused_computation.14 | loop fusion | flops 950400 | bytes 6336000 | tf_op jit(solution)/shard_map/add | solution.py:82
  94.9 10.4 %collective-permute-done.9 = f32[12,102,128]{2,1,0:T(8,128)S(1)} collective-permute-done((f32[12,102,128]{2,1,0:T(8,128)S(1)}, f32[12,102,128]{2,1,0:T(8,128)S(1)}, u32[]{:S(2)}, u32[]{:S(2)}) %collective-permute-start.9) | collective-permute-done | bytes 626720 | tf_op jit(solution)/shard_map/ppermute | solution.py:150
  105.3 2.7 %fusion.49 = f32[12,102,128]{2,1,0:T(8,128)S(1)} fusion(f32[12,102,128]{2,1,0:T(8,128)S(1)} %collective-permute-done.9, f32[12,768,128]{2,1,0:T(8,128)S(1)} %bitcast.42, f32[102,1,768]{2,1,0:T(1,128)S(1)} %copy-done.9), kind=kOutput, calls=%fused_computation.102 | convolution fusion | flops 1444045824 | bytes 6285312 | tf_op jit(solution)/shard_map/rs,ksc->krc/dot_general | solution.py:151
  108.1 1.3 fusion.59
  109.3 2.0 %copy.26 = f32[12,102,3]{1,0,2:T(8,128)} copy(f32[12,102,3]{2,1,0:T(8,128)} %get-tuple-element.39) | data formatting | bytes 29376 | tf_op jit(solution)/shard_map/slice | solution.py:30
  111.3 1.4 copy.27
  112.7 1.9 %collective-permute-start.11 = (f32[12,102,3]{1,0,2:T(8,128)S(1)}, f32[12,102,3]{1,0,2:T(8,128)}, u32[]{:S(2)}, u32[]{:S(2)}) collective-permute-start(f32[12,102,3]{1,0,2:T(8,128)S(1)} %copy.27), channel_id=1, source_target_pairs={{16,0},{32,16},{48,32},{64,48},{80,64},{96,80},{112,96},{128,112},... | collective-permute-start | bytes 44072 | tf_op jit(solution)/shard_map/ppermute | solution.py:33
  114.6 5.1 %collective-permute-start.10 = (f32[12,102,3]{1,0,2:T(8,128)}, f32[12,102,3]{1,0,2:T(8,128)}, u32[]{:S(2)}, u32[]{:S(2)}) collective-permute-start(f32[12,102,3]{1,0,2:T(8,128)} %copy.26), channel_id=1, source_target_pairs={{0,16},{16,32},{32,48},{48,64},{64,80},{80,96},{96,112},{112,128},... | collective-permute-start | bytes 44072 | tf_op jit(solution)/shard_map/ppermute | solution.py:32
  119.7 0.8 slice_negate_fusion.1
  120.5 1.6 %slice.287 = f32[100,132]{1,0:T(8,128)} slice(f32[102,134]{1,0:T(8,128)} %get-tuple-element.19), slice={[1:101], [1:133]} | slice | bytes 105600 | tf_op jit(solution)/shard_map/slice | solution.py:77
  122.1 1.6 %slice.278 = f32[98,130]{1,0:T(8,128)} slice(f32[102,134]{1,0:T(8,128)} %get-tuple-element.19), slice={[2:100], [2:132]} | slice | bytes 101920 | tf_op jit(solution)/shard_map/slice | solution.py:77
  123.8 1.9 %copy.28 = f32[12,102,3]{2,1,0:T(8,128)} copy(f32[12,102,3]{1,0,2:T(8,128)} %collective-permute-done.10) | data formatting | bytes 29376 | tf_op jit(solution)/shard_map/ppermute | solution.py:32
  125.7 1.9 %copy.29 = f32[12,102,3]{2,1,0:T(8,128)} copy(f32[12,102,3]{1,0,2:T(8,128)} %collective-permute-done.11) | data formatting | bytes 29376 | tf_op jit(solution)/shard_map/ppermute | solution.py:33
  127.6 2.3 %slice_subtract_fusion.2 = f32[12,102,134]{2,1,0:T(8,128)S(1)} fusion(f32[39,102,134]{2,1,0:T(8,128)} %copy-done.1, f32[12,102,3]{2,1,0:T(8,128)} %copy.29, f32[12,102,128]{2,1,0:T(8,128)S(1)} %fusion.49, f32[12,102,3]{2,1,0:T(8,128)} %copy.28), kind=kLoop, calls=%fused_computation.41 | loop fusion | flops 492048 | bytes 1968192 | tf_op jit(solution)/shard_map/sub | solution.py:154
  129.9 1.1 fusion.10
  131.1 0.8 fusion.18
  131.9 0.4 fusion.20
  132.3 0.5 copy-done.18
  133.0 2.1 %fusion.2 = f32[24,98,130]{2,1,0:T(8,128)S(1)} fusion(f32[12,100,132]{2,1,0:T(8,128)S(1)} %get-tuple-element.57, f32[12,100,132]{2,1,0:T(8,128)S(1)} %get-tuple-element.56), kind=kLoop, calls=%fused_computation.9 | loop fusion | flops 2140320 | bytes 2490240 | tf_op jit(solution)/shard_map/add | solution.py:82
  135.1 0.8 fusion.6
  136.0 0.8 fusion.22
  136.9 0.4 fusion.25
  137.3 0.5 copy-done.17
  138.0 0.4 copy-done.30
  138.4 1.8 %fusion.58 = (f32[12,96,128]{2,1,0:T(8,128)}, f32[12,96,128]{2,1,0:T(8,128)S(1)}, f32[12,96,128]{2,1,0:T(8,128)}) fusion(f32[12,98,130]{2,1,0:T(8,128)S(1)} %get-tuple-element.52, f32[96]{0:T(128)S(1)} %copy-done.30, f32[12,98,130]{2,1,0:T(8,128)S(1)} %get-tuple-element.51), kind=kLoop, calls=%fused_computation.146 | loop fusion | flops 737280 | bytes 5308800 | tf_op jit(solution)/shard_map/slice | solution.py:183
  140.3 0.9 maximum_multiply_fusion.4
  (90 shorter events, 1.2 us)
Async XLA Ops:
  7.2 0.9 copy-start
  7.2 3.5 %copy-start.6 = (f32[96,1536]{1,0:T(8,128)S(1)}, f32[96,1536]{1,0:T(8,128)}, u32[]{:S(2)}) copy-start(f32[96,1536]{1,0:T(8,128)} %param.20) | copy-start | bytes 1769476
  7.2 75.4 %all-gather.2.cloned.1.call-start = ((), (), s32[]{:S(2)}) async-start(), calls=%async_computation | async-start | bytes 5308416 | tf_op jit(solution)/shard_map/all_gather | solution.py:116
  10.6 20.9 %copy-start.7 = (f32[12,96,128]{2,1,0:T(8,128)S(1)}, f32[12,96,128]{2,1,0:T(8,128)}, u32[]{:S(2)}) copy-start(f32[12,96,128]{2,1,0:T(8,128)} %param.12) | copy-start | bytes 1769476
  10.7 33.8 %collective-permute-start.4 = (f32[3,1536]{1,0:T(4,128)S(1)}, f32[3,1536]{1,0:T(4,128)S(1)}, u32[]{:S(2)}, u32[]{:S(2)}) collective-permute-start(f32[3,1536]{1,0:T(4,128)S(1)} %get-tuple-element.43), channel_id=1, source_target_pairs={{0,1},{1,2},{2,3},{3,4},{4,5},{5,6},{6,7},{7,8},{8,9},{9,10},{10,1... | collective-permute-start | bytes 55304 | tf_op jit(solution)/shard_map/ppermute | solution.py:43
  15.4 40.2 %collective-permute-start.5 = (f32[3,1536]{1,0:T(4,128)S(1)}, f32[3,1536]{1,0:T(4,128)}, u32[]{:S(2)}, u32[]{:S(2)}) collective-permute-start(f32[3,1536]{1,0:T(4,128)S(1)} %get-tuple-element.44), channel_id=1, source_target_pairs={{1,0},{2,1},{3,2},{4,3},{5,4},{6,5},{7,6},{8,7},{9,8},{10,9},{11,1... | collective-permute-start | bytes 55304 | tf_op jit(solution)/shard_map/ppermute | solution.py:44
  21.4 61.1 %collective-permute-start.8 = (f32[3,768]{1,0:T(4,128)S(1)}, f32[3,768]{1,0:T(4,128)}, u32[]{:S(2)}, u32[]{:S(2)}) collective-permute-start(f32[3,768]{1,0:T(4,128)S(1)} %bitcast.43), channel_id=1, source_target_pairs={{1,8},{2,9},{3,10},{4,11},{5,12},{6,13},{7,14},{8,15},{9,0},{10,1}... | collective-permute-start | bytes 27656 | tf_op jit(solution)/shard_map/ppermute | solution.py:144
  24.1 58.4 %collective-permute-start.6 = (f32[3,768]{1,0:T(4,128)}, f32[3,768]{1,0:T(4,128)}, u32[]{:S(2)}, u32[]{:S(2)}) collective-permute-start(f32[3,768]{1,0:T(4,128)} %bitcast.40), channel_id=1, source_target_pairs={{0,9},{1,10},{2,11},{3,12},{4,13},{5,14},{6,15},{7,0},{8,1},{9,2},... | collective-permute-start | bytes 27656 | tf_op jit(solution)/shard_map/ppermute | solution.py:139
  29.5 53.0 %collective-permute-start.7 = (f32[96,768]{1,0:T(8,128)}, f32[96,768]{1,0:T(8,128)}, u32[]{:S(2)}, u32[]{:S(2)}) collective-permute-start(f32[96,768]{1,0:T(8,128)} %bitcast.38), channel_id=1, source_target_pairs={{0,8},{1,9},{2,10},{3,11},{4,12},{5,13},{6,14},{7,15},{8,0},{9,1},... | collective-permute-start | bytes 884744 | tf_op jit(solution)/shard_map/ppermute | solution.py:138
  31.6 5.3 %copy-start.21 = (f32[96,128]{1,0:T(8,128)S(1)}, f32[96,128]{1,0:T(8,128)}, u32[]{:S(2)}) copy-start(f32[96,128]{1,0:T(8,128)} %param.16) | copy-start | bytes 147460
  31.6 5.3 %copy-start.22 = (f32[96,128]{1,0:T(8,128)S(1)}, f32[96,128]{1,0:T(8,128)}, u32[]{:S(2)}) copy-start(f32[96,128]{1,0:T(8,128)} %param.17) | copy-start | bytes 147460
  31.6 5.3 %copy-start.20 = (s32[96,128]{1,0:T(8,128)S(1)}, s32[96,128]{1,0:T(8,128)}, u32[]{:S(2)}) copy-start(s32[96,128]{1,0:T(8,128)} %param.18) | copy-start | bytes 147460
  44.5 21.7 %collective-permute-start.1 = (f32[39,96,3]{1,0,2:T(8,128)S(1)}, f32[39,96,3]{1,0,2:T(8,128)S(1)}, u32[]{:S(2)}, u32[]{:S(2)}) collective-permute-start(f32[39,96,3]{1,0,2:T(8,128)S(1)} %copy.20), channel_id=1, source_target_pairs={{16,0},{32,16},{48,32},{64,48},{80,64},{96,80},{112,96},{128,112},... | collective-permute-start | bytes 134792 | tf_op jit(solution)/shard_map/ppermute | solution.py:33
  55.6 8.6 %collective-permute-start = (f32[39,96,3]{1,0,2:T(8,128)S(1)}, f32[39,96,3]{1,0,2:T(8,128)S(1)}, u32[]{:S(2)}, u32[]{:S(2)}) collective-permute-start(f32[39,96,3]{1,0,2:T(8,128)S(1)} %copy.19), channel_id=1, source_target_pairs={{0,16},{16,32},{32,48},{48,64},{64,80},{80,96},{96,112},{112,128},... | collective-permute-start | bytes 134792 | tf_op jit(solution)/shard_map/ppermute | solution.py:32
  68.0 8.7 %copy-start.8 = (f32[102,2,768]{2,1,0:T(2,128)S(1)}, f32[102,2,768]{2,1,0:T(2,128)}, u32[]{:S(2)}) copy-start(f32[102,2,768]{2,1,0:T(2,128)} %reshape.56) | copy-start | bytes 1880068
  68.0 12.8 %copy-start.2 = (f32[39,96,3]{2,1,0:T(8,128)S(1)}, f32[39,96,3]{2,1,0:T(8,128)}, u32[]{:S(2)}) copy-start(f32[39,96,3]{2,1,0:T(8,128)} %copy.21) | copy-start | bytes 134788
  68.0 12.8 %copy-start.4 = (f32[39,96,3]{2,1,0:T(8,128)S(1)}, f32[39,96,3]{2,1,0:T(8,128)}, u32[]{:S(2)}) copy-start(f32[39,96,3]{2,1,0:T(8,128)} %copy.22) | copy-start | bytes 134788
  69.7 8.1 %collective-permute-start.2 = (f32[39,3,134]{2,1,0:T(4,128)S(1)}, f32[39,3,134]{2,1,0:T(4,128)S(1)}, u32[]{:S(2)}, u32[]{:S(2)}) collective-permute-start(f32[39,3,134]{2,1,0:T(4,128)S(1)} %get-tuple-element.22), channel_id=1, source_target_pairs={{0,1},{1,2},{2,3},{3,4},{4,5},{5,6},{6,7},{7,8},{8,9},{9,10},{10,1... | collective-permute-start | bytes 188144 | tf_op jit(solution)/shard_map/ppermute | solution.py:43
  74.3 6.6 %collective-permute-start.3 = (f32[39,3,134]{2,1,0:T(4,128)S(1)}, f32[39,3,134]{2,1,0:T(4,128)S(1)}, u32[]{:S(2)}, u32[]{:S(2)}) collective-permute-start(f32[39,3,134]{2,1,0:T(4,128)S(1)} %get-tuple-element.23), channel_id=1, source_target_pairs={{1,0},{2,1},{3,2},{4,3},{5,4},{6,5},{7,6},{8,7},{9,8},{10,9},{11,1... | collective-permute-start | bytes 188144 | tf_op jit(solution)/shard_map/ppermute | solution.py:44
  82.6 7.7 %copy-start.3 = (f32[39,96,3]{2,1,0:T(8,128)S(1)}, f32[39,96,3]{2,1,0:T(8,128)}, u32[]{:S(2)}) copy-start(f32[39,96,3]{2,1,0:T(8,128)} %copy.21) | copy-start | bytes 134788
  82.6 7.7 %copy-start.5 = (f32[39,96,3]{2,1,0:T(8,128)S(1)}, f32[39,96,3]{2,1,0:T(8,128)}, u32[]{:S(2)}) copy-start(f32[39,96,3]{2,1,0:T(8,128)} %copy.22) | copy-start | bytes 134788
  88.1 17.2 %collective-permute-start.9 = (f32[12,102,128]{2,1,0:T(8,128)S(1)}, f32[12,102,128]{2,1,0:T(8,128)S(1)}, u32[]{:S(2)}, u32[]{:S(2)}) collective-permute-start(f32[12,102,128]{2,1,0:T(8,128)S(1)} %convolution_bitcast_fusion), channel_id=1, source_target_pairs={{8,0},{0,8},{9,1},{1,9},{10,2},{2,10},{11,3},{3,11},{12,4},{4,12},... | collective-permute-start | bytes 1880072 | tf_op jit(solution)/shard_map/ppermute | solution.py:150
  92.0 3.0 %copy-start.1 = (f32[39,102,134]{2,1,0:T(8,128)}, f32[39,102,134]{2,1,0:T(8,128)S(1)}, u32[]{:S(2)}) copy-start(f32[39,102,134]{2,1,0:T(8,128)S(1)} %pad_maximum_fusion) | copy-start | bytes 6396628
  92.0 13.3 %slice-start = ((s8[4718592]{0:T(1024)(128)(4,1)}), s8[4194304]{0:T(1024)(128)(4,1)S(1)}, s32[]{:S(2)}) async-start(s8[4718592]{0:T(1024)(128)(4,1)} %bitcast.41), calls=%async_computation.1 | async-start | bytes 8388608
  92.8 12.5 %slice-start.1 = ((s8[4718592]{0:T(1024)(128)(4,1)}), s8[524288]{0:T(1024)(128)(4,1)S(1)}, s32[]{:S(2)}) async-start(s8[4718592]{0:T(1024)(128)(4,1)} %bitcast.41), calls=%async_computation.2 | async-start | bytes 1048576
  92.8 12.5 %copy-start.9 = (f32[102,1,768]{2,1,0:T(1,128)S(1)}, f32[102,1,768]{2,1,0:T(1,128)}, u32[]{:S(2)}) copy-start(f32[102,1,768]{2,1,0:T(1,128)} %constant_dynamic-slice_fusion.3) | copy-start | bytes 940036
  112.7 13.0 %collective-permute-start.11 = (f32[12,102,3]{1,0,2:T(8,128)S(1)}, f32[12,102,3]{1,0,2:T(8,128)}, u32[]{:S(2)}, u32[]{:S(2)}) collective-permute-start(f32[12,102,3]{1,0,2:T(8,128)S(1)} %copy.27), channel_id=1, source_target_pairs={{16,0},{32,16},{48,32},{64,48},{80,64},{96,80},{112,96},{128,112},... | collective-permute-start | bytes 44072 | tf_op jit(solution)/shard_map/ppermute | solution.py:33
  114.6 9.1 %collective-permute-start.10 = (f32[12,102,3]{1,0,2:T(8,128)}, f32[12,102,3]{1,0,2:T(8,128)}, u32[]{:S(2)}, u32[]{:S(2)}) collective-permute-start(f32[12,102,3]{1,0,2:T(8,128)} %copy.26), channel_id=1, source_target_pairs={{0,16},{16,32},{32,48},{48,64},{64,80},{80,96},{96,112},{112,128},... | collective-permute-start | bytes 44072 | tf_op jit(solution)/shard_map/ppermute | solution.py:32
  127.5 2.3 %copy-start.14 = (f32[100,132]{1,0:T(8,128)S(1)}, f32[100,132]{1,0:T(8,128)}, u32[]{:S(2)}) copy-start(f32[100,132]{1,0:T(8,128)} %get-tuple-element.61) | copy-start | bytes 158404
  127.5 2.3 %copy-start.15 = (f32[100,132]{1,0:T(8,128)S(1)}, f32[100,132]{1,0:T(8,128)}, u32[]{:S(2)}) copy-start(f32[100,132]{1,0:T(8,128)} %get-tuple-element.62) | copy-start | bytes 158404
  127.5 2.3 %copy-start.31 = (f32[100]{0:T(128)S(1)}, f32[100]{0:T(128)}, u32[]{:S(2)}) copy-start(f32[100]{0:T(128)} %slice_multiply_fusion.8) | copy-start | bytes 1204
  129.8 1.2 copy-start.11
  129.9 1.2 copy-start.12
  129.9 1.2 copy-start.19
  129.9 1.2 copy-start.23
  129.9 1.2 copy-start.24
  129.9 1.2 copy-start.27
  129.9 1.2 copy-start.28
  131.9 0.9 copy-start.18
  133.0 2.1 %copy-start.13 = (f32[98,130]{1,0:T(8,128)S(1)}, f32[98,130]{1,0:T(8,128)}, u32[]{:S(2)}) copy-start(f32[98,130]{1,0:T(8,128)} %get-tuple-element.69) | copy-start | bytes 152884
  135.1 0.9 copy-start.10
  135.1 0.9 copy-start.16
  135.1 0.9 copy-start.25
  135.1 0.9 copy-start.26
  136.9 0.9 copy-start.17
  137.8 0.6 copy-start.30
  138.4 1.9 %copy-start.29 = (f32[6]{0:T(128)S(1)}, f32[6]{0:T(128)}, u32[]{:S(2)}) copy-start(f32[6]{0:T(128)} %constant.107) | copy-start | bytes 76
Sparse Core Ops, SparseCore 0:
  10.8 47.7 all-gather.1

commit v12 on v4

--- a/solution.py
+++ b/solution.py
@@ -48,8 +48,8 @@
 
 
 def slopes(potential_ext, stretch):
-    east_slope = (potential_ext[:, 1:-1, 2:] - potential_ext[:, 1:-1, :-2]) * 0.5 * stretch
-    north_slope = (potential_ext[:, 2:, 1:-1] - potential_ext[:, :-2, 1:-1]) * 0.5
+    east_slope = (potential_ext[:, 2:, 1:-1] - potential_ext[:, :-2, 1:-1]) * 0.5 * stretch
+    north_slope = (potential_ext[:, 1:-1, 2:] - potential_ext[:, 1:-1, :-2]) * 0.5
     return (east_slope, north_slope)
 
 
@@ -87,8 +87,8 @@
 
 
 def surface(east_ext, north_ext, stretch, wet_frac):
-    spread = (east_ext[:, :, 2:] - east_ext[:, :, :-2]) * 0.5 * stretch + (
-        north_ext[:, 2:, :] - north_ext[:, :-2, :]
+    spread = (east_ext[:, 2:, :] - east_ext[:, :-2, :]) * 0.5 * stretch + (
+        north_ext[:, :, 2:] - north_ext[:, :, :-2]
     ) * 0.5
     frequency = jnp.array(FREQS, jnp.float32)[:, None, None]
     return wet_frac * jnp.concatenate([-spread[6:] / frequency, spread[:6] / frequency], axis=0)
@@ -127,22 +127,24 @@
     block = rows_here + spare
     green_blocks = green_ext.reshape(green_ext.shape[0], blocks, rows_here)
     lanes = gathered.reshape(12, blocks, block, columns)[:, :, rows_here : rows_here + 2 * HALO, :rows_here]
-    edge_sal = jnp.einsum("rbj,kbej->kre", green_blocks, lanes, precision=lax.Precision.HIGHEST)
+    edge_sal = jnp.einsum("rbj,kbej->ker", green_blocks, lanes, precision=lax.Precision.HIGHEST)
     size = lax.axis_size("lon")
     up = [(i, (i + 1) % size) for i in range(size)]
     down = [(j, i) for i, j in up]
-    before = lax.ppermute(edge_sal[:, :, HALO:], "lon", up)
-    after = lax.ppermute(edge_sal[:, :, :HALO], "lon", down)
+    before = lax.ppermute(edge_sal[:, HALO:], "lon", up)
+    after = lax.ppermute(edge_sal[:, :HALO], "lon", down)
     green_pad = jnp.pad(green_blocks, ((0, 0), (0, 0), (0, spare))).reshape(green_ext.shape[0], -1)
-    sal = jnp.einsum("rs,ksc->krc", green_pad, gathered, precision=lax.Precision.HIGHEST)
-    sal = jnp.concatenate([before, sal, after], axis=2)
+    sal = jnp.einsum("rs,ksc->kcr", green_pad, gathered, precision=lax.Precision.HIGHEST)
+    sal = jnp.concatenate([before, sal, after], axis=1)
+    stack = jnp.swapaxes(stack, 1, 2)
     potential = stack[:12] - sal
     flows = stack[12:36]
     depth_ext, drag_ext, wet_ext = stack[36], stack[37], stack[38]
 
     first_row = lat_index() * rows_here - HALO
     stretch, coriolis = row_terms(first_row + jnp.arange(rows_here + 2 * HALO), total_rows)
-    east_slope, north_slope = slopes(potential, stretch[1:-1])
+    stretch, coriolis = stretch.T, coriolis.T
+    east_slope, north_slope = slopes(potential, stretch[:, 1:-1])
     flows = relax(
         flows,
         east_slope,
@@ -150,7 +152,7 @@
         inner(depth_ext, 1),
         inner(drag_ext, 1),
         inner(wet_ext, 1),
-        coriolis[1:-1],
+        coriolis[:, 1:-1],
     )
     flows = relax(
         flows,
@@ -159,13 +161,13 @@
         inner(depth_ext, 2),
         inner(drag_ext, 2),
         inner(wet_ext, 2),
-        coriolis[2:-2],
+        coriolis[:, 2:-2],
     )
-    east_ext = flows[:12, 1:-1, :]
-    north_ext = flows[12:, :, 1:-1]
-    elevation_next = surface(east_ext, north_ext, stretch[HALO:-HALO], wet_frac)
-    flows = inner(flows, 1)
-    return (elevation_next, flows[:12], flows[12:])
+    east_ext = flows[:12, :, 1:-1]
+    north_ext = flows[12:, 1:-1, :]
+    elevation_next = surface(east_ext, north_ext, stretch[:, HALO:-HALO], wet_frac.T)
+    flows = jnp.swapaxes(inner(flows, 1), 1, 2)
+    return (jnp.swapaxes(elevation_next, 1, 2), flows[:12], flows[12:])
 
 
 def solution(mesh):

time: 137 us -> 137 us (level)
  local copies, waits for them, and re-layouts: 20.5 us -> 22.1 us
    transpose x0 -> x4, other arithmetic: none -> 6.59 us  [the longest x1 3.94 us: per_device(): stack = jnp.swapaxes(stack, 1, 2)]
    concatenate x2 -> x1, other arithmetic: 2.69 us -> 0.06 us  [widen_lat(): return jnp.concatenate([before, array, after], axis=dim)]
    slice x2 -> x0, other arithmetic: 2.52 us -> none  [the longest x1 1.85 us: per_device(): return (elevation_next, flows[:12], flows[12:])]
    unnamed x68 -> x62, local copies, waits for them, and re-layouts: 2.8 us -> 2.61 us
where the time goes in v12:
time: 137 us; the launch traced here: 136 us
  starting transfers between devices  40 us (29%)
  other arithmetic  27.8 us (20%)
  local copies, waits for them, and re-layouts  22.1 us (16%)
  waiting for transfers between devices  18.4 us (13%)
  between operations  14.7 us (11%)
  matrix products  13.5 us (10%)
    ppermute x1, starting transfers between devices, widen_lon(): after = lax.ppermute(initial, 'lon', down)  10 us
    ppermute x2, starting transfers between devices, widen_lat(): before = lax.ppermute(last, LAT, up)  9.61 us
    dot_general x1, matrix products, per_device(): jnp.einsum('rs,ksc->kcr', green_pad, gathered, precision=lax.Precision.HI...  9.35 us
    ppermute x2, starting transfers between devices, widen_lat(): after = lax.ppermute(initial, LAT, down)  7.52 us
    all_gather x1, waiting for transfers between devices, per_device(): gathered = lax.all_gather(packed, LAT, axis=1, tiled=True)  7.05 us
    ppermute x1, starting transfers between devices, per_device(): after = lax.ppermute(edge_sal[:, :HALO], 'lon', down)  6.9 us
    ppermute x2, waiting for transfers between devices, widen_lat(): after = lax.ppermute(initial, LAT, down)  4.91 us
    slice x2, local copies, waits for them, and re-layouts, widen_lon(): last = lax.slice_in_dim(array, length - width, length, axis=dim)  4.79 us
  transfers between devices with their start and end apart: 9, of which 4 were waited for; matrix products, arithmetic and copies ran while one was open for 30% of the time, Pallas kernels for 0%

profile of v12, /device:TPU:1, one launch (start us, length us, event | category | flops | bytes accessed | tf_op | source)
XLA Modules:
  0.0 136.4 jit_solution(5862694608291991683)
XLA Ops:
  7.2 0.8 fusion.62
  8.0 1.4 %convert_bitcast_fusion = (f32[128,96]{0,1:T(8,128)}, f32[96,128]{1,0:T(8,128)S(1)}) fusion(s32[96,128]{1,0:T(8,128)} %param.18), kind=kLoop, calls=%fused_computation.142 | loop fusion | flops 12288 | bytes 147456 | tf_op jit(solution)/shard_map/transpose | solution.py:168
  9.4 1.7 %fusion.47 = f32[12,96,128]{2,1,0:T(8,128)S(1)} fusion(f32[12,96,128]{2,1,0:T(8,128)} %param.12, f32[96,128]{1,0:T(8,128)S(1)} %get-tuple-element.61, f32[128,128]{1,0:T(8,128)} %param.19), kind=kOutput, calls=%fused_computation.101 | convolution fusion | flops 226639872 | bytes 1294336 | tf_op jit(solution)/shard_map/krj,cj->krc/dot_general | solution.py:112
  11.1 1.2 convolution_bitcast_fusion.1
  12.3 0.9 select_maximum_fusion
  13.3 4.6 %collective-permute-start.4 = (f32[3,1536]{1,0:T(4,128)S(1)}, f32[3,1536]{1,0:T(4,128)S(1)}, u32[]{:S(2)}, u32[]{:S(2)}) collective-permute-start(f32[3,1536]{1,0:T(4,128)S(1)} %get-tuple-element.40), channel_id=1, source_target_pairs={{0,1},{1,2},{2,3},{3,4},{4,5},{5,6},{6,7},{7,8},{8,9},{9,10},{10,1... | collective-permute-start | bytes 55304 | tf_op jit(solution)/shard_map/ppermute | solution.py:40
  17.9 5.6 %collective-permute-start.5 = (f32[3,1536]{1,0:T(4,128)S(1)}, f32[3,1536]{1,0:T(4,128)S(1)}, u32[]{:S(2)}, u32[]{:S(2)}) collective-permute-start(f32[3,1536]{1,0:T(4,128)S(1)} %get-tuple-element.41), channel_id=1, source_target_pairs={{1,0},{2,1},{3,2},{4,3},{5,4},{6,5},{7,6},{8,7},{9,8},{10,9},{11,1... | collective-permute-start | bytes 55304 | tf_op jit(solution)/shard_map/ppermute | solution.py:41
  23.5 1.1 subtract_dynamic-update-slice_fusion
  24.7 1.1 constant_dynamic-update-slice_fusion.1
  25.9 2.6 %fusion.59 = (f32[39,96,3]{2,1,0:T(8,128)}, f32[39,96,3]{2,1,0:T(8,128)}) fusion(f32[39,96,128]{2,1,0:T(8,128)S(1)} %bitcast_dynamic-update-slice_fusion), kind=kLoop, calls=%fused_computation.145 | loop fusion | bytes 179712 | tf_op jit(solution)/shard_map/slice | solution.py:27
  28.6 2.1 %copy.21 = f32[39,96,3]{1,0,2:T(8,128)S(1)} copy(f32[39,96,3]{2,1,0:T(8,128)} %get-tuple-element.35) | data formatting | bytes 89856 | tf_op jit(solution)/shard_map/slice | solution.py:28
  30.7 10.0 %collective-permute-start.1 = (f32[39,96,3]{1,0,2:T(8,128)S(1)}, f32[39,96,3]{1,0,2:T(8,128)S(1)}, u32[]{:S(2)}, u32[]{:S(2)}) collective-permute-start(f32[39,96,3]{1,0,2:T(8,128)S(1)} %copy.21), channel_id=1, source_target_pairs={{16,0},{32,16},{48,32},{64,48},{80,64},{96,80},{112,96},{128,112},... | collective-permute-start | bytes 134792 | tf_op jit(solution)/shard_map/ppermute | solution.py:30
  40.8 2.1 %copy.20 = f32[39,96,3]{1,0,2:T(8,128)S(1)} copy(f32[39,96,3]{2,1,0:T(8,128)} %get-tuple-element.34) | data formatting | bytes 89856 | tf_op jit(solution)/shard_map/slice | solution.py:27
  42.9 1.9 %collective-permute-start = (f32[39,96,3]{1,0,2:T(8,128)S(1)}, f32[39,96,3]{1,0,2:T(8,128)S(1)}, u32[]{:S(2)}, u32[]{:S(2)}) collective-permute-start(f32[39,96,3]{1,0,2:T(8,128)S(1)} %copy.20), channel_id=1, source_target_pairs={{0,16},{16,32},{32,48},{48,64},{64,80},{80,96},{96,112},{112,128},... | collective-permute-start | bytes 134792 | tf_op jit(solution)/shard_map/ppermute | solution.py:29
  44.9 0.1 cosine_divide_fusion
  44.9 0.7 multiply_bitcast_fusion.1
  45.6 0.7 slice_bitcast_fusion.3
  46.2 0.7 multiply_bitcast_fusion.3
  46.9 0.6 multiply_bitcast_fusion.5
  47.6 4.0 %collective-permute-done = f32[39,96,3]{1,0,2:T(8,128)S(1)} collective-permute-done((f32[39,96,3]{1,0,2:T(8,128)S(1)}, f32[39,96,3]{1,0,2:T(8,128)S(1)}, u32[]{:S(2)}, u32[]{:S(2)}) %collective-permute-start) | collective-permute-done | bytes 44960 | tf_op jit(solution)/shard_map/ppermute | solution.py:29
  51.6 1.9 %copy.22 = f32[39,96,3]{2,1,0:T(8,128)} copy(f32[39,96,3]{1,0,2:T(8,128)S(1)} %collective-permute-done) | data formatting | bytes 89856 | tf_op jit(solution)/shard_map/ppermute | solution.py:29
  53.5 1.9 %copy.23 = f32[39,96,3]{2,1,0:T(8,128)} copy(f32[39,96,3]{1,0,2:T(8,128)S(1)} %collective-permute-done.1) | data formatting | bytes 89856 | tf_op jit(solution)/shard_map/ppermute | solution.py:30
  55.4 2.2 %pad_maximum_fusion.5 = (f32[39,3,134]{2,1,0:T(4,128)}, f32[39,3,134]{2,1,0:T(4,128)}) fusion(f32[39,96,3]{2,1,0:T(8,128)} %copy.23, f32[39,96,128]{2,1,0:T(8,128)S(1)} %bitcast_dynamic-update-slice_fusion, f32[39,96,3]{2,1,0:T(8,128)} %copy.22), kind=kLoop, calls=%fused_computation.110 | loop fusion | flops 62712 | bytes 2132208 | tf_op jit(solution)/shard_map/slice | solution.py:38
  57.6 5.0 %collective-permute-start.2 = (f32[39,3,134]{2,1,0:T(4,128)}, f32[39,3,134]{2,1,0:T(4,128)S(1)}, u32[]{:S(2)}, u32[]{:S(2)}) collective-permute-start(f32[39,3,134]{2,1,0:T(4,128)} %get-tuple-element.19), channel_id=1, source_target_pairs={{0,1},{1,2},{2,3},{3,4},{4,5},{5,6},{6,7},{7,8},{8,9},{9,10},{10,1... | collective-permute-start | bytes 188144 | tf_op jit(solution)/shard_map/ppermute | solution.py:40
  62.6 1.9 %collective-permute-start.3 = (f32[39,3,134]{2,1,0:T(4,128)}, f32[39,3,134]{2,1,0:T(4,128)}, u32[]{:S(2)}, u32[]{:S(2)}) collective-permute-start(f32[39,3,134]{2,1,0:T(4,128)} %get-tuple-element.20), channel_id=1, source_target_pairs={{1,0},{2,1},{3,2},{4,3},{5,4},{6,5},{7,6},{8,7},{9,8},{10,9},{11,1... | collective-permute-start | bytes 188144 | tf_op jit(solution)/shard_map/ppermute | solution.py:41
  64.6 0.1 pad_maximum_fusion.2
  64.6 0.3 copy.25
  64.9 1.0 pad.9
  65.9 2.4 %collective-permute-done.2 = f32[39,3,134]{2,1,0:T(4,128)S(1)} collective-permute-done((f32[39,3,134]{2,1,0:T(4,128)}, f32[39,3,134]{2,1,0:T(4,128)S(1)}, u32[]{:S(2)}, u32[]{:S(2)}) %collective-permute-start.2) | collective-permute-done | bytes 62744 | tf_op jit(solution)/shard_map/ppermute | solution.py:40
  68.3 4.9 %collective-permute-done.3 = f32[39,3,134]{2,1,0:T(4,128)} collective-permute-done((f32[39,3,134]{2,1,0:T(4,128)}, f32[39,3,134]{2,1,0:T(4,128)}, u32[]{:S(2)}, u32[]{:S(2)}) %collective-permute-start.3) | collective-permute-done | bytes 62744 | tf_op jit(solution)/shard_map/ppermute | solution.py:41
  73.2 3.9 %maximum_bitcast_fusion = f32[39,134,102]{1,2,0:T(8,128)S(1)} fusion(f32[39,3,134]{2,1,0:T(4,128)} %collective-permute-done.3, f32[39,96,3]{2,1,0:T(8,128)} %copy.23, f32[39,96,128]{2,1,0:T(8,128)S(1)} %bitcast_dynamic-update-slice_fusion, f32[39,96,3]{2,1,0:T(8,128)} %copy.22, f32[39,3,134]{2,1,0:T(4,128)S(1)} %collective-permute-done.2), kind=kLoop, calls=%fused_computation | loop fusion | flops 2132208 | bytes 4264416 | tf_op jit(solution)/shard_map/transpose | solution.py:139
  77.2 0.9 slice.282
  78.1 1.2 slice.270
  79.3 0.8 slice_negate_fusion.1
  80.1 0.8 slice_add_fusion.3
  80.9 0.8 slice_add_fusion.4
  81.7 2.0 %slice_add_fusion = f32[24,132,100]{1,2,0:T(8,128)S(1)} fusion(f32[39,134,102]{1,2,0:T(8,128)S(1)} %maximum_bitcast_fusion), kind=kLoop, calls=%fused_computation.14 | loop fusion | flops 950400 | bytes 6336000 | tf_op jit(solution)/shard_map/add | solution.py:79
  83.7 7.0 %all-gather.2.cloned.1.call-done = f32[12,1664,128]{2,1,0:T(8,128)} async-done(((f32[12,104,128]{2,1,0:T(8,128)}), f32[12,1664,128]{2,1,0:T(8,128)}) %all-gather.2.cloned.1.call-update) | async-done | bytes 10223632 | tf_op jit(solution)/shard_map/all_gather | solution.py:119
  90.8 1.3 slice.276
  92.0 1.3 convolution_bitcast_fusion
  93.3 4.0 %collective-permute-start.6 = (f32[12,3,102]{2,0,1:T(8,128)S(1)}, f32[12,3,102]{2,0,1:T(8,128)S(1)}, u32[]{:S(2)}, u32[]{:S(2)}) collective-permute-start(f32[12,3,102]{2,0,1:T(8,128)S(1)} %get-tuple-element.62), channel_id=1, source_target_pairs={{0,16},{16,32},{32,48},{48,64},{64,80},{80,96},{96,112},{112,128},... | collective-permute-start | bytes 44072 | tf_op jit(solution)/shard_map/ppermute | solution.py:134
  97.3 6.9 %collective-permute-start.7 = (f32[12,3,102]{2,0,1:T(8,128)S(1)}, f32[12,3,102]{2,0,1:T(8,128)S(1)}, u32[]{:S(2)}, u32[]{:S(2)}) collective-permute-start(f32[12,3,102]{2,0,1:T(8,128)S(1)} %get-tuple-element.63), channel_id=1, source_target_pairs={{16,0},{32,16},{48,32},{64,48},{80,64},{96,80},{112,96},{128,112},... | collective-permute-start | bytes 44072 | tf_op jit(solution)/shard_map/ppermute | solution.py:135
  104.2 9.3 %fusion.64 = f32[12,128,102]{1,2,0:T(8,128)S(1)} fusion(f32[12,1664,128]{2,1,0:T(8,128)} %all-gather.2.cloned.1.call-done, f32[102,1664,1]{0,1,2:T(8,128)S(1)} %bitcast.60), kind=kOutput, calls=%fused_computation.150 | convolution fusion | flops 3128426496 | bytes 11529216 | tf_op jit(solution)/shard_map/rs,ksc->kcr/dot_general | solution.py:137
  113.6 1.1 copy.28
  114.7 1.1 copy.27
  115.9 2.3 %slice_subtract_fusion.2 = f32[12,134,102]{1,2,0:T(8,128)S(1)} fusion(f32[39,134,102]{1,2,0:T(8,128)} %copy-done, f32[12,3,102]{1,2,0:T(8,128)} %copy.28, f32[12,128,102]{1,2,0:T(8,128)S(1)} %fusion.64, f32[12,3,102]{1,2,0:T(8,128)} %copy.27), kind=kLoop, calls=%fused_computation.41 | loop fusion | flops 492048 | bytes 1968192 | tf_op jit(solution)/shard_map/sub | solution.py:140
  118.2 1.1 fusion.10
  119.4 0.8 fusion.20
  120.3 0.4 fusion.22
  120.7 0.5 copy-done.12
  121.1 0.2 maximum_multiply_fusion.1
  121.3 2.0 %fusion.2 = f32[24,130,98]{1,2,0:T(8,128)S(1)} fusion(f32[12,132,100]{1,2,0:T(8,128)S(1)} %get-tuple-element.52, f32[12,132,100]{1,2,0:T(8,128)S(1)} %get-tuple-element.51), kind=kLoop, calls=%fused_computation.9 | loop fusion | flops 2140320 | bytes 2490240 | tf_op jit(solution)/shard_map/add | solution.py:79
  123.4 0.8 fusion.6
  124.3 0.0 copy-done.10
  124.3 0.8 fusion.24
  125.1 0.4 fusion.27
  125.5 0.5 copy-done.11
  126.0 0.2 maximum_multiply_fusion.2
  126.3 0.4 fusion.12
  126.6 0.3 copy-done.27
  126.9 0.6 fusion.43
  127.5 1.1 fusion.60
  128.6 0.1 fusion.49
  128.7 0.9 fusion.45
  (69 shorter events, 0.4 us)
Async XLA Ops:
  7.2 3.9 %copy-start.1 = (f32[12,96,128]{2,1,0:T(8,128)S(1)}, f32[12,96,128]{2,1,0:T(8,128)}, u32[]{:S(2)}) copy-start(f32[12,96,128]{2,1,0:T(8,128)} %param.12) | copy-start | bytes 1769476
  7.2 83.6 %all-gather.2.cloned.1.call-start = ((), (), s32[]{:S(2)}) async-start(), calls=%async_computation | async-start | bytes 10862592 | tf_op jit(solution)/shard_map/all_gather | solution.py:119
  11.1 2.1 %copy-start.5 = (f32[96,1536]{1,0:T(8,128)S(1)}, f32[96,1536]{1,0:T(8,128)}, u32[]{:S(2)}) copy-start(f32[96,1536]{1,0:T(8,128)} %param.20) | copy-start | bytes 1769476
  13.3 51.3 %collective-permute-start.4 = (f32[3,1536]{1,0:T(4,128)S(1)}, f32[3,1536]{1,0:T(4,128)S(1)}, u32[]{:S(2)}, u32[]{:S(2)}) collective-permute-start(f32[3,1536]{1,0:T(4,128)S(1)} %get-tuple-element.40), channel_id=1, source_target_pairs={{0,1},{1,2},{2,3},{3,4},{4,5},{5,6},{6,7},{7,8},{8,9},{9,10},{10,1... | collective-permute-start | bytes 55304 | tf_op jit(solution)/shard_map/ppermute | solution.py:40
  17.9 7.9 %copy-start.6 = (f32[12,96,128]{2,1,0:T(8,128)S(1)}, f32[12,96,128]{2,1,0:T(8,128)}, u32[]{:S(2)}) copy-start(f32[12,96,128]{2,1,0:T(8,128)} %param.15) | copy-start | bytes 1769476
  17.9 46.7 %collective-permute-start.5 = (f32[3,1536]{1,0:T(4,128)S(1)}, f32[3,1536]{1,0:T(4,128)S(1)}, u32[]{:S(2)}, u32[]{:S(2)}) collective-permute-start(f32[3,1536]{1,0:T(4,128)S(1)} %get-tuple-element.41), channel_id=1, source_target_pairs={{1,0},{2,1},{3,2},{4,3},{5,4},{6,5},{7,6},{8,7},{9,8},{10,9},{11,1... | collective-permute-start | bytes 55304 | tf_op jit(solution)/shard_map/ppermute | solution.py:41
  24.6 1.2 copy-start.16
  24.6 1.3 copy-start.17
  24.7 1.3 copy-start.15
  30.7 22.8 %collective-permute-start.1 = (f32[39,96,3]{1,0,2:T(8,128)S(1)}, f32[39,96,3]{1,0,2:T(8,128)S(1)}, u32[]{:S(2)}, u32[]{:S(2)}) collective-permute-start(f32[39,96,3]{1,0,2:T(8,128)S(1)} %copy.21), channel_id=1, source_target_pairs={{16,0},{32,16},{48,32},{64,48},{80,64},{96,80},{112,96},{128,112},... | collective-permute-start | bytes 134792 | tf_op jit(solution)/shard_map/ppermute | solution.py:30
  42.9 8.7 %collective-permute-start = (f32[39,96,3]{1,0,2:T(8,128)S(1)}, f32[39,96,3]{1,0,2:T(8,128)S(1)}, u32[]{:S(2)}, u32[]{:S(2)}) collective-permute-start(f32[39,96,3]{1,0,2:T(8,128)S(1)} %copy.20), channel_id=1, source_target_pairs={{0,16},{16,32},{32,48},{48,64},{64,80},{80,96},{96,112},{112,128},... | collective-permute-start | bytes 134792 | tf_op jit(solution)/shard_map/ppermute | solution.py:29
  57.6 10.7 %collective-permute-start.2 = (f32[39,3,134]{2,1,0:T(4,128)}, f32[39,3,134]{2,1,0:T(4,128)S(1)}, u32[]{:S(2)}, u32[]{:S(2)}) collective-permute-start(f32[39,3,134]{2,1,0:T(4,128)} %get-tuple-element.19), channel_id=1, source_target_pairs={{0,1},{1,2},{2,3},{3,4},{4,5},{5,6},{6,7},{7,8},{8,9},{9,10},{10,1... | collective-permute-start | bytes 188144 | tf_op jit(solution)/shard_map/ppermute | solution.py:40
  62.6 10.6 %collective-permute-start.3 = (f32[39,3,134]{2,1,0:T(4,128)}, f32[39,3,134]{2,1,0:T(4,128)}, u32[]{:S(2)}, u32[]{:S(2)}) collective-permute-start(f32[39,3,134]{2,1,0:T(4,128)} %get-tuple-element.20), channel_id=1, source_target_pairs={{1,0},{2,1},{3,2},{4,3},{5,4},{6,5},{7,6},{8,7},{9,8},{10,9},{11,1... | collective-permute-start | bytes 188144 | tf_op jit(solution)/shard_map/ppermute | solution.py:41
  77.2 4.5 %copy-start = (f32[39,134,102]{1,2,0:T(8,128)}, f32[39,134,102]{1,2,0:T(8,128)S(1)}, u32[]{:S(2)}) copy-start(f32[39,134,102]{1,2,0:T(8,128)S(1)} %maximum_bitcast_fusion) | copy-start | bytes 6396628
  90.8 13.4 %copy-start.2 = (f32[102,16,104]{0,2,1:T(8,128)S(1)}, f32[102,16,104]{0,2,1:T(8,128)}, u32[]{:S(2)}) copy-start(f32[102,16,104]{0,2,1:T(8,128)} %pad.9) | copy-start | bytes 2036740
  93.3 21.4 %collective-permute-start.6 = (f32[12,3,102]{2,0,1:T(8,128)S(1)}, f32[12,3,102]{2,0,1:T(8,128)S(1)}, u32[]{:S(2)}, u32[]{:S(2)}) collective-permute-start(f32[12,3,102]{2,0,1:T(8,128)S(1)} %get-tuple-element.62), channel_id=1, source_target_pairs={{0,16},{16,32},{32,48},{48,64},{64,80},{80,96},{96,112},{112,128},... | collective-permute-start | bytes 44072 | tf_op jit(solution)/shard_map/ppermute | solution.py:134
  97.3 16.3 %collective-permute-start.7 = (f32[12,3,102]{2,0,1:T(8,128)S(1)}, f32[12,3,102]{2,0,1:T(8,128)S(1)}, u32[]{:S(2)}, u32[]{:S(2)}) collective-permute-start(f32[12,3,102]{2,0,1:T(8,128)S(1)} %get-tuple-element.63), channel_id=1, source_target_pairs={{16,0},{32,16},{48,32},{64,48},{80,64},{96,80},{112,96},{128,112},... | collective-permute-start | bytes 44072 | tf_op jit(solution)/shard_map/ppermute | solution.py:135
  115.9 2.3 %copy-start.8 = (f32[132,100]{0,1:T(8,128)S(1)}, f32[132,100]{0,1:T(8,128)}, u32[]{:S(2)}) copy-start(f32[132,100]{0,1:T(8,128)} %get-tuple-element.56) | copy-start | bytes 158404
  115.9 2.3 %copy-start.9 = (f32[132,100]{0,1:T(8,128)S(1)}, f32[132,100]{0,1:T(8,128)}, u32[]{:S(2)}) copy-start(f32[132,100]{0,1:T(8,128)} %get-tuple-element.57) | copy-start | bytes 158404
  115.9 2.3 %copy-start.28 = (f32[100]{0:T(128)S(1)}, f32[100]{0:T(128)}, u32[]{:S(2)}) copy-start(f32[100]{0:T(128)} %multiply_bitcast_fusion.5) | copy-start | bytes 1204
  118.1 1.2 copy-start.3
  118.2 1.2 copy-start.4
  118.2 1.2 copy-start.13
  118.2 1.2 copy-start.18
  118.2 1.2 copy-start.19
  118.2 1.2 copy-start.21
  118.2 1.2 copy-start.24
  118.2 1.2 copy-start.25
  120.2 0.9 copy-start.12
  121.3 2.1 %copy-start.7 = (f32[130,98]{0,1:T(8,128)S(1)}, f32[130,98]{0,1:T(8,128)}, u32[]{:S(2)}) copy-start(f32[130,98]{0,1:T(8,128)} %get-tuple-element.70) | copy-start | bytes 152884
  123.4 0.9 copy-start.10
  123.4 0.9 copy-start.20
  123.4 0.9 copy-start.22
  123.4 0.9 copy-start.23
  125.1 0.9 copy-start.11
  126.3 0.7 copy-start.27
  127.5 1.1 copy-start.26
  127.5 1.2 copy-start.14
Sparse Core Ops, SparseCore 0:
  13.4 77.3 all-gather.1

commit v13 on v4

--- a/solution.py
+++ b/solution.py
@@ -126,12 +126,13 @@
     blocks = lat_size()
     block = rows_here + spare
     green_blocks = green_ext.reshape(green_ext.shape[0], blocks, rows_here)
-    lanes = gathered.reshape(12, blocks, block, columns)[:, :, rows_here : rows_here + 2 * HALO, :rows_here]
-    edge_sal = jnp.einsum("rbj,kbej->kre", green_blocks, lanes, precision=lax.Precision.HIGHEST)
+    lanes = gathered.reshape(12, blocks, block, columns)[:, :, rows_here:, :]
+    green_lanes = jnp.pad(green_blocks, ((0, 0), (0, 0), (0, columns - rows_here)))
+    edge_sal = jnp.einsum("rbj,kbej->kre", green_lanes, lanes, precision=lax.Precision.HIGHEST)
     size = lax.axis_size("lon")
     up = [(i, (i + 1) % size) for i in range(size)]
     down = [(j, i) for i, j in up]
-    before = lax.ppermute(edge_sal[:, :, HALO:], "lon", up)
+    before = lax.ppermute(edge_sal[:, :, HALO : 2 * HALO], "lon", up)
     after = lax.ppermute(edge_sal[:, :, :HALO], "lon", down)
     green_pad = jnp.pad(green_blocks, ((0, 0), (0, 0), (0, spare))).reshape(green_ext.shape[0], -1)
     sal = jnp.einsum("rs,ksc->krc", green_pad, gathered, precision=lax.Precision.HIGHEST)

time: 137 us -> 137 us (level)
  waiting for transfers between devices: 18.5 us -> 13.3 us
  local copies, waits for them, and re-layouts: 20.5 us -> 24.5 us
  matrix products: 13.5 us -> 16.2 us
    reshape x0 -> x3, local copies, waits for them, and re-layouts: none -> 3.86 us  [the longest x1 2.42 us: per_device(): jnp.pad(green_blocks, ((0, 0), (0, 0), (0, spare)))]
    ppermute x2, waiting for transfers between devices: 4.93 us -> 2.39 us  [widen_lat(): after = lax.ppermute(initial, LAT, down)]
    ppermute x2, waiting for transfers between devices: 2.4 us -> 0.01 us  [widen_lat(): before = lax.ppermute(last, LAT, up)]
    unnamed x68 -> x72, local copies, waits for them, and re-layouts: 2.8 us -> 4.44 us
  transfers between devices with their start and end apart: 9 -> 9, of which waited for: 4 -> 3; matrix products, arithmetic and copies ran while one was open for 30% -> 33% of each run, Pallas kernels for 0% -> 0%
where the time goes in v13:
time: 137 us; the launch traced here: 136 us
  starting transfers between devices  39.6 us (29%)
  other arithmetic  28.2 us (21%)
  local copies, waits for them, and re-layouts  24.5 us (18%)
  matrix products  16.2 us (12%)
  between operations  14.6 us (11%)
  waiting for transfers between devices  13.3 us (10%)
    dot_general x1, matrix products, per_device(): jnp.einsum('rs,ksc->krc', green_pad, gathered, precision=lax.Precision.HI...  10.1 us
    ppermute x1, starting transfers between devices, widen_lon(): after = lax.ppermute(initial, 'lon', down)  10 us
    ppermute x2, starting transfers between devices, widen_lat(): before = lax.ppermute(last, LAT, up)  9.56 us
    ppermute x2, starting transfers between devices, widen_lat(): after = lax.ppermute(initial, LAT, down)  7.54 us
    ppermute x1, starting transfers between devices, per_device(): after = lax.ppermute(edge_sal[:, :, :HALO], 'lon', down)  6.9 us
    all_gather x1, waiting for transfers between devices, per_device(): gathered = lax.all_gather(packed, LAT, axis=1, tiled=True)  6.69 us
    slice x2, local copies, waits for them, and re-layouts, widen_lon(): last = lax.slice_in_dim(array, length - width, length, axis=dim)  4.81 us
    unnamed x72, local copies, waits for them, and re-layouts  4.44 us
  transfers between devices with their start and end apart: 9, of which 3 were waited for; matrix products, arithmetic and copies ran while one was open for 33% of the time, Pallas kernels for 0%

profile of v13, /device:TPU:1, one launch (start us, length us, event | category | flops | bytes accessed | tf_op | source)
XLA Modules:
  0.0 136.3 jit_solution(11988137792167829539)
XLA Ops:
  7.2 0.7 fusion.63
  7.9 0.8 convert_element_type.12
  8.7 1.8 %fusion.47 = f32[12,96,128]{2,1,0:T(8,128)S(1)} fusion(f32[12,96,128]{2,1,0:T(8,128)} %param.12, f32[96,128]{1,0:T(8,128)S(1)} %convert_element_type.12, f32[128,128]{1,0:T(8,128)} %param.19), kind=kOutput, calls=%fused_computation.101 | convolution fusion | flops 226639872 | bytes 1294336 | tf_op jit(solution)/shard_map/krj,cj->krc/dot_general | solution.py:112
  10.6 2.2 %convolution_bitcast_fusion.2 = f32[12,6,96]{2,1,0:T(8,128)S(1)} fusion(f32[12,96,128]{2,1,0:T(8,128)} %param.12, f32[96,128]{1,0:T(8,128)S(1)} %convert_element_type.12, f32[3,128]{1,0:T(4,128)S(1)} %get-tuple-element.60, f32[3,128]{1,0:T(4,128)S(1)} %get-tuple-element.59), kind=kOutput, calls=%fused_computation.48 | convolution fusion | flops 10765056 | bytes 669696 | tf_op jit(solution)/shard_map/ej,krj->ker/dot_general | solution.py:115
  12.8 0.9 select_maximum_fusion
  13.7 0.8 fusion.62
  14.6 4.6 %collective-permute-start.4 = (f32[3,1536]{1,0:T(4,128)S(1)}, f32[3,1536]{1,0:T(4,128)S(1)}, u32[]{:S(2)}, u32[]{:S(2)}) collective-permute-start(f32[3,1536]{1,0:T(4,128)S(1)} %get-tuple-element.41), channel_id=1, source_target_pairs={{0,1},{1,2},{2,3},{3,4},{4,5},{5,6},{6,7},{7,8},{8,9},{9,10},{10,1... | collective-permute-start | bytes 55304 | tf_op jit(solution)/shard_map/ppermute | solution.py:40
  19.2 5.6 %collective-permute-start.5 = (f32[3,1536]{1,0:T(4,128)S(1)}, f32[3,1536]{1,0:T(4,128)}, u32[]{:S(2)}, u32[]{:S(2)}) collective-permute-start(f32[3,1536]{1,0:T(4,128)S(1)} %get-tuple-element.42), channel_id=1, source_target_pairs={{1,0},{2,1},{3,2},{4,3},{5,4},{6,5},{7,6},{8,7},{9,8},{10,9},{11,1... | collective-permute-start | bytes 55304 | tf_op jit(solution)/shard_map/ppermute | solution.py:41
  24.8 0.1 subtract_dynamic-update-slice_fusion
  24.9 1.1 constant_dynamic-update-slice_fusion.1
  26.0 1.1 constant_dynamic-update-slice_fusion
  27.2 2.6 %fusion.60 = (f32[39,96,3]{2,1,0:T(8,128)}, f32[39,96,3]{2,1,0:T(8,128)}) fusion(f32[39,96,128]{2,1,0:T(8,128)S(1)} %bitcast_dynamic-update-slice_fusion), kind=kLoop, calls=%fused_computation.143 | loop fusion | bytes 179712 | tf_op jit(solution)/shard_map/slice | solution.py:27
  29.8 2.1 %copy.21 = f32[39,96,3]{1,0,2:T(8,128)S(1)} copy(f32[39,96,3]{2,1,0:T(8,128)} %get-tuple-element.35) | data formatting | bytes 89856 | tf_op jit(solution)/shard_map/slice | solution.py:28
  32.0 10.0 %collective-permute-start.1 = (f32[39,96,3]{1,0,2:T(8,128)S(1)}, f32[39,96,3]{1,0,2:T(8,128)S(1)}, u32[]{:S(2)}, u32[]{:S(2)}) collective-permute-start(f32[39,96,3]{1,0,2:T(8,128)S(1)} %copy.21), channel_id=1, source_target_pairs={{16,0},{32,16},{48,32},{64,48},{80,64},{96,80},{112,96},{128,112},... | collective-permute-start | bytes 134792 | tf_op jit(solution)/shard_map/ppermute | solution.py:30
  42.0 2.2 %copy.20 = f32[39,96,3]{1,0,2:T(8,128)S(1)} copy(f32[39,96,3]{2,1,0:T(8,128)} %get-tuple-element.34) | data formatting | bytes 89856 | tf_op jit(solution)/shard_map/slice | solution.py:27
  44.2 1.9 %collective-permute-start = (f32[39,96,3]{1,0,2:T(8,128)S(1)}, f32[39,96,3]{1,0,2:T(8,128)S(1)}, u32[]{:S(2)}, u32[]{:S(2)}) collective-permute-start(f32[39,96,3]{1,0,2:T(8,128)S(1)} %copy.20), channel_id=1, source_target_pairs={{0,16},{16,32},{32,48},{48,64},{64,80},{80,96},{96,112},{112,128},... | collective-permute-start | bytes 134792 | tf_op jit(solution)/shard_map/ppermute | solution.py:29
  46.2 0.6 slice_multiply_fusion.7
  46.8 0.6 fusion.65
  47.4 0.7 broadcast_multiply_fusion.4
  48.1 0.6 slice_multiply_fusion.8
  48.7 4.2 %collective-permute-done = f32[39,96,3]{1,0,2:T(8,128)S(1)} collective-permute-done((f32[39,96,3]{1,0,2:T(8,128)S(1)}, f32[39,96,3]{1,0,2:T(8,128)S(1)}, u32[]{:S(2)}, u32[]{:S(2)}) %collective-permute-start) | collective-permute-done | bytes 44960 | tf_op jit(solution)/shard_map/ppermute | solution.py:29
  52.9 1.9 %copy.22 = f32[39,96,3]{2,1,0:T(8,128)} copy(f32[39,96,3]{1,0,2:T(8,128)S(1)} %collective-permute-done) | data formatting | bytes 89856 | tf_op jit(solution)/shard_map/ppermute | solution.py:29
  54.7 1.9 %copy.23 = f32[39,96,3]{2,1,0:T(8,128)} copy(f32[39,96,3]{1,0,2:T(8,128)S(1)} %collective-permute-done.1) | data formatting | bytes 89856 | tf_op jit(solution)/shard_map/ppermute | solution.py:30
  56.7 2.2 %pad_maximum_fusion.5 = (f32[39,3,134]{2,1,0:T(4,128)}, f32[39,3,134]{2,1,0:T(4,128)}) fusion(f32[39,96,3]{2,1,0:T(8,128)} %copy.23, f32[39,96,128]{2,1,0:T(8,128)S(1)} %bitcast_dynamic-update-slice_fusion, f32[39,96,3]{2,1,0:T(8,128)} %copy.22), kind=kLoop, calls=%fused_computation.110 | loop fusion | flops 62712 | bytes 2132208 | tf_op jit(solution)/shard_map/slice | solution.py:38
  58.9 5.0 %collective-permute-start.2 = (f32[39,3,134]{2,1,0:T(4,128)}, f32[39,3,134]{2,1,0:T(4,128)S(1)}, u32[]{:S(2)}, u32[]{:S(2)}) collective-permute-start(f32[39,3,134]{2,1,0:T(4,128)} %get-tuple-element.22), channel_id=1, source_target_pairs={{0,1},{1,2},{2,3},{3,4},{4,5},{5,6},{6,7},{7,8},{8,9},{9,10},{10,1... | collective-permute-start | bytes 188144 | tf_op jit(solution)/shard_map/ppermute | solution.py:40
  63.9 1.9 %collective-permute-start.3 = (f32[39,3,134]{2,1,0:T(4,128)}, f32[39,3,134]{2,1,0:T(4,128)}, u32[]{:S(2)}, u32[]{:S(2)}) collective-permute-start(f32[39,3,134]{2,1,0:T(4,128)} %get-tuple-element.23), channel_id=1, source_target_pairs={{1,0},{2,1},{3,2},{4,3},{5,4},{6,5},{7,6},{8,7},{9,8},{10,9},{11,1... | collective-permute-start | bytes 188144 | tf_op jit(solution)/shard_map/ppermute | solution.py:41
  65.8 0.6 copy-done.23
  66.4 0.8 pad_maximum_fusion.2
  67.3 0.3 reshape.58
  67.5 1.2 copy.24
  68.7 1.0 pad.14
  69.7 2.4 %reshape.64 = f32[102,1664,1]{1,0,2:T(8,128)} reshape(f32[102,16,104]{2,1,0:T(8,128)} %pad.14) | data formatting | bytes 1357824 | tf_op jit(solution)/shard_map/reshape | solution.py:137
  72.1 2.4 %collective-permute-done.3 = f32[39,3,134]{2,1,0:T(4,128)} collective-permute-done((f32[39,3,134]{2,1,0:T(4,128)}, f32[39,3,134]{2,1,0:T(4,128)}, u32[]{:S(2)}, u32[]{:S(2)}) %collective-permute-start.3) | collective-permute-done | bytes 62744 | tf_op jit(solution)/shard_map/ppermute | solution.py:41
  74.5 1.1 maximum_bitcast_fusion.2
  75.6 0.7 slice.284
  76.4 0.7 slice.274
  77.1 2.6 %pad_maximum_fusion = f32[39,102,134]{2,1,0:T(8,128)S(1)} fusion(f32[39,3,134]{2,1,0:T(4,128)} %collective-permute-done.3, f32[39,96,3]{2,1,0:T(8,128)S(1)} %copy-done.2, f32[39,96,128]{2,1,0:T(8,128)S(1)} %bitcast_dynamic-update-slice_fusion, f32[39,96,3]{2,1,0:T(8,128)S(1)} %copy-done.1, f32[39,3,134]{2,1,0:T(4,128)S(1)} %collective-permute-done.2), kind=kLoop, calls=%fused_computation | loop fusion | flops 2132208 | bytes 4264416 | tf_op jit(solution)/shard_map/concatenate | solution.py:42
  79.7 0.9 slice_negate_fusion.1
  80.6 1.3 slice_add_fusion.3
  82.0 0.8 slice_add_fusion.4
  82.8 2.1 %slice_add_fusion = f32[24,100,132]{2,1,0:T(8,128)S(1)} fusion(f32[39,102,134]{2,1,0:T(8,128)S(1)} %pad_maximum_fusion), kind=kLoop, calls=%fused_computation.14 | loop fusion | flops 950400 | bytes 6336000 | tf_op jit(solution)/shard_map/add | solution.py:79
  84.9 6.7 %all-gather.2.cloned.1.call-done = f32[12,1664,128]{2,1,0:T(8,128)} async-done(((f32[12,104,128]{2,1,0:T(8,128)}), f32[12,1664,128]{2,1,0:T(8,128)}) %all-gather.2.cloned.1.call-update) | async-done | bytes 10223632 | tf_op jit(solution)/shard_map/all_gather | solution.py:119
  91.6 2.0 %convolution_bitcast_fusion.1 = f32[12,102,8]{1,2,0:T(8,128)S(1)} fusion(f32[102,16,96]{2,0,1:T(8,128)S(1)} %copy-done.4, f32[12,16,104,128]{3,2,1,0:T(8,128)} %bitcast.33), kind=kOutput, calls=%fused_computation.47 | convolution fusion | flops 240648192 | bytes 1452288 | tf_op jit(solution)/shard_map/rbj,kbej->kre/dot_general | solution.py:131
  93.6 3.7 %collective-permute-start.6 = (f32[12,102,3]{1,2,0:T(4,128)S(1)}, f32[12,102,3]{1,2,0:T(4,128)S(1)}, u32[]{:S(2)}, u32[]{:S(2)}) collective-permute-start(f32[12,102,3]{1,2,0:T(4,128)S(1)} %get-tuple-element.61), channel_id=1, source_target_pairs={{0,16},{16,32},{32,48},{48,64},{64,80},{80,96},{96,112},{112,128},... | collective-permute-start | bytes 44072 | tf_op jit(solution)/shard_map/ppermute | solution.py:135
  97.3 6.9 %collective-permute-start.7 = (f32[12,102,3]{1,2,0:T(4,128)S(1)}, f32[12,102,3]{1,2,0:T(4,128)S(1)}, u32[]{:S(2)}, u32[]{:S(2)}) collective-permute-start(f32[12,102,3]{1,2,0:T(4,128)S(1)} %get-tuple-element.62), channel_id=1, source_target_pairs={{16,0},{32,16},{48,32},{64,48},{80,64},{96,80},{112,96},{128,112},... | collective-permute-start | bytes 44072 | tf_op jit(solution)/shard_map/ppermute | solution.py:136
  104.2 10.1 %convolution_bitcast_fusion = f32[12,102,128]{2,1,0:T(8,128)} fusion(f32[12,1664,128]{2,1,0:T(8,128)} %all-gather.2.cloned.1.call-done, f32[102,1664,1]{1,0,2:T(8,128)S(1)} %copy-done.5), kind=kOutput, calls=%fused_computation.46 | convolution fusion | flops 3128426496 | bytes 11529216 | tf_op jit(solution)/shard_map/rs,ksc->krc/dot_general | solution.py:138
  114.3 0.3 copy.26
  114.6 1.1 copy.25
  115.8 2.3 %slice_subtract_fusion.2 = f32[12,102,134]{2,1,0:T(8,128)S(1)} fusion(f32[39,102,134]{2,1,0:T(8,128)} %copy-done, f32[12,102,3]{2,1,0:T(8,128)S(1)} %copy.26, f32[12,102,128]{2,1,0:T(8,128)} %convolution_bitcast_fusion, f32[12,102,3]{2,1,0:T(8,128)} %copy.25), kind=kLoop, calls=%fused_computation.41 | loop fusion | flops 492048 | bytes 1968192 | tf_op jit(solution)/shard_map/sub | solution.py:140
  118.2 1.1 fusion.10
  119.3 0.8 fusion.21
  120.2 0.4 fusion.23
  120.6 0.5 copy-done.18
  121.1 0.2 maximum_multiply_fusion.1
  121.3 2.1 %fusion.2 = f32[24,98,130]{2,1,0:T(8,128)S(1)} fusion(f32[12,100,132]{2,1,0:T(8,128)S(1)} %get-tuple-element.53, f32[12,100,132]{2,1,0:T(8,128)S(1)} %get-tuple-element.52), kind=kLoop, calls=%fused_computation.9 | loop fusion | flops 2140320 | bytes 2490240 | tf_op jit(solution)/shard_map/add | solution.py:79
  123.4 0.8 fusion.6
  124.3 0.8 fusion.25
  125.1 0.4 fusion.28
  125.5 0.5 copy-done.17
  126.0 0.2 maximum_multiply_fusion.2
  126.2 0.4 copy-done.32
  126.6 1.8 %fusion.61 = (f32[12,96,128]{2,1,0:T(8,128)}, f32[12,96,128]{2,1,0:T(8,128)S(1)}, f32[12,96,128]{2,1,0:T(8,128)}) fusion(f32[12,98,130]{2,1,0:T(8,128)S(1)} %get-tuple-element.48, f32[96]{0:T(128)S(1)} %copy-done.32, f32[12,98,130]{2,1,0:T(8,128)S(1)} %get-tuple-element.47), kind=kLoop, calls=%fused_computation.144 | loop fusion | flops 737280 | bytes 5308800 | tf_op jit(solution)/shard_map/slice | solution.py:169
  128.5 0.1 fusion.49
  128.6 0.9 maximum_multiply_fusion.4
  (78 shorter events, 0.4 us)
Async XLA Ops:
  7.2 84.4 %all-gather.2.cloned.1.call-start = ((), (), s32[]{:S(2)}) async-start(), calls=%async_computation | async-start | bytes 10862592 | tf_op jit(solution)/shard_map/all_gather | solution.py:119
  8.7 1.8 %copy-start.9 = (f32[96,128]{1,0:T(8,128)}, f32[96,128]{1,0:T(8,128)S(1)}, u32[]{:S(2)}) copy-start(f32[96,128]{1,0:T(8,128)S(1)} %convert_element_type.12) | copy-start | bytes 147460
  8.7 16.1 %copy-start.3 = (f32[12,96,128]{2,1,0:T(8,128)S(1)}, f32[12,96,128]{2,1,0:T(8,128)}, u32[]{:S(2)}) copy-start(f32[12,96,128]{2,1,0:T(8,128)} %param.12) | copy-start | bytes 1769476
  8.7 16.1 %copy-start.12 = (f32[12,96,128]{2,1,0:T(8,128)S(1)}, f32[12,96,128]{2,1,0:T(8,128)}, u32[]{:S(2)}) copy-start(f32[12,96,128]{2,1,0:T(8,128)} %param.13) | copy-start | bytes 1769476
  14.6 51.3 %collective-permute-start.4 = (f32[3,1536]{1,0:T(4,128)S(1)}, f32[3,1536]{1,0:T(4,128)S(1)}, u32[]{:S(2)}, u32[]{:S(2)}) collective-permute-start(f32[3,1536]{1,0:T(4,128)S(1)} %get-tuple-element.41), channel_id=1, source_target_pairs={{0,1},{1,2},{2,3},{3,4},{4,5},{5,6},{6,7},{7,8},{8,9},{9,10},{10,1... | collective-permute-start | bytes 55304 | tf_op jit(solution)/shard_map/ppermute | solution.py:40
  19.2 8.0 %copy-start.21 = (f32[96,128]{1,0:T(8,128)S(1)}, f32[96,128]{1,0:T(8,128)}, u32[]{:S(2)}) copy-start(f32[96,128]{1,0:T(8,128)} %param.16) | copy-start | bytes 147460
  19.2 8.0 %copy-start.22 = (f32[96,128]{1,0:T(8,128)S(1)}, f32[96,128]{1,0:T(8,128)}, u32[]{:S(2)}) copy-start(f32[96,128]{1,0:T(8,128)} %param.17) | copy-start | bytes 147460
  19.2 8.0 %copy-start.20 = (s32[96,128]{1,0:T(8,128)S(1)}, s32[96,128]{1,0:T(8,128)}, u32[]{:S(2)}) copy-start(s32[96,128]{1,0:T(8,128)} %param.18) | copy-start | bytes 147460
  19.2 47.2 %collective-permute-start.5 = (f32[3,1536]{1,0:T(4,128)S(1)}, f32[3,1536]{1,0:T(4,128)}, u32[]{:S(2)}, u32[]{:S(2)}) collective-permute-start(f32[3,1536]{1,0:T(4,128)S(1)} %get-tuple-element.42), channel_id=1, source_target_pairs={{1,0},{2,1},{3,2},{4,3},{5,4},{6,5},{7,6},{8,7},{9,8},{10,9},{11,1... | collective-permute-start | bytes 55304 | tf_op jit(solution)/shard_map/ppermute | solution.py:41
  32.0 22.8 %collective-permute-start.1 = (f32[39,96,3]{1,0,2:T(8,128)S(1)}, f32[39,96,3]{1,0,2:T(8,128)S(1)}, u32[]{:S(2)}, u32[]{:S(2)}) collective-permute-start(f32[39,96,3]{1,0,2:T(8,128)S(1)} %copy.21), channel_id=1, source_target_pairs={{16,0},{32,16},{48,32},{64,48},{80,64},{96,80},{112,96},{128,112},... | collective-permute-start | bytes 134792 | tf_op jit(solution)/shard_map/ppermute | solution.py:30
  44.2 8.7 %collective-permute-start = (f32[39,96,3]{1,0,2:T(8,128)S(1)}, f32[39,96,3]{1,0,2:T(8,128)S(1)}, u32[]{:S(2)}, u32[]{:S(2)}) collective-permute-start(f32[39,96,3]{1,0,2:T(8,128)S(1)} %copy.20), channel_id=1, source_target_pairs={{0,16},{16,32},{32,48},{48,64},{64,80},{80,96},{96,112},{112,128},... | collective-permute-start | bytes 134792 | tf_op jit(solution)/shard_map/ppermute | solution.py:29
  56.7 9.8 %copy-start.11 = (f32[96,1536]{1,0:T(8,128)S(1)}, f32[96,1536]{1,0:T(8,128)}, u32[]{:S(2)}) copy-start(f32[96,1536]{1,0:T(8,128)} %param.20) | copy-start | bytes 1769476
  58.9 13.2 %collective-permute-start.2 = (f32[39,3,134]{2,1,0:T(4,128)}, f32[39,3,134]{2,1,0:T(4,128)S(1)}, u32[]{:S(2)}, u32[]{:S(2)}) collective-permute-start(f32[39,3,134]{2,1,0:T(4,128)} %get-tuple-element.22), channel_id=1, source_target_pairs={{0,1},{1,2},{2,3},{3,4},{4,5},{5,6},{6,7},{7,8},{8,9},{9,10},{10,1... | collective-permute-start | bytes 188144 | tf_op jit(solution)/shard_map/ppermute | solution.py:40
  63.9 10.6 %collective-permute-start.3 = (f32[39,3,134]{2,1,0:T(4,128)}, f32[39,3,134]{2,1,0:T(4,128)}, u32[]{:S(2)}, u32[]{:S(2)}) collective-permute-start(f32[39,3,134]{2,1,0:T(4,128)} %get-tuple-element.23), channel_id=1, source_target_pairs={{1,0},{2,1},{3,2},{4,3},{5,4},{6,5},{7,6},{8,7},{9,8},{10,9},{11,1... | collective-permute-start | bytes 188144 | tf_op jit(solution)/shard_map/ppermute | solution.py:41
  65.8 0.6 copy-start.23
  72.1 5.0 %copy-start.1 = (f32[39,96,3]{2,1,0:T(8,128)S(1)}, f32[39,96,3]{2,1,0:T(8,128)}, u32[]{:S(2)}) copy-start(f32[39,96,3]{2,1,0:T(8,128)} %copy.22) | copy-start | bytes 134788
  72.1 5.0 %copy-start.2 = (f32[39,96,3]{2,1,0:T(8,128)S(1)}, f32[39,96,3]{2,1,0:T(8,128)}, u32[]{:S(2)}) copy-start(f32[39,96,3]{2,1,0:T(8,128)} %copy.23) | copy-start | bytes 134788
  79.7 3.1 %copy-start = (f32[39,102,134]{2,1,0:T(8,128)}, f32[39,102,134]{2,1,0:T(8,128)S(1)}, u32[]{:S(2)}) copy-start(f32[39,102,134]{2,1,0:T(8,128)S(1)} %pad_maximum_fusion) | copy-start | bytes 6396628
  82.8 8.8 %copy-start.4 = (f32[102,16,96]{2,0,1:T(8,128)S(1)}, f32[102,16,96]{2,0,1:T(8,128)}, u32[]{:S(2)}) copy-start(f32[102,16,96]{2,0,1:T(8,128)} %copy.24) | copy-start | bytes 1880068
  91.6 12.6 %copy-start.5 = (f32[102,1664,1]{1,0,2:T(8,128)S(1)}, f32[102,1664,1]{1,0,2:T(8,128)}, u32[]{:S(2)}) copy-start(f32[102,1664,1]{1,0,2:T(8,128)} %reshape.64) | copy-start | bytes 2036740
  93.6 21.0 %collective-permute-start.6 = (f32[12,102,3]{1,2,0:T(4,128)S(1)}, f32[12,102,3]{1,2,0:T(4,128)S(1)}, u32[]{:S(2)}, u32[]{:S(2)}) collective-permute-start(f32[12,102,3]{1,2,0:T(4,128)S(1)} %get-tuple-element.61), channel_id=1, source_target_pairs={{0,16},{16,32},{32,48},{48,64},{64,80},{80,96},{96,112},{112,128},... | collective-permute-start | bytes 44072 | tf_op jit(solution)/shard_map/ppermute | solution.py:135
  97.3 17.0 %collective-permute-start.7 = (f32[12,102,3]{1,2,0:T(4,128)S(1)}, f32[12,102,3]{1,2,0:T(4,128)S(1)}, u32[]{:S(2)}, u32[]{:S(2)}) collective-permute-start(f32[12,102,3]{1,2,0:T(4,128)S(1)} %get-tuple-element.62), channel_id=1, source_target_pairs={{16,0},{32,16},{48,32},{64,48},{80,64},{96,80},{112,96},{128,112},... | collective-permute-start | bytes 44072 | tf_op jit(solution)/shard_map/ppermute | solution.py:136
  115.8 2.3 %copy-start.14 = (f32[100,132]{1,0:T(8,128)S(1)}, f32[100,132]{1,0:T(8,128)}, u32[]{:S(2)}) copy-start(f32[100,132]{1,0:T(8,128)} %get-tuple-element.57) | copy-start | bytes 158404
  115.8 2.3 %copy-start.15 = (f32[100,132]{1,0:T(8,128)S(1)}, f32[100,132]{1,0:T(8,128)}, u32[]{:S(2)}) copy-start(f32[100,132]{1,0:T(8,128)} %get-tuple-element.58) | copy-start | bytes 158404
  115.8 2.3 %copy-start.33 = (f32[100]{0:T(128)S(1)}, f32[100]{0:T(128)}, u32[]{:S(2)}) copy-start(f32[100]{0:T(128)} %slice_multiply_fusion.8) | copy-start | bytes 1204
  118.1 1.2 copy-start.7
  118.1 1.2 copy-start.8
  118.1 1.2 copy-start.19
  118.1 1.2 copy-start.24
  118.1 1.2 copy-start.25
  118.1 1.2 copy-start.26
  118.1 1.2 copy-start.29
  118.1 1.2 copy-start.30
  120.2 0.9 copy-start.18
  121.3 2.1 %copy-start.13 = (f32[98,130]{1,0:T(8,128)S(1)}, f32[98,130]{1,0:T(8,128)}, u32[]{:S(2)}) copy-start(f32[98,130]{1,0:T(8,128)} %get-tuple-element.69) | copy-start | bytes 152884
  123.3 0.9 copy-start.6
  123.3 0.9 copy-start.16
  123.4 0.9 copy-start.27
  123.4 0.9 copy-start.28
  125.1 0.9 copy-start.17
  126.0 0.6 copy-start.32
  126.6 1.9 %copy-start.31 = (f32[6]{0:T(128)S(1)}, f32[6]{0:T(128)}, u32[]{:S(2)}) copy-start(f32[6]{0:T(128)} %constant.50) | copy-start | bytes 76
  126.6 2.0 %copy-start.10 = (f32[96,128]{1,0:T(8,128)S(1)}, f32[96,128]{1,0:T(8,128)}, u32[]{:S(2)}) copy-start(f32[96,128]{1,0:T(8,128)} %copy-done.9) | copy-start | bytes 147460
Sparse Core Ops, SparseCore 0:
  13.8 77.6 all-gather.1
